TPU v7x, 256 devices: a whole 4x4x8 slice. The times are simulated.
256 devices in a mesh: dp: 4 (over x), ctx: 16 (over z, core), mp: 4 (over y).
Axes of the slice: x: 4, y: 4, z: 8, core: 2. Of those that a mesh axis runs over, the one named last changes fastest.
Arguments:
- queries: bfloat16 [65536, 2048], P(('dp', 'ctx'), 'mp'), parts along dimension 0, may hold values from -6 to 6
- keys: bfloat16 [65536, 2048], P(('dp', 'ctx'), 'mp'), parts along dimension 0, may hold values from -6 to 6
- values: bfloat16 [65536, 2048], P(('dp', 'ctx'), 'mp'), parts along dimension 0, may hold values from -6 to 6
- segment_ids: int32 [65536], P(('dp', 'ctx')), parts along dimension 0, may hold values from 0 to 5, never falling along the last dimension, each value on 1 to 8192 neighbouring positions
- norm_gain: float32 [2048], P('mp'), may hold values from 0.5 to 1.5
- out_weight: bfloat16 [2048, 4096], P(None, 'mp'), may hold values from -0.125 to 0.125
Outputs:
- projected: bfloat16 [65536, 4096], P(('dp', 'ctx'), 'mp'), parts along dimension 0
There are 4 independent parts, one for each index of `dp`. A program takes and returns all parts, laid end to end along the dimension named above; an argument that names none is the same for every part. Nothing has to cross between parts.
Inputs may be any that keep to these rules, and one draw needn't show every extreme that they name: `segment_ids`: ids never fall along the stream; 6 segments, each of 1 to 8192 consecutive positions, one of exactly 8192.
All inputs are finite; a program needn't handle non-finite values.
Results may differ from a plain program's by a relative error of at most 0.0053.
Values may be sent and summed in bfloat16 or wider, within the bound.
No kernel may reach another device: no remote copies, remote signals or barrier semaphores. Data moves between devices by JAX's collectives and lax.ppermute only.
A program may use at most 64 MiB of HBM per device.

v0:
```python
import jax
import jax.numpy as jnp
from jax import lax
from jax.sharding import PartitionSpec as P

HEAD = 128


def carried_in(value, axis, join, neutral):
    count, mine = (lax.axis_size(axis), lax.axis_index(axis))
    pieces = jax.tree.map(lambda part: lax.all_gather(part, axis), value)
    so_far = jax.tree.map(
        lambda part, zero: jnp.full_like(part, 0) + jnp.asarray(zero, part.dtype), value, neutral
    )

    def step(position, so_far):
        longer = join(so_far, jax.tree.map(lambda part: part[position], pieces))
        return jax.tree.map(lambda new, old: jnp.where(position < mine, new, old), longer, so_far)

    return lax.fori_loop(0, count - 1, step, so_far)


def features(raw_input):
    return (jax.nn.elu(raw_input.astype(jnp.float32)) + 1.0).astype(jnp.bfloat16)


def join_states(earlier, later):
    early_sum, early_seg = earlier
    later_sum, later_seg = later
    is_blank = later_seg < 0
    linked = early_seg == later_seg
    joined = later_sum + jnp.where(linked, early_sum, 0.0)
    return (jnp.where(is_blank, early_sum, joined), jnp.where(is_blank, early_seg, later_seg))


def per_device(queries, keys, values, segment_ids, norm_gain, out_weight):
    rows_here = queries.shape[0]
    width_here = queries.shape[1]
    heads_here = width_here // HEAD
    feat_query = features(queries).reshape(rows_here, heads_here, HEAD)
    feat_key = features(keys).reshape(rows_here, heads_here, HEAD)
    value_heads = values.reshape(rows_here, heads_here, HEAD)
    final_seg = segment_ids[rows_here - 1]
    in_final = (segment_ids == final_seg).astype(jnp.bfloat16)
    local_sum = jnp.einsum(
        "thd,the->hde",
        feat_key * in_final[:, None, None],
        value_heads,
        preferred_element_type=jnp.float32,
    )
    blank_sum = jnp.zeros_like(local_sum)
    before_sum, before_seg = carried_in(
        (local_sum, final_seg), "ctx", join_states, (blank_sum, jnp.int32(-1))
    )
    position = jnp.arange(rows_here)
    allowed = (position[None, :] <= position[:, None]) & (
        segment_ids[:, None] == segment_ids[None, :]
    )
    scores = jnp.einsum("thd,shd->hts", feat_query, feat_key, preferred_element_type=jnp.float32)
    weights = jnp.where(allowed[None], scores, 0.0).astype(jnp.bfloat16)
    inside = jnp.einsum("hts,she->the", weights, value_heads, preferred_element_type=jnp.float32)
    state_hi = before_sum.astype(jnp.bfloat16)
    state_lo = (before_sum - state_hi.astype(jnp.float32)).astype(jnp.bfloat16)
    carried = jnp.einsum(
        "thd,hde->the", feat_query, state_hi, preferred_element_type=jnp.float32
    ) + jnp.einsum("thd,hde->the", feat_query, state_lo, preferred_element_type=jnp.float32)
    carry_on = (segment_ids == before_seg).astype(jnp.float32)
    numerator = inside + carry_on[:, None, None] * carried
    normed = numerator * lax.rsqrt(jnp.mean(numerator * numerator, axis=-1, keepdims=True) + 1e-06)
    gain_heads = norm_gain.reshape(heads_here, HEAD)
    hidden = (normed * gain_heads[None]).astype(jnp.bfloat16).reshape(rows_here, width_here)
    projected = jnp.dot(
        lax.all_gather(hidden, "mp", axis=1, tiled=True),
        out_weight,
        preferred_element_type=jnp.float32,
    )
    return projected.astype(jnp.bfloat16)


def solution(mesh):
    in_specs = (
        P(("dp", "ctx"), "mp"),
        P(("dp", "ctx"), "mp"),
        P(("dp", "ctx"), "mp"),
        P(("dp", "ctx")),
        P("mp"),
        P(None, "mp"),
    )
    out_specs = P(("dp", "ctx"), "mp")
    return jax.shard_map(
        per_device, mesh=mesh, in_specs=in_specs, out_specs=out_specs, check_vma=False
    )
```

profile of v0, /device:TPU:1, one launch (start us, length us, event | category | flops | bytes accessed | tf_op | source)
XLA Modules:
  0.0 187.0 jit_solution(12356877060179263741)
XLA Ops:
  6.5 1.3 dynamic-slice
  7.9 2.0 %fusion.28 = (s32[1]{0:T(128)}, s32[16]{0:T(128)S(1)}) fusion(s32[1024]{0:T(1024)} %param.11, s32[16]{0:T(128)S(1)} %broadcast.45, u32[]{:T(128)} %bitcast.2), kind=kLoop, calls=%fused_computation.43 | loop fusion | bytes 76 | tf_op jit(solution)/shard_map/slice | solution.py:43
  9.9 1.4 compare_convert_fusion.1
  11.2 2.2 %fusion.6 = bf16[1024,512]{1,0:T(8,128)(2,1)S(1)} fusion(bf16[1024,512]{1,0:T(8,128)(2,1)} %param.9), kind=kLoop, calls=%fused_computation.14 | loop fusion | flops 3145728 | bytes 2097152 | tf_op jit(solution)/shard_map/convert_element_type | solution.py:24
  14.0 1.2 fusion.10
  15.2 14.7 %all-reduce = s32[16]{0:T(128)S(1)} all-reduce(s32[16]{0:T(128)S(1)} %get-tuple-element.151), channel_id=1, replica_groups=mesh['dp'=4,'ctx'=16,'mp'=4] {'ctx'}, use_global_device_ids=true, to_apply=%add | all-reduce | flops 16 | bytes 128
  30.0 1.6 fusion
  31.5 6.9 %fusion.7 = f32[4,1024,128]{1,2,0:T(8,128)S(1)} fusion(bf16[1024,4,128]{0,2,1:T(8,128)(2,1)} %bitcast.55, pred[1024,1024]{1,0:T(8,128)(4,1)} %fusion, bf16[1024,512]{1,0:T(8,128)(2,1)S(1)} %copy-done, bf16[1024,512]{1,0:T(8,128)(2,1)} %param.8), kind=kOutput, calls=%fused_computation.18 | convolution fusion | flops 2159017984 | bytes 6291456 | tf_op jit(solution)/shard_map/hts,she->the/dot_general | solution.py:61
  38.5 23.2 %all-gather.6.cloned.1.call-done = f32[64,128,128]{2,1,0:T(8,128)} async-done(((f32[4,128,128]{2,1,0:T(8,128)}), f32[64,128,128]{2,1,0:T(8,128)}) %all-gather.6.cloned.1.call-update) | async-done | bytes 4194320 | tf_op jit(solution)/shard_map/all_gather | solution.py:11
  61.6 54.6 %while.16 = (s32[]{:T(128)}, f32[4,128,128]{2,1,0:T(8,128)S(1)}, s32[]{:T(128)}, s32[]{:T(128)}, s32[16]{0:T(128)S(1)}, /*index=5*/f32[16,4,128,128]{3,2,1,0:T(8,128)}, s32[]{:T(128)}, s32[]{:T(128)}) while((s32[]{:T(128)}, f32[4,128,128]{2,1,0:T(8,128)S(1)}, s32[]{:T(128)}, s32[]{:T(128)}, s32[16]{0:T(128)S(1)}, ...), condition=%wide.region_1.2_spmd.clone, body=%wide.region_0.1_spmd.clone.sunk | while | flops 327688 | bytes 786615 | solution.py:20
  64.2 1.1 select_select_fusion.2
  67.8 1.1 select_select_fusion.2
  71.4 1.1 select_select_fusion.2
  75.1 1.1 select_select_fusion.2
  78.7 1.1 select_select_fusion.2
  82.4 1.1 select_select_fusion.2
  86.0 1.1 select_select_fusion.2
  89.6 1.1 select_select_fusion.2
  93.3 1.1 select_select_fusion.2
  116.2 2.4 %fusion.15 = f32[4,128,1024]{2,1,0:T(8,128)S(1)} fusion(f32[4,128,128]{2,1,0:T(8,128)S(1)} %get-tuple-element.116, bf16[1024,512]{1,0:T(8,128)(2,1)} %param.8), kind=kOutput, calls=%fused_computation.26 | convolution fusion | flops 137428992 | bytes 3407872 | tf_op jit(solution)/shard_map/thd,hde->the/dot_general | solution.py:64
  118.7 1.4 multiply_reduce_fusion
  120.1 1.2 multiply_convert_fusion
  121.4 49.4 %all-gather.4.cloned.1.call-done = bf16[1024,2048]{0,1:T(8,128)(2,1)} async-done(((bf16[1024,512]{0,1:T(8,128)(2,1)}), bf16[1024,2048]{0,1:T(8,128)(2,1)}) %all-gather.4.cloned.1.call-update) | async-done | bytes 4194320 | tf_op jit(solution)/shard_map/all_gather | solution.py:73
  170.8 9.4 %convolution_convert_fusion = bf16[1024,1024]{1,0:T(8,128)(2,1)} fusion(bf16[1024,2048]{0,1:T(8,128)(2,1)} %all-gather.4.cloned.1.call-done, bf16[2048,1024]{1,0:T(8,128)(2,1)} %param.13), kind=kOutput, calls=%fused_computation.19 | convolution fusion | flops 4296015872 | bytes 10485760 | tf_op jit(solution)/shard_map/dot_general | solution.py:72
  (40 shorter events, 15.9 us)
Async XLA Ops:
  6.5 7.4 %copy-start = (bf16[1024,512]{1,0:T(8,128)(2,1)S(1)}, bf16[1024,512]{1,0:T(8,128)(2,1)}, u32[]{:S(2)}) copy-start(bf16[1024,512]{1,0:T(8,128)(2,1)} %param.10) | copy-start | bytes 3145732
  6.5 55.1 %all-gather.6.cloned.1.call-start = ((), (), s32[]{:S(2)}) async-start(), calls=%async_computation.1 | async-start | bytes 4456448 | tf_op jit(solution)/shard_map/all_gather | solution.py:11
  13.9 16.0 %copy-start.2 = (bf16[1024,512]{0,1:T(8,128)(2,1)}, bf16[1024,512]{0,1:T(8,128)(2,1)S(1)}, u32[]{:S(2)}) copy-start(bf16[1024,512]{0,1:T(8,128)(2,1)S(1)} %copy.23) | copy-start | bytes 3145732
  14.0 16.0 %copy-start.3 = (s32[1024]{0:T(1024)S(1)}, s32[1024]{0:T(1024)}, u32[]{:S(2)}) copy-start(s32[1024]{0:T(1024)} %param.11) | copy-start | bytes 12292
  15.2 155.6 %all-gather.4.cloned.1.call-start = ((), (), s32[]{:S(2)}) async-start(), calls=%async_computation | async-start | bytes 5242880 | tf_op jit(solution)/shard_map/all_gather | solution.py:73
  116.2 2.5 %copy-start.1 = (bf16[1024,512]{1,0:T(8,128)(2,1)S(1)}, bf16[1024,512]{1,0:T(8,128)(2,1)}, u32[]{:S(2)}) copy-start(bf16[1024,512]{1,0:T(8,128)(2,1)} %param.8) | copy-start | bytes 3145732
  118.7 1.4 copy-start.4
Sparse Core Ops, SparseCore 0:
  15.3 46.2 all-gather.5
  121.5 49.1 all-gather.3
where the time goes:
time: 188 us; the launch traced here: 187 us
  waiting for transfers between devices  72.6 us (39%)
  loops' own time  29.6 us (16%)
  other arithmetic  22.5 us (12%)
  matrix products  21.3 us (11%)
  blocking collectives  14.7 us (8%)
  between operations  13.5 us (7%)
  local copies, waits for them, and re-layouts  12.7 us (7%)
    all_gather x1, waiting for transfers between devices, per_device(): lax.all_gather(hidden, 'mp', axis=1, tiled=True)  49.4 us
    another operation x1, loops' own time, carried_in(): return lax.fori_loop(0, count - 1, step, so_far)  29.6 us
    all_gather x1, waiting for transfers between devices, carried_in(): pieces = jax.tree.map(lambda part: lax.all_gather(part, axis), value)  23.2 us
    select_n x15, other arithmetic, step(): jnp.where(position < mine, new, old)  16.2 us
    unnamed x1, blocking collectives  14.7 us
    dot_general x1, matrix products, per_device(): jnp.dot(lax.all_gather(hidden, 'mp', axis=1, tiled=True), out_weight, pre...  9.36 us
    dynamic_slice x15, local copies, waits for them, and re-layouts, step(): longer = join(so_far, jax.tree.map(lambda part: part[position], pieces))  8.79 us
    dot_general x1, matrix products, per_device(): jnp.einsum('hts,she->the', weights, value_heads, preferred_element_type=j...  6.93 us
  transfers between devices with their start and end apart: 2, of which 2 were waited for; matrix products, arithmetic and copies ran while one was open for 5% of the time, Pallas kernels for 0%

commit v1 on v0

--- a/solution.py
+++ b/solution.py
@@ -6,31 +6,29 @@
 HEAD = 128
 
 
-def carried_in(value, axis, join, neutral):
-    count, mine = (lax.axis_size(axis), lax.axis_index(axis))
-    pieces = jax.tree.map(lambda part: lax.all_gather(part, axis), value)
-    so_far = jax.tree.map(
-        lambda part, zero: jnp.full_like(part, 0) + jnp.asarray(zero, part.dtype), value, neutral
-    )
-
-    def step(position, so_far):
-        longer = join(so_far, jax.tree.map(lambda part: part[position], pieces))
-        return jax.tree.map(lambda new, old: jnp.where(position < mine, new, old), longer, so_far)
-
-    return lax.fori_loop(0, count - 1, step, so_far)
-
-
 def features(raw_input):
     return (jax.nn.elu(raw_input.astype(jnp.float32)) + 1.0).astype(jnp.bfloat16)
 
 
-def join_states(earlier, later):
-    early_sum, early_seg = earlier
-    later_sum, later_seg = later
-    is_blank = later_seg < 0
-    linked = early_seg == later_seg
-    joined = later_sum + jnp.where(linked, early_sum, 0.0)
-    return (jnp.where(is_blank, early_sum, joined), jnp.where(is_blank, early_seg, later_seg))
+def carried_in(local_sum, final_seg, axis):
+    count = lax.axis_size(axis)
+    shape = local_sum.shape
+    flat = local_sum.reshape(count, -1)
+    width = flat.shape[1]
+    seg_row = jnp.full((count, HEAD), final_seg.astype(jnp.float32))
+    sent = jnp.concatenate([flat, seg_row], axis=1)
+    pieces = lax.all_to_all(sent, axis, 0, 0, tiled=True)
+    sums = pieces[:, :width]
+    segs = pieces[:, width]
+    block = jnp.arange(count)
+    prev_seg = jnp.concatenate([jnp.full((1,), -1.0, jnp.float32), segs[:-1]])
+    mask = (block[None, :] < block[:, None]) & (segs[None, :] == prev_seg[:, None])
+    carry = jnp.sum(jnp.where(mask[:, :, None], sums[None, :, :], 0.0), axis=1)
+    back = jnp.concatenate([carry, jnp.broadcast_to(prev_seg[:, None], (count, HEAD))], axis=1)
+    mine = lax.all_to_all(back, axis, 0, 0, tiled=True)
+    before_sum = mine[:, :width].reshape(shape)
+    before_seg = mine[0, width]
+    return before_sum, before_seg
 
 
 def per_device(queries, keys, values, segment_ids, norm_gain, out_weight):
@@ -48,10 +46,7 @@
         value_heads,
         preferred_element_type=jnp.float32,
     )
-    blank_sum = jnp.zeros_like(local_sum)
-    before_sum, before_seg = carried_in(
-        (local_sum, final_seg), "ctx", join_states, (blank_sum, jnp.int32(-1))
-    )
+    before_sum, before_seg = carried_in(local_sum, final_seg, "ctx")
     position = jnp.arange(rows_here)
     allowed = (position[None, :] <= position[:, None]) & (
         segment_ids[:, None] == segment_ids[None, :]
@@ -64,7 +59,7 @@
     carried = jnp.einsum(
         "thd,hde->the", feat_query, state_hi, preferred_element_type=jnp.float32
     ) + jnp.einsum("thd,hde->the", feat_query, state_lo, preferred_element_type=jnp.float32)
-    carry_on = (segment_ids == before_seg).astype(jnp.float32)
+    carry_on = (segment_ids.astype(jnp.float32) == before_seg).astype(jnp.float32)
     numerator = inside + carry_on[:, None, None] * carried
     normed = numerator * lax.rsqrt(jnp.mean(numerator * numerator, axis=-1, keepdims=True) + 1e-06)
     gain_heads = norm_gain.reshape(heads_here, HEAD)

time: 188 us -> 126 us (0.67)
  loops' own time: 29.6 us -> 0 us
  blocking collectives: 14.7 us -> 0 us
  other arithmetic: 22.5 us -> 7.99 us
  starting transfers between devices: 0.04 us -> 13.6 us
  waiting for transfers between devices: 72.6 us -> 62.2 us
  local copies, waits for them, and re-layouts: 12.7 us -> 6.64 us
    another operation x1 -> x0, loops' own time: 29.6 us -> none  [carried_in(): return lax.fori_loop(0, count - 1, step, so_far)]
    all_gather x1 -> x0, waiting for transfers between devices: 23.2 us -> none  [carried_in(): pieces = jax.tree.map(lambda part: lax.all_gather(part, axis), value)]
    select_n x15 -> x0, other arithmetic: 16.2 us -> none  [step(): jnp.where(position < mine, new, old)]
    unnamed x1 -> x0, blocking collectives: 14.7 us -> none
    all_to_all x0 -> x2, waiting for transfers between devices: none -> 14.4 us  [the longest x1 10.3 us: carried_in(): pieces = lax.all_to_all(sent, axis, 0, 0, tiled=True)]
    all_to_all x0 -> x2, starting transfers between devices: none -> 13.4 us  [the longest x1 9.98 us: carried_in(): pieces = lax.all_to_all(sent, axis, 0, 0, tiled=True)]
    dynamic_slice x15 -> x0, local copies, waits for them, and re-layouts: 8.79 us -> none  [step(): longer = join(so_far, jax.tree.map(lambda part: part[position], pieces))]
    all_to_all x0 -> x2, local copies, waits for them, and re-layouts: none -> 1.9 us  [the longest x1 1 us: carried_in(): mine = lax.all_to_all(back, axis, 0, 0, tiled=True)]
  transfers between devices with their start and end apart: 2 -> 3, of which waited for: 2 -> 3; matrix products, arithmetic and copies ran while one was open for 5% -> 7% of each run, Pallas kernels for 0% -> 0%
where the time goes in v1:
time: 126 us; the launch traced here: 125 us
  waiting for transfers between devices  62.2 us (49%)
  matrix products  20.6 us (16%)
  between operations  14.2 us (11%)
  starting transfers between devices  13.6 us (11%)
  other arithmetic  7.99 us (6%)
  local copies, waits for them, and re-layouts  6.64 us (5%)
    all_gather x1, waiting for transfers between devices, per_device(): lax.all_gather(hidden, 'mp', axis=1, tiled=True)  47.8 us
    all_to_all x1, waiting for transfers between devices, carried_in(): pieces = lax.all_to_all(sent, axis, 0, 0, tiled=True)  10.3 us
    all_to_all x1, starting transfers between devices, carried_in(): pieces = lax.all_to_all(sent, axis, 0, 0, tiled=True)  9.98 us
    dot_general x1, matrix products, per_device(): jnp.dot(lax.all_gather(hidden, 'mp', axis=1, tiled=True), out_weight, pre...  9.36 us
    dot_general x1, matrix products, per_device(): jnp.einsum('hts,she->the', weights, value_heads, preferred_element_type=j...  6.93 us
    all_to_all x1, waiting for transfers between devices, carried_in(): mine = lax.all_to_all(back, axis, 0, 0, tiled=True)  4.12 us
    all_to_all x1, starting transfers between devices, carried_in(): mine = lax.all_to_all(back, axis, 0, 0, tiled=True)  3.43 us
  transfers between devices with their start and end apart: 3, of which 3 were waited for; matrix products, arithmetic and copies ran while one was open for 7% of the time, Pallas kernels for 0%

profile of v1, /device:TPU:1, one launch (start us, length us, event | category | flops | bytes accessed | tf_op | source)
XLA Modules:
  0.0 125.3 jit_solution(9573553219433462059)
XLA Ops:
  6.5 1.4 %slice.22 = s32[1]{0:T(128)} slice(s32[1024]{0:T(1024)} %param.9), slice={[1023:1024]} | slice | bytes 8 | tf_op jit(solution)/shard_map/slice | solution.py:41
  8.5 1.3 %compare_convert_fusion = bf16[1024]{0:T(1024)(128)(2,1)S(1)} fusion(s32[1024]{0:T(1024)} %param.9, s32[]{:T(128)} %bitcast.1), kind=kLoop, calls=%fused_computation.47 | loop fusion | flops 2048 | bytes 6148 | tf_op jit(solution)/shard_map/convert_element_type | solution.py:42
  9.9 2.2 %fusion.6 = bf16[1024,512]{1,0:T(8,128)(2,1)S(1)} fusion(bf16[1024,512]{1,0:T(8,128)(2,1)} %param.7), kind=kLoop, calls=%fused_computation.13 | loop fusion | flops 3145728 | bytes 2097152 | tf_op jit(solution)/shard_map/convert_element_type | solution.py:10
  12.0 0.5 copy.53
  12.6 0.4 fusion.10
  13.2 0.9 all_to_all.16
  14.1 10.0 %all-to-all-start = ((f32[16,1,4224]{2,1,0:T(1,128)}), f32[16,1,4224]{2,1,0:T(1,128)S(1)}, u32[]{:S(2)}, u32[]{:S(2)}) async-start(f32[16,1,4224]{2,1,0:T(1,128)} %all_to_all.16), calls=%async_computation | async-start | bytes 540672 | tf_op jit(solution)/shard_map/all_to_all | solution.py:20
  24.0 1.6 %fusion = pred[1024,1024]{1,0:T(8,128)(4,1)} fusion(s32[1024]{0:T(1024)S(1)} %copy-done.3), kind=kLoop, calls=%fused_computation.7 | loop fusion | flops 3145728 | bytes 1052672 | tf_op jit(solution)/shard_map/and | solution.py:51
  25.6 10.3 %all-to-all-done = f32[16,1,4224]{2,1,0:T(1,128)S(1)} async-done(((f32[16,1,4224]{2,1,0:T(1,128)}), f32[16,1,4224]{2,1,0:T(1,128)S(1)}, u32[]{:S(2)}, u32[]{:S(2)}) %all-to-all-start) | async-done | bytes 270368 | tf_op jit(solution)/shard_map/all_to_all | solution.py:20
  36.3 0.9 select_reduce_fusion
  37.3 1.0 copy.46
  38.3 3.4 %all-to-all-start.1 = ((f32[16,1,4224]{2,1,0:T(1,128)}), f32[16,1,4224]{2,1,0:T(1,128)S(1)}, u32[]{:S(2)}, u32[]{:S(2)}) async-start(f32[16,1,4224]{2,1,0:T(1,128)} %copy.46), calls=%async_computation.1 | async-start | bytes 540672 | tf_op jit(solution)/shard_map/all_to_all | solution.py:28
  41.8 0.2 all-gather.2.cloned.1.call-start
  42.0 6.9 %fusion.7 = f32[4,1024,128]{1,2,0:T(8,128)S(1)} fusion(bf16[1024,4,128]{0,2,1:T(8,128)(2,1)} %bitcast.58, pred[1024,1024]{1,0:T(8,128)(4,1)} %fusion, bf16[1024,512]{1,0:T(8,128)(2,1)S(1)} %copy-done, bf16[1024,512]{1,0:T(8,128)(2,1)} %param.6), kind=kOutput, calls=%fused_computation.17 | convolution fusion | flops 2159017984 | bytes 6291456 | tf_op jit(solution)/shard_map/hts,she->the/dot_general | solution.py:56
  48.9 4.1 %all-to-all-done.1 = f32[16,1,4224]{2,1,0:T(1,128)S(1)} async-done(((f32[16,1,4224]{2,1,0:T(1,128)}), f32[16,1,4224]{2,1,0:T(1,128)S(1)}, u32[]{:S(2)}, u32[]{:S(2)}) %all-to-all-start.1) | async-done | bytes 270368 | tf_op jit(solution)/shard_map/all_to_all | solution.py:28
  53.1 0.5 slice.32
  53.6 0.7 reshape.121
  54.4 1.1 copy.47
  55.5 0.6 fusion.28
  56.1 2.5 %fusion.13 = f32[4,128,1024]{2,1,0:T(8,128)S(1)} fusion(f32[4,128,128]{1,2,0:T(8,128)S(1)} %copy.47, bf16[1024,512]{1,0:T(8,128)(2,1)} %param.6), kind=kOutput, calls=%fused_computation.24 | convolution fusion | flops 137428992 | bytes 3407872 | tf_op jit(solution)/shard_map/thd,hde->the/dot_general | solution.py:59
  58.6 1.4 %multiply_reduce_fusion = (f32[1024,4]{0,1:T(4,128)S(1)}, f32[1024,4,128]{0,2,1:T(8,128)S(1)}) fusion(f32[4,128,1024]{2,1,0:T(8,128)S(1)} %fusion.13, f32[4,128,128]{1,2,0:T(8,128)S(1)} %copy.47, f32[1024]{0:T(1024)S(1)} %fusion.28, f32[4,1024,128]{1,2,0:T(8,128)S(1)} %fusion.7, bf16[1024,512]{1,0:T(8,128)(2,1)S(1)} %copy-done.1), kind=kOutput, calls=%fused_computation.16 | convolution fusion | flops 140242944 | bytes 7622656 | tf_op jit(solution)/shard_map/thd,hde->the/dot_general | solution.py:61
  60.1 1.2 multiply_convert_fusion
  61.3 47.8 %all-gather.2.cloned.1.call-done = bf16[1024,2048]{0,1:T(8,128)(2,1)} async-done(((bf16[1024,512]{0,1:T(8,128)(2,1)}), bf16[1024,2048]{0,1:T(8,128)(2,1)}) %all-gather.2.cloned.1.call-update) | async-done | bytes 4194320 | tf_op jit(solution)/shard_map/all_gather | solution.py:68
  109.1 9.4 %convolution_convert_fusion = bf16[1024,1024]{1,0:T(8,128)(2,1)} fusion(bf16[1024,2048]{0,1:T(8,128)(2,1)} %all-gather.2.cloned.1.call-done, bf16[2048,1024]{1,0:T(8,128)(2,1)} %param.11), kind=kOutput, calls=%fused_computation.18 | convolution fusion | flops 4296015872 | bytes 10485760 | tf_op jit(solution)/shard_map/dot_general | solution.py:67
  (24 shorter events, 0.7 us)
Async XLA Ops:
  6.5 6.1 %copy-start = (bf16[1024,512]{1,0:T(8,128)(2,1)S(1)}, bf16[1024,512]{1,0:T(8,128)(2,1)}, u32[]{:S(2)}) copy-start(bf16[1024,512]{1,0:T(8,128)(2,1)} %param.8) | copy-start | bytes 3145732
  12.6 1.5 %copy-start.2 = (bf16[1024,512]{0,1:T(8,128)(2,1)}, bf16[1024,512]{0,1:T(8,128)(2,1)S(1)}, u32[]{:S(2)}) copy-start(bf16[1024,512]{0,1:T(8,128)(2,1)S(1)} %copy.53) | copy-start | bytes 3145732
  12.6 11.4 %copy-start.3 = (s32[1024]{0:T(1024)S(1)}, s32[1024]{0:T(1024)}, u32[]{:S(2)}) copy-start(s32[1024]{0:T(1024)} %param.9) | copy-start | bytes 12292
  14.1 21.9 %all-to-all-start = ((f32[16,1,4224]{2,1,0:T(1,128)}), f32[16,1,4224]{2,1,0:T(1,128)S(1)}, u32[]{:S(2)}, u32[]{:S(2)}) async-start(f32[16,1,4224]{2,1,0:T(1,128)} %all_to_all.16), calls=%async_computation | async-start | bytes 540672 | tf_op jit(solution)/shard_map/all_to_all | solution.py:20
  38.3 14.7 %all-to-all-start.1 = ((f32[16,1,4224]{2,1,0:T(1,128)}), f32[16,1,4224]{2,1,0:T(1,128)S(1)}, u32[]{:S(2)}, u32[]{:S(2)}) async-start(f32[16,1,4224]{2,1,0:T(1,128)} %copy.46), calls=%async_computation.1 | async-start | bytes 540672 | tf_op jit(solution)/shard_map/all_to_all | solution.py:28
  41.8 67.4 %all-gather.2.cloned.1.call-start = ((), (), s32[]{:S(2)}) async-start(), calls=%async_computation.2 | async-start | bytes 5242880 | tf_op jit(solution)/shard_map/all_gather | solution.py:68
  56.1 2.5 %copy-start.1 = (bf16[1024,512]{1,0:T(8,128)(2,1)S(1)}, bf16[1024,512]{1,0:T(8,128)(2,1)}, u32[]{:S(2)}) copy-start(bf16[1024,512]{1,0:T(8,128)(2,1)} %param.6) | copy-start | bytes 3145732
  58.6 1.5 %copy-start.4 = (f32[512]{0:T(512)S(1)}, f32[512]{0:T(512)}, u32[]{:S(2)}) copy-start(f32[512]{0:T(512)} %param.10) | copy-start | bytes 6148
Sparse Core Ops, SparseCore 0:
  61.5 47.6 all-gather.1

commit v2 on v1

--- a/solution.py
+++ b/solution.py
@@ -29,6 +29,27 @@
     before_sum = mine[:, :width].reshape(shape)
     before_seg = mine[0, width]
     return before_sum, before_seg
+
+
+def project_gathered(hidden, out_weight, axis):
+    count, mine = lax.axis_size(axis), lax.axis_index(axis)
+    rows, width = hidden.shape
+    half = rows // 2
+    weight_groups = out_weight.reshape(count, width, out_weight.shape[1])
+    ahead = [(j, (j + 1) % count) for j in range(count)]
+    behind = [(j, (j - 1) % count) for j in range(count)]
+
+    def part(block, offset):
+        group = lax.rem(mine + offset + count, count)
+        return jnp.dot(block, weight_groups[group], preferred_element_type=jnp.float32)
+
+    from_left = lax.ppermute(hidden, axis, ahead)
+    from_right = lax.ppermute(hidden, axis, behind)
+    far_top = lax.ppermute(from_left[:half], axis, ahead)
+    far_bottom = lax.ppermute(from_right[half:], axis, behind)
+    total = part(hidden, 0) + part(from_left, -1) + part(from_right, 1)
+    far = jnp.concatenate([part(far_top, 2), part(far_bottom, 2)], axis=0)
+    return total + far
 
 
 def per_device(queries, keys, values, segment_ids, norm_gain, out_weight):
@@ -64,12 +85,7 @@
     normed = numerator * lax.rsqrt(jnp.mean(numerator * numerator, axis=-1, keepdims=True) + 1e-06)
     gain_heads = norm_gain.reshape(heads_here, HEAD)
     hidden = (normed * gain_heads[None]).astype(jnp.bfloat16).reshape(rows_here, width_here)
-    projected = jnp.dot(
-        lax.all_gather(hidden, "mp", axis=1, tiled=True),
-        out_weight,
-        preferred_element_type=jnp.float32,
-    )
-    return projected.astype(jnp.bfloat16)
+    return project_gathered(hidden, out_weight, "mp").astype(jnp.bfloat16)
 
 
 def solution(mesh):

time: 126 us -> 103 us (0.82); the launches traced: 125 us -> 101 us
  waiting for transfers between devices: 62.2 us -> 45.2 us
  between operations: 14.2 us -> 0.89 us
  starting transfers between devices: 13.6 us -> 19.3 us
    all_gather x1 -> x0, waiting for transfers between devices: 47.8 us -> none  [per_device(): lax.all_gather(hidden, 'mp', axis=1, tiled=True)]
    ppermute x0 -> x4, waiting for transfers between devices: none -> 30.5 us  [the longest x1 23.5 us: project_gathered(): from_left = lax.ppermute(hidden, axis, ahead)]
    ppermute x0 -> x4, starting transfers between devices: none -> 5.9 us  [the longest x1 2.72 us: project_gathered(): far_bottom = lax.ppermute(from_right[half:], axis, behind)]
    dot_general x1 -> x5, matrix products: 9.36 us -> 9.64 us  [part(): jnp.dot(block, weight_groups[group], preferred_element_type=jnp.float32)]
  transfers between devices with their start and end apart: 3 -> 6, of which waited for: 3 -> 5; matrix products, arithmetic and copies ran while one was open for 7% -> 15% of each run, Pallas kernels for 0% -> 0%
where the time goes in v2:
time: 103 us; the launch traced here: 101 us
  waiting for transfers between devices  45.2 us (44%)
  matrix products  20.9 us (20%)
  starting transfers between devices  19.3 us (19%)
  local copies, waits for them, and re-layouts  7.72 us (7%)
  other arithmetic  6.98 us (7%)
    ppermute x1, waiting for transfers between devices, project_gathered(): from_left = lax.ppermute(hidden, axis, ahead)  23.5 us
    all_to_all x1, waiting for transfers between devices, carried_in(): pieces = lax.all_to_all(sent, axis, 0, 0, tiled=True)  10.3 us
    all_to_all x1, starting transfers between devices, carried_in(): pieces = lax.all_to_all(sent, axis, 0, 0, tiled=True)  9.97 us
    dot_general x5, matrix products, part(): jnp.dot(block, weight_groups[group], preferred_element_type=jnp.float32)  9.64 us
    dot_general x1, matrix products, per_device(): jnp.einsum('hts,she->the', weights, value_heads, preferred_element_type=j...  6.93 us
    ppermute x1, waiting for transfers between devices, project_gathered(): far_top = lax.ppermute(from_left[:half], axis, ahead)  6.03 us
    all_to_all x1, waiting for transfers between devices, carried_in(): mine = lax.all_to_all(back, axis, 0, 0, tiled=True)  4.35 us
    all_to_all x1, starting transfers between devices, carried_in(): mine = lax.all_to_all(back, axis, 0, 0, tiled=True)  3.43 us
  transfers between devices with their start and end apart: 6, of which 5 were waited for; matrix products, arithmetic and copies ran while one was open for 15% of the time, Pallas kernels for 0%

profile of v2, /device:TPU:1, one launch (start us, length us, event | category | flops | bytes accessed | tf_op | source)
XLA Modules:
  0.0 101.0 jit_solution(55908032406110018)
XLA Ops:
  0.0 1.4 %slice.28 = s32[1]{0:T(128)} slice(s32[1024]{0:T(1024)} %param.9), slice={[1023:1024]} | slice | bytes 8 | tf_op jit(solution)/shard_map/slice | solution.py:62
  2.0 1.3 %compare_convert_fusion = bf16[1024]{0:T(1024)(128)(2,1)S(1)} fusion(s32[1024]{0:T(1024)} %param.9, s32[]{:T(128)} %bitcast.1), kind=kLoop, calls=%fused_computation.62 | loop fusion | flops 2048 | bytes 6148 | tf_op jit(solution)/shard_map/convert_element_type | solution.py:63
  3.3 2.2 %fusion.7 = bf16[1024,512]{1,0:T(8,128)(2,1)S(1)} fusion(bf16[1024,512]{1,0:T(8,128)(2,1)} %param.7), kind=kLoop, calls=%fused_computation.15 | loop fusion | flops 3145728 | bytes 2097152 | tf_op jit(solution)/shard_map/convert_element_type | solution.py:10
  6.6 0.9 all_to_all.16
  7.5 10.0 %all-to-all-start = ((f32[16,1,4224]{2,1,0:T(1,128)}), f32[16,1,4224]{2,1,0:T(1,128)S(1)}, u32[]{:S(2)}, u32[]{:S(2)}) async-start(f32[16,1,4224]{2,1,0:T(1,128)} %all_to_all.16), calls=%async_computation | async-start | bytes 540672 | tf_op jit(solution)/shard_map/all_to_all | solution.py:20
  17.5 1.6 %fusion.1 = pred[1024,1024]{1,0:T(8,128)(4,1)} fusion(s32[1024]{0:T(1024)S(1)} %copy-done.4), kind=kLoop, calls=%fused_computation.9 | loop fusion | flops 3145728 | bytes 1052672 | tf_op jit(solution)/shard_map/and | solution.py:72
  19.1 10.3 %all-to-all-done = f32[16,1,4224]{2,1,0:T(1,128)S(1)} async-done(((f32[16,1,4224]{2,1,0:T(1,128)}), f32[16,1,4224]{2,1,0:T(1,128)S(1)}, u32[]{:S(2)}, u32[]{:S(2)}) %all-to-all-start) | async-done | bytes 270368 | tf_op jit(solution)/shard_map/all_to_all | solution.py:20
  30.8 1.0 copy.46
  31.7 3.4 %all-to-all-start.1 = ((f32[16,1,4224]{2,1,0:T(1,128)}), f32[16,1,4224]{2,1,0:T(1,128)S(1)}, u32[]{:S(2)}, u32[]{:S(2)}) async-start(f32[16,1,4224]{2,1,0:T(1,128)} %copy.46), calls=%async_computation.1 | async-start | bytes 540672 | tf_op jit(solution)/shard_map/all_to_all | solution.py:28
  35.2 6.9 %fusion.8 = f32[4,1024,128]{1,2,0:T(8,128)S(1)} fusion(bf16[1024,4,128]{0,2,1:T(8,128)(2,1)} %bitcast.83, pred[1024,1024]{1,0:T(8,128)(4,1)} %fusion.1, bf16[1024,512]{1,0:T(8,128)(2,1)S(1)} %copy-done, bf16[1024,512]{1,0:T(8,128)(2,1)} %param.6), kind=kOutput, calls=%fused_computation.19 | convolution fusion | flops 2159017984 | bytes 6291456 | tf_op jit(solution)/shard_map/hts,she->the/dot_general | solution.py:77
  42.1 4.3 %all-to-all-done.1 = f32[16,1,4224]{2,1,0:T(1,128)S(1)} async-done(((f32[16,1,4224]{2,1,0:T(1,128)}), f32[16,1,4224]{2,1,0:T(1,128)S(1)}, u32[]{:S(2)}, u32[]{:S(2)}) %all-to-all-start.1) | async-done | bytes 270368 | tf_op jit(solution)/shard_map/all_to_all | solution.py:28
  47.8 1.1 %copy.47 = f32[4,128,128]{1,2,0:T(8,128)S(1)} copy(f32[4,128,128]{2,1,0:T(8,128)} %reshape.124) | data formatting | bytes 524288 | tf_op jit(solution)/shard_map/reshape | solution.py:29
  49.5 2.5 %fusion.14 = f32[4,128,1024]{2,1,0:T(8,128)S(1)} fusion(f32[4,128,128]{1,2,0:T(8,128)S(1)} %copy.47, bf16[1024,512]{1,0:T(8,128)(2,1)} %param.6), kind=kOutput, calls=%fused_computation.25 | convolution fusion | flops 137428992 | bytes 3407872 | tf_op jit(solution)/shard_map/thd,hde->the/dot_general | solution.py:80
  52.0 1.4 %multiply_reduce_fusion = (f32[1024,4]{0,1:T(4,128)S(1)}, f32[1024,4,128]{0,2,1:T(8,128)S(1)}) fusion(f32[4,128,1024]{2,1,0:T(8,128)S(1)} %fusion.14, f32[4,128,128]{1,2,0:T(8,128)S(1)} %copy.47, f32[1024]{0:T(1024)S(1)} %fusion.43, f32[4,1024,128]{1,2,0:T(8,128)S(1)} %fusion.8, bf16[1024,512]{1,0:T(8,128)(2,1)S(1)} %copy-done.2), kind=kOutput, calls=%fused_computation.18 | convolution fusion | flops 140242944 | bytes 7622656 | tf_op jit(solution)/shard_map/thd,hde->the/dot_general | solution.py:82
  53.8 1.6 %collective-permute-start = (bf16[1024,512]{0,1:T(8,128)(2,1)S(1)}, bf16[1024,512]{0,1:T(8,128)(2,1)}, u32[]{:S(2)}, u32[]{:S(2)}) collective-permute-start(bf16[1024,512]{0,1:T(8,128)(2,1)S(1)} %bitcast.74), channel_id=1, source_target_pairs={{0,1},{1,2},{2,3},{3,0},{4,5},{5,6},{6,7},{7,4},{8,9},{9,10},{10,1... | collective-permute-start | bytes 3145736 | tf_op jit(solution)/shard_map/ppermute | solution.py:46
  55.3 1.5 %collective-permute-start.1 = (bf16[1024,512]{0,1:T(8,128)(2,1)S(1)}, bf16[1024,512]{0,1:T(8,128)(2,1)S(1)}, u32[]{:S(2)}, u32[]{:S(2)}) collective-permute-start(bf16[1024,512]{0,1:T(8,128)(2,1)S(1)} %bitcast.75), channel_id=1, source_target_pairs={{0,3},{1,0},{2,1},{3,2},{4,7},{5,4},{6,5},{7,6},{8,11},{9,8},{10,9... | collective-permute-start | bytes 3145736 | tf_op jit(solution)/shard_map/ppermute | solution.py:47
  56.8 23.5 %collective-permute-done = bf16[1024,512]{0,1:T(8,128)(2,1)} collective-permute-done((bf16[1024,512]{0,1:T(8,128)(2,1)S(1)}, bf16[1024,512]{0,1:T(8,128)(2,1)}, u32[]{:S(2)}, u32[]{:S(2)}) %collective-permute-start) | collective-permute-done | bytes 1048608 | tf_op jit(solution)/shard_map/ppermute | solution.py:46
  80.3 1.1 %slice.42 = bf16[512,512]{0,1:T(8,128)(2,1)S(1)} slice(bf16[1024,512]{0,1:T(8,128)(2,1)} %collective-permute-done), slice={[0:512], [0:512]} | slice | bytes 1048576 | tf_op jit(solution)/shard_map/slice | solution.py:48
  81.5 2.7 %fusion.25 = f32[1024,1024]{1,0:T(8,128)S(1)} fusion(bf16[1024,512]{0,1:T(8,128)(2,1)S(1)} %bitcast.76, bf16[4,512,1024]{2,1,0:T(8,128)(2,1)} %bitcast.69, s32[]{:T(128)S(6)} %select_n.43), kind=kOutput, calls=%fused_computation.35 | convolution fusion | flops 1073741824 | bytes 6291460 | tf_op jit(solution)/shard_map/dot_general | solution.py:44
  84.2 2.7 %collective-permute-start.3 = (bf16[512,512]{0,1:T(8,128)(2,1)S(1)}, bf16[512,512]{0,1:T(8,128)(2,1)S(1)}, u32[]{:S(2)}, u32[]{:S(2)}) collective-permute-start(bf16[512,512]{0,1:T(8,128)(2,1)S(1)} %slice.43), channel_id=1, source_target_pairs={{0,3},{1,0},{2,1},{3,2},{4,7},{5,4},{6,5},{7,6},{8,11},{9,8},{10,9... | collective-permute-start | bytes 1572872 | tf_op jit(solution)/shard_map/ppermute | solution.py:49
  87.0 2.5 %fusion.23 = f32[1024,1024]{1,0:T(8,128)S(1)} fusion(bf16[1024,512]{0,1:T(8,128)(2,1)} %collective-permute-done, bf16[4,512,1024]{2,1,0:T(8,128)(2,1)S(1)} %bitcast.70, s32[]{:T(128)S(6)} %select_n.44), kind=kOutput, calls=%fused_computation.33 | convolution fusion | flops 1073741824 | bytes 6291460 | tf_op jit(solution)/shard_map/dot_general | solution.py:44
  89.5 6.0 %collective-permute-done.2 = bf16[512,512]{0,1:T(8,128)(2,1)S(1)} collective-permute-done((bf16[512,512]{0,1:T(8,128)(2,1)S(1)}, bf16[512,512]{0,1:T(8,128)(2,1)S(1)}, u32[]{:S(2)}, u32[]{:S(2)}) %collective-permute-start.2) | collective-permute-done | bytes 524320 | tf_op jit(solution)/shard_map/ppermute | solution.py:48
  96.3 1.0 collective-permute-done.3
  98.0 3.0 %fusion = bf16[1024,1024]{1,0:T(8,128)(2,1)} fusion(f32[512,1024]{1,0:T(8,128)S(1)} %fusion.18, f32[512,1024]{1,0:T(8,128)S(1)} %fusion.20, f32[1024,1024]{1,0:T(8,128)S(1)} %fusion.25, f32[1024,1024]{1,0:T(8,128)S(1)} %fusion.23, bf16[1024,512]{0,1:T(8,128)(2,1)S(1)} %collective-permute-done.1, bf16[4,512,1024]{2,1,0:T(8,128)(2,1)S(1)} %bitcast.73, ...), kind=kOutput, calls=%fused_computation.6 | convolution fusion | flops 1078984704 | bytes 16777220 | tf_op jit(solution)/shard_map/dot_general | solution.py:44
  (37 shorter events, 6.3 us)
Async XLA Ops:
  0.0 6.1 %copy-start = (bf16[1024,512]{1,0:T(8,128)(2,1)S(1)}, bf16[1024,512]{1,0:T(8,128)(2,1)}, u32[]{:S(2)}) copy-start(bf16[1024,512]{1,0:T(8,128)(2,1)} %param.8) | copy-start | bytes 3145732
  6.0 1.5 %copy-start.3 = (bf16[1024,512]{0,1:T(8,128)(2,1)}, bf16[1024,512]{0,1:T(8,128)(2,1)S(1)}, u32[]{:S(2)}) copy-start(bf16[1024,512]{0,1:T(8,128)(2,1)S(1)} %copy.53) | copy-start | bytes 3145732
  6.1 11.4 %copy-start.4 = (s32[1024]{0:T(1024)S(1)}, s32[1024]{0:T(1024)}, u32[]{:S(2)}) copy-start(s32[1024]{0:T(1024)} %param.9) | copy-start | bytes 12292
  7.5 21.8 %all-to-all-start = ((f32[16,1,4224]{2,1,0:T(1,128)}), f32[16,1,4224]{2,1,0:T(1,128)S(1)}, u32[]{:S(2)}, u32[]{:S(2)}) async-start(f32[16,1,4224]{2,1,0:T(1,128)} %all_to_all.16), calls=%async_computation | async-start | bytes 540672 | tf_op jit(solution)/shard_map/all_to_all | solution.py:20
  31.7 14.7 %all-to-all-start.1 = ((f32[16,1,4224]{2,1,0:T(1,128)}), f32[16,1,4224]{2,1,0:T(1,128)S(1)}, u32[]{:S(2)}, u32[]{:S(2)}) async-start(f32[16,1,4224]{2,1,0:T(1,128)} %copy.46), calls=%async_computation.1 | async-start | bytes 540672 | tf_op jit(solution)/shard_map/all_to_all | solution.py:28
  49.5 2.5 %copy-start.2 = (bf16[1024,512]{1,0:T(8,128)(2,1)S(1)}, bf16[1024,512]{1,0:T(8,128)(2,1)}, u32[]{:S(2)}) copy-start(bf16[1024,512]{1,0:T(8,128)(2,1)} %param.6) | copy-start | bytes 3145732
  52.0 1.5 %copy-start.5 = (f32[512]{0:T(512)S(1)}, f32[512]{0:T(512)}, u32[]{:S(2)}) copy-start(f32[512]{0:T(512)} %param.10) | copy-start | bytes 6148
  53.8 26.6 %collective-permute-start = (bf16[1024,512]{0,1:T(8,128)(2,1)S(1)}, bf16[1024,512]{0,1:T(8,128)(2,1)}, u32[]{:S(2)}, u32[]{:S(2)}) collective-permute-start(bf16[1024,512]{0,1:T(8,128)(2,1)S(1)} %bitcast.74), channel_id=1, source_target_pairs={{0,1},{1,2},{2,3},{3,0},{4,5},{5,6},{6,7},{7,4},{8,9},{9,10},{10,1... | collective-permute-start | bytes 3145736 | tf_op jit(solution)/shard_map/ppermute | solution.py:46
  55.3 28.9 %collective-permute-start.1 = (bf16[1024,512]{0,1:T(8,128)(2,1)S(1)}, bf16[1024,512]{0,1:T(8,128)(2,1)S(1)}, u32[]{:S(2)}, u32[]{:S(2)}) collective-permute-start(bf16[1024,512]{0,1:T(8,128)(2,1)S(1)} %bitcast.75), channel_id=1, source_target_pairs={{0,3},{1,0},{2,1},{3,2},{4,7},{5,4},{6,5},{7,6},{8,11},{9,8},{10,9... | collective-permute-start | bytes 3145736 | tf_op jit(solution)/shard_map/ppermute | solution.py:47
  81.4 14.1 %collective-permute-start.2 = (bf16[512,512]{0,1:T(8,128)(2,1)S(1)}, bf16[512,512]{0,1:T(8,128)(2,1)S(1)}, u32[]{:S(2)}, u32[]{:S(2)}) collective-permute-start(bf16[512,512]{0,1:T(8,128)(2,1)S(1)} %slice.42), channel_id=1, source_target_pairs={{0,1},{1,2},{2,3},{3,0},{4,5},{5,6},{6,7},{7,4},{8,9},{9,10},{10,1... | collective-permute-start | bytes 1572872 | tf_op jit(solution)/shard_map/ppermute | solution.py:48
  81.5 5.5 %copy-start.1 = (bf16[2048,1024]{1,0:T(8,128)(2,1)S(1)}, bf16[2048,1024]{1,0:T(8,128)(2,1)}, u32[]{:S(2)}) copy-start(bf16[2048,1024]{1,0:T(8,128)(2,1)} %param.11) | copy-start | bytes 12582916
  84.2 13.0 %collective-permute-start.3 = (bf16[512,512]{0,1:T(8,128)(2,1)S(1)}, bf16[512,512]{0,1:T(8,128)(2,1)S(1)}, u32[]{:S(2)}, u32[]{:S(2)}) collective-permute-start(bf16[512,512]{0,1:T(8,128)(2,1)S(1)} %slice.43), channel_id=1, source_target_pairs={{0,3},{1,0},{2,1},{3,2},{4,7},{5,4},{6,5},{7,6},{8,11},{9,8},{10,9... | collective-permute-start | bytes 1572872 | tf_op jit(solution)/shard_map/ppermute | solution.py:49

commit v3 on v2

--- a/solution.py
+++ b/solution.py
@@ -43,13 +43,21 @@
         group = lax.rem(mine + offset + count, count)
         return jnp.dot(block, weight_groups[group], preferred_element_type=jnp.float32)
 
-    from_left = lax.ppermute(hidden, axis, ahead)
-    from_right = lax.ppermute(hidden, axis, behind)
-    far_top = lax.ppermute(from_left[:half], axis, ahead)
-    far_bottom = lax.ppermute(from_right[half:], axis, behind)
-    total = part(hidden, 0) + part(from_left, -1) + part(from_right, 1)
-    far = jnp.concatenate([part(far_top, 2), part(far_bottom, 2)], axis=0)
-    return total + far
+    top, bottom = hidden[:half], hidden[half:]
+    left_top = lax.ppermute(top, axis, ahead)
+    right_bottom = lax.ppermute(bottom, axis, behind)
+    left_top, right_bottom, top_later, bottom_later = lax.optimization_barrier(
+        (left_top, right_bottom, top, bottom)
+    )
+    left_bottom = lax.ppermute(bottom_later, axis, ahead)
+    right_top = lax.ppermute(top_later, axis, behind)
+    far_top = lax.ppermute(left_top, axis, ahead)
+    far_bottom = lax.ppermute(right_bottom, axis, behind)
+    out_top = part(top, 0) + part(left_top, -1) + part(right_top, 1) + part(far_top, 2)
+    out_bottom = (
+        part(bottom, 0) + part(right_bottom, 1) + part(left_bottom, -1) + part(far_bottom, 2)
+    )
+    return jnp.concatenate([out_top, out_bottom], axis=0)
 
 
 def per_device(queries, keys, values, segment_ids, norm_gain, out_weight):

time: 103 us -> 101 us (0.981); the launches traced: 101 us -> 101 us
  matrix products: 20.9 us -> 17.1 us
  starting transfers between devices: 19.3 us -> 21.8 us
  other arithmetic: 6.98 us -> 8.56 us
    dot_general x5 -> x8, matrix products: 9.64 us -> 5.84 us  [part(): jnp.dot(block, weight_groups[group], preferred_element_type=jnp.float32)]
    ppermute x4 -> x6, starting transfers between devices: 5.9 us -> 8.17 us  [the longest x1 2.7 us: project_gathered(): far_bottom = lax.ppermute(right_bottom, axis, behind)]
    concatenate x0 -> x1, other arithmetic: none -> 1.49 us  [project_gathered(): return jnp.concatenate([out_top, out_bottom], axis=0)]
    ppermute x4 -> x6, waiting for transfers between devices: 30.5 us -> 31 us  [the longest x1 13.6 us: project_gathered(): left_bottom = lax.ppermute(bottom_later, axis, ahead)]
  transfers between devices with their start and end apart: 6 -> 8, of which waited for: 5 -> 5; matrix products, arithmetic and copies ran while one was open for 15% -> 14% of each run, Pallas kernels for 0% -> 0%
where the time goes in v3:
time: 101 us
  waiting for transfers between devices  45.5 us (45%)
  starting transfers between devices  21.8 us (22%)
  matrix products  17.1 us (17%)
  other arithmetic  8.56 us (8%)
  local copies, waits for them, and re-layouts  6.76 us (7%)
    ppermute x1, waiting for transfers between devices, project_gathered(): left_bottom = lax.ppermute(bottom_later, axis, ahead)  13.6 us
    ppermute x1, waiting for transfers between devices, project_gathered(): left_top = lax.ppermute(top, axis, ahead)  10.9 us
    all_to_all x1, waiting for transfers between devices, carried_in(): pieces = lax.all_to_all(sent, axis, 0, 0, tiled=True)  10.3 us
    all_to_all x1, starting transfers between devices, carried_in(): pieces = lax.all_to_all(sent, axis, 0, 0, tiled=True)  9.98 us
    dot_general x1, matrix products, per_device(): jnp.einsum('hts,she->the', weights, value_heads, preferred_element_type=j...  6.92 us
    ppermute x1, waiting for transfers between devices, project_gathered(): right_top = lax.ppermute(top_later, axis, behind)  6.51 us
    dot_general x8, matrix products, part(): jnp.dot(block, weight_groups[group], preferred_element_type=jnp.float32)  5.84 us
    all_to_all x1, waiting for transfers between devices, carried_in(): mine = lax.all_to_all(back, axis, 0, 0, tiled=True)  4.2 us
  transfers between devices with their start and end apart: 8, of which 5 were waited for; matrix products, arithmetic and copies ran while one was open for 14% of the time, Pallas kernels for 0%

profile of v3, /device:TPU:1, one launch (start us, length us, event | category | flops | bytes accessed | tf_op | source)
XLA Modules:
  0.0 100.6 jit_solution(15786246120446828071)
XLA Ops:
  0.0 1.4 %slice.34 = s32[1]{0:T(128)} slice(s32[1024]{0:T(1024)} %param.9), slice={[1023:1024]} | slice | bytes 8 | tf_op jit(solution)/shard_map/slice | solution.py:70
  1.4 1.3 %compare_convert_fusion = bf16[1024]{0:T(1024)(128)(2,1)S(1)} fusion(s32[1024]{0:T(1024)} %param.9, s32[]{:T(128)} %bitcast.1), kind=kLoop, calls=%fused_computation.73 | loop fusion | flops 2048 | bytes 6148 | tf_op jit(solution)/shard_map/convert_element_type | solution.py:71
  3.3 2.2 %fusion.6 = bf16[1024,512]{1,0:T(8,128)(2,1)S(1)} fusion(bf16[1024,512]{1,0:T(8,128)(2,1)} %param.7), kind=kLoop, calls=%fused_computation.13 | loop fusion | flops 3145728 | bytes 2097152 | tf_op jit(solution)/shard_map/convert_element_type | solution.py:10
  6.6 0.9 all_to_all.16
  7.5 10.0 %all-to-all-start = ((f32[16,1,4224]{2,1,0:T(1,128)}), f32[16,1,4224]{2,1,0:T(1,128)S(1)}, u32[]{:S(2)}, u32[]{:S(2)}) async-start(f32[16,1,4224]{2,1,0:T(1,128)} %all_to_all.16), calls=%async_computation | async-start | bytes 540672 | tf_op jit(solution)/shard_map/all_to_all | solution.py:20
  17.5 1.6 %fusion = pred[1024,1024]{1,0:T(8,128)(4,1)} fusion(s32[1024]{0:T(1024)S(1)} %copy-done.4), kind=kLoop, calls=%fused_computation.7 | loop fusion | flops 3145728 | bytes 1052672 | tf_op jit(solution)/shard_map/and | solution.py:80
  19.1 10.3 %all-to-all-done = f32[16,1,4224]{2,1,0:T(1,128)S(1)} async-done(((f32[16,1,4224]{2,1,0:T(1,128)}), f32[16,1,4224]{2,1,0:T(1,128)S(1)}, u32[]{:S(2)}, u32[]{:S(2)}) %all-to-all-start) | async-done | bytes 270368 | tf_op jit(solution)/shard_map/all_to_all | solution.py:20
  29.8 0.9 select_reduce_fusion
  30.8 1.0 copy.46
  31.8 3.6 %all-to-all-start.1 = ((f32[16,1,4224]{2,1,0:T(1,128)}), f32[16,1,4224]{2,1,0:T(1,128)S(1)}, u32[]{:S(2)}, u32[]{:S(2)}) async-start(f32[16,1,4224]{2,1,0:T(1,128)} %copy.46), calls=%async_computation.1 | async-start | bytes 540672 | tf_op jit(solution)/shard_map/all_to_all | solution.py:28
  35.4 6.9 %fusion.7 = f32[4,1024,128]{1,2,0:T(8,128)S(1)} fusion(bf16[1024,4,128]{0,2,1:T(8,128)(2,1)} %bitcast.103, pred[1024,1024]{1,0:T(8,128)(4,1)} %fusion, bf16[1024,512]{1,0:T(8,128)(2,1)S(1)} %copy-done, bf16[1024,512]{1,0:T(8,128)(2,1)} %param.6), kind=kOutput, calls=%fused_computation.20 | convolution fusion | flops 2159017984 | bytes 6291456 | tf_op jit(solution)/shard_map/hts,she->the/dot_general | solution.py:85
  42.3 4.2 %all-to-all-done.1 = f32[16,1,4224]{2,1,0:T(1,128)S(1)} async-done(((f32[16,1,4224]{2,1,0:T(1,128)}), f32[16,1,4224]{2,1,0:T(1,128)S(1)}, u32[]{:S(2)}, u32[]{:S(2)}) %all-to-all-start.1) | async-done | bytes 270368 | tf_op jit(solution)/shard_map/all_to_all | solution.py:28
  47.1 0.7 reshape.124
  47.9 1.1 %copy.47 = f32[4,128,128]{1,2,0:T(8,128)S(1)} copy(f32[4,128,128]{2,1,0:T(8,128)} %reshape.124) | data formatting | bytes 524288 | tf_op jit(solution)/shard_map/reshape | solution.py:29
  49.0 2.5 %fusion.13 = f32[4,128,1024]{2,1,0:T(8,128)S(1)} fusion(f32[4,128,128]{1,2,0:T(8,128)S(1)} %copy.47, bf16[1024,512]{1,0:T(8,128)(2,1)} %param.6), kind=kOutput, calls=%fused_computation.26 | convolution fusion | flops 137428992 | bytes 3407872 | tf_op jit(solution)/shard_map/thd,hde->the/dot_general | solution.py:88
  52.2 1.4 %multiply_reduce_fusion = (f32[1024,4]{0,1:T(4,128)S(1)}, f32[1024,4,128]{0,2,1:T(8,128)S(1)}) fusion(f32[4,128,1024]{2,1,0:T(8,128)S(1)} %fusion.13, f32[4,128,128]{1,2,0:T(8,128)S(1)} %copy.47, f32[1024]{0:T(1024)S(1)} %fusion.56, f32[4,1024,128]{1,2,0:T(8,128)S(1)} %fusion.7, bf16[1024,512]{1,0:T(8,128)(2,1)S(1)} %copy-done.2), kind=kOutput, calls=%fused_computation.19 | convolution fusion | flops 140242944 | bytes 7622656 | tf_op jit(solution)/shard_map/thd,hde->the/dot_general | solution.py:90
  54.0 1.4 %collective-permute-start = (bf16[512,512]{0,1:T(8,128)(2,1)S(1)}, bf16[512,512]{0,1:T(8,128)(2,1)S(1)}, u32[]{:S(2)}, u32[]{:S(2)}) collective-permute-start(bf16[512,512]{0,1:T(8,128)(2,1)S(1)} %bitcast.94), channel_id=1, source_target_pairs={{0,1},{1,2},{2,3},{3,0},{4,5},{5,6},{6,7},{7,4},{8,9},{9,10},{10,1... | collective-permute-start | bytes 1572872 | tf_op jit(solution)/shard_map/ppermute | solution.py:47
  55.4 1.5 %collective-permute-start.1 = (bf16[512,512]{0,1:T(8,128)(2,1)S(1)}, bf16[512,512]{0,1:T(8,128)(2,1)S(1)}, u32[]{:S(2)}, u32[]{:S(2)}) collective-permute-start(bf16[512,512]{0,1:T(8,128)(2,1)S(1)} %bitcast.91), channel_id=1, source_target_pairs={{0,3},{1,0},{2,1},{3,2},{4,7},{5,4},{6,5},{7,6},{8,11},{9,8},{10,9... | collective-permute-start | bytes 1572872 | tf_op jit(solution)/shard_map/ppermute | solution.py:48
  58.4 10.9 %collective-permute-done = bf16[512,512]{0,1:T(8,128)(2,1)S(1)} collective-permute-done((bf16[512,512]{0,1:T(8,128)(2,1)S(1)}, bf16[512,512]{0,1:T(8,128)(2,1)S(1)}, u32[]{:S(2)}, u32[]{:S(2)}) %collective-permute-start) | collective-permute-done | bytes 524320 | tf_op jit(solution)/shard_map/ppermute | solution.py:47
  69.3 2.6 %collective-permute-start.2 = (bf16[512,512]{0,1:T(8,128)(2,1)S(1)}, bf16[512,512]{0,1:T(8,128)(2,1)S(1)}, u32[]{:S(2)}, u32[]{:S(2)}) collective-permute-start(bf16[512,512]{0,1:T(8,128)(2,1)S(1)} %bitcast.96), channel_id=1, source_target_pairs={{0,3},{1,0},{2,1},{3,2},{4,7},{5,4},{6,5},{7,6},{8,11},{9,8},{10,9... | collective-permute-start | bytes 1572872 | tf_op jit(solution)/shard_map/ppermute | solution.py:53
  71.9 2.7 %collective-permute-start.5 = (bf16[512,512]{0,1:T(8,128)(2,1)S(1)}, bf16[512,512]{0,1:T(8,128)(2,1)S(1)}, u32[]{:S(2)}, u32[]{:S(2)}) collective-permute-start(bf16[512,512]{0,1:T(8,128)(2,1)S(1)} %collective-permute-done.1), channel_id=1, source_target_pairs={{0,3},{1,0},{2,1},{3,2},{4,7},{5,4},{6,5},{7,6},{8,11},{9,8},{10,9... | collective-permute-start | bytes 1572872 | tf_op jit(solution)/shard_map/ppermute | solution.py:55
  76.1 6.5 %collective-permute-done.2 = bf16[512,512]{0,1:T(8,128)(2,1)S(1)} collective-permute-done((bf16[512,512]{0,1:T(8,128)(2,1)S(1)}, bf16[512,512]{0,1:T(8,128)(2,1)S(1)}, u32[]{:S(2)}, u32[]{:S(2)}) %collective-permute-start.2) | collective-permute-done | bytes 524320 | tf_op jit(solution)/shard_map/ppermute | solution.py:53
  83.3 13.6 %collective-permute-done.4 = bf16[512,512]{0,1:T(8,128)(2,1)S(1)} collective-permute-done((bf16[512,512]{0,1:T(8,128)(2,1)S(1)}, bf16[512,512]{0,1:T(8,128)(2,1)S(1)}, u32[]{:S(2)}, u32[]{:S(2)}) %collective-permute-start.4) | collective-permute-done | bytes 524320 | tf_op jit(solution)/shard_map/ppermute | solution.py:52
  99.1 1.5 %pad_maximum_fusion = bf16[1024,1024]{1,0:T(8,128)(2,1)} fusion(bf16[512,1024]{1,0:T(8,128)(2,1)S(1)} %add_convert_fusion, bf16[512,1024]{1,0:T(8,128)(2,1)S(1)} %add_convert_fusion.1), kind=kLoop, calls=%fused_computation.14 | loop fusion | flops 4194304 | bytes 4194304 | tf_op jit(solution)/shard_map/concatenate | solution.py:60
  (44 shorter events, 9.1 us)
Async XLA Ops:
  0.0 6.1 %copy-start = (bf16[1024,512]{1,0:T(8,128)(2,1)S(1)}, bf16[1024,512]{1,0:T(8,128)(2,1)}, u32[]{:S(2)}) copy-start(bf16[1024,512]{1,0:T(8,128)(2,1)} %param.8) | copy-start | bytes 3145732
  6.1 1.5 %copy-start.3 = (bf16[1024,512]{0,1:T(8,128)(2,1)}, bf16[1024,512]{0,1:T(8,128)(2,1)S(1)}, u32[]{:S(2)}) copy-start(bf16[1024,512]{0,1:T(8,128)(2,1)S(1)} %copy.53) | copy-start | bytes 3145732
  6.1 11.4 %copy-start.4 = (s32[1024]{0:T(1024)S(1)}, s32[1024]{0:T(1024)}, u32[]{:S(2)}) copy-start(s32[1024]{0:T(1024)} %param.9) | copy-start | bytes 12292
  7.5 21.9 %all-to-all-start = ((f32[16,1,4224]{2,1,0:T(1,128)}), f32[16,1,4224]{2,1,0:T(1,128)S(1)}, u32[]{:S(2)}, u32[]{:S(2)}) async-start(f32[16,1,4224]{2,1,0:T(1,128)} %all_to_all.16), calls=%async_computation | async-start | bytes 540672 | tf_op jit(solution)/shard_map/all_to_all | solution.py:20
  31.8 14.7 %all-to-all-start.1 = ((f32[16,1,4224]{2,1,0:T(1,128)}), f32[16,1,4224]{2,1,0:T(1,128)S(1)}, u32[]{:S(2)}, u32[]{:S(2)}) async-start(f32[16,1,4224]{2,1,0:T(1,128)} %copy.46), calls=%async_computation.1 | async-start | bytes 540672 | tf_op jit(solution)/shard_map/all_to_all | solution.py:28
  49.0 3.2 %copy-start.2 = (bf16[1024,512]{1,0:T(8,128)(2,1)S(1)}, bf16[1024,512]{1,0:T(8,128)(2,1)}, u32[]{:S(2)}) copy-start(bf16[1024,512]{1,0:T(8,128)(2,1)} %param.6) | copy-start | bytes 3145732
  52.2 1.5 %copy-start.5 = (f32[512]{0:T(512)S(1)}, f32[512]{0:T(512)}, u32[]{:S(2)}) copy-start(f32[512]{0:T(512)} %param.10) | copy-start | bytes 6148
  53.7 3.3 %copy-start.1 = (bf16[2048,1024]{1,0:T(8,128)(2,1)S(1)}, bf16[2048,1024]{1,0:T(8,128)(2,1)}, u32[]{:S(2)}) copy-start(bf16[2048,1024]{1,0:T(8,128)(2,1)} %param.11) | copy-start | bytes 12582916
  54.0 15.3 %collective-permute-start = (bf16[512,512]{0,1:T(8,128)(2,1)S(1)}, bf16[512,512]{0,1:T(8,128)(2,1)S(1)}, u32[]{:S(2)}, u32[]{:S(2)}) collective-permute-start(bf16[512,512]{0,1:T(8,128)(2,1)S(1)} %bitcast.94), channel_id=1, source_target_pairs={{0,1},{1,2},{2,3},{3,0},{4,5},{5,6},{6,7},{7,4},{8,9},{9,10},{10,1... | collective-permute-start | bytes 1572872 | tf_op jit(solution)/shard_map/ppermute | solution.py:47
  55.4 13.9 %collective-permute-start.1 = (bf16[512,512]{0,1:T(8,128)(2,1)S(1)}, bf16[512,512]{0,1:T(8,128)(2,1)S(1)}, u32[]{:S(2)}, u32[]{:S(2)}) collective-permute-start(bf16[512,512]{0,1:T(8,128)(2,1)S(1)} %bitcast.91), channel_id=1, source_target_pairs={{0,3},{1,0},{2,1},{3,2},{4,7},{5,4},{6,5},{7,6},{8,11},{9,8},{10,9... | collective-permute-start | bytes 1572872 | tf_op jit(solution)/shard_map/ppermute | solution.py:48
  69.3 13.2 %collective-permute-start.2 = (bf16[512,512]{0,1:T(8,128)(2,1)S(1)}, bf16[512,512]{0,1:T(8,128)(2,1)S(1)}, u32[]{:S(2)}, u32[]{:S(2)}) collective-permute-start(bf16[512,512]{0,1:T(8,128)(2,1)S(1)} %bitcast.96), channel_id=1, source_target_pairs={{0,3},{1,0},{2,1},{3,2},{4,7},{5,4},{6,5},{7,6},{8,11},{9,8},{10,9... | collective-permute-start | bytes 1572872 | tf_op jit(solution)/shard_map/ppermute | solution.py:53
  71.9 25.7 %collective-permute-start.3 = (bf16[512,512]{0,1:T(8,128)(2,1)S(1)}, bf16[512,512]{0,1:T(8,128)(2,1)S(1)}, u32[]{:S(2)}, u32[]{:S(2)}) collective-permute-start(bf16[512,512]{0,1:T(8,128)(2,1)S(1)} %collective-permute-done), channel_id=1, source_target_pairs={{0,1},{1,2},{2,3},{3,0},{4,5},{5,6},{6,7},{7,4},{8,9},{9,10},{10,1... | collective-permute-start | bytes 1572872 | tf_op jit(solution)/shard_map/ppermute | solution.py:54
  71.9 25.0 %collective-permute-start.4 = (bf16[512,512]{0,1:T(8,128)(2,1)S(1)}, bf16[512,512]{0,1:T(8,128)(2,1)S(1)}, u32[]{:S(2)}, u32[]{:S(2)}) collective-permute-start(bf16[512,512]{0,1:T(8,128)(2,1)S(1)} %bitcast.93), channel_id=1, source_target_pairs={{0,1},{1,2},{2,3},{3,0},{4,5},{5,6},{6,7},{7,4},{8,9},{9,10},{10,1... | collective-permute-start | bytes 1572872 | tf_op jit(solution)/shard_map/ppermute | solution.py:52
  71.9 26.5 %collective-permute-start.5 = (bf16[512,512]{0,1:T(8,128)(2,1)S(1)}, bf16[512,512]{0,1:T(8,128)(2,1)S(1)}, u32[]{:S(2)}, u32[]{:S(2)}) collective-permute-start(bf16[512,512]{0,1:T(8,128)(2,1)S(1)} %collective-permute-done.1), channel_id=1, source_target_pairs={{0,3},{1,0},{2,1},{3,2},{4,7},{5,4},{6,5},{7,6},{8,11},{9,8},{10,9... | collective-permute-start | bytes 1572872 | tf_op jit(solution)/shard_map/ppermute | solution.py:55

commit v4 on v3

--- a/solution.py
+++ b/solution.py
@@ -13,21 +13,23 @@
 def carried_in(local_sum, final_seg, axis):
     count = lax.axis_size(axis)
     shape = local_sum.shape
-    flat = local_sum.reshape(count, -1)
-    width = flat.shape[1]
-    seg_row = jnp.full((count, HEAD), final_seg.astype(jnp.float32))
-    sent = jnp.concatenate([flat, seg_row], axis=1)
+    tile = local_sum.size // (count * HEAD)
+    flat = local_sum.reshape(count, tile, HEAD)
+    seg_rows = jnp.full((count, 8, HEAD), final_seg.astype(jnp.float32))
+    sent = jnp.concatenate([flat, seg_rows], axis=1)
     pieces = lax.all_to_all(sent, axis, 0, 0, tiled=True)
-    sums = pieces[:, :width]
-    segs = pieces[:, width]
+    sums = pieces[:, :tile]
+    segs = pieces[:, tile, 0]
     block = jnp.arange(count)
     prev_seg = jnp.concatenate([jnp.full((1,), -1.0, jnp.float32), segs[:-1]])
     mask = (block[None, :] < block[:, None]) & (segs[None, :] == prev_seg[:, None])
-    carry = jnp.sum(jnp.where(mask[:, :, None], sums[None, :, :], 0.0), axis=1)
-    back = jnp.concatenate([carry, jnp.broadcast_to(prev_seg[:, None], (count, HEAD))], axis=1)
+    carry = jnp.sum(jnp.where(mask[:, :, None, None], sums[None], 0.0), axis=1)
+    back = jnp.concatenate(
+        [carry, jnp.broadcast_to(prev_seg[:, None, None], (count, 8, HEAD))], axis=1
+    )
     mine = lax.all_to_all(back, axis, 0, 0, tiled=True)
-    before_sum = mine[:, :width].reshape(shape)
-    before_seg = mine[0, width]
+    before_sum = mine[:, :tile].reshape(shape)
+    before_seg = mine[0, tile, 0]
     return before_sum, before_seg
 
 
@@ -53,11 +55,11 @@
     right_top = lax.ppermute(top_later, axis, behind)
     far_top = lax.ppermute(left_top, axis, ahead)
     far_bottom = lax.ppermute(right_bottom, axis, behind)
-    out_top = part(top, 0) + part(left_top, -1) + part(right_top, 1) + part(far_top, 2)
-    out_bottom = (
-        part(bottom, 0) + part(right_bottom, 1) + part(left_bottom, -1) + part(far_bottom, 2)
-    )
-    return jnp.concatenate([out_top, out_bottom], axis=0)
+    own = jnp.concatenate([part(top, 0), part(bottom, 0)], axis=0)
+    left = jnp.concatenate([part(left_top, -1), part(left_bottom, -1)], axis=0)
+    right = jnp.concatenate([part(right_top, 1), part(right_bottom, 1)], axis=0)
+    far = jnp.concatenate([part(far_top, 2), part(far_bottom, 2)], axis=0)
+    return own + left + right + far
 
 
 def per_device(queries, keys, values, segment_ids, norm_gain, out_weight):

time: 101 us -> 106 us (1.050)
  waiting for transfers between devices: 45.5 us -> 48.6 us
  other arithmetic: 8.56 us -> 10.1 us
    ppermute x1, waiting for transfers between devices: 0.01 us -> 17.5 us  [project_gathered(): far_bottom = lax.ppermute(right_bottom, axis, behind)]
    ppermute x1, waiting for transfers between devices: 13.6 us -> 0.01 us  [project_gathered(): left_bottom = lax.ppermute(bottom_later, axis, ahead)]
    ppermute x1, waiting for transfers between devices: 0.01 us -> 10.2 us  [project_gathered(): right_bottom = lax.ppermute(bottom, axis, behind)]
    ppermute x1, waiting for transfers between devices: 10.9 us -> 3.35 us  [project_gathered(): left_top = lax.ppermute(top, axis, ahead)]
    ppermute x1, waiting for transfers between devices: 6.51 us -> 0.01 us  [project_gathered(): right_top = lax.ppermute(top_later, axis, behind)]
    convert_element_type x0 -> x1, other arithmetic: none -> 2.72 us  [per_device(): return project_gathered(hidden, out_weight, 'mp').astype(jnp.bfloat16)]
    all_to_all x2 -> x0, local copies, waits for them, and re-layouts: 1.88 us -> none  [the longest x1 0.99 us: carried_in(): mine = lax.all_to_all(back, axis, 0, 0, tiled=True)]
    all_to_all x1, waiting for transfers between devices: 4.2 us -> 5.73 us  [carried_in(): mine = lax.all_to_all(back, axis, 0, 0, tiled=True)]
  transfers between devices with their start and end apart: 8 -> 8, of which waited for: 5 -> 6; matrix products, arithmetic and copies ran while one was open for 14% -> 13% of each run, Pallas kernels for 0% -> 0%
where the time goes in v4:
time: 106 us; the launch traced here: 105 us
  waiting for transfers between devices  48.6 us (46%)
  starting transfers between devices  21.6 us (20%)
  matrix products  17.3 us (16%)
  other arithmetic  10.1 us (10%)
  local copies, waits for them, and re-layouts  6.29 us (6%)
    ppermute x1, waiting for transfers between devices, project_gathered(): far_bottom = lax.ppermute(right_bottom, axis, behind)  17.5 us
    all_to_all x1, waiting for transfers between devices, carried_in(): pieces = lax.all_to_all(sent, axis, 0, 0, tiled=True)  11.5 us
    ppermute x1, waiting for transfers between devices, project_gathered(): right_bottom = lax.ppermute(bottom, axis, behind)  10.2 us
    all_to_all x1, starting transfers between devices, carried_in(): pieces = lax.all_to_all(sent, axis, 0, 0, tiled=True)  9.97 us
    dot_general x1, matrix products, per_device(): jnp.einsum('hts,she->the', weights, value_heads, preferred_element_type=j...  6.93 us
    dot_general x8, matrix products, part(): jnp.dot(block, weight_groups[group], preferred_element_type=jnp.float32)  5.95 us
    all_to_all x1, waiting for transfers between devices, carried_in(): mine = lax.all_to_all(back, axis, 0, 0, tiled=True)  5.73 us
    all_to_all x1, starting transfers between devices, carried_in(): mine = lax.all_to_all(back, axis, 0, 0, tiled=True)  3.44 us
  transfers between devices with their start and end apart: 8, of which 6 were waited for; matrix products, arithmetic and copies ran while one was open for 13% of the time, Pallas kernels for 0%

profile of v4, /device:TPU:1, one launch (start us, length us, event | category | flops | bytes accessed | tf_op | source)
XLA Modules:
  0.0 104.8 jit_solution(9330983917759182413)
XLA Ops:
  0.0 1.4 %slice.34 = s32[1]{0:T(128)} slice(s32[1024]{0:T(1024)} %param.9), slice={[1023:1024]} | slice | bytes 8 | tf_op jit(solution)/shard_map/slice | solution.py:72
  2.0 1.3 %compare_convert_fusion = bf16[1024]{0:T(1024)(128)(2,1)S(1)} fusion(s32[1024]{0:T(1024)} %param.9, s32[]{:T(128)} %bitcast.1), kind=kLoop, calls=%fused_computation.72 | loop fusion | flops 2048 | bytes 6148 | tf_op jit(solution)/shard_map/convert_element_type | solution.py:73
  3.3 2.2 %fusion.9 = bf16[1024,512]{1,0:T(8,128)(2,1)S(1)} fusion(bf16[1024,512]{1,0:T(8,128)(2,1)} %param.7), kind=kLoop, calls=%fused_computation.17 | loop fusion | flops 3145728 | bytes 2097152 | tf_op jit(solution)/shard_map/convert_element_type | solution.py:10
  6.5 0.8 concatenate.21
  7.3 10.0 %all-to-all-start = ((f32[16,40,128]{2,1,0:T(8,128)}), f32[16,40,128]{2,1,0:T(8,128)S(1)}, u32[]{:S(2)}, u32[]{:S(2)}) async-start(f32[16,40,128]{2,1,0:T(8,128)} %concatenate.21), calls=%async_computation | async-start | bytes 655360 | tf_op jit(solution)/shard_map/all_to_all | solution.py:20
  17.3 1.6 %fusion.3 = pred[1024,1024]{1,0:T(8,128)(4,1)} fusion(s32[1024]{0:T(1024)S(1)} %copy-done.5), kind=kLoop, calls=%fused_computation.11 | loop fusion | flops 3145728 | bytes 1052672 | tf_op jit(solution)/shard_map/and | solution.py:82
  18.8 11.5 %all-to-all-done = f32[16,40,128]{2,1,0:T(8,128)S(1)} async-done(((f32[16,40,128]{2,1,0:T(8,128)}), f32[16,40,128]{2,1,0:T(8,128)S(1)}, u32[]{:S(2)}, u32[]{:S(2)}) %all-to-all-start) | async-done | bytes 327712 | tf_op jit(solution)/shard_map/all_to_all | solution.py:20
  31.5 0.8 pad_maximum_fusion
  32.3 3.4 %all-to-all-start.1 = ((f32[16,40,128]{2,1,0:T(8,128)}), f32[16,40,128]{2,1,0:T(8,128)S(1)}, u32[]{:S(2)}, u32[]{:S(2)}) async-start(f32[16,40,128]{2,1,0:T(8,128)} %pad_maximum_fusion), calls=%async_computation.1 | async-start | bytes 655360 | tf_op jit(solution)/shard_map/all_to_all | solution.py:30
  35.8 6.9 %fusion.10 = f32[4,1024,128]{1,2,0:T(8,128)S(1)} fusion(bf16[1024,4,128]{0,2,1:T(8,128)(2,1)} %bitcast.88, pred[1024,1024]{1,0:T(8,128)(4,1)} %fusion.3, bf16[1024,512]{1,0:T(8,128)(2,1)S(1)} %copy-done, bf16[1024,512]{1,0:T(8,128)(2,1)} %param.6), kind=kOutput, calls=%fused_computation.21 | convolution fusion | flops 2159017984 | bytes 6291456 | tf_op jit(solution)/shard_map/hts,she->the/dot_general | solution.py:87
  42.7 5.7 %all-to-all-done.1 = f32[16,40,128]{2,1,0:T(8,128)S(1)} async-done(((f32[16,40,128]{2,1,0:T(8,128)}), f32[16,40,128]{2,1,0:T(8,128)S(1)}, u32[]{:S(2)}, u32[]{:S(2)}) %all-to-all-start.1) | async-done | bytes 327712 | tf_op jit(solution)/shard_map/all_to_all | solution.py:30
  49.2 1.8 %copy.46 = f32[4,128,128]{1,2,0:T(8,128)} copy(f32[4,128,128]{2,1,0:T(8,128)} %bitcast.89) | data formatting | bytes 524288 | tf_op jit(solution)/shard_map/reshape | solution.py:31
  52.1 2.6 %fusion.16 = f32[4,128,1024]{2,1,0:T(8,128)S(1)} fusion(f32[4,128,128]{1,2,0:T(8,128)} %copy.46, bf16[1024,512]{1,0:T(8,128)(2,1)} %param.6), kind=kOutput, calls=%fused_computation.27 | convolution fusion | flops 137428992 | bytes 3407872 | tf_op jit(solution)/shard_map/thd,hde->the/dot_general | solution.py:90
  54.7 1.5 %multiply_reduce_fusion = (f32[1024,4]{0,1:T(4,128)S(1)}, f32[1024,4,128]{0,2,1:T(8,128)S(1)}) fusion(f32[4,128,1024]{2,1,0:T(8,128)S(1)} %fusion.16, f32[4,128,128]{1,2,0:T(8,128)S(1)} %copy-done.3, f32[1024]{0:T(1024)S(1)} %fusion.55, f32[4,1024,128]{1,2,0:T(8,128)S(1)} %fusion.10, bf16[1024,512]{1,0:T(8,128)(2,1)S(1)} %copy-done.2), kind=kOutput, calls=%fused_computation.20 | convolution fusion | flops 140242944 | bytes 7622656 | tf_op jit(solution)/shard_map/thd,hde->the/dot_general | solution.py:92
  56.6 2.8 %collective-permute-start.1 = (bf16[512,512]{0,1:T(8,128)(2,1)S(1)}, bf16[512,512]{0,1:T(8,128)(2,1)S(1)}, u32[]{:S(2)}, u32[]{:S(2)}) collective-permute-start(bf16[512,512]{0,1:T(8,128)(2,1)S(1)} %bitcast.81), channel_id=1, source_target_pairs={{0,3},{1,0},{2,1},{3,2},{4,7},{5,4},{6,5},{7,6},{8,11},{9,8},{10,9... | collective-permute-start | bytes 1572872 | tf_op jit(solution)/shard_map/ppermute | solution.py:50
  60.2 0.8 fusion.34
  60.9 10.2 %collective-permute-done.1 = bf16[512,512]{0,1:T(8,128)(2,1)S(1)} collective-permute-done((bf16[512,512]{0,1:T(8,128)(2,1)S(1)}, bf16[512,512]{0,1:T(8,128)(2,1)S(1)}, u32[]{:S(2)}, u32[]{:S(2)}) %collective-permute-start.1) | collective-permute-done | bytes 524320 | tf_op jit(solution)/shard_map/ppermute | solution.py:50
  71.1 3.4 %collective-permute-done = bf16[512,512]{0,1:T(8,128)(2,1)S(1)} collective-permute-done((bf16[512,512]{0,1:T(8,128)(2,1)S(1)}, bf16[512,512]{0,1:T(8,128)(2,1)S(1)}, u32[]{:S(2)}, u32[]{:S(2)}) %collective-permute-start) | collective-permute-done | bytes 524320 | tf_op jit(solution)/shard_map/ppermute | solution.py:49
  74.4 2.7 %collective-permute-start.3 = (bf16[512,512]{0,1:T(8,128)(2,1)S(1)}, bf16[512,512]{0,1:T(8,128)(2,1)S(1)}, u32[]{:S(2)}, u32[]{:S(2)}) collective-permute-start(bf16[512,512]{0,1:T(8,128)(2,1)S(1)} %bitcast.86), channel_id=1, source_target_pairs={{0,3},{1,0},{2,1},{3,2},{4,7},{5,4},{6,5},{7,6},{8,11},{9,8},{10,9... | collective-permute-start | bytes 1572872 | tf_op jit(solution)/shard_map/ppermute | solution.py:55
  77.1 2.7 %collective-permute-start.5 = (bf16[512,512]{0,1:T(8,128)(2,1)S(1)}, bf16[512,512]{0,1:T(8,128)(2,1)S(1)}, u32[]{:S(2)}, u32[]{:S(2)}) collective-permute-start(bf16[512,512]{0,1:T(8,128)(2,1)S(1)} %collective-permute-done.1), channel_id=1, source_target_pairs={{0,3},{1,0},{2,1},{3,2},{4,7},{5,4},{6,5},{7,6},{8,11},{9,8},{10,9... | collective-permute-start | bytes 1572872 | tf_op jit(solution)/shard_map/ppermute | solution.py:57
  80.5 0.8 fusion.30
  81.3 17.5 %collective-permute-done.5 = bf16[512,512]{0,1:T(8,128)(2,1)S(1)} collective-permute-done((bf16[512,512]{0,1:T(8,128)(2,1)S(1)}, bf16[512,512]{0,1:T(8,128)(2,1)S(1)}, u32[]{:S(2)}, u32[]{:S(2)}) %collective-permute-start.5) | collective-permute-done | bytes 524320 | tf_op jit(solution)/shard_map/ppermute | solution.py:57
  101.3 0.8 fusion.28
  102.1 2.7 %fusion.2 = bf16[1024,1024]{1,0:T(8,128)(2,1)} fusion(f32[512,1024]{1,0:T(8,128)S(1)} %fusion.32, f32[512,1024]{1,0:T(8,128)S(1)} %fusion.34, f32[512,1024]{1,0:T(8,128)S(1)} %fusion.28, f32[512,1024]{1,0:T(8,128)S(1)} %fusion.30, f32[512,1024]{1,0:T(8,128)S(1)} %fusion.24, f32[512,1024]{1,0:T(8,128)S(1)} %fusion.26, f32[512,1024]{1,0:T(8,128)S(1)} %fusion.20, ...), kind=kLoop, calls=%fused_computation.8 | loop fusion | flops 8388608 | bytes 18874368 | tf_op jit(solution)/shard_map/convert_element_type | solution.py:98
  (40 shorter events, 8.5 us)
Async XLA Ops:
  0.0 6.1 %copy-start = (bf16[1024,512]{1,0:T(8,128)(2,1)S(1)}, bf16[1024,512]{1,0:T(8,128)(2,1)}, u32[]{:S(2)}) copy-start(bf16[1024,512]{1,0:T(8,128)(2,1)} %param.8) | copy-start | bytes 3145732
  6.0 1.2 %copy-start.4 = (bf16[1024,512]{0,1:T(8,128)(2,1)}, bf16[1024,512]{0,1:T(8,128)(2,1)S(1)}, u32[]{:S(2)}) copy-start(bf16[1024,512]{0,1:T(8,128)(2,1)S(1)} %copy.50) | copy-start | bytes 3145732
  6.1 11.2 %copy-start.5 = (s32[1024]{0:T(1024)S(1)}, s32[1024]{0:T(1024)}, u32[]{:S(2)}) copy-start(s32[1024]{0:T(1024)} %param.9) | copy-start | bytes 12292
  7.3 23.0 %all-to-all-start = ((f32[16,40,128]{2,1,0:T(8,128)}), f32[16,40,128]{2,1,0:T(8,128)S(1)}, u32[]{:S(2)}, u32[]{:S(2)}) async-start(f32[16,40,128]{2,1,0:T(8,128)} %concatenate.21), calls=%async_computation | async-start | bytes 655360 | tf_op jit(solution)/shard_map/all_to_all | solution.py:20
  32.3 16.1 %all-to-all-start.1 = ((f32[16,40,128]{2,1,0:T(8,128)}), f32[16,40,128]{2,1,0:T(8,128)S(1)}, u32[]{:S(2)}, u32[]{:S(2)}) async-start(f32[16,40,128]{2,1,0:T(8,128)} %pad_maximum_fusion), calls=%async_computation.1 | async-start | bytes 655360 | tf_op jit(solution)/shard_map/all_to_all | solution.py:30
  52.1 2.6 %copy-start.2 = (bf16[1024,512]{1,0:T(8,128)(2,1)S(1)}, bf16[1024,512]{1,0:T(8,128)(2,1)}, u32[]{:S(2)}) copy-start(bf16[1024,512]{1,0:T(8,128)(2,1)} %param.6) | copy-start | bytes 3145732
  52.1 2.6 %copy-start.3 = (f32[4,128,128]{1,2,0:T(8,128)S(1)}, f32[4,128,128]{1,2,0:T(8,128)}, u32[]{:S(2)}) copy-start(f32[4,128,128]{1,2,0:T(8,128)} %copy.46) | copy-start | bytes 786436
  54.7 1.5 %copy-start.6 = (f32[512]{0:T(512)S(1)}, f32[512]{0:T(512)}, u32[]{:S(2)}) copy-start(f32[512]{0:T(512)} %param.10) | copy-start | bytes 6148
  56.2 3.2 %copy-start.1 = (bf16[2048,1024]{1,0:T(8,128)(2,1)S(1)}, bf16[2048,1024]{1,0:T(8,128)(2,1)}, u32[]{:S(2)}) copy-start(bf16[2048,1024]{1,0:T(8,128)(2,1)} %param.11) | copy-start | bytes 12582916
  56.6 14.5 %collective-permute-start.1 = (bf16[512,512]{0,1:T(8,128)(2,1)S(1)}, bf16[512,512]{0,1:T(8,128)(2,1)S(1)}, u32[]{:S(2)}, u32[]{:S(2)}) collective-permute-start(bf16[512,512]{0,1:T(8,128)(2,1)S(1)} %bitcast.81), channel_id=1, source_target_pairs={{0,3},{1,0},{2,1},{3,2},{4,7},{5,4},{6,5},{7,6},{8,11},{9,8},{10,9... | collective-permute-start | bytes 1572872 | tf_op jit(solution)/shard_map/ppermute | solution.py:50
  59.4 15.0 %collective-permute-start = (bf16[512,512]{0,1:T(8,128)(2,1)S(1)}, bf16[512,512]{0,1:T(8,128)(2,1)S(1)}, u32[]{:S(2)}, u32[]{:S(2)}) collective-permute-start(bf16[512,512]{0,1:T(8,128)(2,1)S(1)} %bitcast.84), channel_id=1, source_target_pairs={{0,1},{1,2},{2,3},{3,0},{4,5},{5,6},{6,7},{7,4},{8,9},{9,10},{10,1... | collective-permute-start | bytes 1572872 | tf_op jit(solution)/shard_map/ppermute | solution.py:49
  74.4 26.9 %collective-permute-start.2 = (bf16[512,512]{0,1:T(8,128)(2,1)S(1)}, bf16[512,512]{0,1:T(8,128)(2,1)S(1)}, u32[]{:S(2)}, u32[]{:S(2)}) collective-permute-start(bf16[512,512]{0,1:T(8,128)(2,1)S(1)} %bitcast.83), channel_id=1, source_target_pairs={{0,1},{1,2},{2,3},{3,0},{4,5},{5,6},{6,7},{7,4},{8,9},{9,10},{10,1... | collective-permute-start | bytes 1572872 | tf_op jit(solution)/shard_map/ppermute | solution.py:54
  74.4 26.1 %collective-permute-start.3 = (bf16[512,512]{0,1:T(8,128)(2,1)S(1)}, bf16[512,512]{0,1:T(8,128)(2,1)S(1)}, u32[]{:S(2)}, u32[]{:S(2)}) collective-permute-start(bf16[512,512]{0,1:T(8,128)(2,1)S(1)} %bitcast.86), channel_id=1, source_target_pairs={{0,3},{1,0},{2,1},{3,2},{4,7},{5,4},{6,5},{7,6},{8,11},{9,8},{10,9... | collective-permute-start | bytes 1572872 | tf_op jit(solution)/shard_map/ppermute | solution.py:55
  77.1 22.7 %collective-permute-start.4 = (bf16[512,512]{0,1:T(8,128)(2,1)S(1)}, bf16[512,512]{0,1:T(8,128)(2,1)S(1)}, u32[]{:S(2)}, u32[]{:S(2)}) collective-permute-start(bf16[512,512]{0,1:T(8,128)(2,1)S(1)} %collective-permute-done), channel_id=1, source_target_pairs={{0,1},{1,2},{2,3},{3,0},{4,5},{5,6},{6,7},{7,4},{8,9},{9,10},{10,1... | collective-permute-start | bytes 1572872 | tf_op jit(solution)/shard_map/ppermute | solution.py:56
  77.1 21.7 %collective-permute-start.5 = (bf16[512,512]{0,1:T(8,128)(2,1)S(1)}, bf16[512,512]{0,1:T(8,128)(2,1)S(1)}, u32[]{:S(2)}, u32[]{:S(2)}) collective-permute-start(bf16[512,512]{0,1:T(8,128)(2,1)S(1)} %collective-permute-done.1), channel_id=1, source_target_pairs={{0,3},{1,0},{2,1},{3,2},{4,7},{5,4},{6,5},{7,6},{8,11},{9,8},{10,9... | collective-permute-start | bytes 1572872 | tf_op jit(solution)/shard_map/ppermute | solution.py:57

commit v5 on v4

--- a/solution.py
+++ b/solution.py
@@ -10,14 +10,27 @@
     return (jax.nn.elu(raw_input.astype(jnp.float32)) + 1.0).astype(jnp.bfloat16)
 
 
-def carried_in(local_sum, final_seg, axis):
-    count = lax.axis_size(axis)
+def join(early_sum, early_seg, later_sum, later_seg):
+    return later_sum + jnp.where(early_seg == later_seg, early_sum, 0.0)
+
+
+def carried_in(local_sum, final_seg, chips, cores):
+    count = lax.axis_size(chips)
+    core = lax.axis_index(cores)
     shape = local_sum.shape
-    tile = local_sum.size // (count * HEAD)
-    flat = local_sum.reshape(count, tile, HEAD)
-    seg_rows = jnp.full((count, 8, HEAD), final_seg.astype(jnp.float32))
-    sent = jnp.concatenate([flat, seg_rows], axis=1)
-    pieces = lax.all_to_all(sent, axis, 0, 0, tiled=True)
+    flat = local_sum.reshape(2, -1, HEAD)
+    seg = final_seg.astype(jnp.float32)
+    swap = [(0, 1), (1, 0)]
+    other_sum, other_seg = lax.ppermute((flat, seg), cores, swap)
+    first_sum = jnp.where(core == 0, flat, other_sum)
+    first_seg = jnp.where(core == 0, seg, other_seg)
+    last_sum = jnp.where(core == 0, other_sum, flat)
+    last_seg = jnp.where(core == 0, other_seg, seg)
+    chip_sum = join(first_sum, first_seg, last_sum, last_seg)[core]
+    tile = chip_sum.shape[0] // count
+    seg_rows = jnp.full((count, 8, HEAD), last_seg)
+    sent = jnp.concatenate([chip_sum.reshape(count, tile, HEAD), seg_rows], axis=1)
+    pieces = lax.all_to_all(sent, chips, 0, 0, tiled=True)
     sums = pieces[:, :tile]
     segs = pieces[:, tile, 0]
     block = jnp.arange(count)
@@ -27,9 +40,19 @@
     back = jnp.concatenate(
         [carry, jnp.broadcast_to(prev_seg[:, None, None], (count, 8, HEAD))], axis=1
     )
-    mine = lax.all_to_all(back, axis, 0, 0, tiled=True)
-    before_sum = mine[:, :tile].reshape(shape)
-    before_seg = mine[0, tile, 0]
+    mine = lax.all_to_all(back, chips, 0, 0, tiled=True)
+    half_sum = mine[:, :tile].reshape(-1, HEAD)
+    chip_seg = mine[0, tile, 0]
+    other_half = lax.ppermute(half_sum, cores, swap)
+    before_chip = jnp.where(
+        core == 0,
+        jnp.stack([half_sum, other_half]),
+        jnp.stack([other_half, half_sum]),
+    )
+    before_sum = jnp.where(
+        core == 0, before_chip, join(before_chip, chip_seg, first_sum, first_seg)
+    ).reshape(shape)
+    before_seg = jnp.where(core == 0, chip_seg, first_seg)
     return before_sum, before_seg
 
 
@@ -55,11 +78,11 @@
     right_top = lax.ppermute(top_later, axis, behind)
     far_top = lax.ppermute(left_top, axis, ahead)
     far_bottom = lax.ppermute(right_bottom, axis, behind)
-    own = jnp.concatenate([part(top, 0), part(bottom, 0)], axis=0)
-    left = jnp.concatenate([part(left_top, -1), part(left_bottom, -1)], axis=0)
-    right = jnp.concatenate([part(right_top, 1), part(right_bottom, 1)], axis=0)
-    far = jnp.concatenate([part(far_top, 2), part(far_bottom, 2)], axis=0)
-    return own + left + right + far
+    out_top = part(top, 0) + part(left_top, -1) + part(right_top, 1) + part(far_top, 2)
+    out_bottom = (
+        part(bottom, 0) + part(right_bottom, 1) + part(left_bottom, -1) + part(far_bottom, 2)
+    )
+    return jnp.concatenate([out_top, out_bottom], axis=0)
 
 
 def per_device(queries, keys, values, segment_ids, norm_gain, out_weight):
@@ -77,7 +100,7 @@
         value_heads,
         preferred_element_type=jnp.float32,
     )
-    before_sum, before_seg = carried_in(local_sum, final_seg, "ctx")
+    before_sum, before_seg = carried_in(local_sum, final_seg, "cz", "cc")
     position = jnp.arange(rows_here)
     allowed = (position[None, :] <= position[:, None]) & (
         segment_ids[:, None] == segment_ids[None, :]
@@ -99,15 +122,20 @@
 
 
 def solution(mesh):
+    dp, ctx, mp = (mesh.shape[name] for name in ("dp", "ctx", "mp"))
+    split = jax.sharding.Mesh(
+        mesh.devices.reshape(dp, ctx // 2, 2, mp), ("dp", "cz", "cc", "mp")
+    )
+    rows = ("dp", "cz", "cc")
     in_specs = (
-        P(("dp", "ctx"), "mp"),
-        P(("dp", "ctx"), "mp"),
-        P(("dp", "ctx"), "mp"),
-        P(("dp", "ctx")),
+        P(rows, "mp"),
+        P(rows, "mp"),
+        P(rows, "mp"),
+        P(rows),
         P("mp"),
         P(None, "mp"),
     )
-    out_specs = P(("dp", "ctx"), "mp")
+    out_specs = P(rows, "mp")
     return jax.shard_map(
-        per_device, mesh=mesh, in_specs=in_specs, out_specs=out_specs, check_vma=False
+        per_device, mesh=split, in_specs=in_specs, out_specs=out_specs, check_vma=False
     )

time: 106 us -> 100 us (0.943)
  waiting for transfers between devices: 48.6 us -> 39.5 us
  starting transfers between devices: 21.6 us -> 26.1 us
  other arithmetic: 10.1 us -> 7.24 us
  between operations: 0.88 us -> 3.49 us
  local copies, waits for them, and re-layouts: 6.29 us -> 5.17 us
    ppermute x1, waiting for transfers between devices: 17.5 us -> 0.01 us  [project_gathered(): far_bottom = lax.ppermute(right_bottom, axis, behind)]
    ppermute x1, waiting for transfers between devices: 0.01 us -> 13.6 us  [project_gathered(): left_bottom = lax.ppermute(bottom_later, axis, ahead)]
    ppermute x1, waiting for transfers between devices: 10.2 us -> 0.01 us  [project_gathered(): right_bottom = lax.ppermute(bottom, axis, behind)]
    all_to_all x2, waiting for transfers between devices: 17.2 us -> 8.73 us  [the longest x1 7.39 us: carried_in(): pieces = lax.all_to_all(sent, chips, 0, 0, tiled=True)]
    ppermute x0 -> x3, starting transfers between devices: none -> 7.54 us  [the longest x2 4.37 us: carried_in(): other_sum, other_seg = lax.ppermute((flat, seg), cores, swap)]
    ppermute x1, waiting for transfers between devices: 3.35 us -> 10.2 us  [project_gathered(): left_top = lax.ppermute(top, axis, ahead)]
    ppermute x1, waiting for transfers between devices: 0.01 us -> 5.7 us  [project_gathered(): right_top = lax.ppermute(top_later, axis, behind)]
    all_to_all x2, starting transfers between devices: 13.4 us -> 10.5 us  [the longest x1 6.45 us: carried_in(): pieces = lax.all_to_all(sent, chips, 0, 0, tiled=True)]
  transfers between devices with their start and end apart: 8 -> 11, of which waited for: 6 -> 7; matrix products, arithmetic and copies ran while one was open for 13% -> 14% of each run, Pallas kernels for 0% -> 0%
where the time goes in v5:
time: 100 us; the launch traced here: 98.6 us
  waiting for transfers between devices  39.5 us (40%)
  starting transfers between devices  26.1 us (26%)
  matrix products  17 us (17%)
  other arithmetic  7.24 us (7%)
  local copies, waits for them, and re-layouts  5.17 us (5%)
  between operations  3.49 us (3%)
    ppermute x1, waiting for transfers between devices, project_gathered(): left_bottom = lax.ppermute(bottom_later, axis, ahead)  13.6 us
    ppermute x1, waiting for transfers between devices, project_gathered(): left_top = lax.ppermute(top, axis, ahead)  10.2 us
    all_to_all x1, waiting for transfers between devices, carried_in(): pieces = lax.all_to_all(sent, chips, 0, 0, tiled=True)  7.39 us
    dot_general x1, matrix products, per_device(): jnp.einsum('hts,she->the', weights, value_heads, preferred_element_type=j...  6.93 us
    all_to_all x1, starting transfers between devices, carried_in(): pieces = lax.all_to_all(sent, chips, 0, 0, tiled=True)  6.45 us
    dot_general x8, matrix products, part(): jnp.dot(block, weight_groups[group], preferred_element_type=jnp.float32)  5.84 us
    ppermute x1, waiting for transfers between devices, project_gathered(): right_top = lax.ppermute(top_later, axis, behind)  5.7 us
    ppermute x2, starting transfers between devices, carried_in(): other_sum, other_seg = lax.ppermute((flat, seg), cores, swap)  4.37 us
  transfers between devices with their start and end apart: 11, of which 7 were waited for; matrix products, arithmetic and copies ran while one was open for 14% of the time, Pallas kernels for 0%

profile of v5, /device:TPU:1, one launch (start us, length us, event | category | flops | bytes accessed | tf_op | source)
XLA Modules:
  0.0 98.6 jit_solution(8860697933532614960)
XLA Ops:
  0.0 1.4 %slice.34 = s32[1]{0:T(128)} slice(s32[1024]{0:T(1024)} %param.9), slice={[1023:1024]} | slice | bytes 8 | tf_op jit(solution)/shard_map/slice | solution.py:95
  1.4 2.2 %fusion.6 = bf16[1024,512]{1,0:T(8,128)(2,1)S(1)} fusion(bf16[1024,512]{1,0:T(8,128)(2,1)} %param.7), kind=kLoop, calls=%fused_computation.12 | loop fusion | flops 3145728 | bytes 2097152 | tf_op jit(solution)/shard_map/convert_element_type | solution.py:10
  5.2 3.3 %collective-permute-start = (f32[2,256,128]{2,1,0:T(8,128)S(1)}, f32[2,256,128]{2,1,0:T(8,128)S(1)}, u32[]{:S(2)}, u32[]{:S(2)}) collective-permute-start(f32[2,256,128]{2,1,0:T(8,128)S(1)} %bitcast.101), channel_id=1, source_target_pairs={{0,4},{4,0},{1,5},{5,1},{2,6},{6,2},{3,7},{7,3},{8,12},{12,8},{9,1... | collective-permute-start | bytes 786440 | tf_op jit(solution)/shard_map/ppermute | solution.py:24
  9.2 1.0 %collective-permute-start.1 = (f32[]{:T(128)}, f32[]{:T(128)}, u32[]{:S(2)}, u32[]{:S(2)}) collective-permute-start(f32[]{:T(128)} %convert_element_type.47), channel_id=1, source_target_pairs={{0,4},{4,0},{1,5},{5,1},{2,6},{6,2},{3,7},{7,3},{8,12},{12,8},{9,1... | collective-permute-start | bytes 20 | tf_op jit(solution)/shard_map/ppermute | solution.py:24
  12.6 6.5 %all-to-all-start = ((f32[8,40,128]{2,1,0:T(8,128)}), f32[8,40,128]{2,1,0:T(8,128)S(1)}, u32[]{:S(2)}, u32[]{:S(2)}) async-start(f32[8,40,128]{2,1,0:T(8,128)} %concatenate.13), calls=%async_computation | async-start | bytes 327680 | tf_op jit(solution)/shard_map/all_to_all | solution.py:33
  19.0 1.6 %fusion = pred[1024,1024]{1,0:T(8,128)(4,1)} fusion(s32[1024]{0:T(1024)S(1)} %copy-done.4), kind=kLoop, calls=%fused_computation.6 | loop fusion | flops 3145728 | bytes 1052672 | tf_op jit(solution)/shard_map/and | solution.py:105
  20.6 7.4 %all-to-all-done = f32[8,40,128]{2,1,0:T(8,128)S(1)} async-done(((f32[8,40,128]{2,1,0:T(8,128)}), f32[8,40,128]{2,1,0:T(8,128)S(1)}, u32[]{:S(2)}, u32[]{:S(2)}) %all-to-all-start) | async-done | bytes 163872 | tf_op jit(solution)/shard_map/all_to_all | solution.py:33
  29.4 4.0 %all-to-all-start.1 = ((f32[8,40,128]{2,1,0:T(8,128)}), f32[8,40,128]{2,1,0:T(8,128)}, u32[]{:S(2)}, u32[]{:S(2)}) async-start(f32[8,40,128]{2,1,0:T(8,128)} %pad_maximum_fusion.1), calls=%async_computation.1 | async-start | bytes 327680 | tf_op jit(solution)/shard_map/all_to_all | solution.py:43
  33.4 6.9 %fusion.7 = f32[4,1024,128]{1,2,0:T(8,128)S(1)} fusion(bf16[1024,4,128]{0,2,1:T(8,128)(2,1)} %bitcast.100, pred[1024,1024]{1,0:T(8,128)(4,1)} %fusion, bf16[1024,512]{1,0:T(8,128)(2,1)S(1)} %copy-done, bf16[1024,512]{1,0:T(8,128)(2,1)} %param.6), kind=kOutput, calls=%fused_computation.19 | convolution fusion | flops 2159017984 | bytes 6291456 | tf_op jit(solution)/shard_map/hts,she->the/dot_general | solution.py:110
  40.3 1.3 %all-to-all-done.1 = f32[8,40,128]{2,1,0:T(8,128)} async-done(((f32[8,40,128]{2,1,0:T(8,128)}), f32[8,40,128]{2,1,0:T(8,128)}, u32[]{:S(2)}, u32[]{:S(2)}) %all-to-all-start.1) | async-done | bytes 163872 | tf_op jit(solution)/shard_map/all_to_all | solution.py:43
  41.7 1.2 %slice.48 = f32[1,1,1]{2,1,0:T(1,128)} slice(f32[8,40,128]{2,1,0:T(8,128)} %all-to-all-done.1), slice={[0:1], [32:33], [0:1]} | slice | bytes 8 | tf_op jit(solution)/shard_map/slice | solution.py:45
  44.2 0.9 slice.49
  45.1 3.2 %collective-permute-start.2 = (f32[256,128]{1,0:T(8,128)S(1)}, f32[256,128]{1,0:T(8,128)S(1)}, u32[]{:S(2)}, u32[]{:S(2)}) collective-permute-start(f32[256,128]{1,0:T(8,128)S(1)} %bitcast.105), channel_id=1, source_target_pairs={{0,4},{4,0},{1,5},{5,1},{2,6},{6,2},{3,7},{7,3},{8,12},{12,8},{9,1... | collective-permute-start | bytes 393224 | tf_op jit(solution)/shard_map/ppermute | solution.py:46
  48.3 1.0 collective-permute-done.2
  49.3 2.4 %fusion.13 = f32[4,128,1024]{2,1,0:T(8,128)S(1)} fusion(f32[4,128,128]{2,1,0:T(8,128)S(1)} %bitcast.97, bf16[1024,512]{1,0:T(8,128)(2,1)} %param.6), kind=kOutput, calls=%fused_computation.25 | convolution fusion | flops 137428992 | bytes 3407872 | tf_op jit(solution)/shard_map/thd,hde->the/dot_general | solution.py:113
  51.8 1.4 %multiply_reduce_fusion = (f32[1024,4]{0,1:T(4,128)S(1)}, f32[1024,4,128]{0,2,1:T(8,128)S(1)}) fusion(f32[4,128,1024]{2,1,0:T(8,128)S(1)} %fusion.13, f32[4,128,128]{2,1,0:T(8,128)S(1)} %bitcast.98, f32[1024]{0:T(1024)S(1)} %fusion.56, f32[4,1024,128]{1,2,0:T(8,128)S(1)} %fusion.7, bf16[1024,512]{1,0:T(8,128)(2,1)S(1)} %copy-done.2), kind=kOutput, calls=%fused_computation.18 | convolution fusion | flops 140242944 | bytes 7622656 | tf_op jit(solution)/shard_map/thd,hde->the/dot_general | solution.py:115
  53.6 1.4 %collective-permute-start.3 = (bf16[512,512]{0,1:T(8,128)(2,1)S(1)}, bf16[512,512]{0,1:T(8,128)(2,1)S(1)}, u32[]{:S(2)}, u32[]{:S(2)}) collective-permute-start(bf16[512,512]{0,1:T(8,128)(2,1)S(1)} %bitcast.94), channel_id=1, source_target_pairs={{0,1},{1,2},{2,3},{3,0},{4,5},{5,6},{6,7},{7,4},{8,9},{9,10},{10,1... | collective-permute-start | bytes 1572872 | tf_op jit(solution)/shard_map/ppermute | solution.py:72
  54.9 1.5 %collective-permute-start.4 = (bf16[512,512]{0,1:T(8,128)(2,1)S(1)}, bf16[512,512]{0,1:T(8,128)(2,1)S(1)}, u32[]{:S(2)}, u32[]{:S(2)}) collective-permute-start(bf16[512,512]{0,1:T(8,128)(2,1)S(1)} %bitcast.91), channel_id=1, source_target_pairs={{0,3},{1,0},{2,1},{3,2},{4,7},{5,4},{6,5},{7,6},{8,11},{9,8},{10,9... | collective-permute-start | bytes 1572872 | tf_op jit(solution)/shard_map/ppermute | solution.py:73
  57.9 10.2 %collective-permute-done.3 = bf16[512,512]{0,1:T(8,128)(2,1)S(1)} collective-permute-done((bf16[512,512]{0,1:T(8,128)(2,1)S(1)}, bf16[512,512]{0,1:T(8,128)(2,1)S(1)}, u32[]{:S(2)}, u32[]{:S(2)}) %collective-permute-start.3) | collective-permute-done | bytes 524320 | tf_op jit(solution)/shard_map/ppermute | solution.py:72
  68.1 2.5 %collective-permute-start.5 = (bf16[512,512]{0,1:T(8,128)(2,1)S(1)}, bf16[512,512]{0,1:T(8,128)(2,1)S(1)}, u32[]{:S(2)}, u32[]{:S(2)}) collective-permute-start(bf16[512,512]{0,1:T(8,128)(2,1)S(1)} %bitcast.96), channel_id=1, source_target_pairs={{0,3},{1,0},{2,1},{3,2},{4,7},{5,4},{6,5},{7,6},{8,11},{9,8},{10,9... | collective-permute-start | bytes 1572872 | tf_op jit(solution)/shard_map/ppermute | solution.py:78
  70.7 2.7 %collective-permute-start.8 = (bf16[512,512]{0,1:T(8,128)(2,1)S(1)}, bf16[512,512]{0,1:T(8,128)(2,1)S(1)}, u32[]{:S(2)}, u32[]{:S(2)}) collective-permute-start(bf16[512,512]{0,1:T(8,128)(2,1)S(1)} %collective-permute-done.4), channel_id=1, source_target_pairs={{0,3},{1,0},{2,1},{3,2},{4,7},{5,4},{6,5},{7,6},{8,11},{9,8},{10,9... | collective-permute-start | bytes 1572872 | tf_op jit(solution)/shard_map/ppermute | solution.py:80
  74.8 5.7 %collective-permute-done.5 = bf16[512,512]{0,1:T(8,128)(2,1)S(1)} collective-permute-done((bf16[512,512]{0,1:T(8,128)(2,1)S(1)}, bf16[512,512]{0,1:T(8,128)(2,1)S(1)}, u32[]{:S(2)}, u32[]{:S(2)}) %collective-permute-start.5) | collective-permute-done | bytes 524320 | tf_op jit(solution)/shard_map/ppermute | solution.py:78
  81.3 13.6 %collective-permute-done.7 = bf16[512,512]{0,1:T(8,128)(2,1)S(1)} collective-permute-done((bf16[512,512]{0,1:T(8,128)(2,1)S(1)}, bf16[512,512]{0,1:T(8,128)(2,1)S(1)}, u32[]{:S(2)}, u32[]{:S(2)}) %collective-permute-start.7) | collective-permute-done | bytes 524320 | tf_op jit(solution)/shard_map/ppermute | solution.py:77
  97.1 1.5 %pad_maximum_fusion = bf16[1024,1024]{1,0:T(8,128)(2,1)} fusion(bf16[512,1024]{1,0:T(8,128)(2,1)S(1)} %add_convert_fusion, bf16[512,1024]{1,0:T(8,128)(2,1)S(1)} %add_convert_fusion.1), kind=kLoop, calls=%fused_computation.13 | loop fusion | flops 4194304 | bytes 4194304 | tf_op jit(solution)/shard_map/concatenate | solution.py:85
  (46 shorter events, 10.3 us)
Async XLA Ops:
  0.0 4.8 %copy-start = (bf16[1024,512]{1,0:T(8,128)(2,1)S(1)}, bf16[1024,512]{1,0:T(8,128)(2,1)}, u32[]{:S(2)}) copy-start(bf16[1024,512]{1,0:T(8,128)(2,1)} %param.8) | copy-start | bytes 3145732
  1.4 2.7 %copy-start.4 = (s32[1024]{0:T(1024)S(1)}, s32[1024]{0:T(1024)}, u32[]{:S(2)}) copy-start(s32[1024]{0:T(1024)} %param.9) | copy-start | bytes 12292
  4.1 7.8 %copy-start.3 = (bf16[1024,512]{0,1:T(8,128)(2,1)}, bf16[1024,512]{0,1:T(8,128)(2,1)S(1)}, u32[]{:S(2)}) copy-start(bf16[1024,512]{0,1:T(8,128)(2,1)S(1)} %copy.40) | copy-start | bytes 3145732
  5.2 6.6 %collective-permute-start = (f32[2,256,128]{2,1,0:T(8,128)S(1)}, f32[2,256,128]{2,1,0:T(8,128)S(1)}, u32[]{:S(2)}, u32[]{:S(2)}) collective-permute-start(f32[2,256,128]{2,1,0:T(8,128)S(1)} %bitcast.101), channel_id=1, source_target_pairs={{0,4},{4,0},{1,5},{5,1},{2,6},{6,2},{3,7},{7,3},{8,12},{12,8},{9,1... | collective-permute-start | bytes 786440 | tf_op jit(solution)/shard_map/ppermute | solution.py:24
  9.2 1.3 %collective-permute-start.1 = (f32[]{:T(128)}, f32[]{:T(128)}, u32[]{:S(2)}, u32[]{:S(2)}) collective-permute-start(f32[]{:T(128)} %convert_element_type.47), channel_id=1, source_target_pairs={{0,4},{4,0},{1,5},{5,1},{2,6},{6,2},{3,7},{7,3},{8,12},{12,8},{9,1... | collective-permute-start | bytes 20 | tf_op jit(solution)/shard_map/ppermute | solution.py:24
  12.6 15.4 %all-to-all-start = ((f32[8,40,128]{2,1,0:T(8,128)}), f32[8,40,128]{2,1,0:T(8,128)S(1)}, u32[]{:S(2)}, u32[]{:S(2)}) async-start(f32[8,40,128]{2,1,0:T(8,128)} %concatenate.13), calls=%async_computation | async-start | bytes 327680 | tf_op jit(solution)/shard_map/all_to_all | solution.py:33
  29.4 12.3 %all-to-all-start.1 = ((f32[8,40,128]{2,1,0:T(8,128)}), f32[8,40,128]{2,1,0:T(8,128)}, u32[]{:S(2)}, u32[]{:S(2)}) async-start(f32[8,40,128]{2,1,0:T(8,128)} %pad_maximum_fusion.1), calls=%async_computation.1 | async-start | bytes 327680 | tf_op jit(solution)/shard_map/all_to_all | solution.py:43
  45.1 4.2 %collective-permute-start.2 = (f32[256,128]{1,0:T(8,128)S(1)}, f32[256,128]{1,0:T(8,128)S(1)}, u32[]{:S(2)}, u32[]{:S(2)}) collective-permute-start(f32[256,128]{1,0:T(8,128)S(1)} %bitcast.105), channel_id=1, source_target_pairs={{0,4},{4,0},{1,5},{5,1},{2,6},{6,2},{3,7},{7,3},{8,12},{12,8},{9,1... | collective-permute-start | bytes 393224 | tf_op jit(solution)/shard_map/ppermute | solution.py:46
  49.3 2.5 %copy-start.2 = (bf16[1024,512]{1,0:T(8,128)(2,1)S(1)}, bf16[1024,512]{1,0:T(8,128)(2,1)}, u32[]{:S(2)}) copy-start(bf16[1024,512]{1,0:T(8,128)(2,1)} %param.6) | copy-start | bytes 3145732
  51.8 1.4 %copy-start.5 = (f32[512]{0:T(512)S(1)}, f32[512]{0:T(512)}, u32[]{:S(2)}) copy-start(f32[512]{0:T(512)} %param.10) | copy-start | bytes 6148
  53.2 3.3 %copy-start.1 = (bf16[2048,1024]{1,0:T(8,128)(2,1)S(1)}, bf16[2048,1024]{1,0:T(8,128)(2,1)}, u32[]{:S(2)}) copy-start(bf16[2048,1024]{1,0:T(8,128)(2,1)} %param.11) | copy-start | bytes 12582916
  53.6 14.6 %collective-permute-start.3 = (bf16[512,512]{0,1:T(8,128)(2,1)S(1)}, bf16[512,512]{0,1:T(8,128)(2,1)S(1)}, u32[]{:S(2)}, u32[]{:S(2)}) collective-permute-start(bf16[512,512]{0,1:T(8,128)(2,1)S(1)} %bitcast.94), channel_id=1, source_target_pairs={{0,1},{1,2},{2,3},{3,0},{4,5},{5,6},{6,7},{7,4},{8,9},{9,10},{10,1... | collective-permute-start | bytes 1572872 | tf_op jit(solution)/shard_map/ppermute | solution.py:72
  54.9 13.2 %collective-permute-start.4 = (bf16[512,512]{0,1:T(8,128)(2,1)S(1)}, bf16[512,512]{0,1:T(8,128)(2,1)S(1)}, u32[]{:S(2)}, u32[]{:S(2)}) collective-permute-start(bf16[512,512]{0,1:T(8,128)(2,1)S(1)} %bitcast.91), channel_id=1, source_target_pairs={{0,3},{1,0},{2,1},{3,2},{4,7},{5,4},{6,5},{7,6},{8,11},{9,8},{10,9... | collective-permute-start | bytes 1572872 | tf_op jit(solution)/shard_map/ppermute | solution.py:73
  68.1 12.4 %collective-permute-start.5 = (bf16[512,512]{0,1:T(8,128)(2,1)S(1)}, bf16[512,512]{0,1:T(8,128)(2,1)S(1)}, u32[]{:S(2)}, u32[]{:S(2)}) collective-permute-start(bf16[512,512]{0,1:T(8,128)(2,1)S(1)} %bitcast.96), channel_id=1, source_target_pairs={{0,3},{1,0},{2,1},{3,2},{4,7},{5,4},{6,5},{7,6},{8,11},{9,8},{10,9... | collective-permute-start | bytes 1572872 | tf_op jit(solution)/shard_map/ppermute | solution.py:78
  70.7 25.0 %collective-permute-start.6 = (bf16[512,512]{0,1:T(8,128)(2,1)S(1)}, bf16[512,512]{0,1:T(8,128)(2,1)S(1)}, u32[]{:S(2)}, u32[]{:S(2)}) collective-permute-start(bf16[512,512]{0,1:T(8,128)(2,1)S(1)} %collective-permute-done.3), channel_id=1, source_target_pairs={{0,1},{1,2},{2,3},{3,0},{4,5},{5,6},{6,7},{7,4},{8,9},{9,10},{10,1... | collective-permute-start | bytes 1572872 | tf_op jit(solution)/shard_map/ppermute | solution.py:79
  70.7 24.2 %collective-permute-start.7 = (bf16[512,512]{0,1:T(8,128)(2,1)S(1)}, bf16[512,512]{0,1:T(8,128)(2,1)S(1)}, u32[]{:S(2)}, u32[]{:S(2)}) collective-permute-start(bf16[512,512]{0,1:T(8,128)(2,1)S(1)} %bitcast.93), channel_id=1, source_target_pairs={{0,1},{1,2},{2,3},{3,0},{4,5},{5,6},{6,7},{7,4},{8,9},{9,10},{10,1... | collective-permute-start | bytes 1572872 | tf_op jit(solution)/shard_map/ppermute | solution.py:77
  70.7 25.7 %collective-permute-start.8 = (bf16[512,512]{0,1:T(8,128)(2,1)S(1)}, bf16[512,512]{0,1:T(8,128)(2,1)S(1)}, u32[]{:S(2)}, u32[]{:S(2)}) collective-permute-start(bf16[512,512]{0,1:T(8,128)(2,1)S(1)} %collective-permute-done.4), channel_id=1, source_target_pairs={{0,3},{1,0},{2,1},{3,2},{4,7},{5,4},{6,5},{7,6},{8,11},{9,8},{10,9... | collective-permute-start | bytes 1572872 | tf_op jit(solution)/shard_map/ppermute | solution.py:80

commit v6 on v3

--- a/solution.py
+++ b/solution.py
@@ -10,25 +10,27 @@
     return (jax.nn.elu(raw_input.astype(jnp.float32)) + 1.0).astype(jnp.bfloat16)
 
 
-def carried_in(local_sum, final_seg, axis):
+def carried_in(local_sum, final_seg, first_seg, axis):
     count = lax.axis_size(axis)
     shape = local_sum.shape
-    flat = local_sum.reshape(count, -1)
-    width = flat.shape[1]
-    seg_row = jnp.full((count, HEAD), final_seg.astype(jnp.float32))
-    sent = jnp.concatenate([flat, seg_row], axis=1)
+    tile = local_sum.size // (count * HEAD)
+    flat = local_sum.reshape(count, tile, HEAD)
+    seg_rows = jnp.concatenate(
+        [
+            jnp.full((count, 1, HEAD), final_seg.astype(jnp.float32)),
+            jnp.full((count, 7, HEAD), first_seg.astype(jnp.float32)),
+        ],
+        axis=1,
+    )
+    sent = jnp.concatenate([flat, seg_rows], axis=1)
     pieces = lax.all_to_all(sent, axis, 0, 0, tiled=True)
-    sums = pieces[:, :width]
-    segs = pieces[:, width]
+    sums = pieces[:, :tile]
+    last_segs = pieces[:, tile, 0]
+    first_segs = pieces[:, tile + 1, 0]
     block = jnp.arange(count)
-    prev_seg = jnp.concatenate([jnp.full((1,), -1.0, jnp.float32), segs[:-1]])
-    mask = (block[None, :] < block[:, None]) & (segs[None, :] == prev_seg[:, None])
-    carry = jnp.sum(jnp.where(mask[:, :, None], sums[None, :, :], 0.0), axis=1)
-    back = jnp.concatenate([carry, jnp.broadcast_to(prev_seg[:, None], (count, HEAD))], axis=1)
-    mine = lax.all_to_all(back, axis, 0, 0, tiled=True)
-    before_sum = mine[:, :width].reshape(shape)
-    before_seg = mine[0, width]
-    return before_sum, before_seg
+    mask = (block[None, :] < block[:, None]) & (last_segs[None, :] == first_segs[:, None])
+    carry = jnp.sum(jnp.where(mask[:, :, None, None], sums[None], 0.0), axis=1)
+    return lax.all_to_all(carry, axis, 0, 0, tiled=True).reshape(shape)
 
 
 def project_gathered(hidden, out_weight, axis):
@@ -64,7 +66,7 @@
     rows_here = queries.shape[0]
     width_here = queries.shape[1]
     heads_here = width_here // HEAD
-    feat_query = features(queries).reshape(rows_here, heads_here, HEAD)
+    feat_query = lax.optimization_barrier(features(queries)).reshape(rows_here, heads_here, HEAD)
     feat_key = features(keys).reshape(rows_here, heads_here, HEAD)
     value_heads = values.reshape(rows_here, heads_here, HEAD)
     final_seg = segment_ids[rows_here - 1]
@@ -75,7 +77,7 @@
         value_heads,
         preferred_element_type=jnp.float32,
     )
-    before_sum, before_seg = carried_in(local_sum, final_seg, "ctx")
+    before_sum = carried_in(local_sum, final_seg, segment_ids[0], "ctx")
     position = jnp.arange(rows_here)
     allowed = (position[None, :] <= position[:, None]) & (
         segment_ids[:, None] == segment_ids[None, :]
@@ -88,7 +90,7 @@
     carried = jnp.einsum(
         "thd,hde->the", feat_query, state_hi, preferred_element_type=jnp.float32
     ) + jnp.einsum("thd,hde->the", feat_query, state_lo, preferred_element_type=jnp.float32)
-    carry_on = (segment_ids.astype(jnp.float32) == before_seg).astype(jnp.float32)
+    carry_on = (segment_ids == segment_ids[0]).astype(jnp.float32)
     numerator = inside + carry_on[:, None, None] * carried
     normed = numerator * lax.rsqrt(jnp.mean(numerator * numerator, axis=-1, keepdims=True) + 1e-06)
     gain_heads = norm_gain.reshape(heads_here, HEAD)

time: 101 us -> 100 us (0.990)
  matrix products: 17.1 us -> 14.9 us
  other arithmetic: 8.56 us -> 10.6 us
  local copies, waits for them, and re-layouts: 6.76 us -> 5.37 us
    dot_general x1, matrix products: 2.48 us -> 0.43 us  [per_device(): jnp.einsum('thd,hde->the', feat_query, state_hi, preferred_element_type=j...]
    all_to_all x2 -> x0, local copies, waits for them, and re-layouts: 1.88 us -> none  [the longest x1 0.99 us: carried_in(): mine = lax.all_to_all(back, axis, 0, 0, tiled=True)]
    unnamed x14 -> x18, local copies, waits for them, and re-layouts: 0.07 us -> 1.9 us
    convert_element_type x1 -> x2, other arithmetic: 2.16 us -> 3.09 us  [features(): (jax.nn.elu(raw_input.astype(jnp.float32)) + 1.0).astype(jnp.bfloat16)]
    slice x6 -> x3, local copies, waits for them, and re-layouts: 2.21 us -> 1.62 us  [the longest x1 1.4 us: per_device(): carry_on = (segment_ids == segment_ids[0]).astype(jnp.float32)]
    convert_element_type x2 -> x1, other arithmetic: 2.03 us -> 1.97 us  [per_device(): carry_on = (segment_ids == segment_ids[0]).astype(jnp.float32)]
  transfers between devices with their start and end apart: 8 -> 8, of which waited for: 5 -> 5; matrix products, arithmetic and copies ran while one was open for 14% -> 15% of each run, Pallas kernels for 0% -> 0%
where the time goes in v6:
time: 100 us; the launch traced here: 99.1 us
  waiting for transfers between devices  44.6 us (45%)
  starting transfers between devices  22.1 us (22%)
  matrix products  14.9 us (15%)
  other arithmetic  10.6 us (11%)
  local copies, waits for them, and re-layouts  5.37 us (5%)
  between operations  1.52 us (2%)
    ppermute x1, waiting for transfers between devices, project_gathered(): left_bottom = lax.ppermute(bottom_later, axis, ahead)  13.6 us
    ppermute x1, waiting for transfers between devices, project_gathered(): left_top = lax.ppermute(top, axis, ahead)  10.5 us
    all_to_all x1, waiting for transfers between devices, carried_in(): pieces = lax.all_to_all(sent, axis, 0, 0, tiled=True)  10.5 us
    all_to_all x1, starting transfers between devices, carried_in(): pieces = lax.all_to_all(sent, axis, 0, 0, tiled=True)  9.98 us
    dot_general x1, matrix products, per_device(): jnp.einsum('hts,she->the', weights, value_heads, preferred_element_type=j...  7.6 us
    ppermute x1, waiting for transfers between devices, project_gathered(): right_top = lax.ppermute(top_later, axis, behind)  6.42 us
    dot_general x8, matrix products, part(): jnp.dot(block, weight_groups[group], preferred_element_type=jnp.float32)  5.84 us
    all_to_all x1, waiting for transfers between devices, carried_in(): return lax.all_to_all(carry, axis, 0, 0, tiled=True).reshape(shape)  3.54 us
  transfers between devices with their start and end apart: 8, of which 5 were waited for; matrix products, arithmetic and copies ran while one was open for 15% of the time, Pallas kernels for 0%

profile of v6, /device:TPU:1, one launch (start us, length us, event | category | flops | bytes accessed | tf_op | source)
XLA Modules:
  0.0 99.1 jit_solution(17388425313124625269)
XLA Ops:
  0.0 1.4 %fusion.65 = (s32[1]{0:T(128)}, s32[1]{0:T(128)}) fusion(s32[1024]{0:T(1024)} %param.9), kind=kLoop, calls=%fused_computation.80 | loop fusion | bytes 16 | tf_op jit(solution)/shard_map/slice | solution.py:93
  2.1 2.0 %compare_convert_fusion.1 = (f32[1024]{0:T(1024)S(1)}, bf16[1024]{0:T(1024)(128)(2,1)S(1)}) fusion(s32[1024]{0:T(1024)} %param.9, s32[]{:T(128)} %bitcast.1, s32[]{:T(128)} %bitcast.2), kind=kLoop, calls=%fused_computation.69 | loop fusion | flops 4096 | bytes 10248 | tf_op jit(solution)/shard_map/convert_element_type | solution.py:93
  4.7 2.2 %fusion.6 = bf16[1024,512]{1,0:T(8,128)(2,1)S(1)} fusion(bf16[1024,512]{1,0:T(8,128)(2,1)} %param.7), kind=kLoop, calls=%fused_computation.13 | loop fusion | flops 3145728 | bytes 2097152 | tf_op jit(solution)/shard_map/convert_element_type | solution.py:10
  8.0 0.8 maximum_maximum_fusion
  8.8 10.0 %all-to-all-start = ((f32[16,40,128]{2,1,0:T(8,128)}), f32[16,40,128]{2,1,0:T(8,128)S(1)}, u32[]{:S(2)}, u32[]{:S(2)}) async-start(f32[16,40,128]{2,1,0:T(8,128)} %maximum_maximum_fusion), calls=%async_computation | async-start | bytes 655360 | tf_op jit(solution)/shard_map/all_to_all | solution.py:26
  18.8 0.9 fusion.3
  19.8 1.6 %fusion = pred[1024,1024]{1,0:T(8,128)(4,1)} fusion(s32[1024]{0:T(1024)S(1)} %copy-done.7), kind=kLoop, calls=%fused_computation.7 | loop fusion | flops 3145728 | bytes 1052672 | tf_op jit(solution)/shard_map/and | solution.py:82
  21.4 10.5 %all-to-all-done = f32[16,40,128]{2,1,0:T(8,128)S(1)} async-done(((f32[16,40,128]{2,1,0:T(8,128)}), f32[16,40,128]{2,1,0:T(8,128)S(1)}, u32[]{:S(2)}, u32[]{:S(2)}) %all-to-all-start) | async-done | bytes 327712 | tf_op jit(solution)/shard_map/all_to_all | solution.py:26
  32.2 1.3 %select_reduce_fusion = f32[16,32,128]{2,1,0:T(8,128)} fusion(f32[16,32,128]{2,1,0:T(8,128)S(1)} %slice.39, pred[16,16]{1,0:T(8,128)(4,1)S(1)} %fusion.54), kind=kLoop, calls=%fused_computation.5 | loop fusion | flops 2031616 | bytes 524544 | tf_op jit(solution)/shard_map/reduce_sum | solution.py:32
  33.5 3.4 %all-to-all-start.1 = ((f32[16,32,128]{2,1,0:T(8,128)}), f32[16,32,128]{2,1,0:T(8,128)S(1)}, u32[]{:S(2)}, u32[]{:S(2)}) async-start(f32[16,32,128]{2,1,0:T(8,128)} %select_reduce_fusion), calls=%async_computation.1 | async-start | bytes 524288 | tf_op jit(solution)/shard_map/all_to_all | solution.py:33
  36.9 7.6 %fusion.7 = f32[4,1024,128]{1,2,0:T(8,128)} fusion(bf16[1024,4,128]{0,2,1:T(8,128)(2,1)S(1)} %bitcast.95, pred[1024,1024]{1,0:T(8,128)(4,1)} %fusion, bf16[1024,512]{1,0:T(8,128)(2,1)S(1)} %copy-done, bf16[1024,512]{1,0:T(8,128)(2,1)S(1)} %fusion.3), kind=kOutput, calls=%fused_computation.20 | convolution fusion | flops 2155872256 | bytes 6291456 | tf_op jit(solution)/shard_map/hts,she->the/dot_general | solution.py:87
  44.5 3.5 %all-to-all-done.1 = f32[16,32,128]{2,1,0:T(8,128)S(1)} async-done(((f32[16,32,128]{2,1,0:T(8,128)}), f32[16,32,128]{2,1,0:T(8,128)S(1)}, u32[]{:S(2)}, u32[]{:S(2)}) %all-to-all-start.1) | async-done | bytes 262176 | tf_op jit(solution)/shard_map/all_to_all | solution.py:33
  48.8 1.1 %copy.46 = f32[4,128,128]{1,2,0:T(8,128)S(1)} copy(f32[4,128,128]{2,1,0:T(8,128)} %bitcast.96) | data formatting | bytes 524288 | tf_op jit(solution)/shard_map/reshape | solution.py:33
  50.3 1.1 %copy-done.2 = f32[4,1024,128]{1,2,0:T(8,128)S(1)} copy-done((f32[4,1024,128]{1,2,0:T(8,128)S(1)}, f32[4,1024,128]{1,2,0:T(8,128)}, u32[]{:S(2)}) %copy-start.2) | copy-done | bytes 2097176
  52.5 1.4 %collective-permute-start = (bf16[512,512]{0,1:T(8,128)(2,1)S(1)}, bf16[512,512]{0,1:T(8,128)(2,1)S(1)}, u32[]{:S(2)}, u32[]{:S(2)}) collective-permute-start(bf16[512,512]{0,1:T(8,128)(2,1)S(1)} %bitcast.91), channel_id=1, source_target_pairs={{0,1},{1,2},{2,3},{3,0},{4,5},{5,6},{6,7},{7,4},{8,9},{9,10},{10,1... | collective-permute-start | bytes 1572872 | tf_op jit(solution)/shard_map/ppermute | solution.py:49
  53.8 1.7 %collective-permute-start.1 = (bf16[512,512]{0,1:T(8,128)(2,1)S(1)}, bf16[512,512]{0,1:T(8,128)(2,1)S(1)}, u32[]{:S(2)}, u32[]{:S(2)}) collective-permute-start(bf16[512,512]{0,1:T(8,128)(2,1)S(1)} %bitcast.88), channel_id=1, source_target_pairs={{0,3},{1,0},{2,1},{3,2},{4,7},{5,4},{6,5},{7,6},{8,11},{9,8},{10,9... | collective-permute-start | bytes 1572872 | tf_op jit(solution)/shard_map/ppermute | solution.py:50
  57.0 10.5 %collective-permute-done = bf16[512,512]{0,1:T(8,128)(2,1)S(1)} collective-permute-done((bf16[512,512]{0,1:T(8,128)(2,1)S(1)}, bf16[512,512]{0,1:T(8,128)(2,1)S(1)}, u32[]{:S(2)}, u32[]{:S(2)}) %collective-permute-start) | collective-permute-done | bytes 524320 | tf_op jit(solution)/shard_map/ppermute | solution.py:49
  67.5 2.9 %collective-permute-start.2 = (bf16[512,512]{0,1:T(8,128)(2,1)S(1)}, bf16[512,512]{0,1:T(8,128)(2,1)S(1)}, u32[]{:S(2)}, u32[]{:S(2)}) collective-permute-start(bf16[512,512]{0,1:T(8,128)(2,1)S(1)} %bitcast.93), channel_id=1, source_target_pairs={{0,3},{1,0},{2,1},{3,2},{4,7},{5,4},{6,5},{7,6},{8,11},{9,8},{10,9... | collective-permute-start | bytes 1572872 | tf_op jit(solution)/shard_map/ppermute | solution.py:55
  70.4 2.7 %collective-permute-start.5 = (bf16[512,512]{0,1:T(8,128)(2,1)S(1)}, bf16[512,512]{0,1:T(8,128)(2,1)S(1)}, u32[]{:S(2)}, u32[]{:S(2)}) collective-permute-start(bf16[512,512]{0,1:T(8,128)(2,1)S(1)} %collective-permute-done.1), channel_id=1, source_target_pairs={{0,3},{1,0},{2,1},{3,2},{4,7},{5,4},{6,5},{7,6},{8,11},{9,8},{10,9... | collective-permute-start | bytes 1572872 | tf_op jit(solution)/shard_map/ppermute | solution.py:57
  74.6 6.4 %collective-permute-done.2 = bf16[512,512]{0,1:T(8,128)(2,1)S(1)} collective-permute-done((bf16[512,512]{0,1:T(8,128)(2,1)S(1)}, bf16[512,512]{0,1:T(8,128)(2,1)S(1)}, u32[]{:S(2)}, u32[]{:S(2)}) %collective-permute-start.2) | collective-permute-done | bytes 524320 | tf_op jit(solution)/shard_map/ppermute | solution.py:55
  81.7 13.6 %collective-permute-done.4 = bf16[512,512]{0,1:T(8,128)(2,1)S(1)} collective-permute-done((bf16[512,512]{0,1:T(8,128)(2,1)S(1)}, bf16[512,512]{0,1:T(8,128)(2,1)S(1)}, u32[]{:S(2)}, u32[]{:S(2)}) %collective-permute-start.4) | collective-permute-done | bytes 524320 | tf_op jit(solution)/shard_map/ppermute | solution.py:54
  96.1 0.7 add_convert_fusion.1
  96.8 0.7 add_convert_fusion
  97.6 1.5 %pad_maximum_fusion = bf16[1024,1024]{1,0:T(8,128)(2,1)} fusion(bf16[512,1024]{1,0:T(8,128)(2,1)S(1)} %add_convert_fusion, bf16[512,1024]{1,0:T(8,128)(2,1)S(1)} %add_convert_fusion.1), kind=kLoop, calls=%fused_computation.14 | loop fusion | flops 4194304 | bytes 4194304 | tf_op jit(solution)/shard_map/concatenate | solution.py:62
  (41 shorter events, 8.0 us)
Async XLA Ops:
  0.0 7.5 %copy-start = (bf16[1024,512]{1,0:T(8,128)(2,1)S(1)}, bf16[1024,512]{1,0:T(8,128)(2,1)}, u32[]{:S(2)}) copy-start(bf16[1024,512]{1,0:T(8,128)(2,1)} %param.8) | copy-start | bytes 3145732
  7.4 1.5 %copy-start.4 = (bf16[1024,512]{0,1:T(8,128)(2,1)}, bf16[1024,512]{0,1:T(8,128)(2,1)S(1)}, u32[]{:S(2)}) copy-start(bf16[1024,512]{0,1:T(8,128)(2,1)S(1)} %copy.50) | copy-start | bytes 3145732
  7.5 11.3 %copy-start.3 = (bf16[1024,512]{1,0:T(8,128)(2,1)S(1)}, bf16[1024,512]{1,0:T(8,128)(2,1)}, u32[]{:S(2)}) copy-start(bf16[1024,512]{1,0:T(8,128)(2,1)} %param.6) | copy-start | bytes 3145732
  8.0 11.8 %copy-start.7 = (s32[1024]{0:T(1024)S(1)}, s32[1024]{0:T(1024)}, u32[]{:S(2)}) copy-start(s32[1024]{0:T(1024)} %param.9) | copy-start | bytes 12292
  8.8 23.1 %all-to-all-start = ((f32[16,40,128]{2,1,0:T(8,128)}), f32[16,40,128]{2,1,0:T(8,128)S(1)}, u32[]{:S(2)}, u32[]{:S(2)}) async-start(f32[16,40,128]{2,1,0:T(8,128)} %maximum_maximum_fusion), calls=%async_computation | async-start | bytes 655360 | tf_op jit(solution)/shard_map/all_to_all | solution.py:26
  19.8 17.1 %copy-start.5 = (bf16[1024,512]{0,1:T(8,128)(2,1)S(1)}, bf16[1024,512]{0,1:T(8,128)(2,1)}, u32[]{:S(2)}) copy-start(bf16[1024,512]{0,1:T(8,128)(2,1)} %copy-done.4) | copy-start | bytes 3145732
  33.5 14.6 %all-to-all-start.1 = ((f32[16,32,128]{2,1,0:T(8,128)}), f32[16,32,128]{2,1,0:T(8,128)S(1)}, u32[]{:S(2)}, u32[]{:S(2)}) async-start(f32[16,32,128]{2,1,0:T(8,128)} %select_reduce_fusion), calls=%async_computation.1 | async-start | bytes 524288 | tf_op jit(solution)/shard_map/all_to_all | solution.py:33
  48.0 0.7 copy-start.6
  49.8 1.6 %copy-start.2 = (f32[4,1024,128]{1,2,0:T(8,128)S(1)}, f32[4,1024,128]{1,2,0:T(8,128)}, u32[]{:S(2)}) copy-start(f32[4,1024,128]{1,2,0:T(8,128)} %fusion.7) | copy-start | bytes 6291460
  51.4 0.7 copy-start.8
  52.1 3.4 %copy-start.1 = (bf16[2048,1024]{1,0:T(8,128)(2,1)S(1)}, bf16[2048,1024]{1,0:T(8,128)(2,1)}, u32[]{:S(2)}) copy-start(bf16[2048,1024]{1,0:T(8,128)(2,1)} %param.11) | copy-start | bytes 12582916
  52.5 15.1 %collective-permute-start = (bf16[512,512]{0,1:T(8,128)(2,1)S(1)}, bf16[512,512]{0,1:T(8,128)(2,1)S(1)}, u32[]{:S(2)}, u32[]{:S(2)}) collective-permute-start(bf16[512,512]{0,1:T(8,128)(2,1)S(1)} %bitcast.91), channel_id=1, source_target_pairs={{0,1},{1,2},{2,3},{3,0},{4,5},{5,6},{6,7},{7,4},{8,9},{9,10},{10,1... | collective-permute-start | bytes 1572872 | tf_op jit(solution)/shard_map/ppermute | solution.py:49
  53.8 13.7 %collective-permute-start.1 = (bf16[512,512]{0,1:T(8,128)(2,1)S(1)}, bf16[512,512]{0,1:T(8,128)(2,1)S(1)}, u32[]{:S(2)}, u32[]{:S(2)}) collective-permute-start(bf16[512,512]{0,1:T(8,128)(2,1)S(1)} %bitcast.88), channel_id=1, source_target_pairs={{0,3},{1,0},{2,1},{3,2},{4,7},{5,4},{6,5},{7,6},{8,11},{9,8},{10,9... | collective-permute-start | bytes 1572872 | tf_op jit(solution)/shard_map/ppermute | solution.py:50
  67.5 13.5 %collective-permute-start.2 = (bf16[512,512]{0,1:T(8,128)(2,1)S(1)}, bf16[512,512]{0,1:T(8,128)(2,1)S(1)}, u32[]{:S(2)}, u32[]{:S(2)}) collective-permute-start(bf16[512,512]{0,1:T(8,128)(2,1)S(1)} %bitcast.93), channel_id=1, source_target_pairs={{0,3},{1,0},{2,1},{3,2},{4,7},{5,4},{6,5},{7,6},{8,11},{9,8},{10,9... | collective-permute-start | bytes 1572872 | tf_op jit(solution)/shard_map/ppermute | solution.py:55
  70.4 25.6 %collective-permute-start.3 = (bf16[512,512]{0,1:T(8,128)(2,1)S(1)}, bf16[512,512]{0,1:T(8,128)(2,1)S(1)}, u32[]{:S(2)}, u32[]{:S(2)}) collective-permute-start(bf16[512,512]{0,1:T(8,128)(2,1)S(1)} %collective-permute-done), channel_id=1, source_target_pairs={{0,1},{1,2},{2,3},{3,0},{4,5},{5,6},{6,7},{7,4},{8,9},{9,10},{10,1... | collective-permute-start | bytes 1572872 | tf_op jit(solution)/shard_map/ppermute | solution.py:56
  70.4 24.9 %collective-permute-start.4 = (bf16[512,512]{0,1:T(8,128)(2,1)S(1)}, bf16[512,512]{0,1:T(8,128)(2,1)S(1)}, u32[]{:S(2)}, u32[]{:S(2)}) collective-permute-start(bf16[512,512]{0,1:T(8,128)(2,1)S(1)} %bitcast.90), channel_id=1, source_target_pairs={{0,1},{1,2},{2,3},{3,0},{4,5},{5,6},{6,7},{7,4},{8,9},{9,10},{10,1... | collective-permute-start | bytes 1572872 | tf_op jit(solution)/shard_map/ppermute | solution.py:54
  70.4 26.4 %collective-permute-start.5 = (bf16[512,512]{0,1:T(8,128)(2,1)S(1)}, bf16[512,512]{0,1:T(8,128)(2,1)S(1)}, u32[]{:S(2)}, u32[]{:S(2)}) collective-permute-start(bf16[512,512]{0,1:T(8,128)(2,1)S(1)} %collective-permute-done.1), channel_id=1, source_target_pairs={{0,3},{1,0},{2,1},{3,2},{4,7},{5,4},{6,5},{7,6},{8,11},{9,8},{10,9... | collective-permute-start | bytes 1572872 | tf_op jit(solution)/shard_map/ppermute | solution.py:57

commit v7 on v6

--- a/solution.py
+++ b/solution.py
@@ -36,30 +36,35 @@
 def project_gathered(hidden, out_weight, axis):
     count, mine = lax.axis_size(axis), lax.axis_index(axis)
     rows, width = hidden.shape
-    half = rows // 2
-    weight_groups = out_weight.reshape(count, width, out_weight.shape[1])
+    half = width // 2
+    weight_halves = out_weight.reshape(count, 2, half, out_weight.shape[1])
     ahead = [(j, (j + 1) % count) for j in range(count)]
     behind = [(j, (j - 1) % count) for j in range(count)]
 
-    def part(block, offset):
+    def part(block, offset, which):
         group = lax.rem(mine + offset + count, count)
-        return jnp.dot(block, weight_groups[group], preferred_element_type=jnp.float32)
+        return jnp.dot(block, weight_halves[group, which], preferred_element_type=jnp.float32)
 
-    top, bottom = hidden[:half], hidden[half:]
-    left_top = lax.ppermute(top, axis, ahead)
-    right_bottom = lax.ppermute(bottom, axis, behind)
-    left_top, right_bottom, top_later, bottom_later = lax.optimization_barrier(
-        (left_top, right_bottom, top, bottom)
+    first, second = hidden[:, :half], hidden[:, half:]
+    left_first = lax.ppermute(first, axis, ahead)
+    right_second = lax.ppermute(second, axis, behind)
+    left_first, right_second, first_later, second_later = lax.optimization_barrier(
+        (left_first, right_second, first, second)
     )
-    left_bottom = lax.ppermute(bottom_later, axis, ahead)
-    right_top = lax.ppermute(top_later, axis, behind)
-    far_top = lax.ppermute(left_top, axis, ahead)
-    far_bottom = lax.ppermute(right_bottom, axis, behind)
-    out_top = part(top, 0) + part(left_top, -1) + part(right_top, 1) + part(far_top, 2)
-    out_bottom = (
-        part(bottom, 0) + part(right_bottom, 1) + part(left_bottom, -1) + part(far_bottom, 2)
-    )
-    return jnp.concatenate([out_top, out_bottom], axis=0)
+    left_second = lax.ppermute(second_later, axis, ahead)
+    right_first = lax.ppermute(first_later, axis, behind)
+    far_first = lax.ppermute(left_first, axis, ahead)
+    far_second = lax.ppermute(right_second, axis, behind)
+    total = jnp.dot(hidden, out_weight.reshape(count, width, -1)[mine], preferred_element_type=jnp.float32)
+    for block, offset, which in (
+        (left_first, -1, 0),
+        (right_second, 1, 1),
+        (left_second, -1, 1),
+        (right_first, 1, 0),
+        (far_first, 2, 0),
+    ):
+        total = lax.optimization_barrier(total + part(block, offset, which))
+    return total + part(far_second, 2, 1)
 
 
 def per_device(queries, keys, values, segment_ids, norm_gain, out_weight):

time: 100 us -> 99.9 us (level)
  waiting for transfers between devices: 44.6 us -> 41.7 us
  matrix products: 14.9 us -> 17.5 us
  other arithmetic: 10.6 us -> 12.9 us
  starting transfers between devices: 22.1 us -> 20.4 us
    ppermute x6, waiting for transfers between devices: 30.5 us -> 26.6 us  [the longest x1 9.79 us: project_gathered(): left_first = lax.ppermute(first, axis, ahead)]
    add x0 -> x2, other arithmetic: none -> 2.73 us  [project_gathered(): total = lax.optimization_barrier(total + part(block, offset, which))]
    convert_element_type x0 -> x1, other arithmetic: none -> 2.05 us  [per_device(): return project_gathered(hidden, out_weight, 'mp').astype(jnp.bfloat16)]
    ppermute x6, starting transfers between devices: 8.67 us -> 6.96 us  [the longest x1 1.75 us: project_gathered(): right_first = lax.ppermute(first_later, axis, behind)]
    concatenate x1 -> x0, other arithmetic: 1.49 us -> none  [project_gathered(): return jnp.concatenate([out_top, out_bottom], axis=0)]
    dot_general x8 -> x7, matrix products: 5.84 us -> 7.16 us  [the longest x6 4.5 us: part(): jnp.dot(block, weight_halves[group, which], preferred_element_type=jnp.fl...]
    dot_general x1, matrix products: 0.43 us -> 1.66 us  [per_device(): jnp.einsum('thd,the->hde', feat_key * in_final[:, None, None], value_head...]
    all_to_all x1, waiting for transfers between devices: 10.5 us -> 11.5 us  [carried_in(): pieces = lax.all_to_all(sent, axis, 0, 0, tiled=True)]
  transfers between devices with their start and end apart: 8 -> 8, of which waited for: 5 -> 6; matrix products, arithmetic and copies ran while one was open for 15% -> 18% of each run, Pallas kernels for 0% -> 0%
where the time goes in v7:
time: 99.9 us; the launch traced here: 99.4 us
  waiting for transfers between devices  41.7 us (42%)
  starting transfers between devices  20.4 us (20%)
  matrix products  17.5 us (18%)
  other arithmetic  12.9 us (13%)
  local copies, waits for them, and re-layouts  5.43 us (5%)
  between operations  1.47 us (1%)
    all_to_all x1, waiting for transfers between devices, carried_in(): pieces = lax.all_to_all(sent, axis, 0, 0, tiled=True)  11.5 us
    all_to_all x1, starting transfers between devices, carried_in(): pieces = lax.all_to_all(sent, axis, 0, 0, tiled=True)  9.98 us
    ppermute x1, waiting for transfers between devices, project_gathered(): left_first = lax.ppermute(first, axis, ahead)  9.79 us
    ppermute x1, waiting for transfers between devices, project_gathered(): left_second = lax.ppermute(second_later, axis, ahead)  8.47 us
    ppermute x1, waiting for transfers between devices, project_gathered(): far_first = lax.ppermute(left_first, axis, ahead)  8.21 us
    dot_general x1, matrix products, per_device(): jnp.einsum('hts,she->the', weights, value_heads, preferred_element_type=j...  7.6 us
    dot_general x6, matrix products, part(): jnp.dot(block, weight_halves[group, which], preferred_element_type=jnp.fl...  4.5 us
    all_to_all x1, waiting for transfers between devices, carried_in(): return lax.all_to_all(carry, axis, 0, 0, tiled=True).reshape(shape)  3.55 us
  transfers between devices with their start and end apart: 8, of which 6 were waited for; matrix products, arithmetic and copies ran while one was open for 18% of the time, Pallas kernels for 0%

profile of v7, /device:TPU:1, one launch (start us, length us, event | category | flops | bytes accessed | tf_op | source)
XLA Modules:
  0.0 99.4 jit_solution(2327833807711369215)
XLA Ops:
  0.0 1.4 %fusion.57 = (s32[1]{0:T(128)}, s32[1]{0:T(128)}) fusion(s32[1024]{0:T(1024)} %param.9), kind=kLoop, calls=%fused_computation.77 | loop fusion | bytes 16 | tf_op jit(solution)/shard_map/slice | solution.py:98
  2.1 2.0 %compare_convert_fusion.1 = (f32[1024]{0:T(1024)S(1)}, bf16[1024]{0:T(1024)(128)(2,1)S(1)}) fusion(s32[1024]{0:T(1024)} %param.9, s32[]{:T(128)} %bitcast.1, s32[]{:T(128)} %bitcast.2), kind=kLoop, calls=%fused_computation.64 | loop fusion | flops 4096 | bytes 10248 | tf_op jit(solution)/shard_map/convert_element_type | solution.py:98
  4.7 2.2 %fusion.6 = bf16[1024,512]{1,0:T(8,128)(2,1)S(1)} fusion(bf16[1024,512]{1,0:T(8,128)(2,1)} %param.7), kind=kLoop, calls=%fused_computation.17 | loop fusion | flops 3145728 | bytes 2097152 | tf_op jit(solution)/shard_map/convert_element_type | solution.py:10
  6.9 1.3 %copy.50 = bf16[1024,512]{0,1:T(8,128)(2,1)} copy(bf16[1024,512]{1,0:T(8,128)(2,1)S(1)} %fusion.6) | data formatting | bytes 2097152 | tf_op jit(solution)/shard_map/reshape | solution.py:75
  8.4 1.7 %fusion.9 = f32[4,128,128]{2,1,0:T(8,128)S(1)} fusion(bf16[1024,4,128]{0,2,1:T(8,128)(2,1)} %bitcast.85, bf16[1024]{0:T(1024)(128)(2,1)S(1)} %get-tuple-element.18, bf16[1024,512]{1,0:T(8,128)(2,1)S(1)} %copy-done), kind=kOutput, calls=%fused_computation.23 | convolution fusion | flops 134742016 | bytes 2361344 | tf_op jit(solution)/shard_map/thd,the->hde/dot_general | solution.py:79
  10.9 10.0 %all-to-all-start = ((f32[16,40,128]{2,1,0:T(8,128)}), f32[16,40,128]{2,1,0:T(8,128)S(1)}, u32[]{:S(2)}, u32[]{:S(2)}) async-start(f32[16,40,128]{2,1,0:T(8,128)} %maximum_maximum_fusion), calls=%async_computation | async-start | bytes 655360 | tf_op jit(solution)/shard_map/all_to_all | solution.py:26
  22.4 11.5 %all-to-all-done = f32[16,40,128]{2,1,0:T(8,128)S(1)} async-done(((f32[16,40,128]{2,1,0:T(8,128)}), f32[16,40,128]{2,1,0:T(8,128)S(1)}, u32[]{:S(2)}, u32[]{:S(2)}) %all-to-all-start) | async-done | bytes 327712 | tf_op jit(solution)/shard_map/all_to_all | solution.py:26
  34.2 1.2 %select_reduce_fusion = f32[16,32,128]{2,1,0:T(8,128)} fusion(f32[16,32,128]{2,1,0:T(8,128)S(1)} %slice.31, pred[16,16]{1,0:T(8,128)(4,1)S(1)} %fusion.44), kind=kLoop, calls=%fused_computation.6 | loop fusion | flops 2031616 | bytes 524544 | tf_op jit(solution)/shard_map/reduce_sum | solution.py:32
  35.5 3.4 %all-to-all-start.1 = ((f32[16,32,128]{2,1,0:T(8,128)}), f32[16,32,128]{2,1,0:T(8,128)S(1)}, u32[]{:S(2)}, u32[]{:S(2)}) async-start(f32[16,32,128]{2,1,0:T(8,128)} %select_reduce_fusion), calls=%async_computation.1 | async-start | bytes 524288 | tf_op jit(solution)/shard_map/all_to_all | solution.py:33
  38.9 7.6 %fusion.7 = f32[4,1024,128]{1,2,0:T(8,128)} fusion(bf16[1024,4,128]{0,2,1:T(8,128)(2,1)} %bitcast.86, pred[1024,1024]{1,0:T(8,128)(4,1)S(1)} %fusion, bf16[1024,512]{1,0:T(8,128)(2,1)S(1)} %copy-done, bf16[1024,512]{1,0:T(8,128)(2,1)S(1)} %fusion.3), kind=kOutput, calls=%fused_computation.21 | convolution fusion | flops 2155872256 | bytes 6291456 | tf_op jit(solution)/shard_map/hts,she->the/dot_general | solution.py:92
  46.5 3.6 %all-to-all-done.1 = f32[16,32,128]{2,1,0:T(8,128)S(1)} async-done(((f32[16,32,128]{2,1,0:T(8,128)}), f32[16,32,128]{2,1,0:T(8,128)S(1)}, u32[]{:S(2)}, u32[]{:S(2)}) %all-to-all-start.1) | async-done | bytes 262176 | tf_op jit(solution)/shard_map/all_to_all | solution.py:33
  50.7 1.1 %copy-done.2 = f32[4,1024,128]{1,2,0:T(8,128)S(1)} copy-done((f32[4,1024,128]{1,2,0:T(8,128)S(1)}, f32[4,1024,128]{1,2,0:T(8,128)}, u32[]{:S(2)}) %copy-start.2) | copy-done | bytes 2097176
  52.7 1.0 %fusion.56 = (bf16[1024,256]{0,1:T(8,128)(2,1)}, bf16[1024,256]{0,1:T(8,128)(2,1)}) fusion(bf16[1024,512]{0,1:T(8,128)(2,1)S(1)} %bitcast.76), kind=kLoop, calls=%fused_computation.76 | loop fusion | bytes 2097152 | tf_op jit(solution)/shard_map/slice | solution.py:48
  53.8 1.3 %collective-permute-start = (bf16[1024,256]{0,1:T(8,128)(2,1)}, bf16[1024,256]{0,1:T(8,128)(2,1)S(1)}, u32[]{:S(2)}, u32[]{:S(2)}) collective-permute-start(bf16[1024,256]{0,1:T(8,128)(2,1)} %get-tuple-element.12), channel_id=1, source_target_pairs={{0,1},{1,2},{2,3},{3,0},{4,5},{5,6},{6,7},{7,4},{8,9},{9,10},{10,1... | collective-permute-start | bytes 1572872 | tf_op jit(solution)/shard_map/ppermute | solution.py:49
  55.1 1.4 %collective-permute-start.1 = (bf16[1024,256]{0,1:T(8,128)(2,1)}, bf16[1024,256]{0,1:T(8,128)(2,1)S(1)}, u32[]{:S(2)}, u32[]{:S(2)}) collective-permute-start(bf16[1024,256]{0,1:T(8,128)(2,1)} %get-tuple-element.11), channel_id=1, source_target_pairs={{0,3},{1,0},{2,1},{3,2},{4,7},{5,4},{6,5},{7,6},{8,11},{9,8},{10,9... | collective-permute-start | bytes 1572872 | tf_op jit(solution)/shard_map/ppermute | solution.py:50
  56.5 2.7 %fusion.16 = f32[1024,1024]{1,0:T(8,128)S(1)} fusion(bf16[1024,512]{0,1:T(8,128)(2,1)S(1)} %bitcast.77, bf16[4,512,1024]{2,1,0:T(8,128)(2,1)} %bitcast.78, s32[]{:T(128)S(6)} %select_n.45), kind=kOutput, calls=%fused_computation.29 | convolution fusion | flops 1073741824 | bytes 6291460 | tf_op jit(solution)/shard_map/dot_general | solution.py:58
  59.2 9.8 %collective-permute-done = bf16[1024,256]{0,1:T(8,128)(2,1)S(1)} collective-permute-done((bf16[1024,256]{0,1:T(8,128)(2,1)}, bf16[1024,256]{0,1:T(8,128)(2,1)S(1)}, u32[]{:S(2)}, u32[]{:S(2)}) %collective-permute-start) | collective-permute-done | bytes 524320 | tf_op jit(solution)/shard_map/ppermute | solution.py:49
  69.0 1.1 %collective-permute-start.2 = (bf16[1024,256]{0,1:T(8,128)(2,1)}, bf16[1024,256]{0,1:T(8,128)(2,1)S(1)}, u32[]{:S(2)}, u32[]{:S(2)}) collective-permute-start(bf16[1024,256]{0,1:T(8,128)(2,1)} %get-tuple-element.11), channel_id=1, source_target_pairs={{0,1},{1,2},{2,3},{3,0},{4,5},{5,6},{6,7},{7,4},{8,9},{9,10},{10,1... | collective-permute-start | bytes 1572872 | tf_op jit(solution)/shard_map/ppermute | solution.py:54
  71.8 1.8 %collective-permute-start.3 = (bf16[1024,256]{0,1:T(8,128)(2,1)}, bf16[1024,256]{0,1:T(8,128)(2,1)S(1)}, u32[]{:S(2)}, u32[]{:S(2)}) collective-permute-start(bf16[1024,256]{0,1:T(8,128)(2,1)} %get-tuple-element.12), channel_id=1, source_target_pairs={{0,3},{1,0},{2,1},{3,2},{4,7},{5,4},{6,5},{7,6},{8,11},{9,8},{10,9... | collective-permute-start | bytes 1572872 | tf_op jit(solution)/shard_map/ppermute | solution.py:55
  74.7 8.5 %collective-permute-done.2 = bf16[1024,256]{0,1:T(8,128)(2,1)S(1)} collective-permute-done((bf16[1024,256]{0,1:T(8,128)(2,1)}, bf16[1024,256]{0,1:T(8,128)(2,1)S(1)}, u32[]{:S(2)}, u32[]{:S(2)}) %collective-permute-start.2) | collective-permute-done | bytes 524320 | tf_op jit(solution)/shard_map/ppermute | solution.py:54
  84.9 1.4 %add.95 = f32[1024,1024]{1,0:T(8,128)S(1)} add(f32[1024,1024]{1,0:T(8,128)S(1)} %convolution_add_fusion, f32[1024,1024]{1,0:T(8,128)S(1)} %fusion.30) | non-fusion elementwise | flops 1048576 | bytes 12582912 | tf_op jit(solution)/shard_map/add | solution.py:66
  86.2 8.2 %collective-permute-done.4 = bf16[1024,256]{0,1:T(8,128)(2,1)S(1)} collective-permute-done((bf16[1024,256]{0,1:T(8,128)(2,1)S(1)}, bf16[1024,256]{0,1:T(8,128)(2,1)S(1)}, u32[]{:S(2)}, u32[]{:S(2)}) %collective-permute-start.4) | collective-permute-done | bytes 524320 | tf_op jit(solution)/shard_map/ppermute | solution.py:56
  95.2 1.4 %add.98 = f32[1024,1024]{1,0:T(8,128)S(1)} add(f32[1024,1024]{1,0:T(8,128)S(1)} %add.95, f32[1024,1024]{1,0:T(8,128)S(1)} %fusion.28) | non-fusion elementwise | flops 1048576 | bytes 12582912 | tf_op jit(solution)/shard_map/add | solution.py:66
  97.3 2.1 %add_convert_fusion = bf16[1024,1024]{1,0:T(8,128)(2,1)} fusion(f32[1024,1024]{1,0:T(8,128)S(1)} %add.98, f32[1024,1024]{1,0:T(8,128)S(1)} %fusion.26), kind=kLoop, calls=%fused_computation.5 | loop fusion | flops 2097152 | bytes 10485760 | tf_op jit(solution)/shard_map/convert_element_type | solution.py:103
  (36 shorter events, 10.3 us)
Async XLA Ops:
  0.0 8.4 %copy-start = (bf16[1024,512]{1,0:T(8,128)(2,1)S(1)}, bf16[1024,512]{1,0:T(8,128)(2,1)}, u32[]{:S(2)}) copy-start(bf16[1024,512]{1,0:T(8,128)(2,1)} %param.8) | copy-start | bytes 3145732
  4.7 16.2 %copy-start.3 = (bf16[1024,512]{1,0:T(8,128)(2,1)S(1)}, bf16[1024,512]{1,0:T(8,128)(2,1)}, u32[]{:S(2)}) copy-start(bf16[1024,512]{1,0:T(8,128)(2,1)} %param.6) | copy-start | bytes 3145732
  6.9 14.9 %copy-start.4 = (s32[1024]{0:T(1024)S(1)}, s32[1024]{0:T(1024)}, u32[]{:S(2)}) copy-start(s32[1024]{0:T(1024)} %param.9) | copy-start | bytes 12292
  10.9 23.1 %all-to-all-start = ((f32[16,40,128]{2,1,0:T(8,128)}), f32[16,40,128]{2,1,0:T(8,128)S(1)}, u32[]{:S(2)}, u32[]{:S(2)}) async-start(f32[16,40,128]{2,1,0:T(8,128)} %maximum_maximum_fusion), calls=%async_computation | async-start | bytes 655360 | tf_op jit(solution)/shard_map/all_to_all | solution.py:26
  35.5 14.6 %all-to-all-start.1 = ((f32[16,32,128]{2,1,0:T(8,128)}), f32[16,32,128]{2,1,0:T(8,128)S(1)}, u32[]{:S(2)}, u32[]{:S(2)}) async-start(f32[16,32,128]{2,1,0:T(8,128)} %select_reduce_fusion), calls=%async_computation.1 | async-start | bytes 524288 | tf_op jit(solution)/shard_map/all_to_all | solution.py:33
  50.2 1.6 %copy-start.2 = (f32[4,1024,128]{1,2,0:T(8,128)S(1)}, f32[4,1024,128]{1,2,0:T(8,128)}, u32[]{:S(2)}) copy-start(f32[4,1024,128]{1,2,0:T(8,128)} %fusion.7) | copy-start | bytes 6291460
  50.7 1.8 %copy-start.5 = (f32[512]{0:T(512)S(1)}, f32[512]{0:T(512)}, u32[]{:S(2)}) copy-start(f32[512]{0:T(512)} %param.10) | copy-start | bytes 6148
  53.8 15.2 %collective-permute-start = (bf16[1024,256]{0,1:T(8,128)(2,1)}, bf16[1024,256]{0,1:T(8,128)(2,1)S(1)}, u32[]{:S(2)}, u32[]{:S(2)}) collective-permute-start(bf16[1024,256]{0,1:T(8,128)(2,1)} %get-tuple-element.12), channel_id=1, source_target_pairs={{0,1},{1,2},{2,3},{3,0},{4,5},{5,6},{6,7},{7,4},{8,9},{9,10},{10,1... | collective-permute-start | bytes 1572872 | tf_op jit(solution)/shard_map/ppermute | solution.py:49
  55.1 13.9 %collective-permute-start.1 = (bf16[1024,256]{0,1:T(8,128)(2,1)}, bf16[1024,256]{0,1:T(8,128)(2,1)S(1)}, u32[]{:S(2)}, u32[]{:S(2)}) collective-permute-start(bf16[1024,256]{0,1:T(8,128)(2,1)} %get-tuple-element.11), channel_id=1, source_target_pairs={{0,3},{1,0},{2,1},{3,2},{4,7},{5,4},{6,5},{7,6},{8,11},{9,8},{10,9... | collective-permute-start | bytes 1572872 | tf_op jit(solution)/shard_map/ppermute | solution.py:50
  56.5 14.6 %copy-start.1 = (bf16[2048,1024]{1,0:T(8,128)(2,1)S(1)}, bf16[2048,1024]{1,0:T(8,128)(2,1)}, u32[]{:S(2)}) copy-start(bf16[2048,1024]{1,0:T(8,128)(2,1)} %param.11) | copy-start | bytes 12582916
  69.0 14.2 %collective-permute-start.2 = (bf16[1024,256]{0,1:T(8,128)(2,1)}, bf16[1024,256]{0,1:T(8,128)(2,1)S(1)}, u32[]{:S(2)}, u32[]{:S(2)}) collective-permute-start(bf16[1024,256]{0,1:T(8,128)(2,1)} %get-tuple-element.11), channel_id=1, source_target_pairs={{0,1},{1,2},{2,3},{3,0},{4,5},{5,6},{6,7},{7,4},{8,9},{9,10},{10,1... | collective-permute-start | bytes 1572872 | tf_op jit(solution)/shard_map/ppermute | solution.py:54
  70.1 24.4 %collective-permute-start.4 = (bf16[1024,256]{0,1:T(8,128)(2,1)S(1)}, bf16[1024,256]{0,1:T(8,128)(2,1)S(1)}, u32[]{:S(2)}, u32[]{:S(2)}) collective-permute-start(bf16[1024,256]{0,1:T(8,128)(2,1)S(1)} %collective-permute-done), channel_id=1, source_target_pairs={{0,1},{1,2},{2,3},{3,0},{4,5},{5,6},{6,7},{7,4},{8,9},{9,10},{10,1... | collective-permute-start | bytes 1572872 | tf_op jit(solution)/shard_map/ppermute | solution.py:56
  71.8 12.3 %collective-permute-start.3 = (bf16[1024,256]{0,1:T(8,128)(2,1)}, bf16[1024,256]{0,1:T(8,128)(2,1)S(1)}, u32[]{:S(2)}, u32[]{:S(2)}) collective-permute-start(bf16[1024,256]{0,1:T(8,128)(2,1)} %get-tuple-element.12), channel_id=1, source_target_pairs={{0,3},{1,0},{2,1},{3,2},{4,7},{5,4},{6,5},{7,6},{8,11},{9,8},{10,9... | collective-permute-start | bytes 1572872 | tf_op jit(solution)/shard_map/ppermute | solution.py:55
  73.6 23.0 %collective-permute-start.5 = (bf16[1024,256]{0,1:T(8,128)(2,1)S(1)}, bf16[1024,256]{0,1:T(8,128)(2,1)S(1)}, u32[]{:S(2)}, u32[]{:S(2)}) collective-permute-start(bf16[1024,256]{0,1:T(8,128)(2,1)S(1)} %collective-permute-done.1), channel_id=1, source_target_pairs={{0,3},{1,0},{2,1},{3,2},{4,7},{5,4},{6,5},{7,6},{8,11},{9,8},{10,9... | collective-permute-start | bytes 1572872 | tf_op jit(solution)/shard_map/ppermute | solution.py:57

commit v8 on v7

--- a/solution.py
+++ b/solution.py
@@ -77,9 +77,9 @@
     final_seg = segment_ids[rows_here - 1]
     in_final = (segment_ids == final_seg).astype(jnp.bfloat16)
     local_sum = jnp.einsum(
-        "thd,the->hde",
+        "the,thd->hed",
+        value_heads,
         feat_key * in_final[:, None, None],
-        value_heads,
         preferred_element_type=jnp.float32,
     )
     before_sum = carried_in(local_sum, final_seg, segment_ids[0], "ctx")
@@ -93,8 +93,8 @@
     state_hi = before_sum.astype(jnp.bfloat16)
     state_lo = (before_sum - state_hi.astype(jnp.float32)).astype(jnp.bfloat16)
     carried = jnp.einsum(
-        "thd,hde->the", feat_query, state_hi, preferred_element_type=jnp.float32
-    ) + jnp.einsum("thd,hde->the", feat_query, state_lo, preferred_element_type=jnp.float32)
+        "thd,hed->the", feat_query, state_hi, preferred_element_type=jnp.float32
+    ) + jnp.einsum("thd,hed->the", feat_query, state_lo, preferred_element_type=jnp.float32)
     carry_on = (segment_ids == segment_ids[0]).astype(jnp.float32)
     numerator = inside + carry_on[:, None, None] * carried
     normed = numerator * lax.rsqrt(jnp.mean(numerator * numerator, axis=-1, keepdims=True) + 1e-06)

time: 99.9 us -> 97.1 us (0.972)
  local copies, waits for them, and re-layouts: 5.43 us -> 3.36 us
  other arithmetic: 12.9 us -> 11.7 us
    convert_element_type x2 -> x1, other arithmetic: 3.18 us -> 0.94 us  [features(): (jax.nn.elu(raw_input.astype(jnp.float32)) + 1.0).astype(jnp.bfloat16)]
    dot_general x3, matrix products: 2.72 us -> 4.18 us  [the longest x1 3.08 us: per_device(): jnp.einsum('the,thd->hed', value_heads, feat_key * in_final[:, None, None...]
    unnamed x12 -> x10, local copies, waits for them, and re-layouts: 1.16 us -> 0.03 us
  transfers between devices with their start and end apart: 8 -> 8, of which waited for: 6 -> 6; matrix products, arithmetic and copies ran while one was open for 18% -> 19% of each run, Pallas kernels for 0% -> 0%
where the time goes in v8:
time: 97.1 us; the launch traced here: 96.7 us
  waiting for transfers between devices  40.9 us (42%)
  starting transfers between devices  20.9 us (22%)
  matrix products  18.3 us (19%)
  other arithmetic  11.7 us (12%)
  local copies, waits for them, and re-layouts  3.36 us (3%)
  between operations  1.48 us (2%)
    all_to_all x1, waiting for transfers between devices, carried_in(): pieces = lax.all_to_all(sent, axis, 0, 0, tiled=True)  10.6 us
    all_to_all x1, starting transfers between devices, carried_in(): pieces = lax.all_to_all(sent, axis, 0, 0, tiled=True)  9.98 us
    ppermute x1, waiting for transfers between devices, project_gathered(): left_first = lax.ppermute(first, axis, ahead)  9.33 us
    ppermute x1, waiting for transfers between devices, project_gathered(): left_second = lax.ppermute(second_later, axis, ahead)  8.47 us
    ppermute x1, waiting for transfers between devices, project_gathered(): far_first = lax.ppermute(left_first, axis, ahead)  8.28 us
    dot_general x1, matrix products, per_device(): jnp.einsum('hts,she->the', weights, value_heads, preferred_element_type=j...  7 us
    dot_general x6, matrix products, part(): jnp.dot(block, weight_halves[group, which], preferred_element_type=jnp.fl...  4.49 us
    all_to_all x1, waiting for transfers between devices, carried_in(): return lax.all_to_all(carry, axis, 0, 0, tiled=True).reshape(shape)  4.14 us
  transfers between devices with their start and end apart: 8, of which 6 were waited for; matrix products, arithmetic and copies ran while one was open for 19% of the time, Pallas kernels for 0%

profile of v8, /device:TPU:1, one launch (start us, length us, event | category | flops | bytes accessed | tf_op | source)
XLA Modules:
  0.0 96.7 jit_solution(4933915292478560075)
XLA Ops:
  0.0 1.4 %fusion.57 = (s32[1]{0:T(128)}, s32[1]{0:T(128)}) fusion(s32[1024]{0:T(1024)} %param.9), kind=kLoop, calls=%fused_computation.77 | loop fusion | bytes 16 | tf_op jit(solution)/shard_map/slice | solution.py:98
  2.0 2.0 %compare_convert_fusion.1 = (f32[1024]{0:T(1024)S(1)}, bf16[1024]{0:T(1024)(128)(2,1)S(1)}) fusion(s32[1024]{0:T(1024)} %param.9, s32[]{:T(128)} %bitcast.1, s32[]{:T(128)} %bitcast.2), kind=kLoop, calls=%fused_computation.64 | loop fusion | flops 4096 | bytes 10248 | tf_op jit(solution)/shard_map/convert_element_type | solution.py:98
  4.6 1.5 %copy.33 = bf16[1024,512]{0,1:T(8,128)(2,1)S(1)} copy(bf16[1024,512]{1,0:T(8,128)(2,1)} %param.8) | data formatting | bytes 2097152 | tf_op jit(solution)/shard_map/reshape | solution.py:76
  6.3 3.1 %fusion.11 = f32[4,128,128]{1,2,0:T(8,128)S(1)} fusion(bf16[1024,4,128]{0,2,1:T(8,128)(2,1)S(1)} %bitcast.97, bf16[1024]{0:T(1024)(128)(2,1)S(1)} %get-tuple-element.20, bf16[1024,512]{1,0:T(8,128)(2,1)} %param.7), kind=kOutput, calls=%fused_computation.25 | convolution fusion | flops 139460608 | bytes 2361344 | tf_op jit(solution)/shard_map/the,thd->hed/dot_general | solution.py:79
  10.3 10.0 %all-to-all-start = ((f32[16,40,128]{2,1,0:T(8,128)}), f32[16,40,128]{2,1,0:T(8,128)S(1)}, u32[]{:S(2)}, u32[]{:S(2)}) async-start(f32[16,40,128]{2,1,0:T(8,128)} %maximum_maximum_fusion), calls=%async_computation | async-start | bytes 655360 | tf_op jit(solution)/shard_map/all_to_all | solution.py:26
  20.2 0.9 fusion.3
  21.2 1.6 %fusion = pred[1024,1024]{1,0:T(8,128)(4,1)} fusion(s32[1024]{0:T(1024)S(1)} %copy-done.3), kind=kLoop, calls=%fused_computation.8 | loop fusion | flops 3145728 | bytes 1052672 | tf_op jit(solution)/shard_map/and | solution.py:87
  22.8 10.6 %all-to-all-done = f32[16,40,128]{2,1,0:T(8,128)S(1)} async-done(((f32[16,40,128]{2,1,0:T(8,128)}), f32[16,40,128]{2,1,0:T(8,128)S(1)}, u32[]{:S(2)}, u32[]{:S(2)}) %all-to-all-start) | async-done | bytes 327712 | tf_op jit(solution)/shard_map/all_to_all | solution.py:26
  33.6 1.2 %select_reduce_fusion = f32[16,32,128]{2,1,0:T(8,128)} fusion(f32[16,32,128]{2,1,0:T(8,128)S(1)} %slice.31, pred[16,16]{1,0:T(8,128)(4,1)S(1)} %fusion.44), kind=kLoop, calls=%fused_computation.6 | loop fusion | flops 2031616 | bytes 524544 | tf_op jit(solution)/shard_map/reduce_sum | solution.py:32
  34.9 3.4 %all-to-all-start.1 = ((f32[16,32,128]{2,1,0:T(8,128)}), f32[16,32,128]{2,1,0:T(8,128)S(1)}, u32[]{:S(2)}, u32[]{:S(2)}) async-start(f32[16,32,128]{2,1,0:T(8,128)} %select_reduce_fusion), calls=%async_computation.1 | async-start | bytes 524288 | tf_op jit(solution)/shard_map/all_to_all | solution.py:33
  38.3 7.0 %fusion.7 = f32[4,1024,128]{1,2,0:T(8,128)S(1)} fusion(bf16[1024,4,128]{0,2,1:T(8,128)(2,1)} %bitcast.98, pred[1024,1024]{1,0:T(8,128)(4,1)} %fusion, bf16[1024,512]{1,0:T(8,128)(2,1)S(1)} %fusion.3, bf16[1024,512]{1,0:T(8,128)(2,1)} %param.7), kind=kOutput, calls=%fused_computation.21 | convolution fusion | flops 2159017984 | bytes 6291456 | tf_op jit(solution)/shard_map/hts,she->the/dot_general | solution.py:92
  45.3 4.1 %all-to-all-done.1 = f32[16,32,128]{2,1,0:T(8,128)S(1)} async-done(((f32[16,32,128]{2,1,0:T(8,128)}), f32[16,32,128]{2,1,0:T(8,128)S(1)}, u32[]{:S(2)}, u32[]{:S(2)}) %all-to-all-start.1) | async-done | bytes 262176 | tf_op jit(solution)/shard_map/all_to_all | solution.py:33
  51.0 1.4 %collective-permute-start = (bf16[1024,256]{0,1:T(8,128)(2,1)S(1)}, bf16[1024,256]{0,1:T(8,128)(2,1)S(1)}, u32[]{:S(2)}, u32[]{:S(2)}) collective-permute-start(bf16[1024,256]{0,1:T(8,128)(2,1)S(1)} %get-tuple-element.12), channel_id=1, source_target_pairs={{0,1},{1,2},{2,3},{3,0},{4,5},{5,6},{6,7},{7,4},{8,9},{9,10},{10,1... | collective-permute-start | bytes 1572872 | tf_op jit(solution)/shard_map/ppermute | solution.py:49
  52.3 1.7 %collective-permute-start.1 = (bf16[1024,256]{0,1:T(8,128)(2,1)S(1)}, bf16[1024,256]{0,1:T(8,128)(2,1)S(1)}, u32[]{:S(2)}, u32[]{:S(2)}) collective-permute-start(bf16[1024,256]{0,1:T(8,128)(2,1)S(1)} %get-tuple-element.11), channel_id=1, source_target_pairs={{0,3},{1,0},{2,1},{3,2},{4,7},{5,4},{6,5},{7,6},{8,11},{9,8},{10,9... | collective-permute-start | bytes 1572872 | tf_op jit(solution)/shard_map/ppermute | solution.py:50
  54.1 2.7 %fusion.17 = f32[1024,1024]{1,0:T(8,128)S(1)} fusion(bf16[1024,512]{0,1:T(8,128)(2,1)S(1)} %bitcast.89, bf16[4,512,1024]{2,1,0:T(8,128)(2,1)} %bitcast.90, s32[]{:T(128)S(6)} %select_n.45), kind=kOutput, calls=%fused_computation.30 | convolution fusion | flops 1073741824 | bytes 6291460 | tf_op jit(solution)/shard_map/dot_general | solution.py:58
  56.7 9.3 %collective-permute-done = bf16[1024,256]{0,1:T(8,128)(2,1)S(1)} collective-permute-done((bf16[1024,256]{0,1:T(8,128)(2,1)S(1)}, bf16[1024,256]{0,1:T(8,128)(2,1)S(1)}, u32[]{:S(2)}, u32[]{:S(2)}) %collective-permute-start) | collective-permute-done | bytes 524320 | tf_op jit(solution)/shard_map/ppermute | solution.py:49
  66.1 1.1 %collective-permute-start.2 = (bf16[1024,256]{0,1:T(8,128)(2,1)S(1)}, bf16[1024,256]{0,1:T(8,128)(2,1)S(1)}, u32[]{:S(2)}, u32[]{:S(2)}) collective-permute-start(bf16[1024,256]{0,1:T(8,128)(2,1)S(1)} %get-tuple-element.11), channel_id=1, source_target_pairs={{0,1},{1,2},{2,3},{3,0},{4,5},{5,6},{6,7},{7,4},{8,9},{9,10},{10,1... | collective-permute-start | bytes 1572872 | tf_op jit(solution)/shard_map/ppermute | solution.py:54
  67.1 1.0 %collective-permute-start.4 = (bf16[1024,256]{0,1:T(8,128)(2,1)S(1)}, bf16[1024,256]{0,1:T(8,128)(2,1)S(1)}, u32[]{:S(2)}, u32[]{:S(2)}) collective-permute-start(bf16[1024,256]{0,1:T(8,128)(2,1)S(1)} %collective-permute-done), channel_id=1, source_target_pairs={{0,1},{1,2},{2,3},{3,0},{4,5},{5,6},{6,7},{7,4},{8,9},{9,10},{10,1... | collective-permute-start | bytes 1572872 | tf_op jit(solution)/shard_map/ppermute | solution.py:56
  68.9 1.8 %collective-permute-start.3 = (bf16[1024,256]{0,1:T(8,128)(2,1)S(1)}, bf16[1024,256]{0,1:T(8,128)(2,1)S(1)}, u32[]{:S(2)}, u32[]{:S(2)}) collective-permute-start(bf16[1024,256]{0,1:T(8,128)(2,1)S(1)} %get-tuple-element.12), channel_id=1, source_target_pairs={{0,3},{1,0},{2,1},{3,2},{4,7},{5,4},{6,5},{7,6},{8,11},{9,8},{10,9... | collective-permute-start | bytes 1572872 | tf_op jit(solution)/shard_map/ppermute | solution.py:55
  72.0 8.5 %collective-permute-done.2 = bf16[1024,256]{0,1:T(8,128)(2,1)S(1)} collective-permute-done((bf16[1024,256]{0,1:T(8,128)(2,1)S(1)}, bf16[1024,256]{0,1:T(8,128)(2,1)S(1)}, u32[]{:S(2)}, u32[]{:S(2)}) %collective-permute-start.2) | collective-permute-done | bytes 524320 | tf_op jit(solution)/shard_map/ppermute | solution.py:54
  82.1 1.4 %add.95 = f32[1024,1024]{1,0:T(8,128)S(1)} add(f32[1024,1024]{1,0:T(8,128)S(1)} %convolution_add_fusion, f32[1024,1024]{1,0:T(8,128)S(1)} %fusion.31) | non-fusion elementwise | flops 1048576 | bytes 12582912 | tf_op jit(solution)/shard_map/add | solution.py:66
  83.5 8.3 %collective-permute-done.4 = bf16[1024,256]{0,1:T(8,128)(2,1)S(1)} collective-permute-done((bf16[1024,256]{0,1:T(8,128)(2,1)S(1)}, bf16[1024,256]{0,1:T(8,128)(2,1)S(1)}, u32[]{:S(2)}, u32[]{:S(2)}) %collective-permute-start.4) | collective-permute-done | bytes 524320 | tf_op jit(solution)/shard_map/ppermute | solution.py:56
  92.5 1.4 %add.98 = f32[1024,1024]{1,0:T(8,128)S(1)} add(f32[1024,1024]{1,0:T(8,128)S(1)} %add.95, f32[1024,1024]{1,0:T(8,128)S(1)} %fusion.29) | non-fusion elementwise | flops 1048576 | bytes 12582912 | tf_op jit(solution)/shard_map/add | solution.py:66
  94.6 2.1 %add_convert_fusion = bf16[1024,1024]{1,0:T(8,128)(2,1)} fusion(f32[1024,1024]{1,0:T(8,128)S(1)} %add.98, f32[1024,1024]{1,0:T(8,128)S(1)} %fusion.27), kind=kLoop, calls=%fused_computation.5 | loop fusion | flops 2097152 | bytes 10485760 | tf_op jit(solution)/shard_map/convert_element_type | solution.py:103
  (33 shorter events, 8.0 us)
Async XLA Ops:
  6.1 4.1 %copy-start.2 = (bf16[1024,512]{0,1:T(8,128)(2,1)}, bf16[1024,512]{0,1:T(8,128)(2,1)S(1)}, u32[]{:S(2)}) copy-start(bf16[1024,512]{0,1:T(8,128)(2,1)S(1)} %copy.33) | copy-start | bytes 3145732
  6.1 14.1 %copy-start.1 = (bf16[1024,512]{1,0:T(8,128)(2,1)S(1)}, bf16[1024,512]{1,0:T(8,128)(2,1)}, u32[]{:S(2)}) copy-start(bf16[1024,512]{1,0:T(8,128)(2,1)} %param.6) | copy-start | bytes 3145732
  6.3 14.9 %copy-start.3 = (s32[1024]{0:T(1024)S(1)}, s32[1024]{0:T(1024)}, u32[]{:S(2)}) copy-start(s32[1024]{0:T(1024)} %param.9) | copy-start | bytes 12292
  10.3 23.1 %all-to-all-start = ((f32[16,40,128]{2,1,0:T(8,128)}), f32[16,40,128]{2,1,0:T(8,128)S(1)}, u32[]{:S(2)}, u32[]{:S(2)}) async-start(f32[16,40,128]{2,1,0:T(8,128)} %maximum_maximum_fusion), calls=%async_computation | async-start | bytes 655360 | tf_op jit(solution)/shard_map/all_to_all | solution.py:26
  34.9 14.6 %all-to-all-start.1 = ((f32[16,32,128]{2,1,0:T(8,128)}), f32[16,32,128]{2,1,0:T(8,128)S(1)}, u32[]{:S(2)}, u32[]{:S(2)}) async-start(f32[16,32,128]{2,1,0:T(8,128)} %select_reduce_fusion), calls=%async_computation.1 | async-start | bytes 524288 | tf_op jit(solution)/shard_map/all_to_all | solution.py:33
  49.9 0.7 copy-start.4
  51.0 15.1 %collective-permute-start = (bf16[1024,256]{0,1:T(8,128)(2,1)S(1)}, bf16[1024,256]{0,1:T(8,128)(2,1)S(1)}, u32[]{:S(2)}, u32[]{:S(2)}) collective-permute-start(bf16[1024,256]{0,1:T(8,128)(2,1)S(1)} %get-tuple-element.12), channel_id=1, source_target_pairs={{0,1},{1,2},{2,3},{3,0},{4,5},{5,6},{6,7},{7,4},{8,9},{9,10},{10,1... | collective-permute-start | bytes 1572872 | tf_op jit(solution)/shard_map/ppermute | solution.py:49
  52.3 13.7 %collective-permute-start.1 = (bf16[1024,256]{0,1:T(8,128)(2,1)S(1)}, bf16[1024,256]{0,1:T(8,128)(2,1)S(1)}, u32[]{:S(2)}, u32[]{:S(2)}) collective-permute-start(bf16[1024,256]{0,1:T(8,128)(2,1)S(1)} %get-tuple-element.11), channel_id=1, source_target_pairs={{0,3},{1,0},{2,1},{3,2},{4,7},{5,4},{6,5},{7,6},{8,11},{9,8},{10,9... | collective-permute-start | bytes 1572872 | tf_op jit(solution)/shard_map/ppermute | solution.py:50
  54.1 14.1 %copy-start = (bf16[2048,1024]{1,0:T(8,128)(2,1)S(1)}, bf16[2048,1024]{1,0:T(8,128)(2,1)}, u32[]{:S(2)}) copy-start(bf16[2048,1024]{1,0:T(8,128)(2,1)} %param.11) | copy-start | bytes 12582916
  66.1 14.5 %collective-permute-start.2 = (bf16[1024,256]{0,1:T(8,128)(2,1)S(1)}, bf16[1024,256]{0,1:T(8,128)(2,1)S(1)}, u32[]{:S(2)}, u32[]{:S(2)}) collective-permute-start(bf16[1024,256]{0,1:T(8,128)(2,1)S(1)} %get-tuple-element.11), channel_id=1, source_target_pairs={{0,1},{1,2},{2,3},{3,0},{4,5},{5,6},{6,7},{7,4},{8,9},{9,10},{10,1... | collective-permute-start | bytes 1572872 | tf_op jit(solution)/shard_map/ppermute | solution.py:54
  67.1 24.6 %collective-permute-start.4 = (bf16[1024,256]{0,1:T(8,128)(2,1)S(1)}, bf16[1024,256]{0,1:T(8,128)(2,1)S(1)}, u32[]{:S(2)}, u32[]{:S(2)}) collective-permute-start(bf16[1024,256]{0,1:T(8,128)(2,1)S(1)} %collective-permute-done), channel_id=1, source_target_pairs={{0,1},{1,2},{2,3},{3,0},{4,5},{5,6},{6,7},{7,4},{8,9},{9,10},{10,1... | collective-permute-start | bytes 1572872 | tf_op jit(solution)/shard_map/ppermute | solution.py:56
  68.9 12.4 %collective-permute-start.3 = (bf16[1024,256]{0,1:T(8,128)(2,1)S(1)}, bf16[1024,256]{0,1:T(8,128)(2,1)S(1)}, u32[]{:S(2)}, u32[]{:S(2)}) collective-permute-start(bf16[1024,256]{0,1:T(8,128)(2,1)S(1)} %get-tuple-element.12), channel_id=1, source_target_pairs={{0,3},{1,0},{2,1},{3,2},{4,7},{5,4},{6,5},{7,6},{8,11},{9,8},{10,9... | collective-permute-start | bytes 1572872 | tf_op jit(solution)/shard_map/ppermute | solution.py:55
  70.7 23.2 %collective-permute-start.5 = (bf16[1024,256]{0,1:T(8,128)(2,1)S(1)}, bf16[1024,256]{0,1:T(8,128)(2,1)S(1)}, u32[]{:S(2)}, u32[]{:S(2)}) collective-permute-start(bf16[1024,256]{0,1:T(8,128)(2,1)S(1)} %collective-permute-done.1), channel_id=1, source_target_pairs={{0,3},{1,0},{2,1},{3,2},{4,7},{5,4},{6,5},{7,6},{8,11},{9,8},{10,9... | collective-permute-start | bytes 1572872 | tf_op jit(solution)/shard_map/ppermute | solution.py:57

commit v9 on v8

--- a/solution.py
+++ b/solution.py
@@ -41,30 +41,22 @@
     ahead = [(j, (j + 1) % count) for j in range(count)]
     behind = [(j, (j - 1) % count) for j in range(count)]
 
-    def part(block, offset, which):
-        group = lax.rem(mine + offset + count, count)
-        return jnp.dot(block, weight_halves[group, which], preferred_element_type=jnp.float32)
+    def rows_of(offset, which):
+        return weight_halves[lax.rem(mine + offset + count, count), which]
+
+    def dot(block, weight):
+        return jnp.dot(block, weight, preferred_element_type=jnp.float32)
 
     first, second = hidden[:, :half], hidden[:, half:]
     left_first = lax.ppermute(first, axis, ahead)
     right_second = lax.ppermute(second, axis, behind)
-    left_first, right_second, first_later, second_later = lax.optimization_barrier(
-        (left_first, right_second, first, second)
-    )
-    left_second = lax.ppermute(second_later, axis, ahead)
-    right_first = lax.ppermute(first_later, axis, behind)
-    far_first = lax.ppermute(left_first, axis, ahead)
-    far_second = lax.ppermute(right_second, axis, behind)
-    total = jnp.dot(hidden, out_weight.reshape(count, width, -1)[mine], preferred_element_type=jnp.float32)
-    for block, offset, which in (
-        (left_first, -1, 0),
-        (right_second, 1, 1),
-        (left_second, -1, 1),
-        (right_first, 1, 0),
-        (far_first, 2, 0),
-    ):
-        total = lax.optimization_barrier(total + part(block, offset, which))
-    return total + part(far_second, 2, 1)
+    from_left = lax.ppermute(jnp.concatenate([second, left_first], axis=1), axis, ahead)
+    from_right = lax.ppermute(jnp.concatenate([first, right_second], axis=1), axis, behind)
+    left_weight = jnp.concatenate([rows_of(-1, 1), rows_of(2, 0)], axis=0)
+    right_weight = jnp.concatenate([rows_of(1, 0), rows_of(2, 1)], axis=0)
+    total = dot(hidden, out_weight.reshape(count, width, -1)[mine])
+    total = total + dot(left_first, rows_of(-1, 0)) + dot(right_second, rows_of(1, 1))
+    return total + dot(from_left, left_weight) + dot(from_right, right_weight)
 
 
 def per_device(queries, keys, values, segment_ids, norm_gain, out_weight):

time: 97.1 us -> 94.9 us (0.977)
  other arithmetic: 11.7 us -> 7.06 us
  waiting for transfers between devices: 40.9 us -> 44.6 us
  local copies, waits for them, and re-layouts: 3.36 us -> 5.07 us
  starting transfers between devices: 20.9 us -> 19.4 us
  matrix products: 18.3 us -> 16.9 us
    ppermute x4 -> x2, waiting for transfers between devices: 16.8 us -> 19.7 us  [the longest x1 19.7 us: project_gathered(): lax.ppermute(jnp.concatenate([second, left_first], axis=1), axis, ahead)]
    add x2 -> x0, other arithmetic: 2.73 us -> none  [project_gathered(): total = lax.optimization_barrier(total + part(block, offset, which))]
    convert_element_type x1 -> x0, other arithmetic: 2.05 us -> none  [per_device(): return project_gathered(hidden, out_weight, 'mp').astype(jnp.bfloat16)]
    dot_general x1, matrix products: 3.08 us -> 1.36 us  [per_device(): jnp.einsum('the,thd->hed', value_heads, feat_key * in_final[:, None, None...]
    squeeze x0 -> x1, local copies, waits for them, and re-layouts: none -> 1.69 us  [rows_of(): return weight_halves[lax.rem(mine + offset + count, count), which]]
    ppermute x4 -> x2, starting transfers between devices: 4.45 us -> 2.85 us  [the longest x1 2.77 us: project_gathered(): lax.ppermute(jnp.concatenate([first, right_second], axis=1), axis, behind)]
    dot_general x7 -> x5, matrix products: 7.15 us -> 7.39 us  [dot(): return jnp.dot(block, weight, preferred_element_type=jnp.float32)]
  transfers between devices with their start and end apart: 8 -> 6, of which waited for: 6 -> 4; matrix products, arithmetic and copies ran while one was open for 19% -> 16% of each run, Pallas kernels for 0% -> 0%
where the time goes in v9:
time: 94.9 us; the launch traced here: 94.5 us
  waiting for transfers between devices  44.6 us (47%)
  starting transfers between devices  19.4 us (20%)
  matrix products  16.9 us (18%)
  other arithmetic  7.06 us (7%)
  local copies, waits for them, and re-layouts  5.07 us (5%)
  between operations  1.49 us (2%)
    ppermute x1, waiting for transfers between devices, project_gathered(): lax.ppermute(jnp.concatenate([second, left_first], axis=1), axis, ahead)  19.7 us
    all_to_all x1, waiting for transfers between devices, carried_in(): pieces = lax.all_to_all(sent, axis, 0, 0, tiled=True)  10.6 us
    ppermute x1, waiting for transfers between devices, project_gathered(): left_first = lax.ppermute(first, axis, ahead)  10.3 us
    all_to_all x1, starting transfers between devices, carried_in(): pieces = lax.all_to_all(sent, axis, 0, 0, tiled=True)  9.98 us
    dot_general x5, matrix products, dot(): return jnp.dot(block, weight, preferred_element_type=jnp.float32)  7.39 us
    dot_general x1, matrix products, per_device(): jnp.einsum('hts,she->the', weights, value_heads, preferred_element_type=j...  7 us
    all_to_all x1, waiting for transfers between devices, carried_in(): return lax.all_to_all(carry, axis, 0, 0, tiled=True).reshape(shape)  4.14 us
    all_to_all x1, starting transfers between devices, carried_in(): return lax.all_to_all(carry, axis, 0, 0, tiled=True).reshape(shape)  3.43 us
  transfers between devices with their start and end apart: 6, of which 4 were waited for; matrix products, arithmetic and copies ran while one was open for 16% of the time, Pallas kernels for 0%

profile of v9, /device:TPU:1, one launch (start us, length us, event | category | flops | bytes accessed | tf_op | source)
XLA Modules:
  0.0 94.5 jit_solution(12446138084411365766)
XLA Ops:
  0.0 1.4 %fusion.54 = (s32[1]{0:T(128)}, s32[1]{0:T(128)}) fusion(s32[1024]{0:T(1024)} %param.9), kind=kLoop, calls=%fused_computation.75 | loop fusion | bytes 16 | tf_op jit(solution)/shard_map/slice | solution.py:90
  2.7 2.0 %compare_convert_fusion.1 = (f32[1024]{0:T(1024)S(1)}, bf16[1024]{0:T(1024)(128)(2,1)S(1)}) fusion(s32[1024]{0:T(1024)} %param.9, s32[]{:T(128)} %bitcast.1, s32[]{:T(128)} %bitcast.2), kind=kLoop, calls=%fused_computation.66 | loop fusion | flops 4096 | bytes 10248 | tf_op jit(solution)/shard_map/convert_element_type | solution.py:90
  4.8 1.5 %copy.33 = bf16[1024,512]{0,1:T(8,128)(2,1)S(1)} copy(bf16[1024,512]{1,0:T(8,128)(2,1)} %param.8) | data formatting | bytes 2097152 | tf_op jit(solution)/shard_map/reshape | solution.py:68
  6.3 1.4 %fusion.11 = f32[4,128,128]{1,2,0:T(8,128)S(1)} fusion(bf16[1024,4,128]{0,2,1:T(8,128)(2,1)S(1)} %bitcast.88, bf16[1024]{0:T(1024)(128)(2,1)S(1)} %get-tuple-element.16, bf16[1024,512]{1,0:T(8,128)(2,1)S(1)} %copy-done.5), kind=kOutput, calls=%fused_computation.22 | convolution fusion | flops 139460608 | bytes 2361344 | tf_op jit(solution)/shard_map/the,thd->hed/dot_general | solution.py:71
  7.7 0.8 maximum_maximum_fusion
  8.6 10.0 %all-to-all-start = ((f32[16,40,128]{2,1,0:T(8,128)}), f32[16,40,128]{2,1,0:T(8,128)S(1)}, u32[]{:S(2)}, u32[]{:S(2)}) async-start(f32[16,40,128]{2,1,0:T(8,128)} %maximum_maximum_fusion), calls=%async_computation | async-start | bytes 655360 | tf_op jit(solution)/shard_map/all_to_all | solution.py:26
  18.6 0.9 fusion.3
  19.5 1.6 %fusion = pred[1024,1024]{1,0:T(8,128)(4,1)} fusion(s32[1024]{0:T(1024)S(1)} %copy-done.3), kind=kLoop, calls=%fused_computation.8 | loop fusion | flops 3145728 | bytes 1052672 | tf_op jit(solution)/shard_map/and | solution.py:79
  21.1 10.6 %all-to-all-done = f32[16,40,128]{2,1,0:T(8,128)S(1)} async-done(((f32[16,40,128]{2,1,0:T(8,128)}), f32[16,40,128]{2,1,0:T(8,128)S(1)}, u32[]{:S(2)}, u32[]{:S(2)}) %all-to-all-start) | async-done | bytes 327712 | tf_op jit(solution)/shard_map/all_to_all | solution.py:26
  31.9 1.2 %select_reduce_fusion = f32[16,32,128]{2,1,0:T(8,128)} fusion(f32[16,32,128]{2,1,0:T(8,128)S(1)} %slice.31, pred[16,16]{1,0:T(8,128)(4,1)S(1)} %fusion.45), kind=kLoop, calls=%fused_computation.6 | loop fusion | flops 2031616 | bytes 524544 | tf_op jit(solution)/shard_map/reduce_sum | solution.py:32
  33.2 3.4 %all-to-all-start.1 = ((f32[16,32,128]{2,1,0:T(8,128)}), f32[16,32,128]{2,1,0:T(8,128)S(1)}, u32[]{:S(2)}, u32[]{:S(2)}) async-start(f32[16,32,128]{2,1,0:T(8,128)} %select_reduce_fusion), calls=%async_computation.1 | async-start | bytes 524288 | tf_op jit(solution)/shard_map/all_to_all | solution.py:33
  36.6 7.0 %fusion.7 = f32[4,1024,128]{1,2,0:T(8,128)S(1)} fusion(bf16[1024,4,128]{0,2,1:T(8,128)(2,1)} %bitcast.89, pred[1024,1024]{1,0:T(8,128)(4,1)} %fusion, bf16[1024,512]{1,0:T(8,128)(2,1)S(1)} %fusion.3, bf16[1024,512]{1,0:T(8,128)(2,1)} %param.7), kind=kOutput, calls=%fused_computation.18 | convolution fusion | flops 2159017984 | bytes 6291456 | tf_op jit(solution)/shard_map/hts,she->the/dot_general | solution.py:84
  43.6 4.1 %all-to-all-done.1 = f32[16,32,128]{2,1,0:T(8,128)S(1)} async-done(((f32[16,32,128]{2,1,0:T(8,128)}), f32[16,32,128]{2,1,0:T(8,128)S(1)}, u32[]{:S(2)}, u32[]{:S(2)}) %all-to-all-start.1) | async-done | bytes 262176 | tf_op jit(solution)/shard_map/all_to_all | solution.py:33
  49.3 1.4 %collective-permute-start = (bf16[1024,256]{0,1:T(8,128)(2,1)S(1)}, bf16[1024,256]{0,1:T(8,128)(2,1)S(1)}, u32[]{:S(2)}, u32[]{:S(2)}) collective-permute-start(bf16[1024,256]{0,1:T(8,128)(2,1)S(1)} %get-tuple-element.14), channel_id=1, source_target_pairs={{0,1},{1,2},{2,3},{3,0},{4,5},{5,6},{6,7},{7,4},{8,9},{9,10},{10,1... | collective-permute-start | bytes 1572872 | tf_op jit(solution)/shard_map/ppermute | solution.py:51
  50.7 1.7 %collective-permute-start.1 = (bf16[1024,256]{0,1:T(8,128)(2,1)S(1)}, bf16[1024,256]{0,1:T(8,128)(2,1)S(1)}, u32[]{:S(2)}, u32[]{:S(2)}) collective-permute-start(bf16[1024,256]{0,1:T(8,128)(2,1)S(1)} %get-tuple-element.13), channel_id=1, source_target_pairs={{0,3},{1,0},{2,1},{3,2},{4,7},{5,4},{6,5},{7,6},{8,11},{9,8},{10,9... | collective-permute-start | bytes 1572872 | tf_op jit(solution)/shard_map/ppermute | solution.py:52
  52.4 1.7 %dynamic-slice_bitcast_fusion.1 = (bf16[256,1024]{1,0:T(8,128)(2,1)S(1)}, bf16[256,1024]{1,0:T(8,128)(2,1)S(1)}, bf16[256,1024]{1,0:T(8,128)(2,1)S(1)}, bf16[256,1024]{1,0:T(8,128)(2,1)S(1)}) fusion(bf16[4,2,256,1024]{3,2,1,0:T(8,128)(2,1)} %bitcast.84, s32[]{:T(128)S(6)} %select_n.47, s32[]{:T(128)S(6)} %select_n.48, s32[]{:T(128)S(6)} %select_n.46), kind=kLoop, calls=%fused_computation.50 | loop fusion | bytes 4194316 | tf_op jit(solution)/shard_map/squeeze | solution.py:45
  54.1 10.3 %collective-permute-done = bf16[1024,256]{0,1:T(8,128)(2,1)S(1)} collective-permute-done((bf16[1024,256]{0,1:T(8,128)(2,1)S(1)}, bf16[1024,256]{0,1:T(8,128)(2,1)S(1)}, u32[]{:S(2)}, u32[]{:S(2)}) %collective-permute-start) | collective-permute-done | bytes 524320 | tf_op jit(solution)/shard_map/ppermute | solution.py:51
  64.6 2.8 %collective-permute-start.3 = (bf16[1024,512]{0,1:T(8,128)(2,1)S(1)}, bf16[1024,512]{0,1:T(8,128)(2,1)S(1)}, u32[]{:S(2)}, u32[]{:S(2)}) collective-permute-start(bf16[1024,512]{0,1:T(8,128)(2,1)S(1)} %pad_maximum_fusion.1), channel_id=1, source_target_pairs={{0,3},{1,0},{2,1},{3,2},{4,7},{5,4},{6,5},{7,6},{8,11},{9,8},{10,9... | collective-permute-start | bytes 3145736 | tf_op jit(solution)/shard_map/ppermute | solution.py:54
  67.4 1.3 %fusion.27 = f32[1024,1024]{1,0:T(8,128)S(1)} fusion(bf16[1024,512]{0,1:T(8,128)(2,1)S(1)} %bitcast.83, bf16[4,512,1024]{2,1,0:T(8,128)(2,1)S(1)} %bitcast.85, s32[]{:T(128)S(6)} %select_n.45), kind=kOutput, calls=%fused_computation.37 | convolution fusion | flops 1073741824 | bytes 6291460 | tf_op jit(solution)/shard_map/dot_general | solution.py:48
  68.7 0.7 fusion.37
  69.5 0.7 fusion.39
  70.2 19.7 %collective-permute-done.2 = bf16[1024,512]{0,1:T(8,128)(2,1)S(1)} collective-permute-done((bf16[1024,512]{0,1:T(8,128)(2,1)S(1)}, bf16[1024,512]{0,1:T(8,128)(2,1)S(1)}, u32[]{:S(2)}, u32[]{:S(2)}) %collective-permute-start.2) | collective-permute-done | bytes 1048608 | tf_op jit(solution)/shard_map/ppermute | solution.py:53
  89.9 1.3 %fusion.17 = f32[1024,1024]{1,0:T(8,128)S(1)} fusion(bf16[1024,512]{0,1:T(8,128)(2,1)S(1)} %collective-permute-done.2, bf16[256,1024]{1,0:T(8,128)(2,1)S(1)} %get-tuple-element.11, bf16[256,1024]{1,0:T(8,128)(2,1)S(1)} %get-tuple-element.12), kind=kOutput, calls=%fused_computation.28 | convolution fusion | flops 1075838976 | bytes 6291456 | tf_op jit(solution)/shard_map/dot_general | solution.py:48
  91.2 3.3 %add_convert_fusion = bf16[1024,1024]{1,0:T(8,128)(2,1)} fusion(f32[1024,1024]{1,0:T(8,128)S(1)} %fusion.17, f32[1024,1024]{1,0:T(8,128)S(1)} %fusion.37, f32[1024,1024]{1,0:T(8,128)S(1)} %fusion.27, f32[1024,1024]{1,0:T(8,128)S(1)} %fusion.39, bf16[1024,512]{0,1:T(8,128)(2,1)S(1)} %collective-permute-done.3, bf16[256,1024]{1,0:T(8,128)(2,1)S(1)} %get-tuple-element.10, ...), kind=kOutput, calls=%fused_computation.5 | convolution fusion | flops 1081081856 | bytes 20971520 | tf_op jit(solution)/shard_map/dot_general | solution.py:48
  (29 shorter events, 2.2 us)
Async XLA Ops:
  0.0 6.3 %copy-start.5 = (bf16[1024,512]{1,0:T(8,128)(2,1)S(1)}, bf16[1024,512]{1,0:T(8,128)(2,1)}, u32[]{:S(2)}) copy-start(bf16[1024,512]{1,0:T(8,128)(2,1)} %param.7) | copy-start | bytes 3145732
  6.3 1.4 %copy-start.2 = (bf16[1024,512]{0,1:T(8,128)(2,1)}, bf16[1024,512]{0,1:T(8,128)(2,1)S(1)}, u32[]{:S(2)}) copy-start(bf16[1024,512]{0,1:T(8,128)(2,1)S(1)} %copy.33) | copy-start | bytes 3145732
  6.3 12.2 %copy-start.1 = (bf16[1024,512]{1,0:T(8,128)(2,1)S(1)}, bf16[1024,512]{1,0:T(8,128)(2,1)}, u32[]{:S(2)}) copy-start(bf16[1024,512]{1,0:T(8,128)(2,1)} %param.6) | copy-start | bytes 3145732
  7.7 11.8 %copy-start.3 = (s32[1024]{0:T(1024)S(1)}, s32[1024]{0:T(1024)}, u32[]{:S(2)}) copy-start(s32[1024]{0:T(1024)} %param.9) | copy-start | bytes 12292
  8.6 23.0 %all-to-all-start = ((f32[16,40,128]{2,1,0:T(8,128)}), f32[16,40,128]{2,1,0:T(8,128)S(1)}, u32[]{:S(2)}, u32[]{:S(2)}) async-start(f32[16,40,128]{2,1,0:T(8,128)} %maximum_maximum_fusion), calls=%async_computation | async-start | bytes 655360 | tf_op jit(solution)/shard_map/all_to_all | solution.py:26
  33.2 14.6 %all-to-all-start.1 = ((f32[16,32,128]{2,1,0:T(8,128)}), f32[16,32,128]{2,1,0:T(8,128)S(1)}, u32[]{:S(2)}, u32[]{:S(2)}) async-start(f32[16,32,128]{2,1,0:T(8,128)} %select_reduce_fusion), calls=%async_computation.1 | async-start | bytes 524288 | tf_op jit(solution)/shard_map/all_to_all | solution.py:33
  48.2 0.7 copy-start.4
  49.3 15.1 %collective-permute-start = (bf16[1024,256]{0,1:T(8,128)(2,1)S(1)}, bf16[1024,256]{0,1:T(8,128)(2,1)S(1)}, u32[]{:S(2)}, u32[]{:S(2)}) collective-permute-start(bf16[1024,256]{0,1:T(8,128)(2,1)S(1)} %get-tuple-element.14), channel_id=1, source_target_pairs={{0,1},{1,2},{2,3},{3,0},{4,5},{5,6},{6,7},{7,4},{8,9},{9,10},{10,1... | collective-permute-start | bytes 1572872 | tf_op jit(solution)/shard_map/ppermute | solution.py:51
  50.7 13.9 %collective-permute-start.1 = (bf16[1024,256]{0,1:T(8,128)(2,1)S(1)}, bf16[1024,256]{0,1:T(8,128)(2,1)S(1)}, u32[]{:S(2)}, u32[]{:S(2)}) collective-permute-start(bf16[1024,256]{0,1:T(8,128)(2,1)S(1)} %get-tuple-element.13), channel_id=1, source_target_pairs={{0,3},{1,0},{2,1},{3,2},{4,7},{5,4},{6,5},{7,6},{8,11},{9,8},{10,9... | collective-permute-start | bytes 1572872 | tf_op jit(solution)/shard_map/ppermute | solution.py:52
  54.1 13.3 %copy-start = (bf16[2048,1024]{1,0:T(8,128)(2,1)S(1)}, bf16[2048,1024]{1,0:T(8,128)(2,1)}, u32[]{:S(2)}) copy-start(bf16[2048,1024]{1,0:T(8,128)(2,1)} %param.11) | copy-start | bytes 12582916
  64.5 25.4 %collective-permute-start.2 = (bf16[1024,512]{0,1:T(8,128)(2,1)S(1)}, bf16[1024,512]{0,1:T(8,128)(2,1)S(1)}, u32[]{:S(2)}, u32[]{:S(2)}) collective-permute-start(bf16[1024,512]{0,1:T(8,128)(2,1)S(1)} %pad_maximum_fusion), channel_id=1, source_target_pairs={{0,1},{1,2},{2,3},{3,0},{4,5},{5,6},{6,7},{7,4},{8,9},{9,10},{10,1... | collective-permute-start | bytes 3145736 | tf_op jit(solution)/shard_map/ppermute | solution.py:53
  64.6 26.5 %collective-permute-start.3 = (bf16[1024,512]{0,1:T(8,128)(2,1)S(1)}, bf16[1024,512]{0,1:T(8,128)(2,1)S(1)}, u32[]{:S(2)}, u32[]{:S(2)}) collective-permute-start(bf16[1024,512]{0,1:T(8,128)(2,1)S(1)} %pad_maximum_fusion.1), channel_id=1, source_target_pairs={{0,3},{1,0},{2,1},{3,2},{4,7},{5,4},{6,5},{7,6},{8,11},{9,8},{10,9... | collective-permute-start | bytes 3145736 | tf_op jit(solution)/shard_map/ppermute | solution.py:54

commit v10 on v9

--- a/solution.py
+++ b/solution.py
@@ -56,7 +56,9 @@
     right_weight = jnp.concatenate([rows_of(1, 0), rows_of(2, 1)], axis=0)
     total = dot(hidden, out_weight.reshape(count, width, -1)[mine])
     total = total + dot(left_first, rows_of(-1, 0)) + dot(right_second, rows_of(1, 1))
-    return total + dot(from_left, left_weight) + dot(from_right, right_weight)
+    total = lax.optimization_barrier(total)
+    total = lax.optimization_barrier(total + dot(from_left, left_weight))
+    return total + dot(from_right, right_weight)
 
 
 def per_device(queries, keys, values, segment_ids, norm_gain, out_weight):

time: 94.9 us -> 97.4 us (1.026); the launches traced: 94.5 us -> 95.9 us
  waiting for transfers between devices: 44.6 us -> 38.9 us
  other arithmetic: 7.06 us -> 11.5 us
  matrix products: 16.9 us -> 18.5 us
  local copies, waits for them, and re-layouts: 5.07 us -> 6.13 us
    ppermute x1, waiting for transfers between devices: 19.7 us -> 14.9 us  [project_gathered(): lax.ppermute(jnp.concatenate([second, left_first], axis=1), axis, ahead)]
    convert_element_type x0 -> x1, other arithmetic: none -> 2.05 us  [per_device(): return project_gathered(hidden, out_weight, 'mp').astype(jnp.bfloat16)]
    dot_general x5, matrix products: 7.39 us -> 9.03 us  [dot(): return jnp.dot(block, weight, preferred_element_type=jnp.float32)]
    add x0 -> x1, other arithmetic: none -> 1.36 us  [project_gathered(): total = lax.optimization_barrier(total + dot(from_left, left_weight))]
    concatenate x1, other arithmetic: 0.07 us -> 1.11 us  [project_gathered(): jnp.concatenate([first, right_second], axis=1)]
    ppermute x1, waiting for transfers between devices: 10.3 us -> 9.26 us  [project_gathered(): left_first = lax.ppermute(first, axis, ahead)]
    squeeze x1, local copies, waits for them, and re-layouts: 1.69 us -> 2.71 us  [rows_of(): return weight_halves[lax.rem(mine + offset + count, count), which]]
  transfers between devices with their start and end apart: 6 -> 6, of which waited for: 4 -> 4; matrix products, arithmetic and copies ran while one was open for 16% -> 23% of each run, Pallas kernels for 0% -> 0%
where the time goes in v10:
time: 97.4 us; the launch traced here: 95.9 us
  waiting for transfers between devices  38.9 us (40%)
  starting transfers between devices  19.3 us (20%)
  matrix products  18.5 us (19%)
  other arithmetic  11.5 us (12%)
  local copies, waits for them, and re-layouts  6.13 us (6%)
  between operations  1.51 us (2%)
    ppermute x1, waiting for transfers between devices, project_gathered(): lax.ppermute(jnp.concatenate([second, left_first], axis=1), axis, ahead)  14.9 us
    all_to_all x1, waiting for transfers between devices, carried_in(): pieces = lax.all_to_all(sent, axis, 0, 0, tiled=True)  10.5 us
    all_to_all x1, starting transfers between devices, carried_in(): pieces = lax.all_to_all(sent, axis, 0, 0, tiled=True)  9.98 us
    ppermute x1, waiting for transfers between devices, project_gathered(): left_first = lax.ppermute(first, axis, ahead)  9.26 us
    dot_general x5, matrix products, dot(): return jnp.dot(block, weight, preferred_element_type=jnp.float32)  9.03 us
    dot_general x1, matrix products, per_device(): jnp.einsum('hts,she->the', weights, value_heads, preferred_element_type=j...  7 us
    all_to_all x1, waiting for transfers between devices, carried_in(): return lax.all_to_all(carry, axis, 0, 0, tiled=True).reshape(shape)  4.14 us
    all_to_all x1, starting transfers between devices, carried_in(): return lax.all_to_all(carry, axis, 0, 0, tiled=True).reshape(shape)  3.43 us
  transfers between devices with their start and end apart: 6, of which 4 were waited for; matrix products, arithmetic and copies ran while one was open for 23% of the time, Pallas kernels for 0%

profile of v10, /device:TPU:1, one launch (start us, length us, event | category | flops | bytes accessed | tf_op | source)
XLA Modules:
  0.0 95.9 jit_solution(6634814467228278777)
XLA Ops:
  0.0 1.4 %fusion.51 = (s32[1]{0:T(128)}, s32[1]{0:T(128)}) fusion(s32[1024]{0:T(1024)} %param.9), kind=kLoop, calls=%fused_computation.75 | loop fusion | bytes 16 | tf_op jit(solution)/shard_map/slice | solution.py:92
  2.1 2.0 %compare_convert_fusion.1 = (f32[1024]{0:T(1024)S(1)}, bf16[1024]{0:T(1024)(128)(2,1)S(1)}) fusion(s32[1024]{0:T(1024)} %param.9, s32[]{:T(128)} %bitcast.1, s32[]{:T(128)} %bitcast.2), kind=kLoop, calls=%fused_computation.66 | loop fusion | flops 4096 | bytes 10248 | tf_op jit(solution)/shard_map/convert_element_type | solution.py:92
  4.7 1.5 %copy.33 = bf16[1024,512]{0,1:T(8,128)(2,1)S(1)} copy(bf16[1024,512]{1,0:T(8,128)(2,1)} %param.8) | data formatting | bytes 2097152 | tf_op jit(solution)/shard_map/reshape | solution.py:70
  6.4 1.4 %fusion.11 = f32[4,128,128]{1,2,0:T(8,128)S(1)} fusion(bf16[1024,4,128]{0,2,1:T(8,128)(2,1)S(1)} %bitcast.88, bf16[1024]{0:T(1024)(128)(2,1)S(1)} %get-tuple-element.16, bf16[1024,512]{1,0:T(8,128)(2,1)S(1)} %copy-done.7), kind=kOutput, calls=%fused_computation.23 | convolution fusion | flops 139460608 | bytes 2361344 | tf_op jit(solution)/shard_map/the,thd->hed/dot_general | solution.py:73
  8.6 10.0 %all-to-all-start = ((f32[16,40,128]{2,1,0:T(8,128)}), f32[16,40,128]{2,1,0:T(8,128)S(1)}, u32[]{:S(2)}, u32[]{:S(2)}) async-start(f32[16,40,128]{2,1,0:T(8,128)} %maximum_maximum_fusion), calls=%async_computation | async-start | bytes 655360 | tf_op jit(solution)/shard_map/all_to_all | solution.py:26
  19.6 1.6 %fusion = pred[1024,1024]{1,0:T(8,128)(4,1)} fusion(s32[1024]{0:T(1024)S(1)} %copy-done.5), kind=kLoop, calls=%fused_computation.9 | loop fusion | flops 3145728 | bytes 1052672 | tf_op jit(solution)/shard_map/and | solution.py:81
  21.1 10.5 %all-to-all-done = f32[16,40,128]{2,1,0:T(8,128)S(1)} async-done(((f32[16,40,128]{2,1,0:T(8,128)}), f32[16,40,128]{2,1,0:T(8,128)S(1)}, u32[]{:S(2)}, u32[]{:S(2)}) %all-to-all-start) | async-done | bytes 327712 | tf_op jit(solution)/shard_map/all_to_all | solution.py:26
  32.0 1.2 %select_reduce_fusion = f32[16,32,128]{2,1,0:T(8,128)} fusion(f32[16,32,128]{2,1,0:T(8,128)S(1)} %slice.31, pred[16,16]{1,0:T(8,128)(4,1)S(1)} %fusion.42), kind=kLoop, calls=%fused_computation.7 | loop fusion | flops 2031616 | bytes 524544 | tf_op jit(solution)/shard_map/reduce_sum | solution.py:32
  33.2 3.4 %all-to-all-start.1 = ((f32[16,32,128]{2,1,0:T(8,128)}), f32[16,32,128]{2,1,0:T(8,128)S(1)}, u32[]{:S(2)}, u32[]{:S(2)}) async-start(f32[16,32,128]{2,1,0:T(8,128)} %select_reduce_fusion), calls=%async_computation.1 | async-start | bytes 524288 | tf_op jit(solution)/shard_map/all_to_all | solution.py:33
  36.7 7.0 %fusion.7 = f32[4,1024,128]{1,2,0:T(8,128)S(1)} fusion(bf16[1024,4,128]{0,2,1:T(8,128)(2,1)} %bitcast.89, pred[1024,1024]{1,0:T(8,128)(4,1)} %fusion, bf16[1024,512]{1,0:T(8,128)(2,1)S(1)} %fusion.3, bf16[1024,512]{1,0:T(8,128)(2,1)} %param.7), kind=kOutput, calls=%fused_computation.19 | convolution fusion | flops 2159017984 | bytes 6291456 | tf_op jit(solution)/shard_map/hts,she->the/dot_general | solution.py:86
  43.7 4.1 %all-to-all-done.1 = f32[16,32,128]{2,1,0:T(8,128)S(1)} async-done(((f32[16,32,128]{2,1,0:T(8,128)}), f32[16,32,128]{2,1,0:T(8,128)S(1)}, u32[]{:S(2)}, u32[]{:S(2)}) %all-to-all-start.1) | async-done | bytes 262176 | tf_op jit(solution)/shard_map/all_to_all | solution.py:33
  49.3 1.4 %collective-permute-start = (bf16[1024,256]{0,1:T(8,128)(2,1)S(1)}, bf16[1024,256]{0,1:T(8,128)(2,1)S(1)}, u32[]{:S(2)}, u32[]{:S(2)}) collective-permute-start(bf16[1024,256]{0,1:T(8,128)(2,1)S(1)} %get-tuple-element.14), channel_id=1, source_target_pairs={{0,1},{1,2},{2,3},{3,0},{4,5},{5,6},{6,7},{7,4},{8,9},{9,10},{10,1... | collective-permute-start | bytes 1572872 | tf_op jit(solution)/shard_map/ppermute | solution.py:51
  50.7 1.7 %collective-permute-start.1 = (bf16[1024,256]{0,1:T(8,128)(2,1)S(1)}, bf16[1024,256]{0,1:T(8,128)(2,1)}, u32[]{:S(2)}, u32[]{:S(2)}) collective-permute-start(bf16[1024,256]{0,1:T(8,128)(2,1)S(1)} %get-tuple-element.13), channel_id=1, source_target_pairs={{0,3},{1,0},{2,1},{3,2},{4,7},{5,4},{6,5},{7,6},{8,11},{9,8},{10,9... | collective-permute-start | bytes 1572872 | tf_op jit(solution)/shard_map/ppermute | solution.py:52
  52.4 2.7 %dynamic-slice_bitcast_fusion.1 = (bf16[256,1024]{1,0:T(8,128)(2,1)S(1)}, bf16[256,1024]{1,0:T(8,128)(2,1)}, bf16[256,1024]{1,0:T(8,128)(2,1)}, bf16[256,1024]{1,0:T(8,128)(2,1)}) fusion(bf16[4,2,256,1024]{3,2,1,0:T(8,128)(2,1)} %bitcast.84, s32[]{:T(128)S(6)} %select_n.47, s32[]{:T(128)S(6)} %select_n.48, s32[]{:T(128)S(6)} %select_n.46), kind=kLoop, calls=%fused_computation.50 | loop fusion | bytes 4194316 | tf_op jit(solution)/shard_map/squeeze | solution.py:45
  55.2 9.3 %collective-permute-done = bf16[1024,256]{0,1:T(8,128)(2,1)S(1)} collective-permute-done((bf16[1024,256]{0,1:T(8,128)(2,1)S(1)}, bf16[1024,256]{0,1:T(8,128)(2,1)S(1)}, u32[]{:S(2)}, u32[]{:S(2)}) %collective-permute-start) | collective-permute-done | bytes 524320 | tf_op jit(solution)/shard_map/ppermute | solution.py:51
  64.6 2.5 %fusion.25 = f32[1024,1024]{1,0:T(8,128)S(1)} fusion(bf16[1024,512]{0,1:T(8,128)(2,1)S(1)} %bitcast.83, bf16[4,512,1024]{2,1,0:T(8,128)(2,1)} %bitcast.85, s32[]{:T(128)S(6)} %select_n.45), kind=kOutput, calls=%fused_computation.38 | convolution fusion | flops 1073741824 | bytes 6291460 | tf_op jit(solution)/shard_map/dot_general | solution.py:48
  68.3 2.7 %collective-permute-start.3 = (bf16[1024,512]{0,1:T(8,128)(2,1)S(1)}, bf16[1024,512]{0,1:T(8,128)(2,1)S(1)}, u32[]{:S(2)}, u32[]{:S(2)}) collective-permute-start(bf16[1024,512]{0,1:T(8,128)(2,1)S(1)} %pad_maximum_fusion.1), channel_id=1, source_target_pairs={{0,3},{1,0},{2,1},{3,2},{4,7},{5,4},{6,5},{7,6},{8,11},{9,8},{10,9... | collective-permute-start | bytes 3145736 | tf_op jit(solution)/shard_map/ppermute | solution.py:54
  71.0 1.8 %fusion.36 = f32[1024,1024]{1,0:T(8,128)S(1)} fusion(bf16[1024,256]{0,1:T(8,128)(2,1)S(1)} %collective-permute-done, bf16[4,2,256,1024]{3,2,1,0:T(8,128)(2,1)} %bitcast.86, s32[]{:T(128)S(6)} %select_n.46), kind=kOutput, calls=%fused_computation.47 | convolution fusion | flops 536870912 | bytes 5242884 | tf_op jit(solution)/shard_map/dot_general | solution.py:48
  72.8 2.2 %add_add_fusion = f32[1024,1024]{1,0:T(8,128)S(1)} fusion(f32[1024,1024]{1,0:T(8,128)S(1)} %fusion.25, f32[1024,1024]{1,0:T(8,128)S(1)} %fusion.36, bf16[1024,256]{0,1:T(8,128)(2,1)} %collective-permute-done.1, bf16[4,2,256,1024]{3,2,1,0:T(8,128)(2,1)} %bitcast.87, s32[]{:T(128)S(6)} %select_n.47), kind=kOutput, calls=%fused_computation.6 | convolution fusion | flops 538968064 | bytes 13631492 | tf_op jit(solution)/shard_map/dot_general | solution.py:48
  74.9 14.9 %collective-permute-done.2 = bf16[1024,512]{0,1:T(8,128)(2,1)S(1)} collective-permute-done((bf16[1024,512]{0,1:T(8,128)(2,1)S(1)}, bf16[1024,512]{0,1:T(8,128)(2,1)S(1)}, u32[]{:S(2)}, u32[]{:S(2)}) %collective-permute-start.2) | collective-permute-done | bytes 1048608 | tf_op jit(solution)/shard_map/ppermute | solution.py:53
  89.9 1.3 %fusion.17 = f32[1024,1024]{1,0:T(8,128)S(1)} fusion(bf16[1024,512]{0,1:T(8,128)(2,1)S(1)} %collective-permute-done.2, bf16[256,1024]{1,0:T(8,128)(2,1)S(1)} %copy-done.1, bf16[256,1024]{1,0:T(8,128)(2,1)S(1)} %copy-done.2), kind=kOutput, calls=%fused_computation.29 | convolution fusion | flops 1075838976 | bytes 6291456 | tf_op jit(solution)/shard_map/dot_general | solution.py:48
  91.2 1.4 %add.90 = f32[1024,1024]{1,0:T(8,128)S(1)} add(f32[1024,1024]{1,0:T(8,128)S(1)} %add_add_fusion, f32[1024,1024]{1,0:T(8,128)S(1)} %fusion.17) | non-fusion elementwise | flops 1048576 | bytes 12582912 | tf_op jit(solution)/shard_map/add | solution.py:60
  92.6 1.3 %fusion.21 = f32[1024,1024]{1,0:T(8,128)S(1)} fusion(bf16[1024,512]{0,1:T(8,128)(2,1)S(1)} %collective-permute-done.3, bf16[256,1024]{1,0:T(8,128)(2,1)S(1)} %copy-done, bf16[256,1024]{1,0:T(8,128)(2,1)S(1)} %get-tuple-element.9), kind=kOutput, calls=%fused_computation.34 | convolution fusion | flops 1075838976 | bytes 6291456 | tf_op jit(solution)/shard_map/dot_general | solution.py:48
  93.9 2.0 %add_convert_fusion = bf16[1024,1024]{1,0:T(8,128)(2,1)} fusion(f32[1024,1024]{1,0:T(8,128)S(1)} %add.90, f32[1024,1024]{1,0:T(8,128)S(1)} %fusion.21), kind=kLoop, calls=%fused_computation.5 | loop fusion | flops 2097152 | bytes 10485760 | tf_op jit(solution)/shard_map/convert_element_type | solution.py:97
  (35 shorter events, 5.1 us)
Async XLA Ops:
  0.0 6.3 %copy-start.7 = (bf16[1024,512]{1,0:T(8,128)(2,1)S(1)}, bf16[1024,512]{1,0:T(8,128)(2,1)}, u32[]{:S(2)}) copy-start(bf16[1024,512]{1,0:T(8,128)(2,1)} %param.7) | copy-start | bytes 3145732
  6.2 1.6 %copy-start.4 = (bf16[1024,512]{0,1:T(8,128)(2,1)}, bf16[1024,512]{0,1:T(8,128)(2,1)S(1)}, u32[]{:S(2)}) copy-start(bf16[1024,512]{0,1:T(8,128)(2,1)S(1)} %copy.33) | copy-start | bytes 3145732
  6.3 12.2 %copy-start.3 = (bf16[1024,512]{1,0:T(8,128)(2,1)S(1)}, bf16[1024,512]{1,0:T(8,128)(2,1)}, u32[]{:S(2)}) copy-start(bf16[1024,512]{1,0:T(8,128)(2,1)} %param.6) | copy-start | bytes 3145732
  7.8 11.8 %copy-start.5 = (s32[1024]{0:T(1024)S(1)}, s32[1024]{0:T(1024)}, u32[]{:S(2)}) copy-start(s32[1024]{0:T(1024)} %param.9) | copy-start | bytes 12292
  8.6 23.1 %all-to-all-start = ((f32[16,40,128]{2,1,0:T(8,128)}), f32[16,40,128]{2,1,0:T(8,128)S(1)}, u32[]{:S(2)}, u32[]{:S(2)}) async-start(f32[16,40,128]{2,1,0:T(8,128)} %maximum_maximum_fusion), calls=%async_computation | async-start | bytes 655360 | tf_op jit(solution)/shard_map/all_to_all | solution.py:26
  33.2 14.6 %all-to-all-start.1 = ((f32[16,32,128]{2,1,0:T(8,128)}), f32[16,32,128]{2,1,0:T(8,128)S(1)}, u32[]{:S(2)}, u32[]{:S(2)}) async-start(f32[16,32,128]{2,1,0:T(8,128)} %select_reduce_fusion), calls=%async_computation.1 | async-start | bytes 524288 | tf_op jit(solution)/shard_map/all_to_all | solution.py:33
  48.3 0.7 copy-start.6
  49.3 15.1 %collective-permute-start = (bf16[1024,256]{0,1:T(8,128)(2,1)S(1)}, bf16[1024,256]{0,1:T(8,128)(2,1)S(1)}, u32[]{:S(2)}, u32[]{:S(2)}) collective-permute-start(bf16[1024,256]{0,1:T(8,128)(2,1)S(1)} %get-tuple-element.14), channel_id=1, source_target_pairs={{0,1},{1,2},{2,3},{3,0},{4,5},{5,6},{6,7},{7,4},{8,9},{9,10},{10,1... | collective-permute-start | bytes 1572872 | tf_op jit(solution)/shard_map/ppermute | solution.py:51
  50.7 16.4 %collective-permute-start.1 = (bf16[1024,256]{0,1:T(8,128)(2,1)S(1)}, bf16[1024,256]{0,1:T(8,128)(2,1)}, u32[]{:S(2)}, u32[]{:S(2)}) collective-permute-start(bf16[1024,256]{0,1:T(8,128)(2,1)S(1)} %get-tuple-element.13), channel_id=1, source_target_pairs={{0,3},{1,0},{2,1},{3,2},{4,7},{5,4},{6,5},{7,6},{8,11},{9,8},{10,9... | collective-permute-start | bytes 1572872 | tf_op jit(solution)/shard_map/ppermute | solution.py:52
  64.5 25.4 %collective-permute-start.2 = (bf16[1024,512]{0,1:T(8,128)(2,1)S(1)}, bf16[1024,512]{0,1:T(8,128)(2,1)S(1)}, u32[]{:S(2)}, u32[]{:S(2)}) collective-permute-start(bf16[1024,512]{0,1:T(8,128)(2,1)S(1)} %pad_maximum_fusion), channel_id=1, source_target_pairs={{0,1},{1,2},{2,3},{3,0},{4,5},{5,6},{6,7},{7,4},{8,9},{9,10},{10,1... | collective-permute-start | bytes 3145736 | tf_op jit(solution)/shard_map/ppermute | solution.py:53
  68.3 24.3 %collective-permute-start.3 = (bf16[1024,512]{0,1:T(8,128)(2,1)S(1)}, bf16[1024,512]{0,1:T(8,128)(2,1)S(1)}, u32[]{:S(2)}, u32[]{:S(2)}) collective-permute-start(bf16[1024,512]{0,1:T(8,128)(2,1)S(1)} %pad_maximum_fusion.1), channel_id=1, source_target_pairs={{0,3},{1,0},{2,1},{3,2},{4,7},{5,4},{6,5},{7,6},{8,11},{9,8},{10,9... | collective-permute-start | bytes 3145736 | tf_op jit(solution)/shard_map/ppermute | solution.py:54
  72.7 17.1 %copy-start.1 = (bf16[256,1024]{1,0:T(8,128)(2,1)S(1)}, bf16[256,1024]{1,0:T(8,128)(2,1)}, u32[]{:S(2)}) copy-start(bf16[256,1024]{1,0:T(8,128)(2,1)} %get-tuple-element.11) | copy-start | bytes 1572868
  72.8 17.1 %copy-start.2 = (bf16[256,1024]{1,0:T(8,128)(2,1)S(1)}, bf16[256,1024]{1,0:T(8,128)(2,1)}, u32[]{:S(2)}) copy-start(bf16[256,1024]{1,0:T(8,128)(2,1)} %get-tuple-element.12) | copy-start | bytes 1572868
  91.2 1.4 %copy-start = (bf16[256,1024]{1,0:T(8,128)(2,1)S(1)}, bf16[256,1024]{1,0:T(8,128)(2,1)}, u32[]{:S(2)}) copy-start(bf16[256,1024]{1,0:T(8,128)(2,1)} %get-tuple-element.10) | copy-start | bytes 1572868

commit v11 on v9

--- a/solution.py
+++ b/solution.py
@@ -1,6 +1,8 @@
 import jax
 import jax.numpy as jnp
 from jax import lax
+from jax.experimental import pallas as pl
+from jax.experimental.pallas import tpu as pltpu
 from jax.sharding import PartitionSpec as P
 
 HEAD = 128
@@ -10,19 +12,49 @@
     return (jax.nn.elu(raw_input.astype(jnp.float32)) + 1.0).astype(jnp.bfloat16)
 
 
-def carried_in(local_sum, final_seg, first_seg, axis):
+def _payload_kernel(key_ref, value_ref, seg_ref, out_ref):
+    rows, width = key_ref.shape
+    heads = width // HEAD
+    pieces_per_head = HEAD // 32
+    segs = seg_ref[...]
+    last = segs[rows - 1 : rows, :]
+    first = segs[0:1, :]
+    in_final = (segs == last).astype(jnp.float32)
+    seg_rows = jnp.where(
+        lax.broadcasted_iota(jnp.int32, (8, HEAD), 0) == 0,
+        jnp.broadcast_to(last.astype(jnp.float32), (8, HEAD)),
+        jnp.broadcast_to(first.astype(jnp.float32), (8, HEAD)),
+    )
+    for h in range(heads):
+        cols = slice(h * HEAD, (h + 1) * HEAD)
+        raw = key_ref[:, cols].astype(jnp.float32)
+        feat = jnp.where(raw > 0, raw + 1.0, jnp.exp(jnp.minimum(raw, 0.0))).astype(jnp.bfloat16)
+        masked = (feat.astype(jnp.float32) * in_final).astype(jnp.bfloat16)
+        sums = lax.dot_general(
+            value_ref[:, cols], masked, (((0,), (0,)), ((), ())),
+            preferred_element_type=jnp.float32,
+        )
+        for j in range(pieces_per_head):
+            piece = h * pieces_per_head + j
+            out_ref[piece * 40 : piece * 40 + 32, :] = sums[j * 32 : (j + 1) * 32, :]
+            out_ref[piece * 40 + 32 : piece * 40 + 40, :] = seg_rows
+
+
+def scan_payload(keys, values, segment_ids):
+    rows, width = keys.shape
+    count = width // 32
+    out = pl.pallas_call(
+        _payload_kernel,
+        out_shape=jax.ShapeDtypeStruct((count * 40, HEAD), jnp.float32),
+        in_specs=[pl.BlockSpec(memory_space=pltpu.VMEM)] * 3,
+        out_specs=pl.BlockSpec(memory_space=pltpu.VMEM),
+    )(keys, values, segment_ids.reshape(rows, 1))
+    return out.reshape(count, 40, HEAD)
+
+
+def carried_in(sent, shape, axis):
     count = lax.axis_size(axis)
-    shape = local_sum.shape
-    tile = local_sum.size // (count * HEAD)
-    flat = local_sum.reshape(count, tile, HEAD)
-    seg_rows = jnp.concatenate(
-        [
-            jnp.full((count, 1, HEAD), final_seg.astype(jnp.float32)),
-            jnp.full((count, 7, HEAD), first_seg.astype(jnp.float32)),
-        ],
-        axis=1,
-    )
-    sent = jnp.concatenate([flat, seg_rows], axis=1)
+    tile = sent.shape[1] - 8
     pieces = lax.all_to_all(sent, axis, 0, 0, tiled=True)
     sums = pieces[:, :tile]
     last_segs = pieces[:, tile, 0]
@@ -66,15 +98,9 @@
     feat_query = lax.optimization_barrier(features(queries)).reshape(rows_here, heads_here, HEAD)
     feat_key = features(keys).reshape(rows_here, heads_here, HEAD)
     value_heads = values.reshape(rows_here, heads_here, HEAD)
-    final_seg = segment_ids[rows_here - 1]
-    in_final = (segment_ids == final_seg).astype(jnp.bfloat16)
-    local_sum = jnp.einsum(
-        "the,thd->hed",
-        value_heads,
-        feat_key * in_final[:, None, None],
-        preferred_element_type=jnp.float32,
+    before_sum = carried_in(
+        scan_payload(keys, values, segment_ids), (heads_here, HEAD, HEAD), "ctx"
     )
-    before_sum = carried_in(local_sum, final_seg, segment_ids[0], "ctx")
     position = jnp.arange(rows_here)
     allowed = (position[None, :] <= position[:, None]) & (
         segment_ids[:, None] == segment_ids[None, :]

time: 94.9 us -> 91.7 us (0.966)
  Pallas kernels: 0 us -> 3.36 us
  waiting for transfers between devices: 44.6 us -> 42.4 us
  other arithmetic: 7.06 us -> 4.91 us
  matrix products: 16.9 us -> 15.4 us
  between operations: 1.49 us -> 0.16 us
    pallas_call x0 -> x1, Pallas kernels: none -> 3.36 us  [scan_payload(): pl.pallas_call(_payload_kernel, out_shape=jax.ShapeDtypeStruct((count * 4...]
    broadcast_in_dim x1, local copies, waits for them, and re-layouts: 0.01 us -> 1.79 us  [per_device(): segment_ids[:, None] == segment_ids[None, :]]
    dot_general x1 -> x0, matrix products: 1.36 us -> none  [per_device(): jnp.einsum('the,thd->hed', value_heads, feat_key * in_final[:, None, None...]
    all_to_all x1, waiting for transfers between devices: 10.6 us -> 9.22 us  [carried_in(): pieces = lax.all_to_all(sent, axis, 0, 0, tiled=True)]
    convert_element_type x1, other arithmetic: 1.96 us -> 0.65 us  [per_device(): carry_on = (segment_ids == segment_ids[0]).astype(jnp.float32)]
    all_to_all x1, waiting for transfers between devices: 4.14 us -> 2.98 us  [carried_in(): return lax.all_to_all(carry, axis, 0, 0, tiled=True).reshape(shape)]
  transfers between devices with their start and end apart: 6 -> 6, of which waited for: 4 -> 4; matrix products, arithmetic and copies ran while one was open for 16% -> 20% of each run, Pallas kernels for 0% -> 0%
where the time goes in v11:
time: 91.7 us; the launch traced here: 91.3 us
  waiting for transfers between devices  42.4 us (46%)
  starting transfers between devices  19.4 us (21%)
  matrix products  15.4 us (17%)
  local copies, waits for them, and re-layouts  5.65 us (6%)
  other arithmetic  4.91 us (5%)
  Pallas kernels  3.36 us (4%)
    ppermute x1, waiting for transfers between devices, project_gathered(): lax.ppermute(jnp.concatenate([second, left_first], axis=1), axis, ahead)  19.7 us
    ppermute x1, waiting for transfers between devices, project_gathered(): left_first = lax.ppermute(first, axis, ahead)  10.5 us
    all_to_all x1, starting transfers between devices, carried_in(): pieces = lax.all_to_all(sent, axis, 0, 0, tiled=True)  10.1 us
    all_to_all x1, waiting for transfers between devices, carried_in(): pieces = lax.all_to_all(sent, axis, 0, 0, tiled=True)  9.22 us
    dot_general x5, matrix products, dot(): return jnp.dot(block, weight, preferred_element_type=jnp.float32)  7.39 us
    dot_general x1, matrix products, per_device(): jnp.einsum('hts,she->the', weights, value_heads, preferred_element_type=j...  7 us
    all_to_all x1, starting transfers between devices, carried_in(): return lax.all_to_all(carry, axis, 0, 0, tiled=True).reshape(shape)  3.43 us
    pallas_call x1, Pallas kernels, scan_payload(): pl.pallas_call(_payload_kernel, out_shape=jax.ShapeDtypeStruct((count * 4...  3.36 us
  transfers between devices with their start and end apart: 6, of which 4 were waited for; matrix products, arithmetic and copies ran while one was open for 20% of the time, Pallas kernels for 0%

profile of v11, /device:TPU:1, one launch (start us, length us, event | category | flops | bytes accessed | tf_op | source)
XLA Modules:
  0.0 91.3 jit_solution(1676043094473987076)
XLA Ops:
  0.0 1.8 %copy.33.seg_ref = s32[1024,1]{1,0:T(8,128)} copy(s32[1024,1]{0,1:T(1,128)} %bitcast.83) | data formatting | bytes 8192 | tf_op jit(solution)/shard_map/broadcast_in_dim | solution.py:106
  1.8 3.4 %shard_map.64 = f32[640,128]{1,0:T(8,128)} custom-call(bf16[1024,512]{1,0:T(8,128)(2,1)} %key_ref.1, bf16[1024,512]{1,0:T(8,128)(2,1)} %value_ref.1, s32[1024,1]{1,0:T(8,128)} %copy.33.seg_ref), custom_call_target="tpu_custom_call" | custom-call | tf_op jit(solution)/shard_map/pallas_call | solution.py:46
  5.2 10.1 %all-to-all-start = ((f32[16,40,128]{2,1,0:T(8,128)}), f32[16,40,128]{2,1,0:T(8,128)S(1)}, u32[]{:S(2)}, u32[]{:S(2)}) async-start(f32[16,40,128]{2,1,0:T(8,128)} %bitcast.80), calls=%async_computation | async-start | bytes 655360 | tf_op jit(solution)/shard_map/all_to_all | solution.py:58
  15.3 1.3 %copy.36 = bf16[1024,512]{0,1:T(8,128)(2,1)} copy(bf16[1024,512]{1,0:T(8,128)(2,1)S(1)} %copy-done) | data formatting | bytes 2097152 | tf_op jit(solution)/shard_map/reshape | solution.py:100
  16.6 0.9 %fusion.3 = bf16[1024,512]{1,0:T(8,128)(2,1)S(1)} fusion(bf16[1024,512]{1,0:T(8,128)(2,1)S(1)} %copy-done.2), kind=kLoop, calls=%fused_computation.11 | loop fusion | flops 3145728 | bytes 2097152 | tf_op jit(solution)/shard_map/convert_element_type | solution.py:12
  17.6 1.6 %fusion = pred[1024,1024]{1,0:T(8,128)(4,1)} fusion(s32[1024]{0:T(1024)S(1)} %copy-done.3), kind=kLoop, calls=%fused_computation.8 | loop fusion | flops 3145728 | bytes 1052672 | tf_op jit(solution)/shard_map/and | solution.py:105
  19.1 9.2 %all-to-all-done = f32[16,40,128]{2,1,0:T(8,128)S(1)} async-done(((f32[16,40,128]{2,1,0:T(8,128)}), f32[16,40,128]{2,1,0:T(8,128)S(1)}, u32[]{:S(2)}, u32[]{:S(2)}) %all-to-all-start) | async-done | bytes 327712 | tf_op jit(solution)/shard_map/all_to_all | solution.py:58
  28.7 1.2 %select_reduce_fusion = f32[16,32,128]{2,1,0:T(8,128)} fusion(f32[16,32,128]{2,1,0:T(8,128)S(1)} %slice.26, pred[16,16]{1,0:T(8,128)(4,1)S(1)} %fusion.42), kind=kLoop, calls=%fused_computation.6 | loop fusion | flops 2031616 | bytes 524544 | tf_op jit(solution)/shard_map/reduce_sum | solution.py:64
  29.9 3.4 %all-to-all-start.1 = ((f32[16,32,128]{2,1,0:T(8,128)}), f32[16,32,128]{2,1,0:T(8,128)S(1)}, u32[]{:S(2)}, u32[]{:S(2)}) async-start(f32[16,32,128]{2,1,0:T(8,128)} %select_reduce_fusion), calls=%async_computation.1 | async-start | bytes 524288 | tf_op jit(solution)/shard_map/all_to_all | solution.py:65
  33.3 7.0 %fusion.7 = f32[4,1024,128]{1,2,0:T(8,128)S(1)} fusion(bf16[1024,4,128]{0,2,1:T(8,128)(2,1)} %bitcast.81, pred[1024,1024]{1,0:T(8,128)(4,1)} %fusion, bf16[1024,512]{1,0:T(8,128)(2,1)S(1)} %fusion.3, bf16[1024,512]{1,0:T(8,128)(2,1)} %key_ref.1), kind=kOutput, calls=%fused_computation.18 | convolution fusion | flops 2159017984 | bytes 6291456 | tf_op jit(solution)/shard_map/hts,she->the/dot_general | solution.py:110
  40.9 0.6 compare_convert_fusion
  41.5 3.0 %all-to-all-done.1 = f32[16,32,128]{2,1,0:T(8,128)S(1)} async-done(((f32[16,32,128]{2,1,0:T(8,128)}), f32[16,32,128]{2,1,0:T(8,128)S(1)}, u32[]{:S(2)}, u32[]{:S(2)}) %all-to-all-start.1) | async-done | bytes 262176 | tf_op jit(solution)/shard_map/all_to_all | solution.py:65
  45.0 0.6 multiply_reduce_fusion
  46.0 1.4 %collective-permute-start = (bf16[1024,256]{0,1:T(8,128)(2,1)S(1)}, bf16[1024,256]{0,1:T(8,128)(2,1)S(1)}, u32[]{:S(2)}, u32[]{:S(2)}) collective-permute-start(bf16[1024,256]{0,1:T(8,128)(2,1)S(1)} %get-tuple-element.14), channel_id=1, source_target_pairs={{0,1},{1,2},{2,3},{3,0},{4,5},{5,6},{6,7},{7,4},{8,9},{9,10},{10,1... | collective-permute-start | bytes 1572872 | tf_op jit(solution)/shard_map/ppermute | solution.py:83
  47.4 1.5 %collective-permute-start.1 = (bf16[1024,256]{0,1:T(8,128)(2,1)S(1)}, bf16[1024,256]{0,1:T(8,128)(2,1)S(1)}, u32[]{:S(2)}, u32[]{:S(2)}) collective-permute-start(bf16[1024,256]{0,1:T(8,128)(2,1)S(1)} %get-tuple-element.13), channel_id=1, source_target_pairs={{0,3},{1,0},{2,1},{3,2},{4,7},{5,4},{6,5},{7,6},{8,11},{9,8},{10,9... | collective-permute-start | bytes 1572872 | tf_op jit(solution)/shard_map/ppermute | solution.py:84
  48.9 1.7 %dynamic-slice_bitcast_fusion.1 = (bf16[256,1024]{1,0:T(8,128)(2,1)S(1)}, bf16[256,1024]{1,0:T(8,128)(2,1)S(1)}, bf16[256,1024]{1,0:T(8,128)(2,1)S(1)}, bf16[256,1024]{1,0:T(8,128)(2,1)S(1)}) fusion(bf16[4,2,256,1024]{3,2,1,0:T(8,128)(2,1)} %bitcast.76, s32[]{:T(128)S(6)} %select_n.47, s32[]{:T(128)S(6)} %select_n.48, s32[]{:T(128)S(6)} %select_n.46), kind=kLoop, calls=%fused_computation.47 | loop fusion | bytes 4194316 | tf_op jit(solution)/shard_map/squeeze | solution.py:77
  50.6 10.5 %collective-permute-done = bf16[1024,256]{0,1:T(8,128)(2,1)S(1)} collective-permute-done((bf16[1024,256]{0,1:T(8,128)(2,1)S(1)}, bf16[1024,256]{0,1:T(8,128)(2,1)S(1)}, u32[]{:S(2)}, u32[]{:S(2)}) %collective-permute-start) | collective-permute-done | bytes 524320 | tf_op jit(solution)/shard_map/ppermute | solution.py:83
  61.5 2.7 %collective-permute-start.3 = (bf16[1024,512]{0,1:T(8,128)(2,1)S(1)}, bf16[1024,512]{0,1:T(8,128)(2,1)S(1)}, u32[]{:S(2)}, u32[]{:S(2)}) collective-permute-start(bf16[1024,512]{0,1:T(8,128)(2,1)S(1)} %pad_maximum_fusion.1), channel_id=1, source_target_pairs={{0,3},{1,0},{2,1},{3,2},{4,7},{5,4},{6,5},{7,6},{8,11},{9,8},{10,9... | collective-permute-start | bytes 3145736 | tf_op jit(solution)/shard_map/ppermute | solution.py:86
  64.2 1.3 %fusion.28 = f32[1024,1024]{1,0:T(8,128)S(1)} fusion(bf16[1024,512]{0,1:T(8,128)(2,1)S(1)} %bitcast.75, bf16[4,512,1024]{2,1,0:T(8,128)(2,1)S(1)} %bitcast.77, s32[]{:T(128)S(6)} %select_n.45), kind=kOutput, calls=%fused_computation.36 | convolution fusion | flops 1073741824 | bytes 6291460 | tf_op jit(solution)/shard_map/dot_general | solution.py:80
  65.5 0.7 fusion.35
  66.3 0.7 fusion.37
  67.0 19.7 %collective-permute-done.2 = bf16[1024,512]{0,1:T(8,128)(2,1)S(1)} collective-permute-done((bf16[1024,512]{0,1:T(8,128)(2,1)S(1)}, bf16[1024,512]{0,1:T(8,128)(2,1)S(1)}, u32[]{:S(2)}, u32[]{:S(2)}) %collective-permute-start.2) | collective-permute-done | bytes 1048608 | tf_op jit(solution)/shard_map/ppermute | solution.py:85
  86.7 1.3 %fusion.18 = f32[1024,1024]{1,0:T(8,128)S(1)} fusion(bf16[1024,512]{0,1:T(8,128)(2,1)S(1)} %collective-permute-done.2, bf16[256,1024]{1,0:T(8,128)(2,1)S(1)} %get-tuple-element.11, bf16[256,1024]{1,0:T(8,128)(2,1)S(1)} %get-tuple-element.12), kind=kOutput, calls=%fused_computation.27 | convolution fusion | flops 1075838976 | bytes 6291456 | tf_op jit(solution)/shard_map/dot_general | solution.py:80
  88.0 3.3 %add_convert_fusion = bf16[1024,1024]{1,0:T(8,128)(2,1)} fusion(f32[1024,1024]{1,0:T(8,128)S(1)} %fusion.18, f32[1024,1024]{1,0:T(8,128)S(1)} %fusion.35, f32[1024,1024]{1,0:T(8,128)S(1)} %fusion.28, f32[1024,1024]{1,0:T(8,128)S(1)} %fusion.37, bf16[1024,512]{0,1:T(8,128)(2,1)S(1)} %collective-permute-done.3, bf16[256,1024]{1,0:T(8,128)(2,1)S(1)} %get-tuple-element.10, ...), kind=kOutput, calls=%fused_computation.5 | convolution fusion | flops 1081081856 | bytes 20971520 | tf_op jit(solution)/shard_map/dot_general | solution.py:80
  (24 shorter events, 2.1 us)
Async XLA Ops:
  0.0 15.3 %copy-start = (bf16[1024,512]{1,0:T(8,128)(2,1)S(1)}, bf16[1024,512]{1,0:T(8,128)(2,1)}, u32[]{:S(2)}) copy-start(bf16[1024,512]{1,0:T(8,128)(2,1)} %value_ref.1) | copy-start | bytes 3145732
  5.2 11.5 %copy-start.2 = (bf16[1024,512]{1,0:T(8,128)(2,1)S(1)}, bf16[1024,512]{1,0:T(8,128)(2,1)}, u32[]{:S(2)}) copy-start(bf16[1024,512]{1,0:T(8,128)(2,1)} %param.6) | copy-start | bytes 3145732
  5.2 23.2 %all-to-all-start = ((f32[16,40,128]{2,1,0:T(8,128)}), f32[16,40,128]{2,1,0:T(8,128)S(1)}, u32[]{:S(2)}, u32[]{:S(2)}) async-start(f32[16,40,128]{2,1,0:T(8,128)} %bitcast.80), calls=%async_computation | async-start | bytes 655360 | tf_op jit(solution)/shard_map/all_to_all | solution.py:58
  15.3 2.3 %copy-start.3 = (s32[1024]{0:T(1024)S(1)}, s32[1024]{0:T(1024)}, u32[]{:S(2)}) copy-start(s32[1024]{0:T(1024)} %param.9) | copy-start | bytes 12292
  29.9 14.6 %all-to-all-start.1 = ((f32[16,32,128]{2,1,0:T(8,128)}), f32[16,32,128]{2,1,0:T(8,128)S(1)}, u32[]{:S(2)}, u32[]{:S(2)}) async-start(f32[16,32,128]{2,1,0:T(8,128)} %select_reduce_fusion), calls=%async_computation.1 | async-start | bytes 524288 | tf_op jit(solution)/shard_map/all_to_all | solution.py:65
  45.0 0.7 copy-start.4
  46.0 15.1 %collective-permute-start = (bf16[1024,256]{0,1:T(8,128)(2,1)S(1)}, bf16[1024,256]{0,1:T(8,128)(2,1)S(1)}, u32[]{:S(2)}, u32[]{:S(2)}) collective-permute-start(bf16[1024,256]{0,1:T(8,128)(2,1)S(1)} %get-tuple-element.14), channel_id=1, source_target_pairs={{0,1},{1,2},{2,3},{3,0},{4,5},{5,6},{6,7},{7,4},{8,9},{9,10},{10,1... | collective-permute-start | bytes 1572872 | tf_op jit(solution)/shard_map/ppermute | solution.py:83
  47.4 14.1 %collective-permute-start.1 = (bf16[1024,256]{0,1:T(8,128)(2,1)S(1)}, bf16[1024,256]{0,1:T(8,128)(2,1)S(1)}, u32[]{:S(2)}, u32[]{:S(2)}) collective-permute-start(bf16[1024,256]{0,1:T(8,128)(2,1)S(1)} %get-tuple-element.13), channel_id=1, source_target_pairs={{0,3},{1,0},{2,1},{3,2},{4,7},{5,4},{6,5},{7,6},{8,11},{9,8},{10,9... | collective-permute-start | bytes 1572872 | tf_op jit(solution)/shard_map/ppermute | solution.py:84
  50.6 13.6 %copy-start.1 = (bf16[2048,1024]{1,0:T(8,128)(2,1)S(1)}, bf16[2048,1024]{1,0:T(8,128)(2,1)}, u32[]{:S(2)}) copy-start(bf16[2048,1024]{1,0:T(8,128)(2,1)} %param.11) | copy-start | bytes 12582916
  61.1 25.6 %collective-permute-start.2 = (bf16[1024,512]{0,1:T(8,128)(2,1)S(1)}, bf16[1024,512]{0,1:T(8,128)(2,1)S(1)}, u32[]{:S(2)}, u32[]{:S(2)}) collective-permute-start(bf16[1024,512]{0,1:T(8,128)(2,1)S(1)} %pad_maximum_fusion), channel_id=1, source_target_pairs={{0,1},{1,2},{2,3},{3,0},{4,5},{5,6},{6,7},{7,4},{8,9},{9,10},{10,1... | collective-permute-start | bytes 3145736 | tf_op jit(solution)/shard_map/ppermute | solution.py:85
  61.5 26.5 %collective-permute-start.3 = (bf16[1024,512]{0,1:T(8,128)(2,1)S(1)}, bf16[1024,512]{0,1:T(8,128)(2,1)S(1)}, u32[]{:S(2)}, u32[]{:S(2)}) collective-permute-start(bf16[1024,512]{0,1:T(8,128)(2,1)S(1)} %pad_maximum_fusion.1), channel_id=1, source_target_pairs={{0,3},{1,0},{2,1},{3,2},{4,7},{5,4},{6,5},{7,6},{8,11},{9,8},{10,9... | collective-permute-start | bytes 3145736 | tf_op jit(solution)/shard_map/ppermute | solution.py:86

commit v12 on v11

--- a/solution.py
+++ b/solution.py
@@ -17,9 +17,11 @@
     heads = width // HEAD
     pieces_per_head = HEAD // 32
     segs = seg_ref[...]
-    last = segs[rows - 1 : rows, :]
-    first = segs[0:1, :]
-    in_final = (segs == last).astype(jnp.float32)
+    last = segs[-1:, -1:]
+    first = segs[:1, :1]
+    final_from = jnp.sum((segs != last).astype(jnp.int32))
+    rows_at = lax.broadcasted_iota(jnp.int32, (rows, 1), 0)
+    in_final = (rows_at >= final_from).astype(jnp.float32)
     seg_rows = jnp.where(
         lax.broadcasted_iota(jnp.int32, (8, HEAD), 0) == 0,
         jnp.broadcast_to(last.astype(jnp.float32), (8, HEAD)),
@@ -48,7 +50,7 @@
         out_shape=jax.ShapeDtypeStruct((count * 40, HEAD), jnp.float32),
         in_specs=[pl.BlockSpec(memory_space=pltpu.VMEM)] * 3,
         out_specs=pl.BlockSpec(memory_space=pltpu.VMEM),
-    )(keys, values, segment_ids.reshape(rows, 1))
+    )(keys, values, segment_ids.reshape(-1, HEAD))
     return out.reshape(count, 40, HEAD)
 
 

time: 91.7 us -> 90 us (0.981)
  local copies, waits for them, and re-layouts: 5.65 us -> 3.86 us
    broadcast_in_dim x1 -> x0, local copies, waits for them, and re-layouts: 1.79 us -> none  [per_device(): segment_ids[:, None] == segment_ids[None, :]]
where the time goes in v12:
time: 90 us; the launch traced here: 89.7 us
  waiting for transfers between devices  42.4 us (47%)
  starting transfers between devices  19.3 us (21%)
  matrix products  15.4 us (17%)
  other arithmetic  4.91 us (5%)
  local copies, waits for them, and re-layouts  3.86 us (4%)
  Pallas kernels  3.64 us (4%)
    ppermute x1, waiting for transfers between devices, project_gathered(): lax.ppermute(jnp.concatenate([second, left_first], axis=1), axis, ahead)  19.7 us
    ppermute x1, waiting for transfers between devices, project_gathered(): left_first = lax.ppermute(first, axis, ahead)  10.5 us
    all_to_all x1, starting transfers between devices, carried_in(): pieces = lax.all_to_all(sent, axis, 0, 0, tiled=True)  9.98 us
    all_to_all x1, waiting for transfers between devices, carried_in(): pieces = lax.all_to_all(sent, axis, 0, 0, tiled=True)  9.22 us
    dot_general x5, matrix products, dot(): return jnp.dot(block, weight, preferred_element_type=jnp.float32)  7.39 us
    dot_general x1, matrix products, per_device(): jnp.einsum('hts,she->the', weights, value_heads, preferred_element_type=j...  7 us
    pallas_call x1, Pallas kernels, scan_payload(): pl.pallas_call(_payload_kernel, out_shape=jax.ShapeDtypeStruct((count * 4...  3.64 us
    all_to_all x1, starting transfers between devices, carried_in(): return lax.all_to_all(carry, axis, 0, 0, tiled=True).reshape(shape)  3.43 us
  transfers between devices with their start and end apart: 6, of which 4 were waited for; matrix products, arithmetic and copies ran while one was open for 20% of the time, Pallas kernels for 0%

profile of v12, /device:TPU:1, one launch (start us, length us, event | category | flops | bytes accessed | tf_op | source)
XLA Modules:
  0.0 89.7 jit_solution(3054893613365562312)
XLA Ops:
  0.0 3.6 %shard_map.64 = f32[640,128]{1,0:T(8,128)} custom-call(bf16[1024,512]{1,0:T(8,128)(2,1)} %key_ref.1, bf16[1024,512]{1,0:T(8,128)(2,1)} %value_ref.1, s32[8,128]{1,0:T(8,128)} %bitcast.83), custom_call_target="tpu_custom_call" | custom-call | tf_op jit(solution)/shard_map/pallas_call | solution.py:48
  3.6 10.0 %all-to-all-start = ((f32[16,40,128]{2,1,0:T(8,128)}), f32[16,40,128]{2,1,0:T(8,128)S(1)}, u32[]{:S(2)}, u32[]{:S(2)}) async-start(f32[16,40,128]{2,1,0:T(8,128)} %bitcast.80), calls=%async_computation | async-start | bytes 655360 | tf_op jit(solution)/shard_map/all_to_all | solution.py:60
  13.6 1.3 %copy.25 = bf16[1024,512]{0,1:T(8,128)(2,1)} copy(bf16[1024,512]{1,0:T(8,128)(2,1)S(1)} %copy-done) | data formatting | bytes 2097152 | tf_op jit(solution)/shard_map/reshape | solution.py:102
  15.0 0.9 %fusion.3 = bf16[1024,512]{1,0:T(8,128)(2,1)S(1)} fusion(bf16[1024,512]{1,0:T(8,128)(2,1)S(1)} %copy-done.2), kind=kLoop, calls=%fused_computation.11 | loop fusion | flops 3145728 | bytes 2097152 | tf_op jit(solution)/shard_map/convert_element_type | solution.py:12
  15.9 1.6 %fusion = pred[1024,1024]{1,0:T(8,128)(4,1)} fusion(s32[1024]{0:T(1024)S(1)} %copy-done.3), kind=kLoop, calls=%fused_computation.8 | loop fusion | flops 3145728 | bytes 1052672 | tf_op jit(solution)/shard_map/and | solution.py:107
  17.5 9.2 %all-to-all-done = f32[16,40,128]{2,1,0:T(8,128)S(1)} async-done(((f32[16,40,128]{2,1,0:T(8,128)}), f32[16,40,128]{2,1,0:T(8,128)S(1)}, u32[]{:S(2)}, u32[]{:S(2)}) %all-to-all-start) | async-done | bytes 327712 | tf_op jit(solution)/shard_map/all_to_all | solution.py:60
  27.0 1.2 %select_reduce_fusion = f32[16,32,128]{2,1,0:T(8,128)} fusion(f32[16,32,128]{2,1,0:T(8,128)S(1)} %slice.26, pred[16,16]{1,0:T(8,128)(4,1)S(1)} %fusion.42), kind=kLoop, calls=%fused_computation.6 | loop fusion | flops 2031616 | bytes 524544 | tf_op jit(solution)/shard_map/reduce_sum | solution.py:66
  28.3 3.4 %all-to-all-start.1 = ((f32[16,32,128]{2,1,0:T(8,128)}), f32[16,32,128]{2,1,0:T(8,128)S(1)}, u32[]{:S(2)}, u32[]{:S(2)}) async-start(f32[16,32,128]{2,1,0:T(8,128)} %select_reduce_fusion), calls=%async_computation.1 | async-start | bytes 524288 | tf_op jit(solution)/shard_map/all_to_all | solution.py:67
  31.7 7.0 %fusion.7 = f32[4,1024,128]{1,2,0:T(8,128)S(1)} fusion(bf16[1024,4,128]{0,2,1:T(8,128)(2,1)} %bitcast.81, pred[1024,1024]{1,0:T(8,128)(4,1)} %fusion, bf16[1024,512]{1,0:T(8,128)(2,1)S(1)} %fusion.3, bf16[1024,512]{1,0:T(8,128)(2,1)} %key_ref.1), kind=kOutput, calls=%fused_computation.18 | convolution fusion | flops 2159017984 | bytes 6291456 | tf_op jit(solution)/shard_map/hts,she->the/dot_general | solution.py:112
  38.7 0.5 slice.18
  39.2 0.6 compare_convert_fusion
  39.9 3.0 %all-to-all-done.1 = f32[16,32,128]{2,1,0:T(8,128)S(1)} async-done(((f32[16,32,128]{2,1,0:T(8,128)}), f32[16,32,128]{2,1,0:T(8,128)S(1)}, u32[]{:S(2)}, u32[]{:S(2)}) %all-to-all-start.1) | async-done | bytes 262176 | tf_op jit(solution)/shard_map/all_to_all | solution.py:67
  43.3 0.6 multiply_reduce_fusion
  44.3 1.4 %collective-permute-start = (bf16[1024,256]{0,1:T(8,128)(2,1)S(1)}, bf16[1024,256]{0,1:T(8,128)(2,1)S(1)}, u32[]{:S(2)}, u32[]{:S(2)}) collective-permute-start(bf16[1024,256]{0,1:T(8,128)(2,1)S(1)} %get-tuple-element.14), channel_id=1, source_target_pairs={{0,1},{1,2},{2,3},{3,0},{4,5},{5,6},{6,7},{7,4},{8,9},{9,10},{10,1... | collective-permute-start | bytes 1572872 | tf_op jit(solution)/shard_map/ppermute | solution.py:85
  45.7 1.5 %collective-permute-start.1 = (bf16[1024,256]{0,1:T(8,128)(2,1)S(1)}, bf16[1024,256]{0,1:T(8,128)(2,1)S(1)}, u32[]{:S(2)}, u32[]{:S(2)}) collective-permute-start(bf16[1024,256]{0,1:T(8,128)(2,1)S(1)} %get-tuple-element.13), channel_id=1, source_target_pairs={{0,3},{1,0},{2,1},{3,2},{4,7},{5,4},{6,5},{7,6},{8,11},{9,8},{10,9... | collective-permute-start | bytes 1572872 | tf_op jit(solution)/shard_map/ppermute | solution.py:86
  47.2 1.7 %dynamic-slice_bitcast_fusion.1 = (bf16[256,1024]{1,0:T(8,128)(2,1)S(1)}, bf16[256,1024]{1,0:T(8,128)(2,1)S(1)}, bf16[256,1024]{1,0:T(8,128)(2,1)S(1)}, bf16[256,1024]{1,0:T(8,128)(2,1)S(1)}) fusion(bf16[4,2,256,1024]{3,2,1,0:T(8,128)(2,1)} %bitcast.76, s32[]{:T(128)S(6)} %select_n.47, s32[]{:T(128)S(6)} %select_n.48, s32[]{:T(128)S(6)} %select_n.46), kind=kLoop, calls=%fused_computation.47 | loop fusion | bytes 4194316 | tf_op jit(solution)/shard_map/squeeze | solution.py:79
  48.9 10.5 %collective-permute-done = bf16[1024,256]{0,1:T(8,128)(2,1)S(1)} collective-permute-done((bf16[1024,256]{0,1:T(8,128)(2,1)S(1)}, bf16[1024,256]{0,1:T(8,128)(2,1)S(1)}, u32[]{:S(2)}, u32[]{:S(2)}) %collective-permute-start) | collective-permute-done | bytes 524320 | tf_op jit(solution)/shard_map/ppermute | solution.py:85
  59.9 2.7 %collective-permute-start.3 = (bf16[1024,512]{0,1:T(8,128)(2,1)S(1)}, bf16[1024,512]{0,1:T(8,128)(2,1)S(1)}, u32[]{:S(2)}, u32[]{:S(2)}) collective-permute-start(bf16[1024,512]{0,1:T(8,128)(2,1)S(1)} %pad_maximum_fusion.1), channel_id=1, source_target_pairs={{0,3},{1,0},{2,1},{3,2},{4,7},{5,4},{6,5},{7,6},{8,11},{9,8},{10,9... | collective-permute-start | bytes 3145736 | tf_op jit(solution)/shard_map/ppermute | solution.py:88
  62.6 1.3 %fusion.28 = f32[1024,1024]{1,0:T(8,128)S(1)} fusion(bf16[1024,512]{0,1:T(8,128)(2,1)S(1)} %bitcast.75, bf16[4,512,1024]{2,1,0:T(8,128)(2,1)S(1)} %bitcast.77, s32[]{:T(128)S(6)} %select_n.45), kind=kOutput, calls=%fused_computation.36 | convolution fusion | flops 1073741824 | bytes 6291460 | tf_op jit(solution)/shard_map/dot_general | solution.py:82
  63.9 0.7 fusion.35
  64.6 0.7 fusion.37
  65.4 19.7 %collective-permute-done.2 = bf16[1024,512]{0,1:T(8,128)(2,1)S(1)} collective-permute-done((bf16[1024,512]{0,1:T(8,128)(2,1)S(1)}, bf16[1024,512]{0,1:T(8,128)(2,1)S(1)}, u32[]{:S(2)}, u32[]{:S(2)}) %collective-permute-start.2) | collective-permute-done | bytes 1048608 | tf_op jit(solution)/shard_map/ppermute | solution.py:87
  85.1 1.3 %fusion.18 = f32[1024,1024]{1,0:T(8,128)S(1)} fusion(bf16[1024,512]{0,1:T(8,128)(2,1)S(1)} %collective-permute-done.2, bf16[256,1024]{1,0:T(8,128)(2,1)S(1)} %get-tuple-element.11, bf16[256,1024]{1,0:T(8,128)(2,1)S(1)} %get-tuple-element.12), kind=kOutput, calls=%fused_computation.27 | convolution fusion | flops 1075838976 | bytes 6291456 | tf_op jit(solution)/shard_map/dot_general | solution.py:82
  86.4 3.3 %add_convert_fusion = bf16[1024,1024]{1,0:T(8,128)(2,1)} fusion(f32[1024,1024]{1,0:T(8,128)S(1)} %fusion.18, f32[1024,1024]{1,0:T(8,128)S(1)} %fusion.35, f32[1024,1024]{1,0:T(8,128)S(1)} %fusion.28, f32[1024,1024]{1,0:T(8,128)S(1)} %fusion.37, bf16[1024,512]{0,1:T(8,128)(2,1)S(1)} %collective-permute-done.3, bf16[256,1024]{1,0:T(8,128)(2,1)S(1)} %get-tuple-element.10, ...), kind=kOutput, calls=%fused_computation.5 | convolution fusion | flops 1081081856 | bytes 20971520 | tf_op jit(solution)/shard_map/dot_general | solution.py:82
  (23 shorter events, 1.6 us)
Async XLA Ops:
  0.0 13.6 %copy-start = (bf16[1024,512]{1,0:T(8,128)(2,1)S(1)}, bf16[1024,512]{1,0:T(8,128)(2,1)}, u32[]{:S(2)}) copy-start(bf16[1024,512]{1,0:T(8,128)(2,1)} %value_ref.1) | copy-start | bytes 3145732
  0.0 15.0 %copy-start.2 = (bf16[1024,512]{1,0:T(8,128)(2,1)S(1)}, bf16[1024,512]{1,0:T(8,128)(2,1)}, u32[]{:S(2)}) copy-start(bf16[1024,512]{1,0:T(8,128)(2,1)} %param.6) | copy-start | bytes 3145732
  3.6 23.1 %all-to-all-start = ((f32[16,40,128]{2,1,0:T(8,128)}), f32[16,40,128]{2,1,0:T(8,128)S(1)}, u32[]{:S(2)}, u32[]{:S(2)}) async-start(f32[16,40,128]{2,1,0:T(8,128)} %bitcast.80), calls=%async_computation | async-start | bytes 655360 | tf_op jit(solution)/shard_map/all_to_all | solution.py:60
  13.6 2.3 %copy-start.3 = (s32[1024]{0:T(1024)S(1)}, s32[1024]{0:T(1024)}, u32[]{:S(2)}) copy-start(s32[1024]{0:T(1024)} %param.9) | copy-start | bytes 12292
  28.3 14.6 %all-to-all-start.1 = ((f32[16,32,128]{2,1,0:T(8,128)}), f32[16,32,128]{2,1,0:T(8,128)S(1)}, u32[]{:S(2)}, u32[]{:S(2)}) async-start(f32[16,32,128]{2,1,0:T(8,128)} %select_reduce_fusion), calls=%async_computation.1 | async-start | bytes 524288 | tf_op jit(solution)/shard_map/all_to_all | solution.py:67
  43.3 0.7 copy-start.4
  44.3 15.1 %collective-permute-start = (bf16[1024,256]{0,1:T(8,128)(2,1)S(1)}, bf16[1024,256]{0,1:T(8,128)(2,1)S(1)}, u32[]{:S(2)}, u32[]{:S(2)}) collective-permute-start(bf16[1024,256]{0,1:T(8,128)(2,1)S(1)} %get-tuple-element.14), channel_id=1, source_target_pairs={{0,1},{1,2},{2,3},{3,0},{4,5},{5,6},{6,7},{7,4},{8,9},{9,10},{10,1... | collective-permute-start | bytes 1572872 | tf_op jit(solution)/shard_map/ppermute | solution.py:85
  45.7 14.1 %collective-permute-start.1 = (bf16[1024,256]{0,1:T(8,128)(2,1)S(1)}, bf16[1024,256]{0,1:T(8,128)(2,1)S(1)}, u32[]{:S(2)}, u32[]{:S(2)}) collective-permute-start(bf16[1024,256]{0,1:T(8,128)(2,1)S(1)} %get-tuple-element.13), channel_id=1, source_target_pairs={{0,3},{1,0},{2,1},{3,2},{4,7},{5,4},{6,5},{7,6},{8,11},{9,8},{10,9... | collective-permute-start | bytes 1572872 | tf_op jit(solution)/shard_map/ppermute | solution.py:86
  48.9 13.6 %copy-start.1 = (bf16[2048,1024]{1,0:T(8,128)(2,1)S(1)}, bf16[2048,1024]{1,0:T(8,128)(2,1)}, u32[]{:S(2)}) copy-start(bf16[2048,1024]{1,0:T(8,128)(2,1)} %param.11) | copy-start | bytes 12582916
  59.5 25.6 %collective-permute-start.2 = (bf16[1024,512]{0,1:T(8,128)(2,1)S(1)}, bf16[1024,512]{0,1:T(8,128)(2,1)S(1)}, u32[]{:S(2)}, u32[]{:S(2)}) collective-permute-start(bf16[1024,512]{0,1:T(8,128)(2,1)S(1)} %pad_maximum_fusion), channel_id=1, source_target_pairs={{0,1},{1,2},{2,3},{3,0},{4,5},{5,6},{6,7},{7,4},{8,9},{9,10},{10,1... | collective-permute-start | bytes 3145736 | tf_op jit(solution)/shard_map/ppermute | solution.py:87
  59.9 26.5 %collective-permute-start.3 = (bf16[1024,512]{0,1:T(8,128)(2,1)S(1)}, bf16[1024,512]{0,1:T(8,128)(2,1)S(1)}, u32[]{:S(2)}, u32[]{:S(2)}) collective-permute-start(bf16[1024,512]{0,1:T(8,128)(2,1)S(1)} %pad_maximum_fusion.1), channel_id=1, source_target_pairs={{0,3},{1,0},{2,1},{3,2},{4,7},{5,4},{6,5},{7,6},{8,11},{9,8},{10,9... | collective-permute-start | bytes 3145736 | tf_op jit(solution)/shard_map/ppermute | solution.py:88

commit v13 on v12

--- a/solution.py
+++ b/solution.py
@@ -84,13 +84,20 @@
     first, second = hidden[:, :half], hidden[:, half:]
     left_first = lax.ppermute(first, axis, ahead)
     right_second = lax.ppermute(second, axis, behind)
-    from_left = lax.ppermute(jnp.concatenate([second, left_first], axis=1), axis, ahead)
-    from_right = lax.ppermute(jnp.concatenate([first, right_second], axis=1), axis, behind)
-    left_weight = jnp.concatenate([rows_of(-1, 1), rows_of(2, 0)], axis=0)
-    right_weight = jnp.concatenate([rows_of(1, 0), rows_of(2, 1)], axis=0)
-    total = dot(hidden, out_weight.reshape(count, width, -1)[mine])
-    total = total + dot(left_first, rows_of(-1, 0)) + dot(right_second, rows_of(1, 1))
-    return total + dot(from_left, left_weight) + dot(from_right, right_weight)
+    own = dot(hidden, out_weight.reshape(count, width, -1)[mine])
+    to_left, to_right, own = lax.optimization_barrier(
+        (
+            jnp.concatenate([second, left_first], axis=1),
+            jnp.concatenate([first, right_second], axis=1),
+            own,
+        )
+    )
+    from_left = lax.ppermute(to_left, axis, ahead)
+    from_right = lax.ppermute(to_right, axis, behind)
+    total = lax.optimization_barrier(own + dot(left_first, rows_of(-1, 0)))
+    total = lax.optimization_barrier(total + dot(right_second, rows_of(1, 1)))
+    total = total + dot(from_left[:, :half], rows_of(-1, 1)) + dot(from_left[:, half:], rows_of(2, 0))
+    return total + dot(from_right[:, :half], rows_of(1, 0)) + dot(from_right[:, half:], rows_of(2, 1))
 
 
 def per_device(queries, keys, values, segment_ids, norm_gain, out_weight):

time: 90 us -> 91.2 us (1.013)
  waiting for transfers between devices: 42.4 us -> 35.5 us
  matrix products: 15.4 us -> 19.8 us
  other arithmetic: 4.91 us -> 8.59 us
    dot_general x5 -> x7, matrix products: 7.39 us -> 11.7 us  [dot(): return jnp.dot(block, weight, preferred_element_type=jnp.float32)]
    ppermute x2, waiting for transfers between devices: 19.7 us -> 16.7 us  [the longest x1 16.7 us: project_gathered(): from_left = lax.ppermute(to_left, axis, ahead)]
    ppermute x1, waiting for transfers between devices: 10.5 us -> 7.54 us  [project_gathered(): left_first = lax.ppermute(first, axis, ahead)]
    add x0 -> x2, other arithmetic: none -> 2.72 us  [the longest x1 1.36 us: project_gathered(): total = lax.optimization_barrier(total + dot(right_second, rows_of(1, 1)))]
    squeeze x1 -> x0, local copies, waits for them, and re-layouts: 1.69 us -> none  [rows_of(): return weight_halves[lax.rem(mine + offset + count, count), which]]
    concatenate x1, other arithmetic: 0.07 us -> 1.04 us  [project_gathered(): jnp.concatenate([second, left_first], axis=1)]
    reshape x1, local copies, waits for them, and re-layouts: 1.32 us -> 2.26 us  [per_device(): value_heads = values.reshape(rows_here, heads_here, HEAD)]
    all_to_all x1, waiting for transfers between devices: 9.22 us -> 8.29 us  [carried_in(): pieces = lax.all_to_all(sent, axis, 0, 0, tiled=True)]
  transfers between devices with their start and end apart: 6 -> 6, of which waited for: 4 -> 4; matrix products, arithmetic and copies ran while one was open for 20% -> 28% of each run, Pallas kernels for 0% -> 0%
where the time goes in v13:
time: 91.2 us; the launch traced here: 90.8 us
  waiting for transfers between devices  35.5 us (39%)
  matrix products  19.8 us (22%)
  starting transfers between devices  19.2 us (21%)
  other arithmetic  8.59 us (9%)
  local copies, waits for them, and re-layouts  3.92 us (4%)
  Pallas kernels  3.58 us (4%)
    ppermute x1, waiting for transfers between devices, project_gathered(): from_left = lax.ppermute(to_left, axis, ahead)  16.7 us
    dot_general x7, matrix products, dot(): return jnp.dot(block, weight, preferred_element_type=jnp.float32)  11.7 us
    all_to_all x1, starting transfers between devices, carried_in(): pieces = lax.all_to_all(sent, axis, 0, 0, tiled=True)  9.98 us
    all_to_all x1, waiting for transfers between devices, carried_in(): pieces = lax.all_to_all(sent, axis, 0, 0, tiled=True)  8.29 us
    ppermute x1, waiting for transfers between devices, project_gathered(): left_first = lax.ppermute(first, axis, ahead)  7.54 us
    dot_general x1, matrix products, per_device(): jnp.einsum('hts,she->the', weights, value_heads, preferred_element_type=j...  7 us
    pallas_call x1, Pallas kernels, scan_payload(): pl.pallas_call(_payload_kernel, out_shape=jax.ShapeDtypeStruct((count * 4...  3.58 us
    all_to_all x1, starting transfers between devices, carried_in(): return lax.all_to_all(carry, axis, 0, 0, tiled=True).reshape(shape)  3.43 us
  transfers between devices with their start and end apart: 6, of which 4 were waited for; matrix products, arithmetic and copies ran while one was open for 28% of the time, Pallas kernels for 0%

profile of v13, /device:TPU:1, one launch (start us, length us, event | category | flops | bytes accessed | tf_op | source)
XLA Modules:
  0.0 90.8 jit_solution(13590841427008175258)
XLA Ops:
  0.0 3.6 %shard_map.64 = f32[640,128]{1,0:T(8,128)} custom-call(bf16[1024,512]{1,0:T(8,128)(2,1)} %key_ref.1, bf16[1024,512]{1,0:T(8,128)(2,1)} %value_ref.1, s32[8,128]{1,0:T(8,128)} %bitcast.88), custom_call_target="tpu_custom_call" | custom-call | tf_op jit(solution)/shard_map/pallas_call | solution.py:48
  3.6 10.0 %all-to-all-start = ((f32[16,40,128]{2,1,0:T(8,128)}), f32[16,40,128]{2,1,0:T(8,128)S(1)}, u32[]{:S(2)}, u32[]{:S(2)}) async-start(f32[16,40,128]{2,1,0:T(8,128)} %bitcast.85), calls=%async_computation | async-start | bytes 655360 | tf_op jit(solution)/shard_map/all_to_all | solution.py:60
  13.6 2.3 %copy.25 = bf16[1024,512]{0,1:T(8,128)(2,1)} copy(bf16[1024,512]{1,0:T(8,128)(2,1)} %value_ref.1) | data formatting | bytes 2097152 | tf_op jit(solution)/shard_map/reshape | solution.py:109
  15.8 0.9 %fusion.3 = bf16[1024,512]{1,0:T(8,128)(2,1)S(1)} fusion(bf16[1024,512]{1,0:T(8,128)(2,1)S(1)} %copy-done.2), kind=kLoop, calls=%fused_computation.11 | loop fusion | flops 3145728 | bytes 2097152 | tf_op jit(solution)/shard_map/convert_element_type | solution.py:12
  16.8 1.6 %fusion = pred[1024,1024]{1,0:T(8,128)(4,1)} fusion(s32[1024]{0:T(1024)S(1)} %copy-done.3), kind=kLoop, calls=%fused_computation.8 | loop fusion | flops 3145728 | bytes 1052672 | tf_op jit(solution)/shard_map/and | solution.py:114
  18.3 8.3 %all-to-all-done = f32[16,40,128]{2,1,0:T(8,128)S(1)} async-done(((f32[16,40,128]{2,1,0:T(8,128)}), f32[16,40,128]{2,1,0:T(8,128)S(1)}, u32[]{:S(2)}, u32[]{:S(2)}) %all-to-all-start) | async-done | bytes 327712 | tf_op jit(solution)/shard_map/all_to_all | solution.py:60
  26.9 1.2 %select_reduce_fusion = f32[16,32,128]{2,1,0:T(8,128)} fusion(f32[16,32,128]{2,1,0:T(8,128)S(1)} %slice.42, pred[16,16]{1,0:T(8,128)(4,1)S(1)} %fusion.50), kind=kLoop, calls=%fused_computation.6 | loop fusion | flops 2031616 | bytes 524544 | tf_op jit(solution)/shard_map/reduce_sum | solution.py:66
  28.2 3.4 %all-to-all-start.1 = ((f32[16,32,128]{2,1,0:T(8,128)}), f32[16,32,128]{2,1,0:T(8,128)S(1)}, u32[]{:S(2)}, u32[]{:S(2)}) async-start(f32[16,32,128]{2,1,0:T(8,128)} %select_reduce_fusion), calls=%async_computation.1 | async-start | bytes 524288 | tf_op jit(solution)/shard_map/all_to_all | solution.py:67
  31.6 7.0 %fusion.7 = f32[4,1024,128]{1,2,0:T(8,128)S(1)} fusion(bf16[1024,4,128]{0,2,1:T(8,128)(2,1)} %bitcast.86, pred[1024,1024]{1,0:T(8,128)(4,1)} %fusion, bf16[1024,512]{1,0:T(8,128)(2,1)S(1)} %fusion.3, bf16[1024,512]{1,0:T(8,128)(2,1)} %key_ref.1), kind=kOutput, calls=%fused_computation.18 | convolution fusion | flops 2159017984 | bytes 6291456 | tf_op jit(solution)/shard_map/hts,she->the/dot_general | solution.py:119
  39.8 3.0 %all-to-all-done.1 = f32[16,32,128]{2,1,0:T(8,128)S(1)} async-done(((f32[16,32,128]{2,1,0:T(8,128)}), f32[16,32,128]{2,1,0:T(8,128)S(1)}, u32[]{:S(2)}, u32[]{:S(2)}) %all-to-all-start.1) | async-done | bytes 262176 | tf_op jit(solution)/shard_map/all_to_all | solution.py:67
  44.3 1.4 %collective-permute-start = (bf16[1024,256]{0,1:T(8,128)(2,1)S(1)}, bf16[1024,256]{0,1:T(8,128)(2,1)S(1)}, u32[]{:S(2)}, u32[]{:S(2)}) collective-permute-start(bf16[1024,256]{0,1:T(8,128)(2,1)S(1)} %get-tuple-element.16), channel_id=1, source_target_pairs={{0,1},{1,2},{2,3},{3,0},{4,5},{5,6},{6,7},{7,4},{8,9},{9,10},{10,1... | collective-permute-start | bytes 1572872 | tf_op jit(solution)/shard_map/ppermute | solution.py:85
  45.6 1.7 %collective-permute-start.1 = (bf16[1024,256]{0,1:T(8,128)(2,1)S(1)}, bf16[1024,256]{0,1:T(8,128)(2,1)S(1)}, u32[]{:S(2)}, u32[]{:S(2)}) collective-permute-start(bf16[1024,256]{0,1:T(8,128)(2,1)S(1)} %get-tuple-element.15), channel_id=1, source_target_pairs={{0,3},{1,0},{2,1},{3,2},{4,7},{5,4},{6,5},{7,6},{8,11},{9,8},{10,9... | collective-permute-start | bytes 1572872 | tf_op jit(solution)/shard_map/ppermute | solution.py:86
  47.3 4.4 %fusion.18 = f32[1024,1024]{1,0:T(8,128)} fusion(bf16[1024,512]{0,1:T(8,128)(2,1)S(1)} %bitcast.77, bf16[4,512,1024]{2,1,0:T(8,128)(2,1)} %bitcast.78, s32[]{:T(128)S(6)} %select_n.45), kind=kOutput, calls=%fused_computation.28 | convolution fusion | flops 1073741824 | bytes 6291460 | tf_op jit(solution)/shard_map/dot_general | solution.py:82
  51.8 7.5 %collective-permute-done = bf16[1024,256]{0,1:T(8,128)(2,1)S(1)} collective-permute-done((bf16[1024,256]{0,1:T(8,128)(2,1)S(1)}, bf16[1024,256]{0,1:T(8,128)(2,1)S(1)}, u32[]{:S(2)}, u32[]{:S(2)}) %collective-permute-start) | collective-permute-done | bytes 524320 | tf_op jit(solution)/shard_map/ppermute | solution.py:85
  59.3 1.0 %pad_maximum_fusion = bf16[1024,512]{0,1:T(8,128)(2,1)} fusion(bf16[1024,256]{0,1:T(8,128)(2,1)S(1)} %collective-permute-done, bf16[1024,256]{0,1:T(8,128)(2,1)S(1)} %get-tuple-element.15), kind=kLoop, calls=%fused_computation.26 | loop fusion | flops 2097152 | bytes 2097152 | tf_op jit(solution)/shard_map/concatenate | solution.py:90
  60.6 2.6 %collective-permute-start.3 = (bf16[1024,512]{0,1:T(8,128)(2,1)S(1)}, bf16[1024,512]{0,1:T(8,128)(2,1)S(1)}, u32[]{:S(2)}, u32[]{:S(2)}) collective-permute-start(bf16[1024,512]{0,1:T(8,128)(2,1)S(1)} %pad_maximum_fusion.1), channel_id=1, source_target_pairs={{0,3},{1,0},{2,1},{3,2},{4,7},{5,4},{6,5},{7,6},{8,11},{9,8},{10,9... | collective-permute-start | bytes 3145736 | tf_op jit(solution)/shard_map/ppermute | solution.py:96
  63.2 1.8 %fusion.41 = f32[1024,1024]{1,0:T(8,128)S(1)} fusion(bf16[1024,256]{0,1:T(8,128)(2,1)S(1)} %collective-permute-done, bf16[4,2,256,1024]{3,2,1,0:T(8,128)(2,1)} %bitcast.79, s32[]{:T(128)S(6)} %select_n.46), kind=kOutput, calls=%fused_computation.48 | convolution fusion | flops 536870912 | bytes 5242884 | tf_op jit(solution)/shard_map/dot_general | solution.py:82
  65.0 1.4 %add.90 = f32[1024,1024]{1,0:T(8,128)S(1)} add(f32[1024,1024]{1,0:T(8,128)S(1)} %copy-done, f32[1024,1024]{1,0:T(8,128)S(1)} %fusion.41) | non-fusion elementwise | flops 1048576 | bytes 12582912 | tf_op jit(solution)/shard_map/add | solution.py:97
  66.4 0.8 copy-done.1
  67.9 1.4 %add.93 = f32[1024,1024]{1,0:T(8,128)S(1)} add(f32[1024,1024]{1,0:T(8,128)S(1)} %add.90, f32[1024,1024]{1,0:T(8,128)S(1)} %fusion.39) | non-fusion elementwise | flops 1048576 | bytes 12582912 | tf_op jit(solution)/shard_map/add | solution.py:98
  69.3 16.7 %collective-permute-done.2 = bf16[1024,512]{0,1:T(8,128)(2,1)S(1)} collective-permute-done((bf16[1024,512]{0,1:T(8,128)(2,1)}, bf16[1024,512]{0,1:T(8,128)(2,1)S(1)}, u32[]{:S(2)}, u32[]{:S(2)}) %collective-permute-start.2) | collective-permute-done | bytes 1048608 | tf_op jit(solution)/shard_map/ppermute | solution.py:95
  86.0 0.7 fusion.33
  86.8 0.7 fusion.31
  88.3 2.5 %add_convert_fusion = bf16[1024,1024]{1,0:T(8,128)(2,1)} fusion(f32[1024,1024]{1,0:T(8,128)S(1)} %fusion.29, f32[1024,1024]{1,0:T(8,128)S(1)} %fusion.31, f32[1024,1024]{1,0:T(8,128)S(1)} %add.93, f32[1024,1024]{1,0:T(8,128)S(1)} %fusion.33, bf16[1024,512]{0,1:T(8,128)(2,1)S(1)} %collective-permute-done.3, bf16[4,2,256,1024]{3,2,1,0:T(8,128)(2,1)S(1)} %bitcast.84, ...), kind=kOutput, calls=%fused_computation.5 | convolution fusion | flops 542113792 | bytes 19922948 | tf_op jit(solution)/shard_map/dot_general | solution.py:82
  (26 shorter events, 4.6 us)
Async XLA Ops:
  0.0 16.8 %copy-start.3 = (s32[1024]{0:T(1024)S(1)}, s32[1024]{0:T(1024)}, u32[]{:S(2)}) copy-start(s32[1024]{0:T(1024)} %param.9) | copy-start | bytes 12292
  0.0 15.8 %copy-start.2 = (bf16[1024,512]{1,0:T(8,128)(2,1)S(1)}, bf16[1024,512]{1,0:T(8,128)(2,1)}, u32[]{:S(2)}) copy-start(bf16[1024,512]{1,0:T(8,128)(2,1)} %param.6) | copy-start | bytes 3145732
  3.6 23.1 %all-to-all-start = ((f32[16,40,128]{2,1,0:T(8,128)}), f32[16,40,128]{2,1,0:T(8,128)S(1)}, u32[]{:S(2)}, u32[]{:S(2)}) async-start(f32[16,40,128]{2,1,0:T(8,128)} %bitcast.85), calls=%async_computation | async-start | bytes 655360 | tf_op jit(solution)/shard_map/all_to_all | solution.py:60
  28.2 14.6 %all-to-all-start.1 = ((f32[16,32,128]{2,1,0:T(8,128)}), f32[16,32,128]{2,1,0:T(8,128)S(1)}, u32[]{:S(2)}, u32[]{:S(2)}) async-start(f32[16,32,128]{2,1,0:T(8,128)} %select_reduce_fusion), calls=%async_computation.1 | async-start | bytes 524288 | tf_op jit(solution)/shard_map/all_to_all | solution.py:67
  43.2 0.7 copy-start.4
  44.3 15.1 %collective-permute-start = (bf16[1024,256]{0,1:T(8,128)(2,1)S(1)}, bf16[1024,256]{0,1:T(8,128)(2,1)S(1)}, u32[]{:S(2)}, u32[]{:S(2)}) collective-permute-start(bf16[1024,256]{0,1:T(8,128)(2,1)S(1)} %get-tuple-element.16), channel_id=1, source_target_pairs={{0,1},{1,2},{2,3},{3,0},{4,5},{5,6},{6,7},{7,4},{8,9},{9,10},{10,1... | collective-permute-start | bytes 1572872 | tf_op jit(solution)/shard_map/ppermute | solution.py:85
  45.6 14.7 %collective-permute-start.1 = (bf16[1024,256]{0,1:T(8,128)(2,1)S(1)}, bf16[1024,256]{0,1:T(8,128)(2,1)S(1)}, u32[]{:S(2)}, u32[]{:S(2)}) collective-permute-start(bf16[1024,256]{0,1:T(8,128)(2,1)S(1)} %get-tuple-element.15), channel_id=1, source_target_pairs={{0,3},{1,0},{2,1},{3,2},{4,7},{5,4},{6,5},{7,6},{8,11},{9,8},{10,9... | collective-permute-start | bytes 1572872 | tf_op jit(solution)/shard_map/ppermute | solution.py:86
  60.4 25.6 %collective-permute-start.2 = (bf16[1024,512]{0,1:T(8,128)(2,1)}, bf16[1024,512]{0,1:T(8,128)(2,1)S(1)}, u32[]{:S(2)}, u32[]{:S(2)}) collective-permute-start(bf16[1024,512]{0,1:T(8,128)(2,1)} %pad_maximum_fusion), channel_id=1, source_target_pairs={{0,1},{1,2},{2,3},{3,0},{4,5},{5,6},{6,7},{7,4},{8,9},{9,10},{10,1... | collective-permute-start | bytes 3145736 | tf_op jit(solution)/shard_map/ppermute | solution.py:95
  60.6 4.4 %copy-start = (f32[1024,1024]{1,0:T(8,128)S(1)}, f32[1024,1024]{1,0:T(8,128)}, u32[]{:S(2)}) copy-start(f32[1024,1024]{1,0:T(8,128)} %fusion.18) | copy-start | bytes 12582916
  60.6 27.0 %collective-permute-start.3 = (bf16[1024,512]{0,1:T(8,128)(2,1)S(1)}, bf16[1024,512]{0,1:T(8,128)(2,1)S(1)}, u32[]{:S(2)}, u32[]{:S(2)}) collective-permute-start(bf16[1024,512]{0,1:T(8,128)(2,1)S(1)} %pad_maximum_fusion.1), channel_id=1, source_target_pairs={{0,3},{1,0},{2,1},{3,2},{4,7},{5,4},{6,5},{7,6},{8,11},{9,8},{10,9... | collective-permute-start | bytes 3145736 | tf_op jit(solution)/shard_map/ppermute | solution.py:96
  65.0 2.2 %copy-start.1 = (bf16[2048,1024]{1,0:T(8,128)(2,1)S(1)}, bf16[2048,1024]{1,0:T(8,128)(2,1)}, u32[]{:S(2)}) copy-start(bf16[2048,1024]{1,0:T(8,128)(2,1)} %param.11) | copy-start | bytes 12582916

commit v14 on v12

--- a/solution.py
+++ b/solution.py
@@ -88,8 +88,11 @@
     from_right = lax.ppermute(jnp.concatenate([first, right_second], axis=1), axis, behind)
     left_weight = jnp.concatenate([rows_of(-1, 1), rows_of(2, 0)], axis=0)
     right_weight = jnp.concatenate([rows_of(1, 0), rows_of(2, 1)], axis=0)
-    total = dot(hidden, out_weight.reshape(count, width, -1)[mine])
-    total = total + dot(left_first, rows_of(-1, 0)) + dot(right_second, rows_of(1, 1))
+    near = jnp.concatenate([hidden, left_first, right_second], axis=1)
+    near_weight = jnp.concatenate(
+        [out_weight.reshape(count, width, -1)[mine], rows_of(-1, 0), rows_of(1, 1)], axis=0
+    )
+    total = dot(near, near_weight)
     return total + dot(from_left, left_weight) + dot(from_right, right_weight)
 
 

time: 90 us -> 91.9 us (1.021)
  waiting for transfers between devices: 42.4 us -> 36.8 us
  local copies, waits for them, and re-layouts: 3.86 us -> 7.75 us
  other arithmetic: 4.91 us -> 7.95 us
    ppermute x1, waiting for transfers between devices: 19.7 us -> 12.5 us  [project_gathered(): lax.ppermute(jnp.concatenate([second, left_first], axis=1), axis, ahead)]
    squeeze x0 -> x1, local copies, waits for them, and re-layouts: none -> 2.26 us  [project_gathered(): out_weight.reshape(count, width, -1)[mine]]
    concatenate x1, other arithmetic: 0.07 us -> 2.14 us  [project_gathered(): jnp.concatenate([first, right_second], axis=1)]
    ppermute x1, waiting for transfers between devices: 10.5 us -> 12.2 us  [project_gathered(): left_first = lax.ppermute(first, axis, ahead)]
    concatenate x1, other arithmetic: 0.07 us -> 1.03 us  [project_gathered(): jnp.concatenate([second, left_first], axis=1)]
    dot_general x5 -> x3, matrix products: 7.39 us -> 7.35 us  [dot(): return jnp.dot(block, weight, preferred_element_type=jnp.float32)]
  transfers between devices with their start and end apart: 6 -> 6, of which waited for: 4 -> 4; matrix products, arithmetic and copies ran while one was open for 20% -> 27% of each run, Pallas kernels for 0% -> 0%
where the time goes in v14:
time: 91.9 us; the launch traced here: 90.7 us
  waiting for transfers between devices  36.8 us (40%)
  starting transfers between devices  19 us (21%)
  matrix products  15.4 us (17%)
  other arithmetic  7.95 us (9%)
  local copies, waits for them, and re-layouts  7.75 us (8%)
  Pallas kernels  3.66 us (4%)
    ppermute x1, waiting for transfers between devices, project_gathered(): lax.ppermute(jnp.concatenate([second, left_first], axis=1), axis, ahead)  12.5 us
    ppermute x1, waiting for transfers between devices, project_gathered(): left_first = lax.ppermute(first, axis, ahead)  12.2 us
    all_to_all x1, starting transfers between devices, carried_in(): pieces = lax.all_to_all(sent, axis, 0, 0, tiled=True)  9.98 us
    all_to_all x1, waiting for transfers between devices, carried_in(): pieces = lax.all_to_all(sent, axis, 0, 0, tiled=True)  9.22 us
    dot_general x3, matrix products, dot(): return jnp.dot(block, weight, preferred_element_type=jnp.float32)  7.35 us
    dot_general x1, matrix products, per_device(): jnp.einsum('hts,she->the', weights, value_heads, preferred_element_type=j...  7 us
    pallas_call x1, Pallas kernels, scan_payload(): pl.pallas_call(_payload_kernel, out_shape=jax.ShapeDtypeStruct((count * 4...  3.66 us
    all_to_all x1, starting transfers between devices, carried_in(): return lax.all_to_all(carry, axis, 0, 0, tiled=True).reshape(shape)  3.43 us
  transfers between devices with their start and end apart: 6, of which 4 were waited for; matrix products, arithmetic and copies ran while one was open for 27% of the time, Pallas kernels for 0%

profile of v14, /device:TPU:1, one launch (start us, length us, event | category | flops | bytes accessed | tf_op | source)
XLA Modules:
  0.0 90.7 jit_solution(13820071412463313179)
XLA Ops:
  0.0 3.7 %shard_map.64 = f32[640,128]{1,0:T(8,128)} custom-call(bf16[1024,512]{1,0:T(8,128)(2,1)} %key_ref.1, bf16[1024,512]{1,0:T(8,128)(2,1)} %value_ref.1, s32[8,128]{1,0:T(8,128)} %bitcast.75), custom_call_target="tpu_custom_call" | custom-call | tf_op jit(solution)/shard_map/pallas_call | solution.py:48
  3.7 10.0 %all-to-all-start = ((f32[16,40,128]{2,1,0:T(8,128)}), f32[16,40,128]{2,1,0:T(8,128)S(1)}, u32[]{:S(2)}, u32[]{:S(2)}) async-start(f32[16,40,128]{2,1,0:T(8,128)} %bitcast.72), calls=%async_computation | async-start | bytes 655360 | tf_op jit(solution)/shard_map/all_to_all | solution.py:60
  13.7 1.3 %copy.25 = bf16[1024,512]{0,1:T(8,128)(2,1)} copy(bf16[1024,512]{1,0:T(8,128)(2,1)S(1)} %copy-done) | data formatting | bytes 2097152 | tf_op jit(solution)/shard_map/reshape | solution.py:105
  15.0 0.9 %fusion.3 = bf16[1024,512]{1,0:T(8,128)(2,1)S(1)} fusion(bf16[1024,512]{1,0:T(8,128)(2,1)S(1)} %copy-done.2), kind=kLoop, calls=%fused_computation.11 | loop fusion | flops 3145728 | bytes 2097152 | tf_op jit(solution)/shard_map/convert_element_type | solution.py:12
  15.9 1.6 %fusion = pred[1024,1024]{1,0:T(8,128)(4,1)} fusion(s32[1024]{0:T(1024)S(1)} %copy-done.5), kind=kLoop, calls=%fused_computation.8 | loop fusion | flops 3145728 | bytes 1052672 | tf_op jit(solution)/shard_map/and | solution.py:110
  17.5 9.2 %all-to-all-done = f32[16,40,128]{2,1,0:T(8,128)S(1)} async-done(((f32[16,40,128]{2,1,0:T(8,128)}), f32[16,40,128]{2,1,0:T(8,128)S(1)}, u32[]{:S(2)}, u32[]{:S(2)}) %all-to-all-start) | async-done | bytes 327712 | tf_op jit(solution)/shard_map/all_to_all | solution.py:60
  27.0 1.2 %select_reduce_fusion = f32[16,32,128]{2,1,0:T(8,128)} fusion(f32[16,32,128]{2,1,0:T(8,128)S(1)} %slice.26, pred[16,16]{1,0:T(8,128)(4,1)S(1)} %fusion.44), kind=kLoop, calls=%fused_computation.6 | loop fusion | flops 2031616 | bytes 524544 | tf_op jit(solution)/shard_map/reduce_sum | solution.py:66
  28.3 3.4 %all-to-all-start.1 = ((f32[16,32,128]{2,1,0:T(8,128)}), f32[16,32,128]{2,1,0:T(8,128)S(1)}, u32[]{:S(2)}, u32[]{:S(2)}) async-start(f32[16,32,128]{2,1,0:T(8,128)} %select_reduce_fusion), calls=%async_computation.1 | async-start | bytes 524288 | tf_op jit(solution)/shard_map/all_to_all | solution.py:67
  31.7 7.0 %fusion.18 = f32[4,1024,128]{1,2,0:T(8,128)S(1)} fusion(bf16[1024,4,128]{0,2,1:T(8,128)(2,1)} %bitcast.73, pred[1024,1024]{1,0:T(8,128)(4,1)} %fusion, bf16[1024,512]{1,0:T(8,128)(2,1)S(1)} %fusion.3, bf16[1024,512]{1,0:T(8,128)(2,1)} %key_ref.1), kind=kOutput, calls=%fused_computation.29 | convolution fusion | flops 2159017984 | bytes 6291456 | tf_op jit(solution)/shard_map/hts,she->the/dot_general | solution.py:115
  39.2 0.6 compare_convert_fusion
  39.9 3.0 %all-to-all-done.1 = f32[16,32,128]{2,1,0:T(8,128)S(1)} async-done(((f32[16,32,128]{2,1,0:T(8,128)}), f32[16,32,128]{2,1,0:T(8,128)S(1)}, u32[]{:S(2)}, u32[]{:S(2)}) %all-to-all-start.1) | async-done | bytes 262176 | tf_op jit(solution)/shard_map/all_to_all | solution.py:67
  44.4 1.4 %collective-permute-start = (bf16[1024,256]{0,1:T(8,128)(2,1)S(1)}, bf16[1024,256]{0,1:T(8,128)(2,1)S(1)}, u32[]{:S(2)}, u32[]{:S(2)}) collective-permute-start(bf16[1024,256]{0,1:T(8,128)(2,1)S(1)} %get-tuple-element.15), channel_id=1, source_target_pairs={{0,1},{1,2},{2,3},{3,0},{4,5},{5,6},{6,7},{7,4},{8,9},{9,10},{10,1... | collective-permute-start | bytes 1572872 | tf_op jit(solution)/shard_map/ppermute | solution.py:85
  45.7 1.5 %collective-permute-start.1 = (bf16[1024,256]{0,1:T(8,128)(2,1)S(1)}, bf16[1024,256]{0,1:T(8,128)(2,1)}, u32[]{:S(2)}, u32[]{:S(2)}) collective-permute-start(bf16[1024,256]{0,1:T(8,128)(2,1)S(1)} %get-tuple-element.16), channel_id=1, source_target_pairs={{0,3},{1,0},{2,1},{3,2},{4,7},{5,4},{6,5},{7,6},{8,11},{9,8},{10,9... | collective-permute-start | bytes 1572872 | tf_op jit(solution)/shard_map/ppermute | solution.py:86
  47.3 12.2 %collective-permute-done = bf16[1024,256]{0,1:T(8,128)(2,1)S(1)} collective-permute-done((bf16[1024,256]{0,1:T(8,128)(2,1)S(1)}, bf16[1024,256]{0,1:T(8,128)(2,1)S(1)}, u32[]{:S(2)}, u32[]{:S(2)}) %collective-permute-start) | collective-permute-done | bytes 524320 | tf_op jit(solution)/shard_map/ppermute | solution.py:85
  59.4 0.8 copy-done.3
  60.2 1.0 %pad_maximum_fusion = bf16[1024,512]{0,1:T(8,128)(2,1)} fusion(bf16[1024,256]{0,1:T(8,128)(2,1)S(1)} %collective-permute-done, bf16[1024,256]{0,1:T(8,128)(2,1)S(1)} %get-tuple-element.16), kind=kLoop, calls=%fused_computation.37 | loop fusion | flops 2097152 | bytes 2097152 | tf_op jit(solution)/shard_map/concatenate | solution.py:87
  61.4 2.1 %pad_maximum_fusion.1 = bf16[1024,512]{0,1:T(8,128)(2,1)} fusion(bf16[1024,256]{0,1:T(8,128)(2,1)} %collective-permute-done.1, bf16[1024,256]{0,1:T(8,128)(2,1)S(1)} %get-tuple-element.15), kind=kLoop, calls=%fused_computation.42 | loop fusion | flops 2097152 | bytes 2097152 | tf_op jit(solution)/shard_map/concatenate | solution.py:88
  63.5 2.6 %collective-permute-start.3 = (bf16[1024,512]{0,1:T(8,128)(2,1)}, bf16[1024,512]{0,1:T(8,128)(2,1)S(1)}, u32[]{:S(2)}, u32[]{:S(2)}) collective-permute-start(bf16[1024,512]{0,1:T(8,128)(2,1)} %pad_maximum_fusion.1), channel_id=1, source_target_pairs={{0,3},{1,0},{2,1},{3,2},{4,7},{5,4},{6,5},{7,6},{8,11},{9,8},{10,9... | collective-permute-start | bytes 3145736 | tf_op jit(solution)/shard_map/ppermute | solution.py:88
  66.1 2.3 %dynamic-slice_bitcast_fusion = bf16[512,1024]{1,0:T(8,128)(2,1)} fusion(bf16[4,512,1024]{2,1,0:T(8,128)(2,1)} %bitcast.68, s32[]{:T(128)S(6)} %select_n.45), kind=kLoop, calls=%fused_computation.47 | loop fusion | bytes 2097156 | tf_op jit(solution)/shard_map/squeeze | solution.py:93
  68.4 2.5 %dynamic-slice_bitcast_fusion.2 = (bf16[256,1024]{1,0:T(8,128)(2,1)S(1)}, bf16[256,1024]{1,0:T(8,128)(2,1)S(1)}, bf16[256,1024]{1,0:T(8,128)(2,1)S(1)}, bf16[256...) fusion(bf16[4,2,256,1024]{3,2,1,0:T(8,128)(2,1)} %bitcast.69, ...), kind=kLoop, calls=%fused_computation.52 | loop fusion | bytes 6291468 | tf_op jit(solution)/shard_map/squeeze | solution.py:79
  70.9 3.4 %fusion.7 = f32[1024,1024]{1,0:T(8,128)S(1)} fusion(bf16[1024,256]{0,1:T(8,128)(2,1)} %collective-permute-done.1, bf16[1024,256]{0,1:T(8,128)(2,1)S(1)} %copy-done.4, bf16[1024,512]{0,1:T(8,128)(2,1)S(1)} %bitcast.71, bf16[256,1024]{1,0:T(8,128)(2,1)S(1)} %get-tuple-element.13, bf16[256,1024]{1,0:T(8,128)(2,1)S(1)} %get-tuple-element.14, ...), kind=kOutput, calls=%fused_computation.15 | convolution fusion | flops 2160066560 | bytes 8388608 | tf_op jit(solution)/shard_map/dot_general | solution.py:82
  74.3 12.5 %collective-permute-done.2 = bf16[1024,512]{0,1:T(8,128)(2,1)S(1)} collective-permute-done((bf16[1024,512]{0,1:T(8,128)(2,1)}, bf16[1024,512]{0,1:T(8,128)(2,1)S(1)}, u32[]{:S(2)}, u32[]{:S(2)}) %collective-permute-start.2) | collective-permute-done | bytes 1048608 | tf_op jit(solution)/shard_map/ppermute | solution.py:87
  86.8 1.3 %fusion.29 = f32[1024,1024]{1,0:T(8,128)S(1)} fusion(bf16[1024,512]{0,1:T(8,128)(2,1)S(1)} %collective-permute-done.2, bf16[256,1024]{1,0:T(8,128)(2,1)S(1)} %get-tuple-element.11, bf16[256,1024]{1,0:T(8,128)(2,1)S(1)} %get-tuple-element.12), kind=kOutput, calls=%fused_computation.38 | convolution fusion | flops 1075838976 | bytes 6291456 | tf_op jit(solution)/shard_map/dot_general | solution.py:82
  88.1 2.6 %add_convert_fusion = bf16[1024,1024]{1,0:T(8,128)(2,1)} fusion(f32[1024,1024]{1,0:T(8,128)S(1)} %fusion.7, f32[1024,1024]{1,0:T(8,128)S(1)} %fusion.29, bf16[1024,512]{0,1:T(8,128)(2,1)S(1)} %collective-permute-done.3, bf16[256,1024]{1,0:T(8,128)(2,1)S(1)} %get-tuple-element.10, bf16[256,1024]{1,0:T(8,128)(2,1)S(1)} %get-tuple-element.9), kind=kOutput, calls=%fused_computation.5 | convolution fusion | flops 1078984704 | bytes 12582912 | tf_op jit(solution)/shard_map/dot_general | solution.py:82
  (26 shorter events, 2.4 us)
Async XLA Ops:
  0.0 13.6 %copy-start = (bf16[1024,512]{1,0:T(8,128)(2,1)S(1)}, bf16[1024,512]{1,0:T(8,128)(2,1)}, u32[]{:S(2)}) copy-start(bf16[1024,512]{1,0:T(8,128)(2,1)} %value_ref.1) | copy-start | bytes 3145732
  0.0 15.0 %copy-start.2 = (bf16[1024,512]{1,0:T(8,128)(2,1)S(1)}, bf16[1024,512]{1,0:T(8,128)(2,1)}, u32[]{:S(2)}) copy-start(bf16[1024,512]{1,0:T(8,128)(2,1)} %param.6) | copy-start | bytes 3145732
  3.7 23.1 %all-to-all-start = ((f32[16,40,128]{2,1,0:T(8,128)}), f32[16,40,128]{2,1,0:T(8,128)S(1)}, u32[]{:S(2)}, u32[]{:S(2)}) async-start(f32[16,40,128]{2,1,0:T(8,128)} %bitcast.72), calls=%async_computation | async-start | bytes 655360 | tf_op jit(solution)/shard_map/all_to_all | solution.py:60
  13.7 2.3 %copy-start.5 = (s32[1024]{0:T(1024)S(1)}, s32[1024]{0:T(1024)}, u32[]{:S(2)}) copy-start(s32[1024]{0:T(1024)} %param.9) | copy-start | bytes 12292
  28.3 14.6 %all-to-all-start.1 = ((f32[16,32,128]{2,1,0:T(8,128)}), f32[16,32,128]{2,1,0:T(8,128)S(1)}, u32[]{:S(2)}, u32[]{:S(2)}) async-start(f32[16,32,128]{2,1,0:T(8,128)} %select_reduce_fusion), calls=%async_computation.1 | async-start | bytes 524288 | tf_op jit(solution)/shard_map/all_to_all | solution.py:67
  43.3 0.7 copy-start.6
  44.4 15.1 %collective-permute-start = (bf16[1024,256]{0,1:T(8,128)(2,1)S(1)}, bf16[1024,256]{0,1:T(8,128)(2,1)S(1)}, u32[]{:S(2)}, u32[]{:S(2)}) collective-permute-start(bf16[1024,256]{0,1:T(8,128)(2,1)S(1)} %get-tuple-element.15), channel_id=1, source_target_pairs={{0,1},{1,2},{2,3},{3,0},{4,5},{5,6},{6,7},{7,4},{8,9},{9,10},{10,1... | collective-permute-start | bytes 1572872 | tf_op jit(solution)/shard_map/ppermute | solution.py:85
  45.7 15.6 %collective-permute-start.1 = (bf16[1024,256]{0,1:T(8,128)(2,1)S(1)}, bf16[1024,256]{0,1:T(8,128)(2,1)}, u32[]{:S(2)}, u32[]{:S(2)}) collective-permute-start(bf16[1024,256]{0,1:T(8,128)(2,1)S(1)} %get-tuple-element.16), channel_id=1, source_target_pairs={{0,3},{1,0},{2,1},{3,2},{4,7},{5,4},{6,5},{7,6},{8,11},{9,8},{10,9... | collective-permute-start | bytes 1572872 | tf_op jit(solution)/shard_map/ppermute | solution.py:86
  59.4 0.8 copy-start.3
  61.3 25.5 %collective-permute-start.2 = (bf16[1024,512]{0,1:T(8,128)(2,1)}, bf16[1024,512]{0,1:T(8,128)(2,1)S(1)}, u32[]{:S(2)}, u32[]{:S(2)}) collective-permute-start(bf16[1024,512]{0,1:T(8,128)(2,1)} %pad_maximum_fusion), channel_id=1, source_target_pairs={{0,1},{1,2},{2,3},{3,0},{4,5},{5,6},{6,7},{7,4},{8,9},{9,10},{10,1... | collective-permute-start | bytes 3145736 | tf_op jit(solution)/shard_map/ppermute | solution.py:87
  63.5 24.6 %collective-permute-start.3 = (bf16[1024,512]{0,1:T(8,128)(2,1)}, bf16[1024,512]{0,1:T(8,128)(2,1)S(1)}, u32[]{:S(2)}, u32[]{:S(2)}) collective-permute-start(bf16[1024,512]{0,1:T(8,128)(2,1)} %pad_maximum_fusion.1), channel_id=1, source_target_pairs={{0,3},{1,0},{2,1},{3,2},{4,7},{5,4},{6,5},{7,6},{8,11},{9,8},{10,9... | collective-permute-start | bytes 3145736 | tf_op jit(solution)/shard_map/ppermute | solution.py:88
  68.4 2.5 %copy-start.1 = (bf16[512,1024]{1,0:T(8,128)(2,1)S(1)}, bf16[512,1024]{1,0:T(8,128)(2,1)}, u32[]{:S(2)}) copy-start(bf16[512,1024]{1,0:T(8,128)(2,1)} %dynamic-slice_bitcast_fusion) | copy-start | bytes 3145732
  68.4 2.5 %copy-start.4 = (bf16[1024,256]{0,1:T(8,128)(2,1)S(1)}, bf16[1024,256]{0,1:T(8,128)(2,1)}, u32[]{:S(2)}) copy-start(bf16[1024,256]{0,1:T(8,128)(2,1)} %copy-done.3) | copy-start | bytes 1572868

commit v15 on v12

--- a/solution.py
+++ b/solution.py
@@ -63,7 +63,12 @@
     first_segs = pieces[:, tile + 1, 0]
     block = jnp.arange(count)
     mask = (block[None, :] < block[:, None]) & (last_segs[None, :] == first_segs[:, None])
-    carry = jnp.sum(jnp.where(mask[:, :, None, None], sums[None], 0.0), axis=1)
+    carry = jnp.dot(
+        mask.astype(jnp.float32),
+        sums.reshape(count, -1),
+        precision=lax.Precision.HIGHEST,
+        preferred_element_type=jnp.float32,
+    ).reshape(sums.shape)
     return lax.all_to_all(carry, axis, 0, 0, tiled=True).reshape(shape)
 
 

time: 90 us -> 89.9 us (level)
  other arithmetic: 4.91 us -> 3.58 us
    reduce_sum x1 -> x0, other arithmetic: 1.24 us -> none  [carried_in(): carry = jnp.sum(jnp.where(mask[:, :, None, None], sums[None], 0.0), axis=1)]
where the time goes in v15:
time: 89.9 us; the launch traced here: 89.6 us
  waiting for transfers between devices  42.4 us (47%)
  starting transfers between devices  19.3 us (21%)
  matrix products  15.9 us (18%)
  local copies, waits for them, and re-layouts  4.64 us (5%)
  Pallas kernels  3.65 us (4%)
  other arithmetic  3.58 us (4%)
    ppermute x1, waiting for transfers between devices, project_gathered(): lax.ppermute(jnp.concatenate([second, left_first], axis=1), axis, ahead)  19.7 us
    ppermute x1, waiting for transfers between devices, project_gathered(): left_first = lax.ppermute(first, axis, ahead)  10.5 us
    all_to_all x1, starting transfers between devices, carried_in(): pieces = lax.all_to_all(sent, axis, 0, 0, tiled=True)  9.98 us
    all_to_all x1, waiting for transfers between devices, carried_in(): pieces = lax.all_to_all(sent, axis, 0, 0, tiled=True)  9.23 us
    dot_general x5, matrix products, dot(): return jnp.dot(block, weight, preferred_element_type=jnp.float32)  7.39 us
    dot_general x1, matrix products, per_device(): jnp.einsum('hts,she->the', weights, value_heads, preferred_element_type=j...  7 us
    pallas_call x1, Pallas kernels, scan_payload(): pl.pallas_call(_payload_kernel, out_shape=jax.ShapeDtypeStruct((count * 4...  3.65 us
    all_to_all x1, starting transfers between devices, carried_in(): return lax.all_to_all(carry, axis, 0, 0, tiled=True).reshape(shape)  3.43 us
  transfers between devices with their start and end apart: 6, of which 4 were waited for; matrix products, arithmetic and copies ran while one was open for 20% of the time, Pallas kernels for 0%

profile of v15, /device:TPU:1, one launch (start us, length us, event | category | flops | bytes accessed | tf_op | source)
XLA Modules:
  0.0 89.6 jit_solution(3814628046407010363)
XLA Ops:
  0.0 3.7 %shard_map.64 = f32[640,128]{1,0:T(8,128)} custom-call(bf16[1024,512]{1,0:T(8,128)(2,1)} %key_ref.1, bf16[1024,512]{1,0:T(8,128)(2,1)} %value_ref.1, s32[8,128]{1,0:T(8,128)} %bitcast.100), custom_call_target="tpu_custom_call" | custom-call | tf_op jit(solution)/shard_map/pallas_call | solution.py:48
  3.7 10.0 %all-to-all-start = ((f32[16,40,128]{2,1,0:T(8,128)}), f32[16,40,128]{2,1,0:T(8,128)S(1)}, u32[]{:S(2)}, u32[]{:S(2)}) async-start(f32[16,40,128]{2,1,0:T(8,128)} %bitcast.96), calls=%async_computation | async-start | bytes 655360 | tf_op jit(solution)/shard_map/all_to_all | solution.py:60
  13.7 1.3 %copy.32 = bf16[1024,512]{0,1:T(8,128)(2,1)} copy(bf16[1024,512]{1,0:T(8,128)(2,1)S(1)} %copy-done) | data formatting | bytes 2097152 | tf_op jit(solution)/shard_map/reshape | solution.py:107
  15.0 0.9 %fusion.3 = bf16[1024,512]{1,0:T(8,128)(2,1)S(1)} fusion(bf16[1024,512]{1,0:T(8,128)(2,1)S(1)} %copy-done.2), kind=kLoop, calls=%fused_computation.10 | loop fusion | flops 3145728 | bytes 2097152 | tf_op jit(solution)/shard_map/convert_element_type | solution.py:12
  15.9 1.6 %fusion = pred[1024,1024]{1,0:T(8,128)(4,1)} fusion(s32[1024]{0:T(1024)S(1)} %copy-done.3), kind=kLoop, calls=%fused_computation.7 | loop fusion | flops 3145728 | bytes 1052672 | tf_op jit(solution)/shard_map/and | solution.py:112
  17.5 9.2 %all-to-all-done = f32[16,40,128]{2,1,0:T(8,128)S(1)} async-done(((f32[16,40,128]{2,1,0:T(8,128)}), f32[16,40,128]{2,1,0:T(8,128)S(1)}, u32[]{:S(2)}, u32[]{:S(2)}) %all-to-all-start) | async-done | bytes 327712 | tf_op jit(solution)/shard_map/all_to_all | solution.py:60
  27.4 0.8 copy.29
  28.2 3.4 %all-to-all-start.1 = ((f32[16,32,128]{2,1,0:T(8,128)}), f32[16,32,128]{2,1,0:T(8,128)S(1)}, u32[]{:S(2)}, u32[]{:S(2)}) async-start(f32[16,32,128]{2,1,0:T(8,128)} %copy.29), calls=%async_computation.1 | async-start | bytes 524288 | tf_op jit(solution)/shard_map/all_to_all | solution.py:72
  31.6 7.0 %fusion.7 = f32[4,1024,128]{1,2,0:T(8,128)S(1)} fusion(bf16[1024,4,128]{0,2,1:T(8,128)(2,1)} %bitcast.97, pred[1024,1024]{1,0:T(8,128)(4,1)} %fusion, bf16[1024,512]{1,0:T(8,128)(2,1)S(1)} %fusion.3, bf16[1024,512]{1,0:T(8,128)(2,1)} %key_ref.1), kind=kOutput, calls=%fused_computation.17 | convolution fusion | flops 2159017984 | bytes 6291456 | tf_op jit(solution)/shard_map/hts,she->the/dot_general | solution.py:117
  38.6 0.5 slice.18
  39.1 0.6 compare_convert_fusion
  39.8 3.0 %all-to-all-done.1 = f32[16,32,128]{2,1,0:T(8,128)S(1)} async-done(((f32[16,32,128]{2,1,0:T(8,128)}), f32[16,32,128]{2,1,0:T(8,128)S(1)}, u32[]{:S(2)}, u32[]{:S(2)}) %all-to-all-start.1) | async-done | bytes 262176 | tf_op jit(solution)/shard_map/all_to_all | solution.py:72
  43.2 0.6 multiply_reduce_fusion
  44.2 1.4 %collective-permute-start = (bf16[1024,256]{0,1:T(8,128)(2,1)S(1)}, bf16[1024,256]{0,1:T(8,128)(2,1)S(1)}, u32[]{:S(2)}, u32[]{:S(2)}) collective-permute-start(bf16[1024,256]{0,1:T(8,128)(2,1)S(1)} %get-tuple-element.14), channel_id=1, source_target_pairs={{0,1},{1,2},{2,3},{3,0},{4,5},{5,6},{6,7},{7,4},{8,9},{9,10},{10,1... | collective-permute-start | bytes 1572872 | tf_op jit(solution)/shard_map/ppermute | solution.py:90
  45.6 1.5 %collective-permute-start.1 = (bf16[1024,256]{0,1:T(8,128)(2,1)S(1)}, bf16[1024,256]{0,1:T(8,128)(2,1)S(1)}, u32[]{:S(2)}, u32[]{:S(2)}) collective-permute-start(bf16[1024,256]{0,1:T(8,128)(2,1)S(1)} %get-tuple-element.13), channel_id=1, source_target_pairs={{0,3},{1,0},{2,1},{3,2},{4,7},{5,4},{6,5},{7,6},{8,11},{9,8},{10,9... | collective-permute-start | bytes 1572872 | tf_op jit(solution)/shard_map/ppermute | solution.py:91
  47.1 1.7 %dynamic-slice_bitcast_fusion.1 = (bf16[256,1024]{1,0:T(8,128)(2,1)S(1)}, bf16[256,1024]{1,0:T(8,128)(2,1)S(1)}, bf16[256,1024]{1,0:T(8,128)(2,1)S(1)}, bf16[256,1024]{1,0:T(8,128)(2,1)S(1)}) fusion(bf16[4,2,256,1024]{3,2,1,0:T(8,128)(2,1)} %bitcast.92, s32[]{:T(128)S(6)} %select_n.42, s32[]{:T(128)S(6)} %select_n.43, s32[]{:T(128)S(6)} %select_n.41), kind=kLoop, calls=%fused_computation.46 | loop fusion | bytes 4194316 | tf_op jit(solution)/shard_map/squeeze | solution.py:84
  48.8 10.5 %collective-permute-done = bf16[1024,256]{0,1:T(8,128)(2,1)S(1)} collective-permute-done((bf16[1024,256]{0,1:T(8,128)(2,1)S(1)}, bf16[1024,256]{0,1:T(8,128)(2,1)S(1)}, u32[]{:S(2)}, u32[]{:S(2)}) %collective-permute-start) | collective-permute-done | bytes 524320 | tf_op jit(solution)/shard_map/ppermute | solution.py:90
  59.8 2.7 %collective-permute-start.3 = (bf16[1024,512]{0,1:T(8,128)(2,1)S(1)}, bf16[1024,512]{0,1:T(8,128)(2,1)S(1)}, u32[]{:S(2)}, u32[]{:S(2)}) collective-permute-start(bf16[1024,512]{0,1:T(8,128)(2,1)S(1)} %pad_maximum_fusion.1), channel_id=1, source_target_pairs={{0,3},{1,0},{2,1},{3,2},{4,7},{5,4},{6,5},{7,6},{8,11},{9,8},{10,9... | collective-permute-start | bytes 3145736 | tf_op jit(solution)/shard_map/ppermute | solution.py:93
  62.5 1.3 %fusion.28 = f32[1024,1024]{1,0:T(8,128)S(1)} fusion(bf16[1024,512]{0,1:T(8,128)(2,1)S(1)} %bitcast.91, bf16[4,512,1024]{2,1,0:T(8,128)(2,1)S(1)} %bitcast.93, s32[]{:T(128)S(6)} %select_n.40), kind=kOutput, calls=%fused_computation.35 | convolution fusion | flops 1073741824 | bytes 6291460 | tf_op jit(solution)/shard_map/dot_general | solution.py:87
  63.8 0.7 fusion.35
  64.5 0.7 fusion.37
  65.3 19.7 %collective-permute-done.2 = bf16[1024,512]{0,1:T(8,128)(2,1)S(1)} collective-permute-done((bf16[1024,512]{0,1:T(8,128)(2,1)S(1)}, bf16[1024,512]{0,1:T(8,128)(2,1)S(1)}, u32[]{:S(2)}, u32[]{:S(2)}) %collective-permute-start.2) | collective-permute-done | bytes 1048608 | tf_op jit(solution)/shard_map/ppermute | solution.py:92
  85.0 1.3 %fusion.18 = f32[1024,1024]{1,0:T(8,128)S(1)} fusion(bf16[1024,512]{0,1:T(8,128)(2,1)S(1)} %collective-permute-done.2, bf16[256,1024]{1,0:T(8,128)(2,1)S(1)} %get-tuple-element.11, bf16[256,1024]{1,0:T(8,128)(2,1)S(1)} %get-tuple-element.12), kind=kOutput, calls=%fused_computation.26 | convolution fusion | flops 1075838976 | bytes 6291456 | tf_op jit(solution)/shard_map/dot_general | solution.py:87
  86.3 3.3 %add_convert_fusion = bf16[1024,1024]{1,0:T(8,128)(2,1)} fusion(f32[1024,1024]{1,0:T(8,128)S(1)} %fusion.18, f32[1024,1024]{1,0:T(8,128)S(1)} %fusion.35, f32[1024,1024]{1,0:T(8,128)S(1)} %fusion.28, f32[1024,1024]{1,0:T(8,128)S(1)} %fusion.37, bf16[1024,512]{0,1:T(8,128)(2,1)S(1)} %collective-permute-done.3, bf16[256,1024]{1,0:T(8,128)(2,1)S(1)} %get-tuple-element.10, ...), kind=kOutput, calls=%fused_computation.5 | convolution fusion | flops 1081081856 | bytes 20971520 | tf_op jit(solution)/shard_map/dot_general | solution.py:87
  (23 shorter events, 1.9 us)
Async XLA Ops:
  0.0 13.6 %copy-start = (bf16[1024,512]{1,0:T(8,128)(2,1)S(1)}, bf16[1024,512]{1,0:T(8,128)(2,1)}, u32[]{:S(2)}) copy-start(bf16[1024,512]{1,0:T(8,128)(2,1)} %value_ref.1) | copy-start | bytes 3145732
  0.0 15.0 %copy-start.2 = (bf16[1024,512]{1,0:T(8,128)(2,1)S(1)}, bf16[1024,512]{1,0:T(8,128)(2,1)}, u32[]{:S(2)}) copy-start(bf16[1024,512]{1,0:T(8,128)(2,1)} %param.6) | copy-start | bytes 3145732
  3.7 23.1 %all-to-all-start = ((f32[16,40,128]{2,1,0:T(8,128)}), f32[16,40,128]{2,1,0:T(8,128)S(1)}, u32[]{:S(2)}, u32[]{:S(2)}) async-start(f32[16,40,128]{2,1,0:T(8,128)} %bitcast.96), calls=%async_computation | async-start | bytes 655360 | tf_op jit(solution)/shard_map/all_to_all | solution.py:60
  13.6 2.3 %copy-start.3 = (s32[1024]{0:T(1024)S(1)}, s32[1024]{0:T(1024)}, u32[]{:S(2)}) copy-start(s32[1024]{0:T(1024)} %param.9) | copy-start | bytes 12292
  28.2 14.6 %all-to-all-start.1 = ((f32[16,32,128]{2,1,0:T(8,128)}), f32[16,32,128]{2,1,0:T(8,128)S(1)}, u32[]{:S(2)}, u32[]{:S(2)}) async-start(f32[16,32,128]{2,1,0:T(8,128)} %copy.29), calls=%async_computation.1 | async-start | bytes 524288 | tf_op jit(solution)/shard_map/all_to_all | solution.py:72
  43.2 0.7 copy-start.4
  44.2 15.1 %collective-permute-start = (bf16[1024,256]{0,1:T(8,128)(2,1)S(1)}, bf16[1024,256]{0,1:T(8,128)(2,1)S(1)}, u32[]{:S(2)}, u32[]{:S(2)}) collective-permute-start(bf16[1024,256]{0,1:T(8,128)(2,1)S(1)} %get-tuple-element.14), channel_id=1, source_target_pairs={{0,1},{1,2},{2,3},{3,0},{4,5},{5,6},{6,7},{7,4},{8,9},{9,10},{10,1... | collective-permute-start | bytes 1572872 | tf_op jit(solution)/shard_map/ppermute | solution.py:90
  45.6 14.1 %collective-permute-start.1 = (bf16[1024,256]{0,1:T(8,128)(2,1)S(1)}, bf16[1024,256]{0,1:T(8,128)(2,1)S(1)}, u32[]{:S(2)}, u32[]{:S(2)}) collective-permute-start(bf16[1024,256]{0,1:T(8,128)(2,1)S(1)} %get-tuple-element.13), channel_id=1, source_target_pairs={{0,3},{1,0},{2,1},{3,2},{4,7},{5,4},{6,5},{7,6},{8,11},{9,8},{10,9... | collective-permute-start | bytes 1572872 | tf_op jit(solution)/shard_map/ppermute | solution.py:91
  48.8 13.6 %copy-start.1 = (bf16[2048,1024]{1,0:T(8,128)(2,1)S(1)}, bf16[2048,1024]{1,0:T(8,128)(2,1)}, u32[]{:S(2)}) copy-start(bf16[2048,1024]{1,0:T(8,128)(2,1)} %param.11) | copy-start | bytes 12582916
  59.4 25.6 %collective-permute-start.2 = (bf16[1024,512]{0,1:T(8,128)(2,1)S(1)}, bf16[1024,512]{0,1:T(8,128)(2,1)S(1)}, u32[]{:S(2)}, u32[]{:S(2)}) collective-permute-start(bf16[1024,512]{0,1:T(8,128)(2,1)S(1)} %pad_maximum_fusion), channel_id=1, source_target_pairs={{0,1},{1,2},{2,3},{3,0},{4,5},{5,6},{6,7},{7,4},{8,9},{9,10},{10,1... | collective-permute-start | bytes 3145736 | tf_op jit(solution)/shard_map/ppermute | solution.py:92
  59.8 26.5 %collective-permute-start.3 = (bf16[1024,512]{0,1:T(8,128)(2,1)S(1)}, bf16[1024,512]{0,1:T(8,128)(2,1)S(1)}, u32[]{:S(2)}, u32[]{:S(2)}) collective-permute-start(bf16[1024,512]{0,1:T(8,128)(2,1)S(1)} %pad_maximum_fusion.1), channel_id=1, source_target_pairs={{0,3},{1,0},{2,1},{3,2},{4,7},{5,4},{6,5},{7,6},{8,11},{9,8},{10,9... | collective-permute-start | bytes 3145736 | tf_op jit(solution)/shard_map/ppermute | solution.py:93

commit v16 on v12

--- a/solution.py
+++ b/solution.py
@@ -13,8 +13,7 @@
 
 
 def _payload_kernel(key_ref, value_ref, seg_ref, out_ref):
-    rows, width = key_ref.shape
-    heads = width // HEAD
+    rows = key_ref.shape[0]
     pieces_per_head = HEAD // 32
     segs = seg_ref[...]
     last = segs[-1:, -1:]
@@ -27,30 +26,34 @@
         jnp.broadcast_to(last.astype(jnp.float32), (8, HEAD)),
         jnp.broadcast_to(first.astype(jnp.float32), (8, HEAD)),
     )
-    for h in range(heads):
-        cols = slice(h * HEAD, (h + 1) * HEAD)
-        raw = key_ref[:, cols].astype(jnp.float32)
-        feat = jnp.where(raw > 0, raw + 1.0, jnp.exp(jnp.minimum(raw, 0.0))).astype(jnp.bfloat16)
-        masked = (feat.astype(jnp.float32) * in_final).astype(jnp.bfloat16)
-        sums = lax.dot_general(
-            value_ref[:, cols], masked, (((0,), (0,)), ((), ())),
-            preferred_element_type=jnp.float32,
-        )
-        for j in range(pieces_per_head):
-            piece = h * pieces_per_head + j
-            out_ref[piece * 40 : piece * 40 + 32, :] = sums[j * 32 : (j + 1) * 32, :]
-            out_ref[piece * 40 + 32 : piece * 40 + 40, :] = seg_rows
+    raw = key_ref[...].astype(jnp.float32)
+    feat = jnp.where(raw > 0, raw + 1.0, jnp.exp(jnp.minimum(raw, 0.0))).astype(jnp.bfloat16)
+    masked = (feat.astype(jnp.float32) * in_final).astype(jnp.bfloat16)
+    sums = lax.dot_general(
+        value_ref[...], masked, (((0,), (0,)), ((), ())),
+        preferred_element_type=jnp.float32,
+    )
+    for j in range(pieces_per_head):
+        out_ref[j * 40 : j * 40 + 32, :] = sums[j * 32 : (j + 1) * 32, :]
+        out_ref[j * 40 + 32 : j * 40 + 40, :] = seg_rows
 
 
 def scan_payload(keys, values, segment_ids):
     rows, width = keys.shape
     count = width // 32
+    heads = width // HEAD
+    seg_tiles = segment_ids.reshape(-1, HEAD)
     out = pl.pallas_call(
         _payload_kernel,
         out_shape=jax.ShapeDtypeStruct((count * 40, HEAD), jnp.float32),
-        in_specs=[pl.BlockSpec(memory_space=pltpu.VMEM)] * 3,
-        out_specs=pl.BlockSpec(memory_space=pltpu.VMEM),
-    )(keys, values, segment_ids.reshape(-1, HEAD))
+        grid=(heads,),
+        in_specs=[
+            pl.BlockSpec((rows, HEAD), lambda h: (0, h)),
+            pl.BlockSpec((rows, HEAD), lambda h: (0, h)),
+            pl.BlockSpec(seg_tiles.shape, lambda h: (0, 0)),
+        ],
+        out_specs=pl.BlockSpec((count // heads * 40, HEAD), lambda h: (h, 0)),
+    )(keys, values, seg_tiles)
     return out.reshape(count, 40, HEAD)
 
 

time: 90 us -> 90.9 us (1.010)
  Pallas kernels: 3.64 us -> 4.68 us
    pallas_call x1, Pallas kernels: 3.64 us -> 4.68 us  [scan_payload(): pl.pallas_call(_payload_kernel, out_shape=jax.ShapeDtypeStruct((count * 4...]
where the time goes in v16:
time: 90.9 us; the launch traced here: 90.5 us
  waiting for transfers between devices  42.2 us (46%)
  starting transfers between devices  19.3 us (21%)
  matrix products  15.5 us (17%)
  other arithmetic  4.91 us (5%)
  Pallas kernels  4.68 us (5%)
  local copies, waits for them, and re-layouts  3.85 us (4%)
    ppermute x1, waiting for transfers between devices, project_gathered(): lax.ppermute(jnp.concatenate([second, left_first], axis=1), axis, ahead)  19.5 us
    ppermute x1, waiting for transfers between devices, project_gathered(): left_first = lax.ppermute(first, axis, ahead)  10.5 us
    all_to_all x1, starting transfers between devices, carried_in(): pieces = lax.all_to_all(sent, axis, 0, 0, tiled=True)  9.98 us
    all_to_all x1, waiting for transfers between devices, carried_in(): pieces = lax.all_to_all(sent, axis, 0, 0, tiled=True)  9.22 us
    dot_general x5, matrix products, dot(): return jnp.dot(block, weight, preferred_element_type=jnp.float32)  7.39 us
    dot_general x1, matrix products, per_device(): jnp.einsum('hts,she->the', weights, value_heads, preferred_element_type=j...  7 us
    pallas_call x1, Pallas kernels, scan_payload(): pl.pallas_call(_payload_kernel, out_shape=jax.ShapeDtypeStruct((count * 4...  4.68 us
    all_to_all x1, starting transfers between devices, carried_in(): return lax.all_to_all(carry, axis, 0, 0, tiled=True).reshape(shape)  3.43 us
  transfers between devices with their start and end apart: 6, of which 4 were waited for; matrix products, arithmetic and copies ran while one was open for 20% of the time, Pallas kernels for 0%

profile of v16, /device:TPU:1, one launch (start us, length us, event | category | flops | bytes accessed | tf_op | source)
XLA Modules:
  0.0 90.5 jit_solution(11397804951228693942)
XLA Ops:
  0.0 4.7 %shard_map.64 = f32[640,128]{1,0:T(8,128)} custom-call(bf16[1024,512]{1,0:T(8,128)(2,1)} %key_ref.1, bf16[1024,512]{1,0:T(8,128)(2,1)} %value_ref.1, s32[8,128]{1,0:T(8,128)} %bitcast.83), custom_call_target="tpu_custom_call" | custom-call | tf_op jit(solution)/shard_map/pallas_call | solution.py:46
  4.7 10.0 %all-to-all-start = ((f32[16,40,128]{2,1,0:T(8,128)}), f32[16,40,128]{2,1,0:T(8,128)S(1)}, u32[]{:S(2)}, u32[]{:S(2)}) async-start(f32[16,40,128]{2,1,0:T(8,128)} %bitcast.80), calls=%async_computation | async-start | bytes 655360 | tf_op jit(solution)/shard_map/all_to_all | solution.py:63
  14.7 1.3 %copy.25 = bf16[1024,512]{0,1:T(8,128)(2,1)} copy(bf16[1024,512]{1,0:T(8,128)(2,1)S(1)} %copy-done) | data formatting | bytes 2097152 | tf_op jit(solution)/shard_map/reshape | solution.py:105
  16.0 0.9 %fusion.3 = bf16[1024,512]{1,0:T(8,128)(2,1)S(1)} fusion(bf16[1024,512]{1,0:T(8,128)(2,1)S(1)} %copy-done.2), kind=kLoop, calls=%fused_computation.11 | loop fusion | flops 3145728 | bytes 2097152 | tf_op jit(solution)/shard_map/convert_element_type | solution.py:12
  16.9 1.6 %fusion = pred[1024,1024]{1,0:T(8,128)(4,1)} fusion(s32[1024]{0:T(1024)S(1)} %copy-done.3), kind=kLoop, calls=%fused_computation.8 | loop fusion | flops 3145728 | bytes 1052672 | tf_op jit(solution)/shard_map/and | solution.py:110
  18.5 9.2 %all-to-all-done = f32[16,40,128]{2,1,0:T(8,128)S(1)} async-done(((f32[16,40,128]{2,1,0:T(8,128)}), f32[16,40,128]{2,1,0:T(8,128)S(1)}, u32[]{:S(2)}, u32[]{:S(2)}) %all-to-all-start) | async-done | bytes 327712 | tf_op jit(solution)/shard_map/all_to_all | solution.py:63
  28.0 1.2 %select_reduce_fusion = f32[16,32,128]{2,1,0:T(8,128)} fusion(f32[16,32,128]{2,1,0:T(8,128)S(1)} %slice.26, pred[16,16]{1,0:T(8,128)(4,1)S(1)} %fusion.42), kind=kLoop, calls=%fused_computation.6 | loop fusion | flops 2031616 | bytes 524544 | tf_op jit(solution)/shard_map/reduce_sum | solution.py:69
  29.3 3.4 %all-to-all-start.1 = ((f32[16,32,128]{2,1,0:T(8,128)}), f32[16,32,128]{2,1,0:T(8,128)S(1)}, u32[]{:S(2)}, u32[]{:S(2)}) async-start(f32[16,32,128]{2,1,0:T(8,128)} %select_reduce_fusion), calls=%async_computation.1 | async-start | bytes 524288 | tf_op jit(solution)/shard_map/all_to_all | solution.py:70
  32.7 7.0 %fusion.7 = f32[4,1024,128]{1,2,0:T(8,128)S(1)} fusion(bf16[1024,4,128]{0,2,1:T(8,128)(2,1)} %bitcast.81, pred[1024,1024]{1,0:T(8,128)(4,1)} %fusion, bf16[1024,512]{1,0:T(8,128)(2,1)S(1)} %fusion.3, bf16[1024,512]{1,0:T(8,128)(2,1)} %key_ref.1), kind=kOutput, calls=%fused_computation.18 | convolution fusion | flops 2159017984 | bytes 6291456 | tf_op jit(solution)/shard_map/hts,she->the/dot_general | solution.py:115
  39.7 0.5 slice.18
  40.2 0.6 compare_convert_fusion
  40.9 3.0 %all-to-all-done.1 = f32[16,32,128]{2,1,0:T(8,128)S(1)} async-done(((f32[16,32,128]{2,1,0:T(8,128)}), f32[16,32,128]{2,1,0:T(8,128)S(1)}, u32[]{:S(2)}, u32[]{:S(2)}) %all-to-all-start.1) | async-done | bytes 262176 | tf_op jit(solution)/shard_map/all_to_all | solution.py:70
  44.4 0.6 multiply_reduce_fusion
  45.4 1.4 %collective-permute-start = (bf16[1024,256]{0,1:T(8,128)(2,1)S(1)}, bf16[1024,256]{0,1:T(8,128)(2,1)S(1)}, u32[]{:S(2)}, u32[]{:S(2)}) collective-permute-start(bf16[1024,256]{0,1:T(8,128)(2,1)S(1)} %get-tuple-element.14), channel_id=1, source_target_pairs={{0,1},{1,2},{2,3},{3,0},{4,5},{5,6},{6,7},{7,4},{8,9},{9,10},{10,1... | collective-permute-start | bytes 1572872 | tf_op jit(solution)/shard_map/ppermute | solution.py:88
  46.8 1.5 %collective-permute-start.1 = (bf16[1024,256]{0,1:T(8,128)(2,1)S(1)}, bf16[1024,256]{0,1:T(8,128)(2,1)S(1)}, u32[]{:S(2)}, u32[]{:S(2)}) collective-permute-start(bf16[1024,256]{0,1:T(8,128)(2,1)S(1)} %get-tuple-element.13), channel_id=1, source_target_pairs={{0,3},{1,0},{2,1},{3,2},{4,7},{5,4},{6,5},{7,6},{8,11},{9,8},{10,9... | collective-permute-start | bytes 1572872 | tf_op jit(solution)/shard_map/ppermute | solution.py:89
  48.3 1.7 %dynamic-slice_bitcast_fusion.1 = (bf16[256,1024]{1,0:T(8,128)(2,1)S(1)}, bf16[256,1024]{1,0:T(8,128)(2,1)S(1)}, bf16[256,1024]{1,0:T(8,128)(2,1)S(1)}, bf16[256,1024]{1,0:T(8,128)(2,1)S(1)}) fusion(bf16[4,2,256,1024]{3,2,1,0:T(8,128)(2,1)} %bitcast.76, s32[]{:T(128)S(6)} %select_n.47, s32[]{:T(128)S(6)} %select_n.48, s32[]{:T(128)S(6)} %select_n.46), kind=kLoop, calls=%fused_computation.47 | loop fusion | bytes 4194316 | tf_op jit(solution)/shard_map/squeeze | solution.py:82
  50.0 10.5 %collective-permute-done = bf16[1024,256]{0,1:T(8,128)(2,1)S(1)} collective-permute-done((bf16[1024,256]{0,1:T(8,128)(2,1)S(1)}, bf16[1024,256]{0,1:T(8,128)(2,1)S(1)}, u32[]{:S(2)}, u32[]{:S(2)}) %collective-permute-start) | collective-permute-done | bytes 524320 | tf_op jit(solution)/shard_map/ppermute | solution.py:88
  60.7 2.9 %collective-permute-start.3 = (bf16[1024,512]{0,1:T(8,128)(2,1)S(1)}, bf16[1024,512]{0,1:T(8,128)(2,1)S(1)}, u32[]{:S(2)}, u32[]{:S(2)}) collective-permute-start(bf16[1024,512]{0,1:T(8,128)(2,1)S(1)} %pad_maximum_fusion.1), channel_id=1, source_target_pairs={{0,3},{1,0},{2,1},{3,2},{4,7},{5,4},{6,5},{7,6},{8,11},{9,8},{10,9... | collective-permute-start | bytes 3145736 | tf_op jit(solution)/shard_map/ppermute | solution.py:91
  63.6 1.3 %fusion.28 = f32[1024,1024]{1,0:T(8,128)S(1)} fusion(bf16[1024,512]{0,1:T(8,128)(2,1)S(1)} %bitcast.75, bf16[4,512,1024]{2,1,0:T(8,128)(2,1)S(1)} %bitcast.77, s32[]{:T(128)S(6)} %select_n.45), kind=kOutput, calls=%fused_computation.36 | convolution fusion | flops 1073741824 | bytes 6291460 | tf_op jit(solution)/shard_map/dot_general | solution.py:85
  64.9 0.7 fusion.35
  65.7 0.7 fusion.37
  66.4 19.5 %collective-permute-done.2 = bf16[1024,512]{0,1:T(8,128)(2,1)S(1)} collective-permute-done((bf16[1024,512]{0,1:T(8,128)(2,1)S(1)}, bf16[1024,512]{0,1:T(8,128)(2,1)S(1)}, u32[]{:S(2)}, u32[]{:S(2)}) %collective-permute-start.2) | collective-permute-done | bytes 1048608 | tf_op jit(solution)/shard_map/ppermute | solution.py:90
  85.9 1.3 %fusion.18 = f32[1024,1024]{1,0:T(8,128)S(1)} fusion(bf16[1024,512]{0,1:T(8,128)(2,1)S(1)} %collective-permute-done.2, bf16[256,1024]{1,0:T(8,128)(2,1)S(1)} %get-tuple-element.11, bf16[256,1024]{1,0:T(8,128)(2,1)S(1)} %get-tuple-element.12), kind=kOutput, calls=%fused_computation.27 | convolution fusion | flops 1075838976 | bytes 6291456 | tf_op jit(solution)/shard_map/dot_general | solution.py:85
  87.2 3.3 %add_convert_fusion = bf16[1024,1024]{1,0:T(8,128)(2,1)} fusion(f32[1024,1024]{1,0:T(8,128)S(1)} %fusion.18, f32[1024,1024]{1,0:T(8,128)S(1)} %fusion.35, f32[1024,1024]{1,0:T(8,128)S(1)} %fusion.28, f32[1024,1024]{1,0:T(8,128)S(1)} %fusion.37, bf16[1024,512]{0,1:T(8,128)(2,1)S(1)} %collective-permute-done.3, bf16[256,1024]{1,0:T(8,128)(2,1)S(1)} %get-tuple-element.10, ...), kind=kOutput, calls=%fused_computation.5 | convolution fusion | flops 1081081856 | bytes 20971520 | tf_op jit(solution)/shard_map/dot_general | solution.py:85
  (23 shorter events, 1.4 us)
Async XLA Ops:
  0.0 14.7 %copy-start = (bf16[1024,512]{1,0:T(8,128)(2,1)S(1)}, bf16[1024,512]{1,0:T(8,128)(2,1)}, u32[]{:S(2)}) copy-start(bf16[1024,512]{1,0:T(8,128)(2,1)} %value_ref.1) | copy-start | bytes 3145732
  0.0 16.0 %copy-start.2 = (bf16[1024,512]{1,0:T(8,128)(2,1)S(1)}, bf16[1024,512]{1,0:T(8,128)(2,1)}, u32[]{:S(2)}) copy-start(bf16[1024,512]{1,0:T(8,128)(2,1)} %param.6) | copy-start | bytes 3145732
  4.7 23.1 %all-to-all-start = ((f32[16,40,128]{2,1,0:T(8,128)}), f32[16,40,128]{2,1,0:T(8,128)S(1)}, u32[]{:S(2)}, u32[]{:S(2)}) async-start(f32[16,40,128]{2,1,0:T(8,128)} %bitcast.80), calls=%async_computation | async-start | bytes 655360 | tf_op jit(solution)/shard_map/all_to_all | solution.py:63
  14.7 2.3 %copy-start.3 = (s32[1024]{0:T(1024)S(1)}, s32[1024]{0:T(1024)}, u32[]{:S(2)}) copy-start(s32[1024]{0:T(1024)} %param.9) | copy-start | bytes 12292
  29.3 14.6 %all-to-all-start.1 = ((f32[16,32,128]{2,1,0:T(8,128)}), f32[16,32,128]{2,1,0:T(8,128)S(1)}, u32[]{:S(2)}, u32[]{:S(2)}) async-start(f32[16,32,128]{2,1,0:T(8,128)} %select_reduce_fusion), calls=%async_computation.1 | async-start | bytes 524288 | tf_op jit(solution)/shard_map/all_to_all | solution.py:70
  44.4 0.7 copy-start.4
  45.4 15.1 %collective-permute-start = (bf16[1024,256]{0,1:T(8,128)(2,1)S(1)}, bf16[1024,256]{0,1:T(8,128)(2,1)S(1)}, u32[]{:S(2)}, u32[]{:S(2)}) collective-permute-start(bf16[1024,256]{0,1:T(8,128)(2,1)S(1)} %get-tuple-element.14), channel_id=1, source_target_pairs={{0,1},{1,2},{2,3},{3,0},{4,5},{5,6},{6,7},{7,4},{8,9},{9,10},{10,1... | collective-permute-start | bytes 1572872 | tf_op jit(solution)/shard_map/ppermute | solution.py:88
  46.8 13.9 %collective-permute-start.1 = (bf16[1024,256]{0,1:T(8,128)(2,1)S(1)}, bf16[1024,256]{0,1:T(8,128)(2,1)S(1)}, u32[]{:S(2)}, u32[]{:S(2)}) collective-permute-start(bf16[1024,256]{0,1:T(8,128)(2,1)S(1)} %get-tuple-element.13), channel_id=1, source_target_pairs={{0,3},{1,0},{2,1},{3,2},{4,7},{5,4},{6,5},{7,6},{8,11},{9,8},{10,9... | collective-permute-start | bytes 1572872 | tf_op jit(solution)/shard_map/ppermute | solution.py:89
  50.0 13.6 %copy-start.1 = (bf16[2048,1024]{1,0:T(8,128)(2,1)S(1)}, bf16[2048,1024]{1,0:T(8,128)(2,1)}, u32[]{:S(2)}) copy-start(bf16[2048,1024]{1,0:T(8,128)(2,1)} %param.11) | copy-start | bytes 12582916
  60.5 25.4 %collective-permute-start.2 = (bf16[1024,512]{0,1:T(8,128)(2,1)S(1)}, bf16[1024,512]{0,1:T(8,128)(2,1)S(1)}, u32[]{:S(2)}, u32[]{:S(2)}) collective-permute-start(bf16[1024,512]{0,1:T(8,128)(2,1)S(1)} %pad_maximum_fusion), channel_id=1, source_target_pairs={{0,1},{1,2},{2,3},{3,0},{4,5},{5,6},{6,7},{7,4},{8,9},{9,10},{10,1... | collective-permute-start | bytes 3145736 | tf_op jit(solution)/shard_map/ppermute | solution.py:90
  60.7 26.5 %collective-permute-start.3 = (bf16[1024,512]{0,1:T(8,128)(2,1)S(1)}, bf16[1024,512]{0,1:T(8,128)(2,1)S(1)}, u32[]{:S(2)}, u32[]{:S(2)}) collective-permute-start(bf16[1024,512]{0,1:T(8,128)(2,1)S(1)} %pad_maximum_fusion.1), channel_id=1, source_target_pairs={{0,3},{1,0},{2,1},{3,2},{4,7},{5,4},{6,5},{7,6},{8,11},{9,8},{10,9... | collective-permute-start | bytes 3145736 | tf_op jit(solution)/shard_map/ppermute | solution.py:91

commit v17 on v15

--- a/solution.py
+++ b/solution.py
@@ -21,7 +21,7 @@
     first = segs[:1, :1]
     final_from = jnp.sum((segs != last).astype(jnp.int32))
     rows_at = lax.broadcasted_iota(jnp.int32, (rows, 1), 0)
-    in_final = (rows_at >= final_from).astype(jnp.float32)
+    in_final = rows_at >= final_from
     seg_rows = jnp.where(
         lax.broadcasted_iota(jnp.int32, (8, HEAD), 0) == 0,
         jnp.broadcast_to(last.astype(jnp.float32), (8, HEAD)),
@@ -31,7 +31,7 @@
         cols = slice(h * HEAD, (h + 1) * HEAD)
         raw = key_ref[:, cols].astype(jnp.float32)
         feat = jnp.where(raw > 0, raw + 1.0, jnp.exp(jnp.minimum(raw, 0.0))).astype(jnp.bfloat16)
-        masked = (feat.astype(jnp.float32) * in_final).astype(jnp.bfloat16)
+        masked = jnp.where(in_final, feat, jnp.zeros_like(feat))
         sums = lax.dot_general(
             value_ref[:, cols], masked, (((0,), (0,)), ((), ())),
             preferred_element_type=jnp.float32,

time: 89.9 us -> 89.8 us (level)
  no operation moved by 1% of the time
where the time goes in v17:
time: 89.8 us; the launch traced here: 89.5 us
  waiting for transfers between devices  42.4 us (47%)
  starting transfers between devices  19.3 us (21%)
  matrix products  15.9 us (18%)
  local copies, waits for them, and re-layouts  4.64 us (5%)
  other arithmetic  3.58 us (4%)
  Pallas kernels  3.57 us (4%)
    ppermute x1, waiting for transfers between devices, project_gathered(): lax.ppermute(jnp.concatenate([second, left_first], axis=1), axis, ahead)  19.7 us
    ppermute x1, waiting for transfers between devices, project_gathered(): left_first = lax.ppermute(first, axis, ahead)  10.5 us
    all_to_all x1, starting transfers between devices, carried_in(): pieces = lax.all_to_all(sent, axis, 0, 0, tiled=True)  9.99 us
    all_to_all x1, waiting for transfers between devices, carried_in(): pieces = lax.all_to_all(sent, axis, 0, 0, tiled=True)  9.23 us
    dot_general x5, matrix products, dot(): return jnp.dot(block, weight, preferred_element_type=jnp.float32)  7.39 us
    dot_general x1, matrix products, per_device(): jnp.einsum('hts,she->the', weights, value_heads, preferred_element_type=j...  7 us
    pallas_call x1, Pallas kernels, scan_payload(): pl.pallas_call(_payload_kernel, out_shape=jax.ShapeDtypeStruct((count * 4...  3.57 us
    all_to_all x1, starting transfers between devices, carried_in(): return lax.all_to_all(carry, axis, 0, 0, tiled=True).reshape(shape)  3.43 us
  transfers between devices with their start and end apart: 6, of which 4 were waited for; matrix products, arithmetic and copies ran while one was open for 20% of the time, Pallas kernels for 0%

profile of v17, /device:TPU:1, one launch (start us, length us, event | category | flops | bytes accessed | tf_op | source)
XLA Modules:
  0.0 89.5 jit_solution(5459248170284557203)
XLA Ops:
  0.0 3.6 %shard_map.64 = f32[640,128]{1,0:T(8,128)} custom-call(bf16[1024,512]{1,0:T(8,128)(2,1)} %key_ref.1, bf16[1024,512]{1,0:T(8,128)(2,1)} %value_ref.1, s32[8,128]{1,0:T(8,128)} %bitcast.100), custom_call_target="tpu_custom_call" | custom-call | tf_op jit(solution)/shard_map/pallas_call | solution.py:48
  3.6 10.0 %all-to-all-start = ((f32[16,40,128]{2,1,0:T(8,128)}), f32[16,40,128]{2,1,0:T(8,128)S(1)}, u32[]{:S(2)}, u32[]{:S(2)}) async-start(f32[16,40,128]{2,1,0:T(8,128)} %bitcast.96), calls=%async_computation | async-start | bytes 655360 | tf_op jit(solution)/shard_map/all_to_all | solution.py:60
  13.6 1.3 %copy.32 = bf16[1024,512]{0,1:T(8,128)(2,1)} copy(bf16[1024,512]{1,0:T(8,128)(2,1)S(1)} %copy-done) | data formatting | bytes 2097152 | tf_op jit(solution)/shard_map/reshape | solution.py:107
  14.9 0.9 %fusion.3 = bf16[1024,512]{1,0:T(8,128)(2,1)S(1)} fusion(bf16[1024,512]{1,0:T(8,128)(2,1)S(1)} %copy-done.2), kind=kLoop, calls=%fused_computation.10 | loop fusion | flops 3145728 | bytes 2097152 | tf_op jit(solution)/shard_map/convert_element_type | solution.py:12
  15.8 1.6 %fusion = pred[1024,1024]{1,0:T(8,128)(4,1)} fusion(s32[1024]{0:T(1024)S(1)} %copy-done.3), kind=kLoop, calls=%fused_computation.7 | loop fusion | flops 3145728 | bytes 1052672 | tf_op jit(solution)/shard_map/and | solution.py:112
  17.4 9.2 %all-to-all-done = f32[16,40,128]{2,1,0:T(8,128)S(1)} async-done(((f32[16,40,128]{2,1,0:T(8,128)}), f32[16,40,128]{2,1,0:T(8,128)S(1)}, u32[]{:S(2)}, u32[]{:S(2)}) %all-to-all-start) | async-done | bytes 327712 | tf_op jit(solution)/shard_map/all_to_all | solution.py:60
  27.3 0.8 copy.29
  28.1 3.4 %all-to-all-start.1 = ((f32[16,32,128]{2,1,0:T(8,128)}), f32[16,32,128]{2,1,0:T(8,128)S(1)}, u32[]{:S(2)}, u32[]{:S(2)}) async-start(f32[16,32,128]{2,1,0:T(8,128)} %copy.29), calls=%async_computation.1 | async-start | bytes 524288 | tf_op jit(solution)/shard_map/all_to_all | solution.py:72
  31.5 7.0 %fusion.7 = f32[4,1024,128]{1,2,0:T(8,128)S(1)} fusion(bf16[1024,4,128]{0,2,1:T(8,128)(2,1)} %bitcast.97, pred[1024,1024]{1,0:T(8,128)(4,1)} %fusion, bf16[1024,512]{1,0:T(8,128)(2,1)S(1)} %fusion.3, bf16[1024,512]{1,0:T(8,128)(2,1)} %key_ref.1), kind=kOutput, calls=%fused_computation.17 | convolution fusion | flops 2159017984 | bytes 6291456 | tf_op jit(solution)/shard_map/hts,she->the/dot_general | solution.py:117
  38.5 0.5 slice.18
  39.0 0.6 compare_convert_fusion
  39.7 3.0 %all-to-all-done.1 = f32[16,32,128]{2,1,0:T(8,128)S(1)} async-done(((f32[16,32,128]{2,1,0:T(8,128)}), f32[16,32,128]{2,1,0:T(8,128)S(1)}, u32[]{:S(2)}, u32[]{:S(2)}) %all-to-all-start.1) | async-done | bytes 262176 | tf_op jit(solution)/shard_map/all_to_all | solution.py:72
  43.2 0.6 multiply_reduce_fusion
  44.2 1.4 %collective-permute-start = (bf16[1024,256]{0,1:T(8,128)(2,1)S(1)}, bf16[1024,256]{0,1:T(8,128)(2,1)S(1)}, u32[]{:S(2)}, u32[]{:S(2)}) collective-permute-start(bf16[1024,256]{0,1:T(8,128)(2,1)S(1)} %get-tuple-element.14), channel_id=1, source_target_pairs={{0,1},{1,2},{2,3},{3,0},{4,5},{5,6},{6,7},{7,4},{8,9},{9,10},{10,1... | collective-permute-start | bytes 1572872 | tf_op jit(solution)/shard_map/ppermute | solution.py:90
  45.5 1.5 %collective-permute-start.1 = (bf16[1024,256]{0,1:T(8,128)(2,1)S(1)}, bf16[1024,256]{0,1:T(8,128)(2,1)S(1)}, u32[]{:S(2)}, u32[]{:S(2)}) collective-permute-start(bf16[1024,256]{0,1:T(8,128)(2,1)S(1)} %get-tuple-element.13), channel_id=1, source_target_pairs={{0,3},{1,0},{2,1},{3,2},{4,7},{5,4},{6,5},{7,6},{8,11},{9,8},{10,9... | collective-permute-start | bytes 1572872 | tf_op jit(solution)/shard_map/ppermute | solution.py:91
  47.1 1.7 %dynamic-slice_bitcast_fusion.1 = (bf16[256,1024]{1,0:T(8,128)(2,1)S(1)}, bf16[256,1024]{1,0:T(8,128)(2,1)S(1)}, bf16[256,1024]{1,0:T(8,128)(2,1)S(1)}, bf16[256,1024]{1,0:T(8,128)(2,1)S(1)}) fusion(bf16[4,2,256,1024]{3,2,1,0:T(8,128)(2,1)} %bitcast.92, s32[]{:T(128)S(6)} %select_n.42, s32[]{:T(128)S(6)} %select_n.43, s32[]{:T(128)S(6)} %select_n.41), kind=kLoop, calls=%fused_computation.46 | loop fusion | bytes 4194316 | tf_op jit(solution)/shard_map/squeeze | solution.py:84
  48.8 10.5 %collective-permute-done = bf16[1024,256]{0,1:T(8,128)(2,1)S(1)} collective-permute-done((bf16[1024,256]{0,1:T(8,128)(2,1)S(1)}, bf16[1024,256]{0,1:T(8,128)(2,1)S(1)}, u32[]{:S(2)}, u32[]{:S(2)}) %collective-permute-start) | collective-permute-done | bytes 524320 | tf_op jit(solution)/shard_map/ppermute | solution.py:90
  59.7 2.7 %collective-permute-start.3 = (bf16[1024,512]{0,1:T(8,128)(2,1)S(1)}, bf16[1024,512]{0,1:T(8,128)(2,1)S(1)}, u32[]{:S(2)}, u32[]{:S(2)}) collective-permute-start(bf16[1024,512]{0,1:T(8,128)(2,1)S(1)} %pad_maximum_fusion.1), channel_id=1, source_target_pairs={{0,3},{1,0},{2,1},{3,2},{4,7},{5,4},{6,5},{7,6},{8,11},{9,8},{10,9... | collective-permute-start | bytes 3145736 | tf_op jit(solution)/shard_map/ppermute | solution.py:93
  62.4 1.3 %fusion.28 = f32[1024,1024]{1,0:T(8,128)S(1)} fusion(bf16[1024,512]{0,1:T(8,128)(2,1)S(1)} %bitcast.91, bf16[4,512,1024]{2,1,0:T(8,128)(2,1)S(1)} %bitcast.93, s32[]{:T(128)S(6)} %select_n.40), kind=kOutput, calls=%fused_computation.35 | convolution fusion | flops 1073741824 | bytes 6291460 | tf_op jit(solution)/shard_map/dot_general | solution.py:87
  63.7 0.7 fusion.35
  64.4 0.7 fusion.37
  65.2 19.7 %collective-permute-done.2 = bf16[1024,512]{0,1:T(8,128)(2,1)S(1)} collective-permute-done((bf16[1024,512]{0,1:T(8,128)(2,1)S(1)}, bf16[1024,512]{0,1:T(8,128)(2,1)S(1)}, u32[]{:S(2)}, u32[]{:S(2)}) %collective-permute-start.2) | collective-permute-done | bytes 1048608 | tf_op jit(solution)/shard_map/ppermute | solution.py:92
  84.9 1.3 %fusion.18 = f32[1024,1024]{1,0:T(8,128)S(1)} fusion(bf16[1024,512]{0,1:T(8,128)(2,1)S(1)} %collective-permute-done.2, bf16[256,1024]{1,0:T(8,128)(2,1)S(1)} %get-tuple-element.11, bf16[256,1024]{1,0:T(8,128)(2,1)S(1)} %get-tuple-element.12), kind=kOutput, calls=%fused_computation.26 | convolution fusion | flops 1075838976 | bytes 6291456 | tf_op jit(solution)/shard_map/dot_general | solution.py:87
  86.2 3.3 %add_convert_fusion = bf16[1024,1024]{1,0:T(8,128)(2,1)} fusion(f32[1024,1024]{1,0:T(8,128)S(1)} %fusion.18, f32[1024,1024]{1,0:T(8,128)S(1)} %fusion.35, f32[1024,1024]{1,0:T(8,128)S(1)} %fusion.28, f32[1024,1024]{1,0:T(8,128)S(1)} %fusion.37, bf16[1024,512]{0,1:T(8,128)(2,1)S(1)} %collective-permute-done.3, bf16[256,1024]{1,0:T(8,128)(2,1)S(1)} %get-tuple-element.10, ...), kind=kOutput, calls=%fused_computation.5 | convolution fusion | flops 1081081856 | bytes 20971520 | tf_op jit(solution)/shard_map/dot_general | solution.py:87
  (23 shorter events, 1.9 us)
Async XLA Ops:
  0.0 13.6 %copy-start = (bf16[1024,512]{1,0:T(8,128)(2,1)S(1)}, bf16[1024,512]{1,0:T(8,128)(2,1)}, u32[]{:S(2)}) copy-start(bf16[1024,512]{1,0:T(8,128)(2,1)} %value_ref.1) | copy-start | bytes 3145732
  0.0 14.9 %copy-start.2 = (bf16[1024,512]{1,0:T(8,128)(2,1)S(1)}, bf16[1024,512]{1,0:T(8,128)(2,1)}, u32[]{:S(2)}) copy-start(bf16[1024,512]{1,0:T(8,128)(2,1)} %param.6) | copy-start | bytes 3145732
  3.6 23.1 %all-to-all-start = ((f32[16,40,128]{2,1,0:T(8,128)}), f32[16,40,128]{2,1,0:T(8,128)S(1)}, u32[]{:S(2)}, u32[]{:S(2)}) async-start(f32[16,40,128]{2,1,0:T(8,128)} %bitcast.96), calls=%async_computation | async-start | bytes 655360 | tf_op jit(solution)/shard_map/all_to_all | solution.py:60
  13.6 2.3 %copy-start.3 = (s32[1024]{0:T(1024)S(1)}, s32[1024]{0:T(1024)}, u32[]{:S(2)}) copy-start(s32[1024]{0:T(1024)} %param.9) | copy-start | bytes 12292
  28.1 14.6 %all-to-all-start.1 = ((f32[16,32,128]{2,1,0:T(8,128)}), f32[16,32,128]{2,1,0:T(8,128)S(1)}, u32[]{:S(2)}, u32[]{:S(2)}) async-start(f32[16,32,128]{2,1,0:T(8,128)} %copy.29), calls=%async_computation.1 | async-start | bytes 524288 | tf_op jit(solution)/shard_map/all_to_all | solution.py:72
  43.1 0.7 copy-start.4
  44.2 15.1 %collective-permute-start = (bf16[1024,256]{0,1:T(8,128)(2,1)S(1)}, bf16[1024,256]{0,1:T(8,128)(2,1)S(1)}, u32[]{:S(2)}, u32[]{:S(2)}) collective-permute-start(bf16[1024,256]{0,1:T(8,128)(2,1)S(1)} %get-tuple-element.14), channel_id=1, source_target_pairs={{0,1},{1,2},{2,3},{3,0},{4,5},{5,6},{6,7},{7,4},{8,9},{9,10},{10,1... | collective-permute-start | bytes 1572872 | tf_op jit(solution)/shard_map/ppermute | solution.py:90
  45.5 14.0 %collective-permute-start.1 = (bf16[1024,256]{0,1:T(8,128)(2,1)S(1)}, bf16[1024,256]{0,1:T(8,128)(2,1)S(1)}, u32[]{:S(2)}, u32[]{:S(2)}) collective-permute-start(bf16[1024,256]{0,1:T(8,128)(2,1)S(1)} %get-tuple-element.13), channel_id=1, source_target_pairs={{0,3},{1,0},{2,1},{3,2},{4,7},{5,4},{6,5},{7,6},{8,11},{9,8},{10,9... | collective-permute-start | bytes 1572872 | tf_op jit(solution)/shard_map/ppermute | solution.py:91
  48.8 13.6 %copy-start.1 = (bf16[2048,1024]{1,0:T(8,128)(2,1)S(1)}, bf16[2048,1024]{1,0:T(8,128)(2,1)}, u32[]{:S(2)}) copy-start(bf16[2048,1024]{1,0:T(8,128)(2,1)} %param.11) | copy-start | bytes 12582916
  59.3 25.6 %collective-permute-start.2 = (bf16[1024,512]{0,1:T(8,128)(2,1)S(1)}, bf16[1024,512]{0,1:T(8,128)(2,1)S(1)}, u32[]{:S(2)}, u32[]{:S(2)}) collective-permute-start(bf16[1024,512]{0,1:T(8,128)(2,1)S(1)} %pad_maximum_fusion), channel_id=1, source_target_pairs={{0,1},{1,2},{2,3},{3,0},{4,5},{5,6},{6,7},{7,4},{8,9},{9,10},{10,1... | collective-permute-start | bytes 3145736 | tf_op jit(solution)/shard_map/ppermute | solution.py:92
  59.7 26.5 %collective-permute-start.3 = (bf16[1024,512]{0,1:T(8,128)(2,1)S(1)}, bf16[1024,512]{0,1:T(8,128)(2,1)S(1)}, u32[]{:S(2)}, u32[]{:S(2)}) collective-permute-start(bf16[1024,512]{0,1:T(8,128)(2,1)S(1)} %pad_maximum_fusion.1), channel_id=1, source_target_pairs={{0,3},{1,0},{2,1},{3,2},{4,7},{5,4},{6,5},{7,6},{8,11},{9,8},{10,9... | collective-permute-start | bytes 3145736 | tf_op jit(solution)/shard_map/ppermute | solution.py:93

commit v18 on v12

--- a/solution.py
+++ b/solution.py
@@ -90,7 +90,8 @@
     right_weight = jnp.concatenate([rows_of(1, 0), rows_of(2, 1)], axis=0)
     total = dot(hidden, out_weight.reshape(count, width, -1)[mine])
     total = total + dot(left_first, rows_of(-1, 0)) + dot(right_second, rows_of(1, 1))
-    return total + dot(from_left, left_weight) + dot(from_right, right_weight)
+    far_weight = jnp.concatenate([left_weight, right_weight], axis=0)
+    return total + dot(jnp.concatenate([from_left, from_right], axis=1), far_weight)
 
 
 def per_device(queries, keys, values, segment_ids, norm_gain, out_weight):

time: 90 us -> 93.1 us (1.034); the launches traced: 89.7 us -> 91.7 us
  matrix products: 15.4 us -> 19.8 us
  waiting for transfers between devices: 42.4 us -> 38.9 us
  other arithmetic: 4.91 us -> 6.87 us
    ppermute x1, waiting for transfers between devices: 19.7 us -> 14.5 us  [project_gathered(): lax.ppermute(jnp.concatenate([second, left_first], axis=1), axis, ahead)]
    dot_general x5 -> x4, matrix products: 7.39 us -> 11.7 us  [dot(): return jnp.dot(block, weight, preferred_element_type=jnp.float32)]
    ppermute x1, waiting for transfers between devices: 10.5 us -> 12.2 us  [project_gathered(): left_first = lax.ppermute(first, axis, ahead)]
    concatenate x1, other arithmetic: 0.07 us -> 1.05 us  [project_gathered(): jnp.concatenate([second, left_first], axis=1)]
    concatenate x1, other arithmetic: 0.07 us -> 1.04 us  [project_gathered(): jnp.concatenate([first, right_second], axis=1)]
  transfers between devices with their start and end apart: 6 -> 6, of which waited for: 4 -> 4; matrix products, arithmetic and copies ran while one was open for 20% -> 23% of each run, Pallas kernels for 0% -> 0%
where the time goes in v18:
time: 93.1 us; the launch traced here: 91.7 us
  waiting for transfers between devices  38.9 us (42%)
  matrix products  19.8 us (21%)
  starting transfers between devices  19 us (20%)
  other arithmetic  6.87 us (7%)
  Pallas kernels  3.66 us (4%)
  local copies, waits for them, and re-layouts  3.38 us (4%)
    ppermute x1, waiting for transfers between devices, project_gathered(): lax.ppermute(jnp.concatenate([second, left_first], axis=1), axis, ahead)  14.5 us
    ppermute x1, waiting for transfers between devices, project_gathered(): left_first = lax.ppermute(first, axis, ahead)  12.2 us
    dot_general x4, matrix products, dot(): return jnp.dot(block, weight, preferred_element_type=jnp.float32)  11.7 us
    all_to_all x1, starting transfers between devices, carried_in(): pieces = lax.all_to_all(sent, axis, 0, 0, tiled=True)  9.98 us
    all_to_all x1, waiting for transfers between devices, carried_in(): pieces = lax.all_to_all(sent, axis, 0, 0, tiled=True)  9.22 us
    dot_general x1, matrix products, per_device(): jnp.einsum('hts,she->the', weights, value_heads, preferred_element_type=j...  7 us
    pallas_call x1, Pallas kernels, scan_payload(): pl.pallas_call(_payload_kernel, out_shape=jax.ShapeDtypeStruct((count * 4...  3.66 us
    all_to_all x1, starting transfers between devices, carried_in(): return lax.all_to_all(carry, axis, 0, 0, tiled=True).reshape(shape)  3.43 us
  transfers between devices with their start and end apart: 6, of which 4 were waited for; matrix products, arithmetic and copies ran while one was open for 23% of the time, Pallas kernels for 0%

profile of v18, /device:TPU:1, one launch (start us, length us, event | category | flops | bytes accessed | tf_op | source)
XLA Modules:
  0.0 91.7 jit_solution(14823255512928524825)
XLA Ops:
  0.0 3.7 %shard_map.64 = f32[640,128]{1,0:T(8,128)} custom-call(bf16[1024,512]{1,0:T(8,128)(2,1)} %key_ref.1, bf16[1024,512]{1,0:T(8,128)(2,1)} %value_ref.1, s32[8,128]{1,0:T(8,128)} %bitcast.81), custom_call_target="tpu_custom_call" | custom-call | tf_op jit(solution)/shard_map/pallas_call | solution.py:48
  3.7 10.0 %all-to-all-start = ((f32[16,40,128]{2,1,0:T(8,128)}), f32[16,40,128]{2,1,0:T(8,128)S(1)}, u32[]{:S(2)}, u32[]{:S(2)}) async-start(f32[16,40,128]{2,1,0:T(8,128)} %bitcast.78), calls=%async_computation | async-start | bytes 655360 | tf_op jit(solution)/shard_map/all_to_all | solution.py:60
  13.7 1.3 %copy.25 = bf16[1024,512]{0,1:T(8,128)(2,1)} copy(bf16[1024,512]{1,0:T(8,128)(2,1)S(1)} %copy-done) | data formatting | bytes 2097152 | tf_op jit(solution)/shard_map/reshape | solution.py:103
  15.0 0.9 %fusion.3 = bf16[1024,512]{1,0:T(8,128)(2,1)S(1)} fusion(bf16[1024,512]{1,0:T(8,128)(2,1)S(1)} %copy-done.2), kind=kLoop, calls=%fused_computation.11 | loop fusion | flops 3145728 | bytes 2097152 | tf_op jit(solution)/shard_map/convert_element_type | solution.py:12
  15.9 1.6 %fusion = pred[1024,1024]{1,0:T(8,128)(4,1)} fusion(s32[1024]{0:T(1024)S(1)} %copy-done.5), kind=kLoop, calls=%fused_computation.8 | loop fusion | flops 3145728 | bytes 1052672 | tf_op jit(solution)/shard_map/and | solution.py:108
  17.5 9.2 %all-to-all-done = f32[16,40,128]{2,1,0:T(8,128)S(1)} async-done(((f32[16,40,128]{2,1,0:T(8,128)}), f32[16,40,128]{2,1,0:T(8,128)S(1)}, u32[]{:S(2)}, u32[]{:S(2)}) %all-to-all-start) | async-done | bytes 327712 | tf_op jit(solution)/shard_map/all_to_all | solution.py:60
  27.0 1.2 %select_reduce_fusion = f32[16,32,128]{2,1,0:T(8,128)} fusion(f32[16,32,128]{2,1,0:T(8,128)S(1)} %slice.26, pred[16,16]{1,0:T(8,128)(4,1)S(1)} %fusion.47), kind=kLoop, calls=%fused_computation.6 | loop fusion | flops 2031616 | bytes 524544 | tf_op jit(solution)/shard_map/reduce_sum | solution.py:66
  28.3 3.4 %all-to-all-start.1 = ((f32[16,32,128]{2,1,0:T(8,128)}), f32[16,32,128]{2,1,0:T(8,128)S(1)}, u32[]{:S(2)}, u32[]{:S(2)}) async-start(f32[16,32,128]{2,1,0:T(8,128)} %select_reduce_fusion), calls=%async_computation.1 | async-start | bytes 524288 | tf_op jit(solution)/shard_map/all_to_all | solution.py:67
  31.7 7.0 %fusion.18 = f32[4,1024,128]{1,2,0:T(8,128)S(1)} fusion(bf16[1024,4,128]{0,2,1:T(8,128)(2,1)} %bitcast.79, pred[1024,1024]{1,0:T(8,128)(4,1)} %fusion, bf16[1024,512]{1,0:T(8,128)(2,1)S(1)} %fusion.3, bf16[1024,512]{1,0:T(8,128)(2,1)} %key_ref.1), kind=kOutput, calls=%fused_computation.29 | convolution fusion | flops 2159017984 | bytes 6291456 | tf_op jit(solution)/shard_map/hts,she->the/dot_general | solution.py:113
  39.2 0.6 compare_convert_fusion
  39.9 3.0 %all-to-all-done.1 = f32[16,32,128]{2,1,0:T(8,128)S(1)} async-done(((f32[16,32,128]{2,1,0:T(8,128)}), f32[16,32,128]{2,1,0:T(8,128)S(1)}, u32[]{:S(2)}, u32[]{:S(2)}) %all-to-all-start.1) | async-done | bytes 262176 | tf_op jit(solution)/shard_map/all_to_all | solution.py:67
  43.4 0.6 multiply_reduce_fusion
  44.4 1.4 %collective-permute-start = (bf16[1024,256]{0,1:T(8,128)(2,1)S(1)}, bf16[1024,256]{0,1:T(8,128)(2,1)S(1)}, u32[]{:S(2)}, u32[]{:S(2)}) collective-permute-start(bf16[1024,256]{0,1:T(8,128)(2,1)S(1)} %get-tuple-element.13), channel_id=1, source_target_pairs={{0,1},{1,2},{2,3},{3,0},{4,5},{5,6},{6,7},{7,4},{8,9},{9,10},{10,1... | collective-permute-start | bytes 1572872 | tf_op jit(solution)/shard_map/ppermute | solution.py:85
  45.7 1.5 %collective-permute-start.1 = (bf16[1024,256]{0,1:T(8,128)(2,1)S(1)}, bf16[1024,256]{0,1:T(8,128)(2,1)S(1)}, u32[]{:S(2)}, u32[]{:S(2)}) collective-permute-start(bf16[1024,256]{0,1:T(8,128)(2,1)S(1)} %get-tuple-element.14), channel_id=1, source_target_pairs={{0,3},{1,0},{2,1},{3,2},{4,7},{5,4},{6,5},{7,6},{8,11},{9,8},{10,9... | collective-permute-start | bytes 1572872 | tf_op jit(solution)/shard_map/ppermute | solution.py:86
  47.3 12.2 %collective-permute-done = bf16[1024,256]{0,1:T(8,128)(2,1)S(1)} collective-permute-done((bf16[1024,256]{0,1:T(8,128)(2,1)S(1)}, bf16[1024,256]{0,1:T(8,128)(2,1)S(1)}, u32[]{:S(2)}, u32[]{:S(2)}) %collective-permute-start) | collective-permute-done | bytes 524320 | tf_op jit(solution)/shard_map/ppermute | solution.py:85
  59.4 1.1 %pad_maximum_fusion = bf16[1024,512]{0,1:T(8,128)(2,1)} fusion(bf16[1024,256]{0,1:T(8,128)(2,1)S(1)} %collective-permute-done, bf16[1024,256]{0,1:T(8,128)(2,1)S(1)} %get-tuple-element.14), kind=kLoop, calls=%fused_computation.37 | loop fusion | flops 2097152 | bytes 2097152 | tf_op jit(solution)/shard_map/concatenate | solution.py:87
  60.5 1.0 %pad_maximum_fusion.1 = bf16[1024,512]{0,1:T(8,128)(2,1)} fusion(bf16[1024,256]{0,1:T(8,128)(2,1)S(1)} %collective-permute-done.1, bf16[1024,256]{0,1:T(8,128)(2,1)S(1)} %get-tuple-element.13), kind=kLoop, calls=%fused_computation.38 | loop fusion | flops 2097152 | bytes 2097152 | tf_op jit(solution)/shard_map/concatenate | solution.py:88
  61.5 2.7 %collective-permute-start.3 = (bf16[1024,512]{0,1:T(8,128)(2,1)}, bf16[1024,512]{0,1:T(8,128)(2,1)}, u32[]{:S(2)}, u32[]{:S(2)}) collective-permute-start(bf16[1024,512]{0,1:T(8,128)(2,1)} %pad_maximum_fusion.1), channel_id=1, source_target_pairs={{0,3},{1,0},{2,1},{3,2},{4,7},{5,4},{6,5},{7,6},{8,11},{9,8},{10,9... | collective-permute-start | bytes 3145736 | tf_op jit(solution)/shard_map/ppermute | solution.py:88
  64.2 1.2 %dynamic-slice_bitcast_fusion.3 = (bf16[256,1024]{1,0:T(8,128)(2,1)S(1)}, bf16[256,1024]{1,0:T(8,128)(2,1)S(1)}, bf16[256,1024]{1,0:T(8,128)(2,1)}, bf16[256,1024]{1,0:T(8,128)(2,1)}) fusion(bf16[4,2,256,1024]{3,2,1,0:T(8,128)(2,1)S(1)} %bitcast.77, s32[]{:T(128)S(6)} %select_n.46, s32[]{:T(128)S(6)} %select_n.48, s32[]{:T(128)S(6)} %select_n.47), kind=kLoop, calls=%fused_computation.52 | loop fusion | bytes 4194316 | tf_op jit(solution)/shard_map/squeeze | solution.py:79
  65.4 2.5 %fusion.33 = f32[1024,1024]{1,0:T(8,128)S(1)} fusion(bf16[1024,512]{0,1:T(8,128)(2,1)S(1)} %bitcast.73, bf16[4,512,1024]{2,1,0:T(8,128)(2,1)} %bitcast.74, s32[]{:T(128)S(6)} %select_n.45), kind=kOutput, calls=%fused_computation.39 | convolution fusion | flops 1073741824 | bytes 6291460 | tf_op jit(solution)/shard_map/dot_general | solution.py:82
  67.9 1.8 %fusion.40 = f32[1024,1024]{1,0:T(8,128)S(1)} fusion(bf16[1024,256]{0,1:T(8,128)(2,1)S(1)} %collective-permute-done.1, bf16[4,2,256,1024]{3,2,1,0:T(8,128)(2,1)} %bitcast.75, s32[]{:T(128)S(6)} %select_n.47), kind=kOutput, calls=%fused_computation.45 | convolution fusion | flops 536870912 | bytes 5242884 | tf_op jit(solution)/shard_map/dot_general | solution.py:82
  69.8 1.9 %fusion.42 = f32[1024,1024]{1,0:T(8,128)S(1)} fusion(bf16[1024,256]{0,1:T(8,128)(2,1)S(1)} %collective-permute-done, bf16[4,2,256,1024]{3,2,1,0:T(8,128)(2,1)} %bitcast.76, s32[]{:T(128)S(6)} %select_n.46), kind=kOutput, calls=%fused_computation.47 | convolution fusion | flops 536870912 | bytes 5242884 | tf_op jit(solution)/shard_map/dot_general | solution.py:82
  71.6 14.5 %collective-permute-done.2 = bf16[1024,512]{0,1:T(8,128)(2,1)} collective-permute-done((bf16[1024,512]{0,1:T(8,128)(2,1)}, bf16[1024,512]{0,1:T(8,128)(2,1)}, u32[]{:S(2)}, u32[]{:S(2)}) %collective-permute-start.2) | collective-permute-done | bytes 1048608 | tf_op jit(solution)/shard_map/ppermute | solution.py:87
  86.1 5.5 %add_convert_fusion = bf16[1024,1024]{1,0:T(8,128)(2,1)} fusion(f32[1024,1024]{1,0:T(8,128)S(1)} %fusion.40, f32[1024,1024]{1,0:T(8,128)S(1)} %fusion.33, f32[1024,1024]{1,0:T(8,128)S(1)} %fusion.42, bf16[256,1024]{1,0:T(8,128)(2,1)S(1)} %get-tuple-element.10, bf16[256,1024]{1,0:T(8,128)(2,1)S(1)} %copy-done.3, bf16[256,1024]{1,0:T(8,128)(2,1)S(1)} %copy-done.4, ...), kind=kOutput, calls=%fused_computation.5 | convolution fusion | flops 2164260864 | bytes 18874368 | tf_op jit(solution)/shard_map/dot_general | solution.py:82
  (26 shorter events, 1.7 us)
Async XLA Ops:
  0.0 13.6 %copy-start = (bf16[1024,512]{1,0:T(8,128)(2,1)S(1)}, bf16[1024,512]{1,0:T(8,128)(2,1)}, u32[]{:S(2)}) copy-start(bf16[1024,512]{1,0:T(8,128)(2,1)} %value_ref.1) | copy-start | bytes 3145732
  0.0 15.0 %copy-start.2 = (bf16[1024,512]{1,0:T(8,128)(2,1)S(1)}, bf16[1024,512]{1,0:T(8,128)(2,1)}, u32[]{:S(2)}) copy-start(bf16[1024,512]{1,0:T(8,128)(2,1)} %param.6) | copy-start | bytes 3145732
  3.7 23.1 %all-to-all-start = ((f32[16,40,128]{2,1,0:T(8,128)}), f32[16,40,128]{2,1,0:T(8,128)S(1)}, u32[]{:S(2)}, u32[]{:S(2)}) async-start(f32[16,40,128]{2,1,0:T(8,128)} %bitcast.78), calls=%async_computation | async-start | bytes 655360 | tf_op jit(solution)/shard_map/all_to_all | solution.py:60
  13.7 2.3 %copy-start.5 = (s32[1024]{0:T(1024)S(1)}, s32[1024]{0:T(1024)}, u32[]{:S(2)}) copy-start(s32[1024]{0:T(1024)} %param.9) | copy-start | bytes 12292
  28.3 14.6 %all-to-all-start.1 = ((f32[16,32,128]{2,1,0:T(8,128)}), f32[16,32,128]{2,1,0:T(8,128)S(1)}, u32[]{:S(2)}, u32[]{:S(2)}) async-start(f32[16,32,128]{2,1,0:T(8,128)} %select_reduce_fusion), calls=%async_computation.1 | async-start | bytes 524288 | tf_op jit(solution)/shard_map/all_to_all | solution.py:67
  43.3 0.7 copy-start.6
  44.4 15.1 %collective-permute-start = (bf16[1024,256]{0,1:T(8,128)(2,1)S(1)}, bf16[1024,256]{0,1:T(8,128)(2,1)S(1)}, u32[]{:S(2)}, u32[]{:S(2)}) collective-permute-start(bf16[1024,256]{0,1:T(8,128)(2,1)S(1)} %get-tuple-element.13), channel_id=1, source_target_pairs={{0,1},{1,2},{2,3},{3,0},{4,5},{5,6},{6,7},{7,4},{8,9},{9,10},{10,1... | collective-permute-start | bytes 1572872 | tf_op jit(solution)/shard_map/ppermute | solution.py:85
  45.7 14.8 %collective-permute-start.1 = (bf16[1024,256]{0,1:T(8,128)(2,1)S(1)}, bf16[1024,256]{0,1:T(8,128)(2,1)S(1)}, u32[]{:S(2)}, u32[]{:S(2)}) collective-permute-start(bf16[1024,256]{0,1:T(8,128)(2,1)S(1)} %get-tuple-element.14), channel_id=1, source_target_pairs={{0,3},{1,0},{2,1},{3,2},{4,7},{5,4},{6,5},{7,6},{8,11},{9,8},{10,9... | collective-permute-start | bytes 1572872 | tf_op jit(solution)/shard_map/ppermute | solution.py:86
  47.3 16.9 %copy-start.1 = (bf16[2048,1024]{1,0:T(8,128)(2,1)S(1)}, bf16[2048,1024]{1,0:T(8,128)(2,1)}, u32[]{:S(2)}) copy-start(bf16[2048,1024]{1,0:T(8,128)(2,1)} %param.11) | copy-start | bytes 12582916
  60.5 25.6 %collective-permute-start.2 = (bf16[1024,512]{0,1:T(8,128)(2,1)}, bf16[1024,512]{0,1:T(8,128)(2,1)}, u32[]{:S(2)}, u32[]{:S(2)}) collective-permute-start(bf16[1024,512]{0,1:T(8,128)(2,1)} %pad_maximum_fusion), channel_id=1, source_target_pairs={{0,1},{1,2},{2,3},{3,0},{4,5},{5,6},{6,7},{7,4},{8,9},{9,10},{10,1... | collective-permute-start | bytes 3145736 | tf_op jit(solution)/shard_map/ppermute | solution.py:87
  61.5 24.6 %collective-permute-start.3 = (bf16[1024,512]{0,1:T(8,128)(2,1)}, bf16[1024,512]{0,1:T(8,128)(2,1)}, u32[]{:S(2)}, u32[]{:S(2)}) collective-permute-start(bf16[1024,512]{0,1:T(8,128)(2,1)} %pad_maximum_fusion.1), channel_id=1, source_target_pairs={{0,3},{1,0},{2,1},{3,2},{4,7},{5,4},{6,5},{7,6},{8,11},{9,8},{10,9... | collective-permute-start | bytes 3145736 | tf_op jit(solution)/shard_map/ppermute | solution.py:88
  69.7 16.4 %copy-start.3 = (bf16[256,1024]{1,0:T(8,128)(2,1)S(1)}, bf16[256,1024]{1,0:T(8,128)(2,1)}, u32[]{:S(2)}) copy-start(bf16[256,1024]{1,0:T(8,128)(2,1)} %get-tuple-element.11) | copy-start | bytes 1572868
  69.7 16.4 %copy-start.4 = (bf16[256,1024]{1,0:T(8,128)(2,1)S(1)}, bf16[256,1024]{1,0:T(8,128)(2,1)}, u32[]{:S(2)}) copy-start(bf16[256,1024]{1,0:T(8,128)(2,1)} %get-tuple-element.12) | copy-start | bytes 1572868

commit v19 on v12

--- a/solution.py
+++ b/solution.py
@@ -21,7 +21,7 @@
     first = segs[:1, :1]
     final_from = jnp.sum((segs != last).astype(jnp.int32))
     rows_at = lax.broadcasted_iota(jnp.int32, (rows, 1), 0)
-    in_final = (rows_at >= final_from).astype(jnp.float32)
+    in_final = rows_at >= final_from
     seg_rows = jnp.where(
         lax.broadcasted_iota(jnp.int32, (8, HEAD), 0) == 0,
         jnp.broadcast_to(last.astype(jnp.float32), (8, HEAD)),
@@ -31,7 +31,7 @@
         cols = slice(h * HEAD, (h + 1) * HEAD)
         raw = key_ref[:, cols].astype(jnp.float32)
         feat = jnp.where(raw > 0, raw + 1.0, jnp.exp(jnp.minimum(raw, 0.0))).astype(jnp.bfloat16)
-        masked = (feat.astype(jnp.float32) * in_final).astype(jnp.bfloat16)
+        masked = jnp.where(in_final, feat, jnp.zeros_like(feat))
         sums = lax.dot_general(
             value_ref[:, cols], masked, (((0,), (0,)), ((), ())),
             preferred_element_type=jnp.float32,

time: 90 us -> 89.9 us (level)
  no operation moved by 1% of the time
where the time goes in v19:
time: 89.9 us; the launch traced here: 89.6 us
  waiting for transfers between devices  42.4 us (47%)
  starting transfers between devices  19.3 us (21%)
  matrix products  15.5 us (17%)
  other arithmetic  4.91 us (5%)
  local copies, waits for them, and re-layouts  3.85 us (4%)
  Pallas kernels  3.56 us (4%)
    ppermute x1, waiting for transfers between devices, project_gathered(): lax.ppermute(jnp.concatenate([second, left_first], axis=1), axis, ahead)  19.7 us
    ppermute x1, waiting for transfers between devices, project_gathered(): left_first = lax.ppermute(first, axis, ahead)  10.5 us
    all_to_all x1, starting transfers between devices, carried_in(): pieces = lax.all_to_all(sent, axis, 0, 0, tiled=True)  9.99 us
    all_to_all x1, waiting for transfers between devices, carried_in(): pieces = lax.all_to_all(sent, axis, 0, 0, tiled=True)  9.22 us
    dot_general x5, matrix products, dot(): return jnp.dot(block, weight, preferred_element_type=jnp.float32)  7.39 us
    dot_general x1, matrix products, per_device(): jnp.einsum('hts,she->the', weights, value_heads, preferred_element_type=j...  7 us
    pallas_call x1, Pallas kernels, scan_payload(): pl.pallas_call(_payload_kernel, out_shape=jax.ShapeDtypeStruct((count * 4...  3.56 us
    all_to_all x1, starting transfers between devices, carried_in(): return lax.all_to_all(carry, axis, 0, 0, tiled=True).reshape(shape)  3.43 us
  transfers between devices with their start and end apart: 6, of which 4 were waited for; matrix products, arithmetic and copies ran while one was open for 20% of the time, Pallas kernels for 0%

profile of v19, /device:TPU:1, one launch (start us, length us, event | category | flops | bytes accessed | tf_op | source)
XLA Modules:
  0.0 89.6 jit_solution(17233220718314540383)
XLA Ops:
  0.0 3.6 %shard_map.64 = f32[640,128]{1,0:T(8,128)} custom-call(bf16[1024,512]{1,0:T(8,128)(2,1)} %key_ref.1, bf16[1024,512]{1,0:T(8,128)(2,1)} %value_ref.1, s32[8,128]{1,0:T(8,128)} %bitcast.83), custom_call_target="tpu_custom_call" | custom-call | tf_op jit(solution)/shard_map/pallas_call | solution.py:48
  3.6 10.0 %all-to-all-start = ((f32[16,40,128]{2,1,0:T(8,128)}), f32[16,40,128]{2,1,0:T(8,128)S(1)}, u32[]{:S(2)}, u32[]{:S(2)}) async-start(f32[16,40,128]{2,1,0:T(8,128)} %bitcast.80), calls=%async_computation | async-start | bytes 655360 | tf_op jit(solution)/shard_map/all_to_all | solution.py:60
  13.6 1.3 %copy.25 = bf16[1024,512]{0,1:T(8,128)(2,1)} copy(bf16[1024,512]{1,0:T(8,128)(2,1)S(1)} %copy-done) | data formatting | bytes 2097152 | tf_op jit(solution)/shard_map/reshape | solution.py:102
  14.9 0.9 %fusion.3 = bf16[1024,512]{1,0:T(8,128)(2,1)S(1)} fusion(bf16[1024,512]{1,0:T(8,128)(2,1)S(1)} %copy-done.2), kind=kLoop, calls=%fused_computation.11 | loop fusion | flops 3145728 | bytes 2097152 | tf_op jit(solution)/shard_map/convert_element_type | solution.py:12
  15.8 1.6 %fusion = pred[1024,1024]{1,0:T(8,128)(4,1)} fusion(s32[1024]{0:T(1024)S(1)} %copy-done.3), kind=kLoop, calls=%fused_computation.8 | loop fusion | flops 3145728 | bytes 1052672 | tf_op jit(solution)/shard_map/and | solution.py:107
  17.4 9.2 %all-to-all-done = f32[16,40,128]{2,1,0:T(8,128)S(1)} async-done(((f32[16,40,128]{2,1,0:T(8,128)}), f32[16,40,128]{2,1,0:T(8,128)S(1)}, u32[]{:S(2)}, u32[]{:S(2)}) %all-to-all-start) | async-done | bytes 327712 | tf_op jit(solution)/shard_map/all_to_all | solution.py:60
  26.9 1.2 %select_reduce_fusion = f32[16,32,128]{2,1,0:T(8,128)} fusion(f32[16,32,128]{2,1,0:T(8,128)S(1)} %slice.26, pred[16,16]{1,0:T(8,128)(4,1)S(1)} %fusion.42), kind=kLoop, calls=%fused_computation.6 | loop fusion | flops 2031616 | bytes 524544 | tf_op jit(solution)/shard_map/reduce_sum | solution.py:66
  28.2 3.4 %all-to-all-start.1 = ((f32[16,32,128]{2,1,0:T(8,128)}), f32[16,32,128]{2,1,0:T(8,128)S(1)}, u32[]{:S(2)}, u32[]{:S(2)}) async-start(f32[16,32,128]{2,1,0:T(8,128)} %select_reduce_fusion), calls=%async_computation.1 | async-start | bytes 524288 | tf_op jit(solution)/shard_map/all_to_all | solution.py:67
  31.6 7.0 %fusion.7 = f32[4,1024,128]{1,2,0:T(8,128)S(1)} fusion(bf16[1024,4,128]{0,2,1:T(8,128)(2,1)} %bitcast.81, pred[1024,1024]{1,0:T(8,128)(4,1)} %fusion, bf16[1024,512]{1,0:T(8,128)(2,1)S(1)} %fusion.3, bf16[1024,512]{1,0:T(8,128)(2,1)} %key_ref.1), kind=kOutput, calls=%fused_computation.18 | convolution fusion | flops 2159017984 | bytes 6291456 | tf_op jit(solution)/shard_map/hts,she->the/dot_general | solution.py:112
  38.6 0.5 slice.18
  39.1 0.6 compare_convert_fusion
  39.8 3.0 %all-to-all-done.1 = f32[16,32,128]{2,1,0:T(8,128)S(1)} async-done(((f32[16,32,128]{2,1,0:T(8,128)}), f32[16,32,128]{2,1,0:T(8,128)S(1)}, u32[]{:S(2)}, u32[]{:S(2)}) %all-to-all-start.1) | async-done | bytes 262176 | tf_op jit(solution)/shard_map/all_to_all | solution.py:67
  43.2 0.6 multiply_reduce_fusion
  44.3 1.4 %collective-permute-start = (bf16[1024,256]{0,1:T(8,128)(2,1)S(1)}, bf16[1024,256]{0,1:T(8,128)(2,1)S(1)}, u32[]{:S(2)}, u32[]{:S(2)}) collective-permute-start(bf16[1024,256]{0,1:T(8,128)(2,1)S(1)} %get-tuple-element.14), channel_id=1, source_target_pairs={{0,1},{1,2},{2,3},{3,0},{4,5},{5,6},{6,7},{7,4},{8,9},{9,10},{10,1... | collective-permute-start | bytes 1572872 | tf_op jit(solution)/shard_map/ppermute | solution.py:85
  45.6 1.5 %collective-permute-start.1 = (bf16[1024,256]{0,1:T(8,128)(2,1)S(1)}, bf16[1024,256]{0,1:T(8,128)(2,1)S(1)}, u32[]{:S(2)}, u32[]{:S(2)}) collective-permute-start(bf16[1024,256]{0,1:T(8,128)(2,1)S(1)} %get-tuple-element.13), channel_id=1, source_target_pairs={{0,3},{1,0},{2,1},{3,2},{4,7},{5,4},{6,5},{7,6},{8,11},{9,8},{10,9... | collective-permute-start | bytes 1572872 | tf_op jit(solution)/shard_map/ppermute | solution.py:86
  47.2 1.7 %dynamic-slice_bitcast_fusion.1 = (bf16[256,1024]{1,0:T(8,128)(2,1)S(1)}, bf16[256,1024]{1,0:T(8,128)(2,1)S(1)}, bf16[256,1024]{1,0:T(8,128)(2,1)S(1)}, bf16[256,1024]{1,0:T(8,128)(2,1)S(1)}) fusion(bf16[4,2,256,1024]{3,2,1,0:T(8,128)(2,1)} %bitcast.76, s32[]{:T(128)S(6)} %select_n.47, s32[]{:T(128)S(6)} %select_n.48, s32[]{:T(128)S(6)} %select_n.46), kind=kLoop, calls=%fused_computation.47 | loop fusion | bytes 4194316 | tf_op jit(solution)/shard_map/squeeze | solution.py:79
  48.9 10.5 %collective-permute-done = bf16[1024,256]{0,1:T(8,128)(2,1)S(1)} collective-permute-done((bf16[1024,256]{0,1:T(8,128)(2,1)S(1)}, bf16[1024,256]{0,1:T(8,128)(2,1)S(1)}, u32[]{:S(2)}, u32[]{:S(2)}) %collective-permute-start) | collective-permute-done | bytes 524320 | tf_op jit(solution)/shard_map/ppermute | solution.py:85
  59.8 2.7 %collective-permute-start.3 = (bf16[1024,512]{0,1:T(8,128)(2,1)S(1)}, bf16[1024,512]{0,1:T(8,128)(2,1)S(1)}, u32[]{:S(2)}, u32[]{:S(2)}) collective-permute-start(bf16[1024,512]{0,1:T(8,128)(2,1)S(1)} %pad_maximum_fusion.1), channel_id=1, source_target_pairs={{0,3},{1,0},{2,1},{3,2},{4,7},{5,4},{6,5},{7,6},{8,11},{9,8},{10,9... | collective-permute-start | bytes 3145736 | tf_op jit(solution)/shard_map/ppermute | solution.py:88
  62.5 1.3 %fusion.28 = f32[1024,1024]{1,0:T(8,128)S(1)} fusion(bf16[1024,512]{0,1:T(8,128)(2,1)S(1)} %bitcast.75, bf16[4,512,1024]{2,1,0:T(8,128)(2,1)S(1)} %bitcast.77, s32[]{:T(128)S(6)} %select_n.45), kind=kOutput, calls=%fused_computation.36 | convolution fusion | flops 1073741824 | bytes 6291460 | tf_op jit(solution)/shard_map/dot_general | solution.py:82
  63.8 0.7 fusion.35
  64.5 0.7 fusion.37
  65.3 19.7 %collective-permute-done.2 = bf16[1024,512]{0,1:T(8,128)(2,1)S(1)} collective-permute-done((bf16[1024,512]{0,1:T(8,128)(2,1)S(1)}, bf16[1024,512]{0,1:T(8,128)(2,1)S(1)}, u32[]{:S(2)}, u32[]{:S(2)}) %collective-permute-start.2) | collective-permute-done | bytes 1048608 | tf_op jit(solution)/shard_map/ppermute | solution.py:87
  85.0 1.3 %fusion.18 = f32[1024,1024]{1,0:T(8,128)S(1)} fusion(bf16[1024,512]{0,1:T(8,128)(2,1)S(1)} %collective-permute-done.2, bf16[256,1024]{1,0:T(8,128)(2,1)S(1)} %get-tuple-element.11, bf16[256,1024]{1,0:T(8,128)(2,1)S(1)} %get-tuple-element.12), kind=kOutput, calls=%fused_computation.27 | convolution fusion | flops 1075838976 | bytes 6291456 | tf_op jit(solution)/shard_map/dot_general | solution.py:82
  86.3 3.3 %add_convert_fusion = bf16[1024,1024]{1,0:T(8,128)(2,1)} fusion(f32[1024,1024]{1,0:T(8,128)S(1)} %fusion.18, f32[1024,1024]{1,0:T(8,128)S(1)} %fusion.35, f32[1024,1024]{1,0:T(8,128)S(1)} %fusion.28, f32[1024,1024]{1,0:T(8,128)S(1)} %fusion.37, bf16[1024,512]{0,1:T(8,128)(2,1)S(1)} %collective-permute-done.3, bf16[256,1024]{1,0:T(8,128)(2,1)S(1)} %get-tuple-element.10, ...), kind=kOutput, calls=%fused_computation.5 | convolution fusion | flops 1081081856 | bytes 20971520 | tf_op jit(solution)/shard_map/dot_general | solution.py:82
  (23 shorter events, 1.6 us)
Async XLA Ops:
  0.0 13.6 %copy-start = (bf16[1024,512]{1,0:T(8,128)(2,1)S(1)}, bf16[1024,512]{1,0:T(8,128)(2,1)}, u32[]{:S(2)}) copy-start(bf16[1024,512]{1,0:T(8,128)(2,1)} %value_ref.1) | copy-start | bytes 3145732
  0.0 14.9 %copy-start.2 = (bf16[1024,512]{1,0:T(8,128)(2,1)S(1)}, bf16[1024,512]{1,0:T(8,128)(2,1)}, u32[]{:S(2)}) copy-start(bf16[1024,512]{1,0:T(8,128)(2,1)} %param.6) | copy-start | bytes 3145732
  3.6 23.1 %all-to-all-start = ((f32[16,40,128]{2,1,0:T(8,128)}), f32[16,40,128]{2,1,0:T(8,128)S(1)}, u32[]{:S(2)}, u32[]{:S(2)}) async-start(f32[16,40,128]{2,1,0:T(8,128)} %bitcast.80), calls=%async_computation | async-start | bytes 655360 | tf_op jit(solution)/shard_map/all_to_all | solution.py:60
  13.6 2.3 %copy-start.3 = (s32[1024]{0:T(1024)S(1)}, s32[1024]{0:T(1024)}, u32[]{:S(2)}) copy-start(s32[1024]{0:T(1024)} %param.9) | copy-start | bytes 12292
  28.2 14.6 %all-to-all-start.1 = ((f32[16,32,128]{2,1,0:T(8,128)}), f32[16,32,128]{2,1,0:T(8,128)S(1)}, u32[]{:S(2)}, u32[]{:S(2)}) async-start(f32[16,32,128]{2,1,0:T(8,128)} %select_reduce_fusion), calls=%async_computation.1 | async-start | bytes 524288 | tf_op jit(solution)/shard_map/all_to_all | solution.py:67
  43.2 0.7 copy-start.4
  44.3 15.1 %collective-permute-start = (bf16[1024,256]{0,1:T(8,128)(2,1)S(1)}, bf16[1024,256]{0,1:T(8,128)(2,1)S(1)}, u32[]{:S(2)}, u32[]{:S(2)}) collective-permute-start(bf16[1024,256]{0,1:T(8,128)(2,1)S(1)} %get-tuple-element.14), channel_id=1, source_target_pairs={{0,1},{1,2},{2,3},{3,0},{4,5},{5,6},{6,7},{7,4},{8,9},{9,10},{10,1... | collective-permute-start | bytes 1572872 | tf_op jit(solution)/shard_map/ppermute | solution.py:85
  45.6 14.1 %collective-permute-start.1 = (bf16[1024,256]{0,1:T(8,128)(2,1)S(1)}, bf16[1024,256]{0,1:T(8,128)(2,1)S(1)}, u32[]{:S(2)}, u32[]{:S(2)}) collective-permute-start(bf16[1024,256]{0,1:T(8,128)(2,1)S(1)} %get-tuple-element.13), channel_id=1, source_target_pairs={{0,3},{1,0},{2,1},{3,2},{4,7},{5,4},{6,5},{7,6},{8,11},{9,8},{10,9... | collective-permute-start | bytes 1572872 | tf_op jit(solution)/shard_map/ppermute | solution.py:86
  48.9 13.6 %copy-start.1 = (bf16[2048,1024]{1,0:T(8,128)(2,1)S(1)}, bf16[2048,1024]{1,0:T(8,128)(2,1)}, u32[]{:S(2)}) copy-start(bf16[2048,1024]{1,0:T(8,128)(2,1)} %param.11) | copy-start | bytes 12582916
  59.4 25.6 %collective-permute-start.2 = (bf16[1024,512]{0,1:T(8,128)(2,1)S(1)}, bf16[1024,512]{0,1:T(8,128)(2,1)S(1)}, u32[]{:S(2)}, u32[]{:S(2)}) collective-permute-start(bf16[1024,512]{0,1:T(8,128)(2,1)S(1)} %pad_maximum_fusion), channel_id=1, source_target_pairs={{0,1},{1,2},{2,3},{3,0},{4,5},{5,6},{6,7},{7,4},{8,9},{9,10},{10,1... | collective-permute-start | bytes 3145736 | tf_op jit(solution)/shard_map/ppermute | solution.py:87
  59.8 26.5 %collective-permute-start.3 = (bf16[1024,512]{0,1:T(8,128)(2,1)S(1)}, bf16[1024,512]{0,1:T(8,128)(2,1)S(1)}, u32[]{:S(2)}, u32[]{:S(2)}) collective-permute-start(bf16[1024,512]{0,1:T(8,128)(2,1)S(1)} %pad_maximum_fusion.1), channel_id=1, source_target_pairs={{0,3},{1,0},{2,1},{3,2},{4,7},{5,4},{6,5},{7,6},{8,11},{9,8},{10,9... | collective-permute-start | bytes 3145736 | tf_op jit(solution)/shard_map/ppermute | solution.py:88
